TPU v7x, 256 devices: a whole 4x4x8 slice. The times are simulated.
256 devices in a mesh: users: 64 (over y_lo, x, z), panel: 4 (over y_hi, core).
Axes of the slice: x: 4, y: 4 (y_hi: 2, y_lo: 2; y = y_hi * 2 + y_lo), z: 8, core: 2. Of those that a mesh axis runs over, the one named last changes fastest.
Arguments:
- user_emb0: float32 [65536, 128], P('users'), may hold values from -6 to 6
- item_base: float32 [4, 8192, 128], P('panel'), may hold values from -6 to 6
- weight_tiles: bfloat16 [64, 128, 128], replicated, may hold values from -0.02734375 to 0.02734375
- blk_user: int32 [64, 4, 384], P('users', 'panel'), may hold values from 0 to 7
- blk_item: int32 [64, 4, 384], P('users', 'panel'), may hold values from 0 to 63
- blk_weight: int32 [64, 4, 384], P('users', 'panel'), may hold values from 0 to 63
Outputs:
- user_out: float32 [65536, 128], P('users')
- item_emb: float32 [4, 8192, 128], P('panel', 'users')
All inputs are finite; a program needn't handle non-finite values.
Results may differ from a plain program's by a relative error of at most 0.0036.
Values may be sent and summed in bfloat16 or wider, within the bound.
No kernel may reach another device: no remote copies, remote signals or barrier semaphores. Data moves between devices by JAX's collectives and lax.ppermute only.
A program may use at most 128 MiB of HBM per device.

v0:
```python
import jax
import jax.numpy as jnp
from jax import lax
from jax.sharding import PartitionSpec as P

teleport = 0.2


def item_terms(user_tiles, users, items, weights, weight_tiles, n_items):
    group_size = min(users.shape[0], 128)
    pieces = (
        users.reshape(-1, group_size),
        items.reshape(-1, group_size),
        weights.reshape(-1, group_size),
    )

    def item_add_group(totals, lists):
        tiles = weight_tiles[lists[2]]
        rows = user_tiles[lists[0]]
        products = jnp.einsum("gab,gae->gbe", tiles, rows, preferred_element_type=jnp.float32)
        return (totals + jax.ops.segment_sum(products, lists[1], num_segments=n_items), None)

    start = jnp.zeros((n_items, user_tiles.shape[1], user_tiles.shape[2]), jnp.float32)
    totals, unused = lax.scan(item_add_group, start, pieces)
    return totals


def user_terms(item_tiles, users, items, weights, weight_tiles, n_tiles):
    group_size = min(users.shape[0], 128)
    pieces = (
        users.reshape(-1, group_size),
        items.reshape(-1, group_size),
        weights.reshape(-1, group_size),
    )

    def user_add_group(totals, lists):
        tiles = weight_tiles[lists[2]]
        rows = item_tiles[lists[1]]
        products = jnp.einsum("gab,gbe->gae", tiles, rows, preferred_element_type=jnp.float32)
        return (totals + jax.ops.segment_sum(products, lists[0], num_segments=n_tiles), None)

    start = jnp.zeros((n_tiles, item_tiles.shape[1], item_tiles.shape[2]), jnp.float32)
    totals, unused = lax.scan(user_add_group, start, pieces)
    return totals


def per_device(user_emb0, item_base, weight_tiles, blk_user, blk_item, blk_weight):
    tile_rows = weight_tiles.shape[1]
    width = user_emb0.shape[1]
    n_users = lax.axis_size("users")
    user_tiles = user_emb0.astype(jnp.bfloat16).reshape(-1, tile_rows, width)
    n_user_tiles = user_tiles.shape[0]
    user_list = blk_user.reshape(-1)
    item_list = blk_item.reshape(-1)
    weight_list = blk_weight.reshape(-1)
    partial_value = item_terms(user_tiles, user_list, item_list, weight_list, weight_tiles, n_users)
    partial_flat = partial_value.reshape(n_users * tile_rows, width)
    panel_base = item_base[0]
    position = lax.axis_index("users")
    totals = lax.psum(partial_flat, "users")
    panel_emb = (1.0 - teleport) * totals + teleport * panel_base
    own_emb = lax.dynamic_slice_in_dim(panel_emb, position * tile_rows, tile_rows, 0)
    panel_bf = panel_emb.astype(jnp.bfloat16)
    item_tiles = panel_bf.reshape(n_users, tile_rows, width)
    user_part = user_terms(
        item_tiles, user_list, item_list, weight_list, weight_tiles, n_user_tiles
    )
    user_sum = lax.psum(user_part, "panel")
    user_out = (1.0 - teleport) * user_sum.reshape(-1, width) + teleport * user_emb0
    return (user_out, own_emb[None])


def solution(mesh):
    placed = (
        P("users", None),
        P("panel", None, None),
        P(),
        P("users", "panel", None),
        P("users", "panel", None),
        P("users", "panel", None),
    )
    return jax.shard_map(
        per_device,
        mesh=mesh,
        in_specs=placed,
        out_specs=(P("users", None), P("panel", "users", None)),
        check_vma=False,
    )
```

profile of v0, /device:TPU:1, one launch (start us, length us, event | category | flops | bytes accessed | tf_op | source)
XLA Modules:
  0.0 918.8 jit_solution(14164029038932604751)
XLA Ops:
  10.5 2.4 broadcast.84
  13.0 120.8 %while.20 = (s32[]{:T(128)}, f32[64,128,128]{2,1,0:T(8,128)}, s32[3,128]{1,0:T(4,128)S(1)}, s32[3,128]{1,0:T(4,128)S(1)}, bf16[64,128,128]{2,1,0:T(8,128)(2,1)S(...) while((s32[]{:T(128)}, f32[64,128,128]{2,1,0:T(8,128)}, ...), condition=%wide.region_2.3_spmd, body=%wide.region_0.2_spmd.sunk | while | flops 538970880 | bytes 58734172 | solution.py:24
  13.0 3.1 gather_fusion
  16.1 3.0 gather_fusion.1
  19.1 8.2 fusion.31
  27.3 25.9 %scatter_fusion = f32[64,128,128]{2,1,0:T(8,128)} fusion(f32[64,128,128]{2,1,0:T(8,128)} %get-tuple-element.215, s32[128]{0:T(128)S(1)} %fusion.29, f32[128,128,128]{2,1,0:T(8,128)} %fusion.31), kind=kCustom, calls=%fused_computation.4.clone.1 | custom fusion | flops 2097152 | bytes 25166336 | tf_op jit(solution)/shard_map/while/body/eval_jaxpr/scatter-add | solution.py:21
  53.2 3.1 gather_fusion
  56.3 3.0 gather_fusion.1
  59.4 8.2 fusion.31
  67.6 25.7 %scatter_fusion = f32[64,128,128]{2,1,0:T(8,128)} fusion(f32[64,128,128]{2,1,0:T(8,128)} %get-tuple-element.215, s32[128]{0:T(128)S(1)} %fusion.29, f32[128,128,128]{2,1,0:T(8,128)} %fusion.31), kind=kCustom, calls=%fused_computation.4.clone.1 | custom fusion | flops 2097152 | bytes 25166336 | tf_op jit(solution)/shard_map/while/body/eval_jaxpr/scatter-add | solution.py:21
  93.3 3.1 gather_fusion
  96.4 3.0 gather_fusion.1
  99.5 8.2 fusion.31
  107.7 26.0 %scatter_fusion = f32[64,128,128]{2,1,0:T(8,128)} fusion(f32[64,128,128]{2,1,0:T(8,128)} %get-tuple-element.215, s32[128]{0:T(128)S(1)} %fusion.29, f32[128,128,128]{2,1,0:T(8,128)} %fusion.31), kind=kCustom, calls=%fused_computation.4.clone.1 | custom fusion | flops 2097152 | bytes 25166336 | tf_op jit(solution)/shard_map/while/body/eval_jaxpr/scatter-add | solution.py:21
  133.8 577.4 %all-reduce.3.cloned.1.call-done = f32[8192,128]{1,0:T(8,128)} async-done(((f32[8192,128]{1,0:T(8,128)}), f32[8192,128]{1,0:T(8,128)}) %all-reduce.3.cloned.1.call-update) | async-done | bytes 4194320 | tf_op jit(solution)/shard_map/psum | solution.py:60
  711.2 7.0 fusion.10
  718.2 98.0 %while.21 = (s32[]{:T(128)}, f32[8,128,128]{2,1,0:T(8,128)S(1)}, s32[3,128]{1,0:T(4,128)S(1)}, s32[3,128]{1,0:T(4,128)S(1)}, bf16[64,128,128]{2,1,0:T(8,128)(2,1...) while((s32[]{:T(128)}, f32[8,128,128]{2,1,0:T(8,128)S(1)}, ...), condition=%wide.region_6.7_spmd, body=%wide.region_4.6_spmd.sunk | while | flops 538970880 | bytes 58734172 | solution.py:43
  718.3 3.0 gather_fusion.2
  721.3 4.6 gather_fusion.3
  725.9 7.9 fusion.36
  733.9 17.0 %scatter_fusion.1 = f32[8,128,128]{2,1,0:T(8,128)S(1)} fusion(f32[8,128,128]{2,1,0:T(8,128)S(1)} %get-tuple-element.239, s32[128]{0:T(128)S(1)} %fusion.34, f32[128,128,128]{2,1,0:T(8,128)} %fusion.36), kind=kCustom, calls=%fused_computation.5.clone.1 | custom fusion | flops 2097152 | bytes 25166336 | tf_op jit(solution)/shard_map/while/body/eval_jaxpr/scatter-add | solution.py:40
  750.9 3.0 gather_fusion.2
  754.0 4.6 gather_fusion.3
  758.6 7.9 fusion.36
  766.5 17.0 %scatter_fusion.1 = f32[8,128,128]{2,1,0:T(8,128)S(1)} fusion(f32[8,128,128]{2,1,0:T(8,128)S(1)} %get-tuple-element.239, s32[128]{0:T(128)S(1)} %fusion.34, f32[128,128,128]{2,1,0:T(8,128)} %fusion.36), kind=kCustom, calls=%fused_computation.5.clone.1 | custom fusion | flops 2097152 | bytes 25166336 | tf_op jit(solution)/shard_map/while/body/eval_jaxpr/scatter-add | solution.py:40
  783.6 3.0 gather_fusion.2
  786.6 4.6 gather_fusion.3
  791.2 7.9 fusion.36
  799.2 17.0 %scatter_fusion.1 = f32[8,128,128]{2,1,0:T(8,128)S(1)} fusion(f32[8,128,128]{2,1,0:T(8,128)S(1)} %get-tuple-element.239, s32[128]{0:T(128)S(1)} %fusion.34, f32[128,128,128]{2,1,0:T(8,128)} %fusion.36), kind=kCustom, calls=%fused_computation.5.clone.1 | custom fusion | flops 2097152 | bytes 25166336 | tf_op jit(solution)/shard_map/while/body/eval_jaxpr/scatter-add | solution.py:40
  817.0 1.5 dynamic-slice_bitcast_fusion
  818.5 91.5 %all-reduce.5.cloned.1.call-done = f32[8,128,128]{2,1,0:T(8,128)} async-done(((f32[8,128,128]{2,1,0:T(8,128)}), f32[8,128,128]{2,1,0:T(8,128)}) %all-reduce.5.cloned.1.call-update) | async-done | bytes 524304 | tf_op jit(solution)/shard_map/psum | solution.py:68
  910.0 1.1 broadcast_multiply_fusion
  (40 shorter events, 5.3 us)
Async XLA Ops:
  7.2 5.8 copy-start.1
  7.2 704.0 %all-reduce.3.cloned.1.call-start = ((), (), s32[]{:S(2)}) async-start(), calls=%async_computation | async-start | bytes 8388608 | tf_op jit(solution)/shard_map/psum | solution.py:60
  133.8 776.2 %all-reduce.5.cloned.1.call-start = ((), (), s32[]{:S(2)}) async-start(), calls=%async_computation.1 | async-start | bytes 1048576 | tf_op jit(solution)/shard_map/psum | solution.py:68
  718.2 192.9 %copy-start.2 = (f32[1024,128]{1,0:T(8,128)S(1)}, f32[1024,128]{1,0:T(8,128)}, u32[]{:S(2)}) copy-start(f32[1024,128]{1,0:T(8,128)} %param.10) | copy-start | bytes 1572868
  816.2 0.8 copy-start
Sparse Core Ops, SparseCore 0:
  133.9 577.2 all-reduce.2
  817.2 92.7 all-reduce.4
where the time goes:
time: 921 us; the launch traced here: 919 us
  waiting for transfers between devices  669 us (73%)
  other arithmetic  141 us (15%)
  matrix products  48.5 us (5%)
  local copies, waits for them, and re-layouts  46 us (5%)
  between operations  14.1 us (2%)
    psum x1, waiting for transfers between devices, per_device(): totals = lax.psum(partial_flat, 'users')  577 us
    psum x1, waiting for transfers between devices, per_device(): user_sum = lax.psum(user_part, 'panel')  91.5 us
    scatter-add x3, other arithmetic, item_add_group(): jax.ops.segment_sum(products, lists[1], num_segments=n_items)  77.7 us
    scatter-add x3, other arithmetic, user_add_group(): jax.ops.segment_sum(products, lists[0], num_segments=n_tiles)  51.1 us
    dot_general x3, matrix products, item_add_group(): jnp.einsum('gab,gae->gbe', tiles, rows, preferred_element_type=jnp.float32)  24.7 us
    dot_general x3, matrix products, user_add_group(): jnp.einsum('gab,gbe->gae', tiles, rows, preferred_element_type=jnp.float32)  23.8 us
  transfers between devices with their start and end apart: 2, of which 2 were waited for; matrix products, arithmetic and copies ran while one was open for 0% of the time, Pallas kernels for 0%

commit v1 on v0

v1 whole, which is shorter than its diff:
```python
import jax
import jax.numpy as jnp
from jax import lax
from jax.experimental import pallas as pl
from jax.experimental.pallas import tpu as pltpu
from jax.sharding import Mesh
from jax.sharding import PartitionSpec as P

teleport = 0.2

USER_AXES = ("ylo", "x", "z")
PANEL_AXES = ("yhi", "core")


def block_sum_kernel(a_index_ref, b_index_ref, out_index_ref, a_ref, b_ref, o_ref):
    o_ref[...] = jnp.zeros(o_ref.shape, o_ref.dtype)
    n_blocks = a_index_ref.shape[0]

    def body(k, carry):
        a = a_ref[a_index_ref[k]]
        b = b_ref[b_index_ref[k]]
        o_ref[out_index_ref[k]] += jnp.dot(a, b, preferred_element_type=jnp.float32)
        return carry

    lax.fori_loop(0, n_blocks, body, 0)


def block_sums(lists, a_tiles, b_tiles, n_out):
    tile = a_tiles.shape[1]
    width = b_tiles.shape[2]
    return pl.pallas_call(
        block_sum_kernel,
        grid_spec=pltpu.PrefetchScalarGridSpec(
            num_scalar_prefetch=3,
            grid=(1,),
            in_specs=[
                pl.BlockSpec(a_tiles.shape, lambda i, *_: (0, 0, 0)),
                pl.BlockSpec(b_tiles.shape, lambda i, *_: (0, 0, 0)),
            ],
            out_specs=pl.BlockSpec((n_out, tile, width), lambda i, *_: (0, 0, 0)),
        ),
        out_shape=jax.ShapeDtypeStruct((n_out, tile, width), jnp.float32),
    )(lists[0], lists[1], lists[2], a_tiles, b_tiles)


def ring_reduce_scatter(x, axis, n):
    i = lax.axis_index(axis)
    h = x.shape[1] // 2
    xl, xr = x[:, :h], x[:, h:]
    right = [(j, (j + 1) % n) for j in range(n)]
    left = [(j, (j - 1) % n) for j in range(n)]
    bl = lax.dynamic_index_in_dim(xl, (i - 1) % n, 0, keepdims=False)
    br = lax.dynamic_index_in_dim(xr, (i + 1) % n, 0, keepdims=False)
    for s in range(n - 1):
        rl = lax.ppermute(bl, axis, right)
        rr = lax.ppermute(br, axis, left)
        bl = rl + lax.dynamic_index_in_dim(xl, (i - s - 2) % n, 0, keepdims=False)
        br = rr + lax.dynamic_index_in_dim(xr, (i + s + 2) % n, 0, keepdims=False)
    return jnp.concatenate([bl, br], 0)


def ring_all_gather(x, axis, n):
    i = lax.axis_index(axis)
    h = x.shape[0] // 2
    right = [(j, (j + 1) % n) for j in range(n)]
    left = [(j, (j - 1) % n) for j in range(n)]
    out = jnp.zeros((n,) + x.shape, x.dtype)
    out = lax.dynamic_update_index_in_dim(out, x, i, 0)
    bl, br = x[:h], x[h:]
    zeros = (0,) * (x.ndim - 1)
    for s in range(n - 1):
        bl = lax.ppermute(bl, axis, right)
        br = lax.ppermute(br, axis, left)
        out = lax.dynamic_update_slice(out, bl[None], ((i - s - 1) % n, 0) + zeros)
        out = lax.dynamic_update_slice(out, br[None], ((i + s + 1) % n, h) + zeros)
    return out


def per_device(user_emb0, item_base, weight_tiles, blk_user, blk_item, blk_weight, *, sizes):
    n_ylo, n_x, n_z, n_yhi, n_core = sizes
    n_users = n_ylo * n_x * n_z
    tile_rows = weight_tiles.shape[1]
    width = user_emb0.shape[1]
    user_tiles = user_emb0.astype(jnp.bfloat16).reshape(-1, tile_rows, width)
    n_user_tiles = user_tiles.shape[0]
    lists = (blk_user.reshape(-1), blk_item.reshape(-1), blk_weight.reshape(-1))
    weights_t = jnp.swapaxes(weight_tiles, 1, 2)

    partial = block_sums(
        (lists[2], lists[0], lists[1]), weights_t, user_tiles, n_users
    )
    x = partial.reshape(n_ylo, n_x, n_z, tile_rows, width)
    x = x.transpose(2, 1, 0, 3, 4).reshape(n_z, n_x * n_ylo * tile_rows, width)
    x = ring_reduce_scatter(x, "z", n_z)
    x = ring_reduce_scatter(x.reshape(n_x, n_ylo * tile_rows, width), "x", n_x)
    own_sum = ring_reduce_scatter(x.reshape(n_ylo, tile_rows, width), "ylo", n_ylo)

    position = lax.axis_index(USER_AXES)
    own_base = lax.dynamic_slice_in_dim(item_base[0], position * tile_rows, tile_rows, 0)
    own_emb = (1.0 - teleport) * own_sum + teleport * own_base
    own_bf = own_emb.astype(jnp.bfloat16)
    spread = jnp.broadcast_to(own_bf[None], (n_users, tile_rows, width))
    item_tiles = lax.all_to_all(spread, USER_AXES, 0, 0, tiled=True)

    user_part = block_sums(
        (lists[2], lists[1], lists[0]), weight_tiles, item_tiles, n_user_tiles
    )
    y = user_part.reshape(n_core, -1, width)
    y = ring_reduce_scatter(y, "core", n_core)
    y = ring_reduce_scatter(y.reshape(n_yhi, -1, width), "yhi", n_yhi)
    y = ring_all_gather(y, "yhi", n_yhi).reshape(-1, width)
    y = ring_all_gather(y, "core", n_core).reshape(-1, width)
    user_out = (1.0 - teleport) * y + teleport * user_emb0
    return (user_out, own_emb[None])


def solution(mesh):
    import functools

    sizes = (2, 4, 8, 2, 2)
    fine = Mesh(mesh.devices.reshape(sizes), USER_AXES + PANEL_AXES)
    placed = (
        P(USER_AXES, None),
        P(PANEL_AXES, None, None),
        P(),
        P(USER_AXES, PANEL_AXES, None),
        P(USER_AXES, PANEL_AXES, None),
        P(USER_AXES, PANEL_AXES, None),
    )
    return jax.shard_map(
        functools.partial(per_device, sizes=sizes),
        mesh=fine,
        in_specs=placed,
        out_specs=(P(USER_AXES, None), P(PANEL_AXES, USER_AXES, None)),
        check_vma=False,
    )
```

time: 921 us -> 298 us (0.32)
  waiting for transfers between devices: 669 us -> 77 us
  other arithmetic: 141 us -> 20.9 us
  Pallas kernels: 0 us -> 114 us
  starting transfers between devices: 0.08 us -> 70.5 us
  matrix products: 48.5 us -> 0 us
  local copies, waits for them, and re-layouts: 46 us -> 13.8 us
  between operations: 14.1 us -> 1.09 us
    psum x2 -> x0, waiting for transfers between devices: 669 us -> none  [the longest x1 577 us: per_device(): totals = lax.psum(partial_flat, 'users')]
    scatter-add x6 -> x0, other arithmetic: 129 us -> none  [the longest x3 77.7 us: item_add_group(): jax.ops.segment_sum(products, lists[1], num_segments=n_items)]
    pallas_call x0 -> x2, Pallas kernels: none -> 114 us  [block_sums(): pl.pallas_call(block_sum_kernel, grid_spec=pltpu.PrefetchScalarGridSpec(n...]
    ppermute x0 -> x30, starting transfers between devices: none -> 60.6 us  [the longest x13 28.1 us: ring_reduce_scatter(): rr = lax.ppermute(br, axis, left)]
    dot_general x6 -> x0, matrix products: 48.5 us -> none  [the longest x3 24.7 us: item_add_group(): jnp.einsum('gab,gae->gbe', tiles, rows, preferred_element_type=jnp.float32)]
    gather x12 -> x0, local copies, waits for them, and re-layouts: 41.2 us -> none  [the longest x3 13.8 us: user_add_group(): rows = item_tiles[lists[1]]]
    ppermute x0 -> x30, waiting for transfers between devices: none -> 40.8 us  [the longest x13 34.3 us: ring_reduce_scatter(): rl = lax.ppermute(bl, axis, right)]
    all_to_all x0 -> x1, waiting for transfers between devices: none -> 36.2 us  [per_device(): item_tiles = lax.all_to_all(spread, USER_AXES, 0, 0, tiled=True)]
  transfers between devices with their start and end apart: 2 -> 31, of which waited for: 2 -> 20; matrix products, arithmetic and copies ran while one was open for 0% -> 4% of each run, Pallas kernels for 0% -> 0%
where the time goes in v1:
time: 298 us; the launch traced here: 297 us
  Pallas kernels  114 us (38%)
  waiting for transfers between devices  77 us (26%)
  starting transfers between devices  70.5 us (24%)
  other arithmetic  20.9 us (7%)
  local copies, waits for them, and re-layouts  13.8 us (5%)
    pallas_call x2, Pallas kernels, block_sums(): pl.pallas_call(block_sum_kernel, grid_spec=pltpu.PrefetchScalarGridSpec(n...  114 us
    all_to_all x1, waiting for transfers between devices, per_device(): item_tiles = lax.all_to_all(spread, USER_AXES, 0, 0, tiled=True)  36.2 us
    ppermute x13, waiting for transfers between devices, ring_reduce_scatter(): rl = lax.ppermute(bl, axis, right)  34.3 us
    ppermute x13, starting transfers between devices, ring_reduce_scatter(): rr = lax.ppermute(br, axis, left)  28.1 us
    ppermute x13, starting transfers between devices, ring_reduce_scatter(): rl = lax.ppermute(bl, axis, right)  25.1 us
    all_to_all x1, starting transfers between devices, per_device(): item_tiles = lax.all_to_all(spread, USER_AXES, 0, 0, tiled=True)  9.89 us
    add x12, other arithmetic, ring_reduce_scatter(): bl = rl + lax.dynamic_index_in_dim(xl, (i - s - 2) % n, 0, keepdims=False)  7.14 us
    add x12, other arithmetic, ring_reduce_scatter(): br = rr + lax.dynamic_index_in_dim(xr, (i + s + 2) % n, 0, keepdims=False)  6.7 us
  transfers between devices with their start and end apart: 31, of which 20 were waited for; matrix products, arithmetic and copies ran while one was open for 4% of the time, Pallas kernels for 0%

profile of v1, /device:TPU:1, one launch (start us, length us, event | category | flops | bytes accessed | tf_op | source)
XLA Modules:
  0.0 297.5 jit_solution(16261124238965531734)
XLA Ops:
  4.5 4.1 %copy.9 = bf16[64,128,128]{1,2,0:T(8,128)(2,1)} copy(bf16[64,128,128]{2,1,0:T(8,128)(2,1)} %a_ref.1) | data formatting | bytes 4194304 | tf_op args[2]
  9.4 57.5 %shard_map.77 = f32[64,128,128]{2,1,0:T(8,128)} custom-call(s32[384]{0:T(512)} %reduce.a_index_ref, s32[384]{0:T(512)} %reduce.2.b_index_ref.out_index_ref, s32[384]{0:T(512)} %reduce.1.out_index_ref.b_index_ref, bf16[64,128,128]{2,1,0:T(8,128)(2,1)} %bitcast.115, bf16[8,128,128]{2,1,0:T(8,128)(2,1)} %bitcast.120), custom_call_target="tpu_custom_call" | custom-call | tf_op jit(solution)/shard_map/pallas_call | solution.py:31
  66.9 2.5 copy.10
  69.3 1.6 fusion.5
  72.0 2.5 collective-permute-start
  74.5 4.1 %collective-permute-start.7 = (f32[512,128]{1,0:T(8,128)S(1)}, f32[512,128]{1,0:T(8,128)}, u32[]{:S(2)}, u32[]{:S(2)}) collective-permute-start(f32[512,128]{1,0:T(8,128)S(1)} %dynamic-slice_bitcast_fusion), channel_id=1, source_target_pairs={{0,28},{4,0},{8,4},{12,8},{16,12},{20,16},{24,20},{28,24},{1,29},{... | collective-permute-start | bytes 786440 | tf_op jit(solution)/shard_map/ppermute | solution.py:56
  78.6 5.9 %collective-permute-done = f32[512,128]{1,0:T(8,128)S(1)} collective-permute-done((f32[512,128]{1,0:T(8,128)S(1)}, f32[512,128]{1,0:T(8,128)S(1)}, u32[]{:S(2)}, u32[]{:S(2)}) %collective-permute-start) | collective-permute-done | bytes 262176 | tf_op jit(solution)/shard_map/ppermute | solution.py:55
  86.5 2.7 collective-permute-start.8
  89.2 4.1 %collective-permute-done.1 = f32[512,128]{1,0:T(8,128)S(1)} collective-permute-done((f32[512,128]{1,0:T(8,128)S(1)}, f32[512,128]{1,0:T(8,128)S(1)}, u32[]{:S(2)}, u32[]{:S(2)}) %collective-permute-start.1) | collective-permute-done | bytes 262176 | tf_op jit(solution)/shard_map/ppermute | solution.py:55
  95.4 2.7 collective-permute-start.9
  98.1 3.3 %collective-permute-done.2 = f32[512,128]{1,0:T(8,128)} collective-permute-done((f32[512,128]{1,0:T(8,128)S(1)}, f32[512,128]{1,0:T(8,128)}, u32[]{:S(2)}, u32[]{:S(2)}) %collective-permute-start.2) | collective-permute-done | bytes 262176 | tf_op jit(solution)/shard_map/ppermute | solution.py:55
  103.6 2.7 collective-permute-start.10
  106.3 2.7 collective-permute-done.3
  111.1 2.8 collective-permute-start.11
  113.9 2.7 collective-permute-done.4
  118.5 2.6 collective-permute-start.12
  121.2 3.1 %collective-permute-done.5 = f32[512,128]{1,0:T(8,128)} collective-permute-done((f32[512,128]{1,0:T(8,128)S(1)}, f32[512,128]{1,0:T(8,128)}, u32[]{:S(2)}, u32[]{:S(2)}) %collective-permute-start.5) | collective-permute-done | bytes 262176 | tf_op jit(solution)/shard_map/ppermute | solution.py:55
  126.5 2.9 collective-permute-start.13
  129.4 3.4 %collective-permute-done.6 = f32[512,128]{1,0:T(8,128)S(1)} collective-permute-done((f32[512,128]{1,0:T(8,128)S(1)}, f32[512,128]{1,0:T(8,128)S(1)}, u32[]{:S(2)}, u32[]{:S(2)}) %collective-permute-start.6) | collective-permute-done | bytes 262176 | tf_op jit(solution)/shard_map/ppermute | solution.py:55
  137.6 1.9 collective-permute-done.14
  139.7 2.6 collective-permute-start.18
  144.1 2.7 collective-permute-start.19
  154.4 1.9 broadcast_in_dim.38
  156.3 9.9 %all-to-all-start = ((bf16[64,128,128]{2,1,0:T(8,128)(2,1)}), bf16[64,128,128]{2,1,0:T(8,128)(2,1)S(1)}, u32[]{:S(2)}, u32[]{:S(2)}) async-start(bf16[64,128,128]{2,1,0:T(8,128)(2,1)} %broadcast_in_dim.38), calls=%async_computation | async-start | bytes 4194304 | tf_op jit(solution)/shard_map/all_to_all | solution.py:103
  166.2 36.2 %all-to-all-done.b_ref = bf16[64,128,128]{2,1,0:T(8,128)(2,1)S(1)} async-done(((bf16[64,128,128]{2,1,0:T(8,128)(2,1)}), bf16[64,128,128]{2,1,0:T(8,128)(2,1)S(1)}, u32[]{:S(2)}, u32[]{:S(2)}) %all-to-all-start) | async-done | bytes 2097184 | tf_op jit(solution)/shard_map/all_to_all | solution.py:103
  203.7 56.7 %shard_map.78 = f32[8,128,128]{2,1,0:T(8,128)} custom-call(s32[384]{0:T(512)} %reduce.a_index_ref, s32[384]{0:T(512)} %reduce.1.out_index_ref.b_index_ref, s32[384]{0:T(512)} %reduce.2.b_index_ref.out_index_ref, bf16[64,128,128]{2,1,0:T(8,128)(2,1)} %a_ref.1, bf16[64,128,128]{2,1,0:T(8,128)(2,1)} %copy-done), custom_call_target="tpu_custom_call" | custom-call | tf_op jit(solution)/shard_map/pallas_call | solution.py:31
  261.6 16.3 %collective-permute-start.22 = (f32[256,128]{1,0:T(8,128)S(1)}, f32[256,128]{1,0:T(8,128)S(1)}, u32[]{:S(2)}, u32[]{:S(2)}) collective-permute-start(f32[256,128]{1,0:T(8,128)S(1)} %dynamic-slice_bitcast_fusion.3), channel_id=1, source_target_pairs={{0,1},{1,0},{2,3},{3,2},{4,5},{5,4},{6,7},{7,6},{8,9},{9,8},{10,11... | collective-permute-start | bytes 393224 | tf_op jit(solution)/shard_map/ppermute | solution.py:55
  279.4 2.8 collective-permute-start.24
  282.4 2.0 collective-permute-done.24
  284.5 2.8 collective-permute-start.26
  289.2 2.8 collective-permute-done.27
  292.1 3.1 %collective-permute-start.28 = (f32[256,128]{1,0:T(8,128)S(1)}, f32[256,128]{1,0:T(8,128)S(1)}, u32[]{:S(2)}, u32[]{:S(2)}) collective-permute-start(f32[256,128]{1,0:T(8,128)S(1)} %get-tuple-element.11), channel_id=1, source_target_pairs={{0,1},{1,0},{2,3},{3,2},{4,5},{5,4},{6,7},{7,6},{8,9},{9,8},{10,11... | collective-permute-start | bytes 393224 | tf_op jit(solution)/shard_map/ppermute | solution.py:72
  (99 shorter events, 40.4 us)
Async XLA Ops:
  4.5 4.1 %copy-start.1 = (f32[1024,128]{1,0:T(8,128)S(1)}, f32[1024,128]{1,0:T(8,128)}, u32[]{:S(2)}) copy-start(f32[1024,128]{1,0:T(8,128)} %param.6) | copy-start | bytes 1572868
  72.0 12.5 %collective-permute-start = (f32[512,128]{1,0:T(8,128)S(1)}, f32[512,128]{1,0:T(8,128)S(1)}, u32[]{:S(2)}, u32[]{:S(2)}) collective-permute-start(f32[512,128]{1,0:T(8,128)S(1)} %dynamic-slice_bitcast_fusion.1), channel_id=1, source_target_pairs={{0,4},{4,8},{8,12},{12,16},{16,20},{20,24},{24,28},{28,0},{1,5},{5... | collective-permute-start | bytes 786440 | tf_op jit(solution)/shard_map/ppermute | solution.py:55
  74.5 11.0 %collective-permute-start.7 = (f32[512,128]{1,0:T(8,128)S(1)}, f32[512,128]{1,0:T(8,128)}, u32[]{:S(2)}, u32[]{:S(2)}) collective-permute-start(f32[512,128]{1,0:T(8,128)S(1)} %dynamic-slice_bitcast_fusion), channel_id=1, source_target_pairs={{0,28},{4,0},{8,4},{12,8},{16,12},{20,16},{24,20},{28,24},{1,29},{... | collective-permute-start | bytes 786440 | tf_op jit(solution)/shard_map/ppermute | solution.py:56
  85.4 7.9 %collective-permute-start.1 = (f32[512,128]{1,0:T(8,128)S(1)}, f32[512,128]{1,0:T(8,128)S(1)}, u32[]{:S(2)}, u32[]{:S(2)}) collective-permute-start(f32[512,128]{1,0:T(8,128)S(1)} %bitcast_add_fusion.14), channel_id=1, source_target_pairs={{0,4},{4,8},{8,12},{12,16},{16,20},{20,24},{24,28},{28,0},{1,5},{5... | collective-permute-start | bytes 786440 | tf_op jit(solution)/shard_map/ppermute | solution.py:55
  86.5 7.9 %collective-permute-start.8 = (f32[512,128]{1,0:T(8,128)S(1)}, f32[512,128]{1,0:T(8,128)}, u32[]{:S(2)}, u32[]{:S(2)}) collective-permute-start(f32[512,128]{1,0:T(8,128)S(1)} %bitcast_add_fusion.7), channel_id=1, source_target_pairs={{0,28},{4,0},{8,4},{12,8},{16,12},{20,16},{24,20},{28,24},{1,29},{... | collective-permute-start | bytes 786440 | tf_op jit(solution)/shard_map/ppermute | solution.py:56
  94.3 7.2 %collective-permute-start.2 = (f32[512,128]{1,0:T(8,128)S(1)}, f32[512,128]{1,0:T(8,128)}, u32[]{:S(2)}, u32[]{:S(2)}) collective-permute-start(f32[512,128]{1,0:T(8,128)S(1)} %bitcast_add_fusion.13), channel_id=1, source_target_pairs={{0,4},{4,8},{8,12},{12,16},{16,20},{20,24},{24,28},{28,0},{1,5},{5... | collective-permute-start | bytes 786440 | tf_op jit(solution)/shard_map/ppermute | solution.py:55
  95.4 7.2 %collective-permute-start.9 = (f32[512,128]{1,0:T(8,128)S(1)}, f32[512,128]{1,0:T(8,128)}, u32[]{:S(2)}, u32[]{:S(2)}) collective-permute-start(f32[512,128]{1,0:T(8,128)S(1)} %bitcast_add_fusion.6), channel_id=1, source_target_pairs={{0,28},{4,0},{8,4},{12,8},{16,12},{20,16},{24,20},{28,24},{1,29},{... | collective-permute-start | bytes 786440 | tf_op jit(solution)/shard_map/ppermute | solution.py:56
  102.5 6.5 %collective-permute-start.3 = (f32[512,128]{1,0:T(8,128)S(1)}, f32[512,128]{1,0:T(8,128)S(1)}, u32[]{:S(2)}, u32[]{:S(2)}) collective-permute-start(f32[512,128]{1,0:T(8,128)S(1)} %bitcast_add_fusion.12), channel_id=1, source_target_pairs={{0,4},{4,8},{8,12},{12,16},{16,20},{20,24},{24,28},{28,0},{1,5},{5... | collective-permute-start | bytes 786440 | tf_op jit(solution)/shard_map/ppermute | solution.py:55
  103.6 6.5 %collective-permute-start.10 = (f32[512,128]{1,0:T(8,128)S(1)}, f32[512,128]{1,0:T(8,128)}, u32[]{:S(2)}, u32[]{:S(2)}) collective-permute-start(f32[512,128]{1,0:T(8,128)S(1)} %bitcast_add_fusion.5), channel_id=1, source_target_pairs={{0,28},{4,0},{8,4},{12,8},{16,12},{20,16},{24,20},{28,24},{1,29},{... | collective-permute-start | bytes 786440 | tf_op jit(solution)/shard_map/ppermute | solution.py:56
  110.0 6.6 %collective-permute-start.4 = (f32[512,128]{1,0:T(8,128)S(1)}, f32[512,128]{1,0:T(8,128)}, u32[]{:S(2)}, u32[]{:S(2)}) collective-permute-start(f32[512,128]{1,0:T(8,128)S(1)} %bitcast_add_fusion.11), channel_id=1, source_target_pairs={{0,4},{4,8},{8,12},{12,16},{16,20},{20,24},{24,28},{28,0},{1,5},{5... | collective-permute-start | bytes 786440 | tf_op jit(solution)/shard_map/ppermute | solution.py:55
  111.1 6.7 %collective-permute-start.11 = (f32[512,128]{1,0:T(8,128)S(1)}, f32[512,128]{1,0:T(8,128)S(1)}, u32[]{:S(2)}, u32[]{:S(2)}) collective-permute-start(f32[512,128]{1,0:T(8,128)S(1)} %bitcast_add_fusion.4), channel_id=1, source_target_pairs={{0,28},{4,0},{8,4},{12,8},{16,12},{20,16},{24,20},{28,24},{1,29},{... | collective-permute-start | bytes 786440 | tf_op jit(solution)/shard_map/ppermute | solution.py:56
  117.7 6.6 %collective-permute-start.5 = (f32[512,128]{1,0:T(8,128)S(1)}, f32[512,128]{1,0:T(8,128)}, u32[]{:S(2)}, u32[]{:S(2)}) collective-permute-start(f32[512,128]{1,0:T(8,128)S(1)} %bitcast_add_fusion.10), channel_id=1, source_target_pairs={{0,4},{4,8},{8,12},{12,16},{16,20},{20,24},{24,28},{28,0},{1,5},{5... | collective-permute-start | bytes 786440 | tf_op jit(solution)/shard_map/ppermute | solution.py:55
  118.5 6.9 %collective-permute-start.12 = (f32[512,128]{1,0:T(8,128)}, f32[512,128]{1,0:T(8,128)}, u32[]{:S(2)}, u32[]{:S(2)}) collective-permute-start(f32[512,128]{1,0:T(8,128)} %bitcast_add_fusion.3), channel_id=1, source_target_pairs={{0,28},{4,0},{8,4},{12,8},{16,12},{20,16},{24,20},{28,24},{1,29},{... | collective-permute-start | bytes 786440 | tf_op jit(solution)/shard_map/ppermute | solution.py:56
  125.4 7.4 %collective-permute-start.6 = (f32[512,128]{1,0:T(8,128)S(1)}, f32[512,128]{1,0:T(8,128)S(1)}, u32[]{:S(2)}, u32[]{:S(2)}) collective-permute-start(f32[512,128]{1,0:T(8,128)S(1)} %bitcast_add_fusion.9), channel_id=1, source_target_pairs={{0,4},{4,8},{8,12},{12,16},{16,20},{20,24},{24,28},{28,0},{1,5},{5... | collective-permute-start | bytes 786440 | tf_op jit(solution)/shard_map/ppermute | solution.py:55
  126.5 7.3 %collective-permute-start.13 = (f32[512,128]{1,0:T(8,128)S(1)}, f32[512,128]{1,0:T(8,128)}, u32[]{:S(2)}, u32[]{:S(2)}) collective-permute-start(f32[512,128]{1,0:T(8,128)S(1)} %bitcast_add_fusion.2), channel_id=1, source_target_pairs={{0,28},{4,0},{8,4},{12,8},{16,12},{20,16},{24,20},{28,24},{1,29},{... | collective-permute-start | bytes 786440 | tf_op jit(solution)/shard_map/ppermute | solution.py:56
  134.8 4.7 %collective-permute-start.14 = (f32[128,128]{1,0:T(8,128)S(1)}, f32[128,128]{1,0:T(8,128)S(1)}, u32[]{:S(2)}, u32[]{:S(2)}) collective-permute-start(f32[128,128]{1,0:T(8,128)S(1)} %dynamic-slice_bitcast_fusion.7), channel_id=1, source_target_pairs={{0,32},{32,64},{64,96},{96,0},{1,33},{33,65},{65,97},{97,1},{2,34}... | collective-permute-start | bytes 196616 | tf_op jit(solution)/shard_map/ppermute | solution.py:55
  136.1 3.6 %collective-permute-start.17 = (f32[128,128]{1,0:T(8,128)S(1)}, f32[128,128]{1,0:T(8,128)S(1)}, u32[]{:S(2)}, u32[]{:S(2)}) collective-permute-start(f32[128,128]{1,0:T(8,128)S(1)} %dynamic-slice_bitcast_fusion.6), channel_id=1, source_target_pairs={{0,96},{32,0},{64,32},{96,64},{1,97},{33,1},{65,33},{97,65},{2,98}... | collective-permute-start | bytes 196616 | tf_op jit(solution)/shard_map/ppermute | solution.py:56
  139.5 4.4 %collective-permute-start.15 = (f32[128,128]{1,0:T(8,128)S(1)}, f32[128,128]{1,0:T(8,128)S(1)}, u32[]{:S(2)}, u32[]{:S(2)}) collective-permute-start(f32[128,128]{1,0:T(8,128)S(1)} %bitcast_add_fusion.24), channel_id=1, source_target_pairs={{0,32},{32,64},{64,96},{96,0},{1,33},{33,65},{65,97},{97,1},{2,34}... | collective-permute-start | bytes 196616 | tf_op jit(solution)/shard_map/ppermute | solution.py:55
  139.7 4.3 %collective-permute-start.18 = (f32[128,128]{1,0:T(8,128)S(1)}, f32[128,128]{1,0:T(8,128)S(1)}, u32[]{:S(2)}, u32[]{:S(2)}) collective-permute-start(f32[128,128]{1,0:T(8,128)S(1)} %bitcast_add_fusion.21), channel_id=1, source_target_pairs={{0,96},{32,0},{64,32},{96,64},{1,97},{33,1},{65,33},{97,65},{2,98}... | collective-permute-start | bytes 196616 | tf_op jit(solution)/shard_map/ppermute | solution.py:56
  144.0 4.4 %collective-permute-start.16 = (f32[128,128]{1,0:T(8,128)S(1)}, f32[128,128]{1,0:T(8,128)S(1)}, u32[]{:S(2)}, u32[]{:S(2)}) collective-permute-start(f32[128,128]{1,0:T(8,128)S(1)} %bitcast_add_fusion.23), channel_id=1, source_target_pairs={{0,32},{32,64},{64,96},{96,0},{1,33},{33,65},{65,97},{97,1},{2,34}... | collective-permute-start | bytes 196616 | tf_op jit(solution)/shard_map/ppermute | solution.py:55
  144.1 4.3 %collective-permute-start.19 = (f32[128,128]{1,0:T(8,128)S(1)}, f32[128,128]{1,0:T(8,128)S(1)}, u32[]{:S(2)}, u32[]{:S(2)}) collective-permute-start(f32[128,128]{1,0:T(8,128)S(1)} %bitcast_add_fusion.20), channel_id=1, source_target_pairs={{0,96},{32,0},{64,32},{96,64},{1,97},{33,1},{65,33},{97,65},{2,98}... | collective-permute-start | bytes 196616 | tf_op jit(solution)/shard_map/ppermute | solution.py:56
  148.5 2.9 collective-permute-start.20
  149.9 3.1 %collective-permute-start.21 = (f32[64,128]{1,0:T(8,128)S(1)}, f32[64,128]{1,0:T(8,128)S(1)}, u32[]{:S(2)}, u32[]{:S(2)}) collective-permute-start(f32[64,128]{1,0:T(8,128)S(1)} %dynamic-slice_bitcast_fusion.8), channel_id=1, source_target_pairs={{0,128},{128,0},{1,129},{129,1},{2,130},{130,2},{3,131},{131,3},{4... | collective-permute-start | bytes 98312 | tf_op jit(solution)/shard_map/ppermute | solution.py:56
  156.3 46.1 %all-to-all-start = ((bf16[64,128,128]{2,1,0:T(8,128)(2,1)}), bf16[64,128,128]{2,1,0:T(8,128)(2,1)S(1)}, u32[]{:S(2)}, u32[]{:S(2)}) async-start(bf16[64,128,128]{2,1,0:T(8,128)(2,1)} %broadcast_in_dim.38), calls=%async_computation | async-start | bytes 4194304 | tf_op jit(solution)/shard_map/all_to_all | solution.py:103
  261.6 17.2 %collective-permute-start.22 = (f32[256,128]{1,0:T(8,128)S(1)}, f32[256,128]{1,0:T(8,128)S(1)}, u32[]{:S(2)}, u32[]{:S(2)}) collective-permute-start(f32[256,128]{1,0:T(8,128)S(1)} %dynamic-slice_bitcast_fusion.3), channel_id=1, source_target_pairs={{0,1},{1,0},{2,3},{3,2},{4,5},{5,4},{6,7},{7,6},{8,9},{9,8},{10,11... | collective-permute-start | bytes 393224 | tf_op jit(solution)/shard_map/ppermute | solution.py:55
  277.8 1.4 collective-permute-start.23
  279.4 5.1 %collective-permute-start.24 = (f32[128,128]{1,0:T(8,128)S(1)}, f32[128,128]{1,0:T(8,128)S(1)}, u32[]{:S(2)}, u32[]{:S(2)}) collective-permute-start(f32[128,128]{1,0:T(8,128)S(1)} %dynamic-slice_bitcast_fusion.5), channel_id=1, source_target_pairs={{0,2},{2,0},{1,3},{3,1},{4,6},{6,4},{5,7},{7,5},{8,10},{10,8},{9,1... | collective-permute-start | bytes 196616 | tf_op jit(solution)/shard_map/ppermute | solution.py:55
  282.2 5.1 %collective-permute-start.25 = (f32[128,128]{1,0:T(8,128)S(1)}, f32[128,128]{1,0:T(8,128)S(1)}, u32[]{:S(2)}, u32[]{:S(2)}) collective-permute-start(f32[128,128]{1,0:T(8,128)S(1)} %dynamic-slice_bitcast_fusion.4), channel_id=1, source_target_pairs={{0,2},{2,0},{1,3},{3,1},{4,6},{6,4},{5,7},{7,5},{8,10},{10,8},{9,1... | collective-permute-start | bytes 196616 | tf_op jit(solution)/shard_map/ppermute | solution.py:56
  284.5 4.7 %collective-permute-start.26 = (f32[128,128]{1,0:T(8,128)S(1)}, f32[128,128]{1,0:T(8,128)S(1)}, u32[]{:S(2)}, u32[]{:S(2)}) collective-permute-start(f32[128,128]{1,0:T(8,128)S(1)} %bitcast_add_fusion.18), channel_id=1, source_target_pairs={{0,2},{2,0},{1,3},{3,1},{4,6},{6,4},{5,7},{7,5},{8,10},{10,8},{9,1... | collective-permute-start | bytes 196616 | tf_op jit(solution)/shard_map/ppermute | solution.py:72
  287.3 4.7 %collective-permute-start.27 = (f32[128,128]{1,0:T(8,128)S(1)}, f32[128,128]{1,0:T(8,128)S(1)}, u32[]{:S(2)}, u32[]{:S(2)}) collective-permute-start(f32[128,128]{1,0:T(8,128)S(1)} %bitcast_add_fusion.17), channel_id=1, source_target_pairs={{0,2},{2,0},{1,3},{3,1},{4,6},{6,4},{5,7},{7,5},{8,10},{10,8},{9,1... | collective-permute-start | bytes 196616 | tf_op jit(solution)/shard_map/ppermute | solution.py:73
  292.1 4.1 %collective-permute-start.28 = (f32[256,128]{1,0:T(8,128)S(1)}, f32[256,128]{1,0:T(8,128)S(1)}, u32[]{:S(2)}, u32[]{:S(2)}) collective-permute-start(f32[256,128]{1,0:T(8,128)S(1)} %get-tuple-element.11), channel_id=1, source_target_pairs={{0,1},{1,0},{2,3},{3,2},{4,5},{5,4},{6,7},{7,6},{8,9},{9,8},{10,11... | collective-permute-start | bytes 393224 | tf_op jit(solution)/shard_map/ppermute | solution.py:72
  295.2 1.3 collective-permute-start.29
  (1 other events, 1.4 us)

commit v2 on v1

--- a/solution.py
+++ b/solution.py
@@ -22,7 +22,7 @@
         o_ref[out_index_ref[k]] += jnp.dot(a, b, preferred_element_type=jnp.float32)
         return carry
 
-    lax.fori_loop(0, n_blocks, body, 0)
+    lax.fori_loop(0, n_blocks, body, 0, unroll=8)
 
 
 def block_sums(lists, a_tiles, b_tiles, n_out):

time: 298 us -> 215 us (0.72)
  Pallas kernels: 114 us -> 30.5 us
    pallas_call x2, Pallas kernels: 114 us -> 30.5 us  [block_sums(): pl.pallas_call(block_sum_kernel, grid_spec=pltpu.PrefetchScalarGridSpec(n...]
  transfers between devices with their start and end apart: 31 -> 31, of which waited for: 20 -> 20; matrix products, arithmetic and copies ran while one was open for 4% -> 6% of each run, Pallas kernels for 0% -> 0%
where the time goes in v2:
time: 215 us; the launch traced here: 214 us
  waiting for transfers between devices  76.9 us (36%)
  starting transfers between devices  70.5 us (33%)
  Pallas kernels  30.5 us (14%)
  other arithmetic  20.9 us (10%)
  local copies, waits for them, and re-layouts  13.8 us (6%)
    all_to_all x1, waiting for transfers between devices, per_device(): item_tiles = lax.all_to_all(spread, USER_AXES, 0, 0, tiled=True)  36.2 us
    ppermute x13, waiting for transfers between devices, ring_reduce_scatter(): rl = lax.ppermute(bl, axis, right)  34.3 us
    pallas_call x2, Pallas kernels, block_sums(): pl.pallas_call(block_sum_kernel, grid_spec=pltpu.PrefetchScalarGridSpec(n...  30.5 us
    ppermute x13, starting transfers between devices, ring_reduce_scatter(): rr = lax.ppermute(br, axis, left)  27.9 us
    ppermute x13, starting transfers between devices, ring_reduce_scatter(): rl = lax.ppermute(bl, axis, right)  25.2 us
    all_to_all x1, starting transfers between devices, per_device(): item_tiles = lax.all_to_all(spread, USER_AXES, 0, 0, tiled=True)  9.92 us
    add x12, other arithmetic, ring_reduce_scatter(): bl = rl + lax.dynamic_index_in_dim(xl, (i - s - 2) % n, 0, keepdims=False)  7.14 us
    add x12, other arithmetic, ring_reduce_scatter(): br = rr + lax.dynamic_index_in_dim(xr, (i + s + 2) % n, 0, keepdims=False)  6.7 us
  transfers between devices with their start and end apart: 31, of which 20 were waited for; matrix products, arithmetic and copies ran while one was open for 6% of the time, Pallas kernels for 0%

profile of v2, /device:TPU:1, one launch (start us, length us, event | category | flops | bytes accessed | tf_op | source)
XLA Modules:
  0.0 213.8 jit_solution(672952840523606506)
XLA Ops:
  4.5 4.1 %copy.9 = bf16[64,128,128]{1,2,0:T(8,128)(2,1)} copy(bf16[64,128,128]{2,1,0:T(8,128)(2,1)} %a_ref.1) | data formatting | bytes 4194304 | tf_op args[2]
  9.4 15.6 %shard_map.77 = f32[64,128,128]{2,1,0:T(8,128)} custom-call(s32[384]{0:T(512)} %reduce.a_index_ref, s32[384]{0:T(512)} %reduce.2.b_index_ref.out_index_ref, s32[384]{0:T(512)} %reduce.1.out_index_ref.b_index_ref, bf16[64,128,128]{2,1,0:T(8,128)(2,1)} %bitcast.115, bf16[8,128,128]{2,1,0:T(8,128)(2,1)} %bitcast.120), custom_call_target="tpu_custom_call" | custom-call | tf_op jit(solution)/shard_map/pallas_call | solution.py:31
  25.0 2.5 %copy.10 = f32[2,4,8,128,128]{4,3,0,1,2:T(8,128)S(1)} copy(f32[2,4,8,128,128]{4,3,2,1,0:T(8,128)} %bitcast.114) | data formatting | bytes 8388608 | tf_op jit(solution)/shard_map/reshape | solution.py:92
  27.5 1.6 fusion.5
  30.1 2.5 %collective-permute-start = (f32[512,128]{1,0:T(8,128)S(1)}, f32[512,128]{1,0:T(8,128)S(1)}, u32[]{:S(2)}, u32[]{:S(2)}) collective-permute-start(f32[512,128]{1,0:T(8,128)S(1)} %dynamic-slice_bitcast_fusion.1), channel_id=1, source_target_pairs={{0,4},{4,8},{8,12},{12,16},{16,20},{20,24},{24,28},{28,0},{1,5},{5... | collective-permute-start | bytes 786440 | tf_op jit(solution)/shard_map/ppermute | solution.py:55
  32.6 4.1 %collective-permute-start.7 = (f32[512,128]{1,0:T(8,128)S(1)}, f32[512,128]{1,0:T(8,128)}, u32[]{:S(2)}, u32[]{:S(2)}) collective-permute-start(f32[512,128]{1,0:T(8,128)S(1)} %dynamic-slice_bitcast_fusion), channel_id=1, source_target_pairs={{0,28},{4,0},{8,4},{12,8},{16,12},{20,16},{24,20},{28,24},{1,29},{... | collective-permute-start | bytes 786440 | tf_op jit(solution)/shard_map/ppermute | solution.py:56
  36.7 5.9 %collective-permute-done = f32[512,128]{1,0:T(8,128)S(1)} collective-permute-done((f32[512,128]{1,0:T(8,128)S(1)}, f32[512,128]{1,0:T(8,128)S(1)}, u32[]{:S(2)}, u32[]{:S(2)}) %collective-permute-start) | collective-permute-done | bytes 262176 | tf_op jit(solution)/shard_map/ppermute | solution.py:55
  44.6 2.7 %collective-permute-start.8 = (f32[512,128]{1,0:T(8,128)S(1)}, f32[512,128]{1,0:T(8,128)}, u32[]{:S(2)}, u32[]{:S(2)}) collective-permute-start(f32[512,128]{1,0:T(8,128)S(1)} %bitcast_add_fusion.7), channel_id=1, source_target_pairs={{0,28},{4,0},{8,4},{12,8},{16,12},{20,16},{24,20},{28,24},{1,29},{... | collective-permute-start | bytes 786440 | tf_op jit(solution)/shard_map/ppermute | solution.py:56
  47.3 4.1 %collective-permute-done.1 = f32[512,128]{1,0:T(8,128)S(1)} collective-permute-done((f32[512,128]{1,0:T(8,128)S(1)}, f32[512,128]{1,0:T(8,128)S(1)}, u32[]{:S(2)}, u32[]{:S(2)}) %collective-permute-start.1) | collective-permute-done | bytes 262176 | tf_op jit(solution)/shard_map/ppermute | solution.py:55
  53.5 2.7 %collective-permute-start.9 = (f32[512,128]{1,0:T(8,128)S(1)}, f32[512,128]{1,0:T(8,128)}, u32[]{:S(2)}, u32[]{:S(2)}) collective-permute-start(f32[512,128]{1,0:T(8,128)S(1)} %bitcast_add_fusion.6), channel_id=1, source_target_pairs={{0,28},{4,0},{8,4},{12,8},{16,12},{20,16},{24,20},{28,24},{1,29},{... | collective-permute-start | bytes 786440 | tf_op jit(solution)/shard_map/ppermute | solution.py:56
  56.2 3.3 %collective-permute-done.2 = f32[512,128]{1,0:T(8,128)} collective-permute-done((f32[512,128]{1,0:T(8,128)S(1)}, f32[512,128]{1,0:T(8,128)}, u32[]{:S(2)}, u32[]{:S(2)}) %collective-permute-start.2) | collective-permute-done | bytes 262176 | tf_op jit(solution)/shard_map/ppermute | solution.py:55
  61.7 2.7 %collective-permute-start.10 = (f32[512,128]{1,0:T(8,128)S(1)}, f32[512,128]{1,0:T(8,128)}, u32[]{:S(2)}, u32[]{:S(2)}) collective-permute-start(f32[512,128]{1,0:T(8,128)S(1)} %bitcast_add_fusion.5), channel_id=1, source_target_pairs={{0,28},{4,0},{8,4},{12,8},{16,12},{20,16},{24,20},{28,24},{1,29},{... | collective-permute-start | bytes 786440 | tf_op jit(solution)/shard_map/ppermute | solution.py:56
  64.4 2.7 %collective-permute-done.3 = f32[512,128]{1,0:T(8,128)S(1)} collective-permute-done((f32[512,128]{1,0:T(8,128)S(1)}, f32[512,128]{1,0:T(8,128)S(1)}, u32[]{:S(2)}, u32[]{:S(2)}) %collective-permute-start.3) | collective-permute-done | bytes 262176 | tf_op jit(solution)/shard_map/ppermute | solution.py:55
  69.2 2.8 %collective-permute-start.11 = (f32[512,128]{1,0:T(8,128)S(1)}, f32[512,128]{1,0:T(8,128)S(1)}, u32[]{:S(2)}, u32[]{:S(2)}) collective-permute-start(f32[512,128]{1,0:T(8,128)S(1)} %bitcast_add_fusion.4), channel_id=1, source_target_pairs={{0,28},{4,0},{8,4},{12,8},{16,12},{20,16},{24,20},{28,24},{1,29},{... | collective-permute-start | bytes 786440 | tf_op jit(solution)/shard_map/ppermute | solution.py:56
  72.0 2.7 %collective-permute-done.4 = f32[512,128]{1,0:T(8,128)} collective-permute-done((f32[512,128]{1,0:T(8,128)S(1)}, f32[512,128]{1,0:T(8,128)}, u32[]{:S(2)}, u32[]{:S(2)}) %collective-permute-start.4) | collective-permute-done | bytes 262176 | tf_op jit(solution)/shard_map/ppermute | solution.py:55
  76.6 2.6 %collective-permute-start.12 = (f32[512,128]{1,0:T(8,128)}, f32[512,128]{1,0:T(8,128)}, u32[]{:S(2)}, u32[]{:S(2)}) collective-permute-start(f32[512,128]{1,0:T(8,128)} %bitcast_add_fusion.3), channel_id=1, source_target_pairs={{0,28},{4,0},{8,4},{12,8},{16,12},{20,16},{24,20},{28,24},{1,29},{... | collective-permute-start | bytes 786440 | tf_op jit(solution)/shard_map/ppermute | solution.py:56
  79.3 3.1 %collective-permute-done.5 = f32[512,128]{1,0:T(8,128)} collective-permute-done((f32[512,128]{1,0:T(8,128)S(1)}, f32[512,128]{1,0:T(8,128)}, u32[]{:S(2)}, u32[]{:S(2)}) %collective-permute-start.5) | collective-permute-done | bytes 262176 | tf_op jit(solution)/shard_map/ppermute | solution.py:55
  84.5 2.9 %collective-permute-start.13 = (f32[512,128]{1,0:T(8,128)S(1)}, f32[512,128]{1,0:T(8,128)}, u32[]{:S(2)}, u32[]{:S(2)}) collective-permute-start(f32[512,128]{1,0:T(8,128)S(1)} %bitcast_add_fusion.2), channel_id=1, source_target_pairs={{0,28},{4,0},{8,4},{12,8},{16,12},{20,16},{24,20},{28,24},{1,29},{... | collective-permute-start | bytes 786440 | tf_op jit(solution)/shard_map/ppermute | solution.py:56
  87.5 3.4 %collective-permute-done.6 = f32[512,128]{1,0:T(8,128)S(1)} collective-permute-done((f32[512,128]{1,0:T(8,128)S(1)}, f32[512,128]{1,0:T(8,128)S(1)}, u32[]{:S(2)}, u32[]{:S(2)}) %collective-permute-start.6) | collective-permute-done | bytes 262176 | tf_op jit(solution)/shard_map/ppermute | solution.py:55
  95.7 1.9 collective-permute-done.14
  97.9 2.6 %collective-permute-start.18 = (f32[128,128]{1,0:T(8,128)S(1)}, f32[128,128]{1,0:T(8,128)S(1)}, u32[]{:S(2)}, u32[]{:S(2)}) collective-permute-start(f32[128,128]{1,0:T(8,128)S(1)} %bitcast_add_fusion.21), channel_id=1, source_target_pairs={{0,96},{32,0},{64,32},{96,64},{1,97},{33,1},{65,33},{97,65},{2,98}... | collective-permute-start | bytes 196616 | tf_op jit(solution)/shard_map/ppermute | solution.py:56
  102.2 2.7 %collective-permute-start.19 = (f32[128,128]{1,0:T(8,128)S(1)}, f32[128,128]{1,0:T(8,128)S(1)}, u32[]{:S(2)}, u32[]{:S(2)}) collective-permute-start(f32[128,128]{1,0:T(8,128)S(1)} %bitcast_add_fusion.20), channel_id=1, source_target_pairs={{0,96},{32,0},{64,32},{96,64},{1,97},{33,1},{65,33},{97,65},{2,98}... | collective-permute-start | bytes 196616 | tf_op jit(solution)/shard_map/ppermute | solution.py:56
  112.5 1.9 broadcast_in_dim.38
  114.4 9.9 %all-to-all-start = ((bf16[64,128,128]{2,1,0:T(8,128)(2,1)}), bf16[64,128,128]{2,1,0:T(8,128)(2,1)S(1)}, u32[]{:S(2)}, u32[]{:S(2)}) async-start(bf16[64,128,128]{2,1,0:T(8,128)(2,1)} %broadcast_in_dim.38), calls=%async_computation | async-start | bytes 4194304 | tf_op jit(solution)/shard_map/all_to_all | solution.py:103
  124.3 36.2 %all-to-all-done.b_ref = bf16[64,128,128]{2,1,0:T(8,128)(2,1)S(1)} async-done(((bf16[64,128,128]{2,1,0:T(8,128)(2,1)}), bf16[64,128,128]{2,1,0:T(8,128)(2,1)S(1)}, u32[]{:S(2)}, u32[]{:S(2)}) %all-to-all-start) | async-done | bytes 2097184 | tf_op jit(solution)/shard_map/all_to_all | solution.py:103
  161.9 14.9 %shard_map.78 = f32[8,128,128]{2,1,0:T(8,128)} custom-call(s32[384]{0:T(512)} %reduce.a_index_ref, s32[384]{0:T(512)} %reduce.1.out_index_ref.b_index_ref, s32[384]{0:T(512)} %reduce.2.b_index_ref.out_index_ref, bf16[64,128,128]{2,1,0:T(8,128)(2,1)} %a_ref.1, bf16[64,128,128]{2,1,0:T(8,128)(2,1)} %copy-done), custom_call_target="tpu_custom_call" | custom-call | tf_op jit(solution)/shard_map/pallas_call | solution.py:31
  177.8 16.2 %collective-permute-start.22 = (f32[256,128]{1,0:T(8,128)S(1)}, f32[256,128]{1,0:T(8,128)S(1)}, u32[]{:S(2)}, u32[]{:S(2)}) collective-permute-start(f32[256,128]{1,0:T(8,128)S(1)} %dynamic-slice_bitcast_fusion.3), channel_id=1, source_target_pairs={{0,1},{1,0},{2,3},{3,2},{4,5},{5,4},{6,7},{7,6},{8,9},{9,8},{10,11... | collective-permute-start | bytes 393224 | tf_op jit(solution)/shard_map/ppermute | solution.py:55
  195.6 2.9 %collective-permute-start.24 = (f32[128,128]{1,0:T(8,128)S(1)}, f32[128,128]{1,0:T(8,128)S(1)}, u32[]{:S(2)}, u32[]{:S(2)}) collective-permute-start(f32[128,128]{1,0:T(8,128)S(1)} %dynamic-slice_bitcast_fusion.5), channel_id=1, source_target_pairs={{0,2},{2,0},{1,3},{3,1},{4,6},{6,4},{5,7},{7,5},{8,10},{10,8},{9,1... | collective-permute-start | bytes 196616 | tf_op jit(solution)/shard_map/ppermute | solution.py:55
  198.7 2.0 collective-permute-done.24
  200.7 2.9 %collective-permute-start.26 = (f32[128,128]{1,0:T(8,128)S(1)}, f32[128,128]{1,0:T(8,128)S(1)}, u32[]{:S(2)}, u32[]{:S(2)}) collective-permute-start(f32[128,128]{1,0:T(8,128)S(1)} %bitcast_add_fusion.18), channel_id=1, source_target_pairs={{0,2},{2,0},{1,3},{3,1},{4,6},{6,4},{5,7},{7,5},{8,10},{10,8},{9,1... | collective-permute-start | bytes 196616 | tf_op jit(solution)/shard_map/ppermute | solution.py:72
  205.4 2.9 %collective-permute-done.27 = f32[128,128]{1,0:T(8,128)S(1)} collective-permute-done((f32[128,128]{1,0:T(8,128)S(1)}, f32[128,128]{1,0:T(8,128)S(1)}, u32[]{:S(2)}, u32[]{:S(2)}) %collective-permute-start.27) | collective-permute-done | bytes 65568 | tf_op jit(solution)/shard_map/ppermute | solution.py:73
  208.4 3.1 %collective-permute-start.28 = (f32[256,128]{1,0:T(8,128)S(1)}, f32[256,128]{1,0:T(8,128)S(1)}, u32[]{:S(2)}, u32[]{:S(2)}) collective-permute-start(f32[256,128]{1,0:T(8,128)S(1)} %get-tuple-element.11), channel_id=1, source_target_pairs={{0,1},{1,0},{2,3},{3,2},{4,5},{5,4},{6,7},{7,6},{8,9},{9,8},{10,11... | collective-permute-start | bytes 393224 | tf_op jit(solution)/shard_map/ppermute | solution.py:72
  (99 shorter events, 40.4 us)
Async XLA Ops:
  4.5 4.1 %copy-start.1 = (f32[1024,128]{1,0:T(8,128)S(1)}, f32[1024,128]{1,0:T(8,128)}, u32[]{:S(2)}) copy-start(f32[1024,128]{1,0:T(8,128)} %param.6) | copy-start | bytes 1572868
  30.1 12.5 %collective-permute-start = (f32[512,128]{1,0:T(8,128)S(1)}, f32[512,128]{1,0:T(8,128)S(1)}, u32[]{:S(2)}, u32[]{:S(2)}) collective-permute-start(f32[512,128]{1,0:T(8,128)S(1)} %dynamic-slice_bitcast_fusion.1), channel_id=1, source_target_pairs={{0,4},{4,8},{8,12},{12,16},{16,20},{20,24},{24,28},{28,0},{1,5},{5... | collective-permute-start | bytes 786440 | tf_op jit(solution)/shard_map/ppermute | solution.py:55
  32.6 11.0 %collective-permute-start.7 = (f32[512,128]{1,0:T(8,128)S(1)}, f32[512,128]{1,0:T(8,128)}, u32[]{:S(2)}, u32[]{:S(2)}) collective-permute-start(f32[512,128]{1,0:T(8,128)S(1)} %dynamic-slice_bitcast_fusion), channel_id=1, source_target_pairs={{0,28},{4,0},{8,4},{12,8},{16,12},{20,16},{24,20},{28,24},{1,29},{... | collective-permute-start | bytes 786440 | tf_op jit(solution)/shard_map/ppermute | solution.py:56
  43.5 7.9 %collective-permute-start.1 = (f32[512,128]{1,0:T(8,128)S(1)}, f32[512,128]{1,0:T(8,128)S(1)}, u32[]{:S(2)}, u32[]{:S(2)}) collective-permute-start(f32[512,128]{1,0:T(8,128)S(1)} %bitcast_add_fusion.14), channel_id=1, source_target_pairs={{0,4},{4,8},{8,12},{12,16},{16,20},{20,24},{24,28},{28,0},{1,5},{5... | collective-permute-start | bytes 786440 | tf_op jit(solution)/shard_map/ppermute | solution.py:55
  44.6 7.9 %collective-permute-start.8 = (f32[512,128]{1,0:T(8,128)S(1)}, f32[512,128]{1,0:T(8,128)}, u32[]{:S(2)}, u32[]{:S(2)}) collective-permute-start(f32[512,128]{1,0:T(8,128)S(1)} %bitcast_add_fusion.7), channel_id=1, source_target_pairs={{0,28},{4,0},{8,4},{12,8},{16,12},{20,16},{24,20},{28,24},{1,29},{... | collective-permute-start | bytes 786440 | tf_op jit(solution)/shard_map/ppermute | solution.py:56
  52.4 7.1 %collective-permute-start.2 = (f32[512,128]{1,0:T(8,128)S(1)}, f32[512,128]{1,0:T(8,128)}, u32[]{:S(2)}, u32[]{:S(2)}) collective-permute-start(f32[512,128]{1,0:T(8,128)S(1)} %bitcast_add_fusion.13), channel_id=1, source_target_pairs={{0,4},{4,8},{8,12},{12,16},{16,20},{20,24},{24,28},{28,0},{1,5},{5... | collective-permute-start | bytes 786440 | tf_op jit(solution)/shard_map/ppermute | solution.py:55
  53.5 7.2 %collective-permute-start.9 = (f32[512,128]{1,0:T(8,128)S(1)}, f32[512,128]{1,0:T(8,128)}, u32[]{:S(2)}, u32[]{:S(2)}) collective-permute-start(f32[512,128]{1,0:T(8,128)S(1)} %bitcast_add_fusion.6), channel_id=1, source_target_pairs={{0,28},{4,0},{8,4},{12,8},{16,12},{20,16},{24,20},{28,24},{1,29},{... | collective-permute-start | bytes 786440 | tf_op jit(solution)/shard_map/ppermute | solution.py:56
  60.6 6.5 %collective-permute-start.3 = (f32[512,128]{1,0:T(8,128)S(1)}, f32[512,128]{1,0:T(8,128)S(1)}, u32[]{:S(2)}, u32[]{:S(2)}) collective-permute-start(f32[512,128]{1,0:T(8,128)S(1)} %bitcast_add_fusion.12), channel_id=1, source_target_pairs={{0,4},{4,8},{8,12},{12,16},{16,20},{20,24},{24,28},{28,0},{1,5},{5... | collective-permute-start | bytes 786440 | tf_op jit(solution)/shard_map/ppermute | solution.py:55
  61.7 6.5 %collective-permute-start.10 = (f32[512,128]{1,0:T(8,128)S(1)}, f32[512,128]{1,0:T(8,128)}, u32[]{:S(2)}, u32[]{:S(2)}) collective-permute-start(f32[512,128]{1,0:T(8,128)S(1)} %bitcast_add_fusion.5), channel_id=1, source_target_pairs={{0,28},{4,0},{8,4},{12,8},{16,12},{20,16},{24,20},{28,24},{1,29},{... | collective-permute-start | bytes 786440 | tf_op jit(solution)/shard_map/ppermute | solution.py:56
  68.1 6.6 %collective-permute-start.4 = (f32[512,128]{1,0:T(8,128)S(1)}, f32[512,128]{1,0:T(8,128)}, u32[]{:S(2)}, u32[]{:S(2)}) collective-permute-start(f32[512,128]{1,0:T(8,128)S(1)} %bitcast_add_fusion.11), channel_id=1, source_target_pairs={{0,4},{4,8},{8,12},{12,16},{16,20},{20,24},{24,28},{28,0},{1,5},{5... | collective-permute-start | bytes 786440 | tf_op jit(solution)/shard_map/ppermute | solution.py:55
  69.2 6.7 %collective-permute-start.11 = (f32[512,128]{1,0:T(8,128)S(1)}, f32[512,128]{1,0:T(8,128)S(1)}, u32[]{:S(2)}, u32[]{:S(2)}) collective-permute-start(f32[512,128]{1,0:T(8,128)S(1)} %bitcast_add_fusion.4), channel_id=1, source_target_pairs={{0,28},{4,0},{8,4},{12,8},{16,12},{20,16},{24,20},{28,24},{1,29},{... | collective-permute-start | bytes 786440 | tf_op jit(solution)/shard_map/ppermute | solution.py:56
  75.8 6.6 %collective-permute-start.5 = (f32[512,128]{1,0:T(8,128)S(1)}, f32[512,128]{1,0:T(8,128)}, u32[]{:S(2)}, u32[]{:S(2)}) collective-permute-start(f32[512,128]{1,0:T(8,128)S(1)} %bitcast_add_fusion.10), channel_id=1, source_target_pairs={{0,4},{4,8},{8,12},{12,16},{16,20},{20,24},{24,28},{28,0},{1,5},{5... | collective-permute-start | bytes 786440 | tf_op jit(solution)/shard_map/ppermute | solution.py:55
  76.6 6.9 %collective-permute-start.12 = (f32[512,128]{1,0:T(8,128)}, f32[512,128]{1,0:T(8,128)}, u32[]{:S(2)}, u32[]{:S(2)}) collective-permute-start(f32[512,128]{1,0:T(8,128)} %bitcast_add_fusion.3), channel_id=1, source_target_pairs={{0,28},{4,0},{8,4},{12,8},{16,12},{20,16},{24,20},{28,24},{1,29},{... | collective-permute-start | bytes 786440 | tf_op jit(solution)/shard_map/ppermute | solution.py:56
  83.5 7.4 %collective-permute-start.6 = (f32[512,128]{1,0:T(8,128)S(1)}, f32[512,128]{1,0:T(8,128)S(1)}, u32[]{:S(2)}, u32[]{:S(2)}) collective-permute-start(f32[512,128]{1,0:T(8,128)S(1)} %bitcast_add_fusion.9), channel_id=1, source_target_pairs={{0,4},{4,8},{8,12},{12,16},{16,20},{20,24},{24,28},{28,0},{1,5},{5... | collective-permute-start | bytes 786440 | tf_op jit(solution)/shard_map/ppermute | solution.py:55
  84.5 7.3 %collective-permute-start.13 = (f32[512,128]{1,0:T(8,128)S(1)}, f32[512,128]{1,0:T(8,128)}, u32[]{:S(2)}, u32[]{:S(2)}) collective-permute-start(f32[512,128]{1,0:T(8,128)S(1)} %bitcast_add_fusion.2), channel_id=1, source_target_pairs={{0,28},{4,0},{8,4},{12,8},{16,12},{20,16},{24,20},{28,24},{1,29},{... | collective-permute-start | bytes 786440 | tf_op jit(solution)/shard_map/ppermute | solution.py:56
  92.9 4.7 %collective-permute-start.14 = (f32[128,128]{1,0:T(8,128)S(1)}, f32[128,128]{1,0:T(8,128)S(1)}, u32[]{:S(2)}, u32[]{:S(2)}) collective-permute-start(f32[128,128]{1,0:T(8,128)S(1)} %dynamic-slice_bitcast_fusion.7), channel_id=1, source_target_pairs={{0,32},{32,64},{64,96},{96,0},{1,33},{33,65},{65,97},{97,1},{2,34}... | collective-permute-start | bytes 196616 | tf_op jit(solution)/shard_map/ppermute | solution.py:55
  94.3 3.6 %collective-permute-start.17 = (f32[128,128]{1,0:T(8,128)S(1)}, f32[128,128]{1,0:T(8,128)S(1)}, u32[]{:S(2)}, u32[]{:S(2)}) collective-permute-start(f32[128,128]{1,0:T(8,128)S(1)} %dynamic-slice_bitcast_fusion.6), channel_id=1, source_target_pairs={{0,96},{32,0},{64,32},{96,64},{1,97},{33,1},{65,33},{97,65},{2,98}... | collective-permute-start | bytes 196616 | tf_op jit(solution)/shard_map/ppermute | solution.py:56
  97.6 4.4 %collective-permute-start.15 = (f32[128,128]{1,0:T(8,128)S(1)}, f32[128,128]{1,0:T(8,128)S(1)}, u32[]{:S(2)}, u32[]{:S(2)}) collective-permute-start(f32[128,128]{1,0:T(8,128)S(1)} %bitcast_add_fusion.24), channel_id=1, source_target_pairs={{0,32},{32,64},{64,96},{96,0},{1,33},{33,65},{65,97},{97,1},{2,34}... | collective-permute-start | bytes 196616 | tf_op jit(solution)/shard_map/ppermute | solution.py:55
  97.9 4.3 %collective-permute-start.18 = (f32[128,128]{1,0:T(8,128)S(1)}, f32[128,128]{1,0:T(8,128)S(1)}, u32[]{:S(2)}, u32[]{:S(2)}) collective-permute-start(f32[128,128]{1,0:T(8,128)S(1)} %bitcast_add_fusion.21), channel_id=1, source_target_pairs={{0,96},{32,0},{64,32},{96,64},{1,97},{33,1},{65,33},{97,65},{2,98}... | collective-permute-start | bytes 196616 | tf_op jit(solution)/shard_map/ppermute | solution.py:56
  102.0 4.4 %collective-permute-start.16 = (f32[128,128]{1,0:T(8,128)S(1)}, f32[128,128]{1,0:T(8,128)S(1)}, u32[]{:S(2)}, u32[]{:S(2)}) collective-permute-start(f32[128,128]{1,0:T(8,128)S(1)} %bitcast_add_fusion.23), channel_id=1, source_target_pairs={{0,32},{32,64},{64,96},{96,0},{1,33},{33,65},{65,97},{97,1},{2,34}... | collective-permute-start | bytes 196616 | tf_op jit(solution)/shard_map/ppermute | solution.py:55
  102.2 4.3 %collective-permute-start.19 = (f32[128,128]{1,0:T(8,128)S(1)}, f32[128,128]{1,0:T(8,128)S(1)}, u32[]{:S(2)}, u32[]{:S(2)}) collective-permute-start(f32[128,128]{1,0:T(8,128)S(1)} %bitcast_add_fusion.20), channel_id=1, source_target_pairs={{0,96},{32,0},{64,32},{96,64},{1,97},{33,1},{65,33},{97,65},{2,98}... | collective-permute-start | bytes 196616 | tf_op jit(solution)/shard_map/ppermute | solution.py:56
  106.6 2.9 %collective-permute-start.20 = (f32[64,128]{1,0:T(8,128)S(1)}, f32[64,128]{1,0:T(8,128)S(1)}, u32[]{:S(2)}, u32[]{:S(2)}) collective-permute-start(f32[64,128]{1,0:T(8,128)S(1)} %dynamic-slice_bitcast_fusion.9), channel_id=1, source_target_pairs={{0,128},{128,0},{1,129},{129,1},{2,130},{130,2},{3,131},{131,3},{4... | collective-permute-start | bytes 98312 | tf_op jit(solution)/shard_map/ppermute | solution.py:55
  108.0 3.1 %collective-permute-start.21 = (f32[64,128]{1,0:T(8,128)S(1)}, f32[64,128]{1,0:T(8,128)S(1)}, u32[]{:S(2)}, u32[]{:S(2)}) collective-permute-start(f32[64,128]{1,0:T(8,128)S(1)} %dynamic-slice_bitcast_fusion.8), channel_id=1, source_target_pairs={{0,128},{128,0},{1,129},{129,1},{2,130},{130,2},{3,131},{131,3},{4... | collective-permute-start | bytes 98312 | tf_op jit(solution)/shard_map/ppermute | solution.py:56
  114.4 46.1 %all-to-all-start = ((bf16[64,128,128]{2,1,0:T(8,128)(2,1)}), bf16[64,128,128]{2,1,0:T(8,128)(2,1)S(1)}, u32[]{:S(2)}, u32[]{:S(2)}) async-start(bf16[64,128,128]{2,1,0:T(8,128)(2,1)} %broadcast_in_dim.38), calls=%async_computation | async-start | bytes 4194304 | tf_op jit(solution)/shard_map/all_to_all | solution.py:103
  177.8 17.2 %collective-permute-start.22 = (f32[256,128]{1,0:T(8,128)S(1)}, f32[256,128]{1,0:T(8,128)S(1)}, u32[]{:S(2)}, u32[]{:S(2)}) collective-permute-start(f32[256,128]{1,0:T(8,128)S(1)} %dynamic-slice_bitcast_fusion.3), channel_id=1, source_target_pairs={{0,1},{1,0},{2,3},{3,2},{4,5},{5,4},{6,7},{7,6},{8,9},{9,8},{10,11... | collective-permute-start | bytes 393224 | tf_op jit(solution)/shard_map/ppermute | solution.py:55
  194.1 1.4 collective-permute-start.23
  195.6 5.1 %collective-permute-start.24 = (f32[128,128]{1,0:T(8,128)S(1)}, f32[128,128]{1,0:T(8,128)S(1)}, u32[]{:S(2)}, u32[]{:S(2)}) collective-permute-start(f32[128,128]{1,0:T(8,128)S(1)} %dynamic-slice_bitcast_fusion.5), channel_id=1, source_target_pairs={{0,2},{2,0},{1,3},{3,1},{4,6},{6,4},{5,7},{7,5},{8,10},{10,8},{9,1... | collective-permute-start | bytes 196616 | tf_op jit(solution)/shard_map/ppermute | solution.py:55
  198.5 5.1 %collective-permute-start.25 = (f32[128,128]{1,0:T(8,128)S(1)}, f32[128,128]{1,0:T(8,128)S(1)}, u32[]{:S(2)}, u32[]{:S(2)}) collective-permute-start(f32[128,128]{1,0:T(8,128)S(1)} %dynamic-slice_bitcast_fusion.4), channel_id=1, source_target_pairs={{0,2},{2,0},{1,3},{3,1},{4,6},{6,4},{5,7},{7,5},{8,10},{10,8},{9,1... | collective-permute-start | bytes 196616 | tf_op jit(solution)/shard_map/ppermute | solution.py:56
  200.7 4.7 %collective-permute-start.26 = (f32[128,128]{1,0:T(8,128)S(1)}, f32[128,128]{1,0:T(8,128)S(1)}, u32[]{:S(2)}, u32[]{:S(2)}) collective-permute-start(f32[128,128]{1,0:T(8,128)S(1)} %bitcast_add_fusion.18), channel_id=1, source_target_pairs={{0,2},{2,0},{1,3},{3,1},{4,6},{6,4},{5,7},{7,5},{8,10},{10,8},{9,1... | collective-permute-start | bytes 196616 | tf_op jit(solution)/shard_map/ppermute | solution.py:72
  203.6 4.7 %collective-permute-start.27 = (f32[128,128]{1,0:T(8,128)S(1)}, f32[128,128]{1,0:T(8,128)S(1)}, u32[]{:S(2)}, u32[]{:S(2)}) collective-permute-start(f32[128,128]{1,0:T(8,128)S(1)} %bitcast_add_fusion.17), channel_id=1, source_target_pairs={{0,2},{2,0},{1,3},{3,1},{4,6},{6,4},{5,7},{7,5},{8,10},{10,8},{9,1... | collective-permute-start | bytes 196616 | tf_op jit(solution)/shard_map/ppermute | solution.py:73
  208.4 4.1 %collective-permute-start.28 = (f32[256,128]{1,0:T(8,128)S(1)}, f32[256,128]{1,0:T(8,128)S(1)}, u32[]{:S(2)}, u32[]{:S(2)}) collective-permute-start(f32[256,128]{1,0:T(8,128)S(1)} %get-tuple-element.11), channel_id=1, source_target_pairs={{0,1},{1,0},{2,3},{3,2},{4,5},{5,4},{6,7},{7,6},{8,9},{9,8},{10,11... | collective-permute-start | bytes 393224 | tf_op jit(solution)/shard_map/ppermute | solution.py:72
  211.5 1.3 collective-permute-start.29
  (1 other events, 1.4 us)

commit v3 on v2

--- a/solution.py
+++ b/solution.py
@@ -12,26 +12,26 @@
 PANEL_AXES = ("yhi", "core")
 
 
-def block_sum_kernel(a_index_ref, b_index_ref, out_index_ref, a_ref, b_ref, o_ref):
+def block_sum_kernel(index_ref, a_ref, b_ref, o_ref):
     o_ref[...] = jnp.zeros(o_ref.shape, o_ref.dtype)
-    n_blocks = a_index_ref.shape[0]
+    n_blocks = index_ref.shape[0] // 3
 
     def body(k, carry):
-        a = a_ref[a_index_ref[k]]
-        b = b_ref[b_index_ref[k]]
-        o_ref[out_index_ref[k]] += jnp.dot(a, b, preferred_element_type=jnp.float32)
+        a = a_ref[index_ref[k]]
+        b = b_ref[index_ref[n_blocks + k]]
+        o_ref[index_ref[2 * n_blocks + k]] += jnp.dot(a, b, preferred_element_type=jnp.float32)
         return carry
 
     lax.fori_loop(0, n_blocks, body, 0, unroll=8)
 
 
-def block_sums(lists, a_tiles, b_tiles, n_out):
+def block_sums(index, a_tiles, b_tiles, n_out):
     tile = a_tiles.shape[1]
     width = b_tiles.shape[2]
     return pl.pallas_call(
         block_sum_kernel,
         grid_spec=pltpu.PrefetchScalarGridSpec(
-            num_scalar_prefetch=3,
+            num_scalar_prefetch=1,
             grid=(1,),
             in_specs=[
                 pl.BlockSpec(a_tiles.shape, lambda i, *_: (0, 0, 0)),
@@ -40,7 +40,7 @@
             out_specs=pl.BlockSpec((n_out, tile, width), lambda i, *_: (0, 0, 0)),
         ),
         out_shape=jax.ShapeDtypeStruct((n_out, tile, width), jnp.float32),
-    )(lists[0], lists[1], lists[2], a_tiles, b_tiles)
+    )(index, a_tiles, b_tiles)
 
 
 def ring_reduce_scatter(x, axis, n):
@@ -83,28 +83,33 @@
     width = user_emb0.shape[1]
     user_tiles = user_emb0.astype(jnp.bfloat16).reshape(-1, tile_rows, width)
     n_user_tiles = user_tiles.shape[0]
-    lists = (blk_user.reshape(-1), blk_item.reshape(-1), blk_weight.reshape(-1))
+    users_list = blk_user.reshape(-1)
+    items_list = blk_item.reshape(-1)
+    weights_list = blk_weight.reshape(-1)
     weights_t = jnp.swapaxes(weight_tiles, 1, 2)
 
-    partial = block_sums(
-        (lists[2], lists[0], lists[1]), weights_t, user_tiles, n_users
-    )
-    x = partial.reshape(n_ylo, n_x, n_z, tile_rows, width)
-    x = x.transpose(2, 1, 0, 3, 4).reshape(n_z, n_x * n_ylo * tile_rows, width)
+    item_ylo = items_list // (n_x * n_z)
+    item_x = (items_list // n_z) % n_x
+    item_z = items_list % n_z
+    item_slot = (item_z * n_ylo + item_ylo) * n_x + item_x
+    item_index = jnp.concatenate([weights_list, users_list, item_slot])
+    partial = block_sums(item_index, weights_t, user_tiles, n_users)
+    x = partial.reshape(n_z, n_ylo * n_x * tile_rows, width)
     x = ring_reduce_scatter(x, "z", n_z)
-    x = ring_reduce_scatter(x.reshape(n_x, n_ylo * tile_rows, width), "x", n_x)
-    own_sum = ring_reduce_scatter(x.reshape(n_ylo, tile_rows, width), "ylo", n_ylo)
+    x = lax.all_to_all(x.reshape(n_ylo * n_x, tile_rows, width), ("ylo", "x"), 0, 0, tiled=True)
+    own_sum = x.sum(0)
 
     position = lax.axis_index(USER_AXES)
     own_base = lax.dynamic_slice_in_dim(item_base[0], position * tile_rows, tile_rows, 0)
     own_emb = (1.0 - teleport) * own_sum + teleport * own_base
     own_bf = own_emb.astype(jnp.bfloat16)
-    spread = jnp.broadcast_to(own_bf[None], (n_users, tile_rows, width))
-    item_tiles = lax.all_to_all(spread, USER_AXES, 0, 0, tiled=True)
+    t = lax.all_to_all(jnp.broadcast_to(own_bf[None], (n_z, tile_rows, width)), "z", 0, 0, tiled=True)
+    t = jnp.broadcast_to(t[None], (n_ylo * n_x, n_z, tile_rows, width))
+    t = lax.all_to_all(t, ("ylo", "x"), 0, 0, tiled=True)
+    item_tiles = t.reshape(n_users, tile_rows, width)
 
-    user_part = block_sums(
-        (lists[2], lists[1], lists[0]), weight_tiles, item_tiles, n_user_tiles
-    )
+    user_index = jnp.concatenate([weights_list, items_list, users_list])
+    user_part = block_sums(user_index, weight_tiles, item_tiles, n_user_tiles)
     y = user_part.reshape(n_core, -1, width)
     y = ring_reduce_scatter(y, "core", n_core)
     y = ring_reduce_scatter(y.reshape(n_yhi, -1, width), "yhi", n_yhi)

time: 215 us -> 193 us (0.90)
  waiting for transfers between devices: 76.9 us -> 55.7 us
  blocking collectives: 0 us -> 15.2 us
  starting transfers between devices: 70.5 us -> 55.9 us
    all_to_all x0 -> x1, blocking collectives: none -> 15.2 us  [per_device(): lax.all_to_all(jnp.broadcast_to(own_bf[None], (n_z, tile_rows, width)), '...]
    all_to_all x1 -> x2, waiting for transfers between devices: 36.2 us -> 23.7 us  [the longest x1 16.2 us: per_device(): t = lax.all_to_all(t, ('ylo', 'x'), 0, 0, tiled=True)]
    ppermute x13 -> x9, waiting for transfers between devices: 34.3 us -> 26.8 us  [ring_reduce_scatter(): rl = lax.ppermute(bl, axis, right)]
    ppermute x13 -> x9, starting transfers between devices: 25.2 us -> 18.1 us  [ring_reduce_scatter(): rl = lax.ppermute(bl, axis, right)]
    ppermute x13 -> x9, starting transfers between devices: 27.9 us -> 21.5 us  [ring_reduce_scatter(): rr = lax.ppermute(br, axis, left)]
    reshape x1 -> x0, local copies, waits for them, and re-layouts: 2.46 us -> none  [per_device(): x = partial.reshape(n_ylo, n_x, n_z, tile_rows, width)]
    slice x5 -> x3, local copies, waits for them, and re-layouts: 2.78 us -> 5.06 us  [ring_reduce_scatter(): xl, xr = (x[:, :h], x[:, h:])]
    all_to_all x1 -> x2, starting transfers between devices: 9.92 us -> 8.64 us  [the longest x1 5.04 us: per_device(): lax.all_to_all(x.reshape(n_ylo * n_x, tile_rows, width), ('ylo', 'x'), 0,...]
  transfers between devices with their start and end apart: 31 -> 24, of which waited for: 20 -> 17; matrix products, arithmetic and copies ran while one was open for 6% -> 7% of each run, Pallas kernels for 0% -> 0%
where the time goes in v3:
time: 193 us; the launch traced here: 192 us
  starting transfers between devices  55.9 us (29%)
  waiting for transfers between devices  55.7 us (29%)
  Pallas kernels  30.3 us (16%)
  other arithmetic  20.6 us (11%)
  blocking collectives  15.2 us (8%)
  local copies, waits for them, and re-layouts  13.6 us (7%)
    pallas_call x2, Pallas kernels, block_sums(): pl.pallas_call(block_sum_kernel, grid_spec=pltpu.PrefetchScalarGridSpec(n...  30.3 us
    ppermute x9, waiting for transfers between devices, ring_reduce_scatter(): rl = lax.ppermute(bl, axis, right)  26.8 us
    ppermute x9, starting transfers between devices, ring_reduce_scatter(): rr = lax.ppermute(br, axis, left)  21.5 us
    ppermute x9, starting transfers between devices, ring_reduce_scatter(): rl = lax.ppermute(bl, axis, right)  18.1 us
    all_to_all x1, waiting for transfers between devices, per_device(): t = lax.all_to_all(t, ('ylo', 'x'), 0, 0, tiled=True)  16.2 us
    all_to_all x1, blocking collectives, per_device(): lax.all_to_all(jnp.broadcast_to(own_bf[None], (n_z, tile_rows, width)), '...  15.2 us
    all_to_all x1, waiting for transfers between devices, per_device(): lax.all_to_all(x.reshape(n_ylo * n_x, tile_rows, width), ('ylo', 'x'), 0,...  7.54 us
    add x9, other arithmetic, ring_reduce_scatter(): bl = rl + lax.dynamic_index_in_dim(xl, (i - s - 2) % n, 0, keepdims=False)  6.95 us
  transfers between devices with their start and end apart: 24, of which 17 were waited for; matrix products, arithmetic and copies ran while one was open for 7% of the time, Pallas kernels for 0%

profile of v3, /device:TPU:1, one launch (start us, length us, event | category | flops | bytes accessed | tf_op | source)
XLA Modules:
  0.0 192.3 jit_solution(967551599730323483)
XLA Ops:
  2.8 4.1 %copy.8 = bf16[64,128,128]{1,2,0:T(8,128)(2,1)} copy(bf16[64,128,128]{2,1,0:T(8,128)(2,1)} %a_ref.1) | data formatting | bytes 4194304 | tf_op args[2]
  8.3 15.5 %shard_map.77 = f32[64,128,128]{2,1,0:T(8,128)} custom-call(s32[1152]{0:T(1024)} %get-tuple-element.12.index_ref, bf16[64,128,128]{2,1,0:T(8,128)(2,1)} %bitcast.83, bf16[8,128,128]{2,1,0:T(8,128)(2,1)} %bitcast.86), custom_call_target="tpu_custom_call" | custom-call | tf_op jit(solution)/shard_map/pallas_call | solution.py:31
  23.8 4.0 %fusion.10 = (f32[8,512,128]{2,1,0:T(8,128)}, f32[8,512,128]{2,1,0:T(8,128)S(1)}) fusion(f32[8,1024,128]{2,1,0:T(8,128)} %bitcast.81), kind=kLoop, calls=%fused_computation.62 | loop fusion | bytes 8388608 | tf_op jit(solution)/shard_map/slice | solution.py:49
  28.7 2.5 %collective-permute-start = (f32[512,128]{1,0:T(8,128)S(1)}, f32[512,128]{1,0:T(8,128)S(1)}, u32[]{:S(2)}, u32[]{:S(2)}) collective-permute-start(f32[512,128]{1,0:T(8,128)S(1)} %dynamic-slice_bitcast_fusion.1), channel_id=1, source_target_pairs={{0,4},{4,8},{8,12},{12,16},{16,20},{20,24},{24,28},{28,0},{1,5},{5... | collective-permute-start | bytes 786440 | tf_op jit(solution)/shard_map/ppermute | solution.py:55
  31.2 4.1 %collective-permute-start.7 = (f32[512,128]{1,0:T(8,128)S(1)}, f32[512,128]{1,0:T(8,128)}, u32[]{:S(2)}, u32[]{:S(2)}) collective-permute-start(f32[512,128]{1,0:T(8,128)S(1)} %dynamic-slice_bitcast_fusion), channel_id=1, source_target_pairs={{0,28},{4,0},{8,4},{12,8},{16,12},{20,16},{24,20},{28,24},{1,29},{... | collective-permute-start | bytes 786440 | tf_op jit(solution)/shard_map/ppermute | solution.py:56
  35.3 5.8 %collective-permute-done = f32[512,128]{1,0:T(8,128)S(1)} collective-permute-done((f32[512,128]{1,0:T(8,128)S(1)}, f32[512,128]{1,0:T(8,128)S(1)}, u32[]{:S(2)}, u32[]{:S(2)}) %collective-permute-start) | collective-permute-done | bytes 262176 | tf_op jit(solution)/shard_map/ppermute | solution.py:55
  43.2 2.7 %collective-permute-start.8 = (f32[512,128]{1,0:T(8,128)S(1)}, f32[512,128]{1,0:T(8,128)}, u32[]{:S(2)}, u32[]{:S(2)}) collective-permute-start(f32[512,128]{1,0:T(8,128)S(1)} %bitcast_add_fusion.7), channel_id=1, source_target_pairs={{0,28},{4,0},{8,4},{12,8},{16,12},{20,16},{24,20},{28,24},{1,29},{... | collective-permute-start | bytes 786440 | tf_op jit(solution)/shard_map/ppermute | solution.py:56
  46.0 4.1 %collective-permute-done.1 = f32[512,128]{1,0:T(8,128)S(1)} collective-permute-done((f32[512,128]{1,0:T(8,128)S(1)}, f32[512,128]{1,0:T(8,128)S(1)}, u32[]{:S(2)}, u32[]{:S(2)}) %collective-permute-start.1) | collective-permute-done | bytes 262176 | tf_op jit(solution)/shard_map/ppermute | solution.py:55
  52.1 2.7 %collective-permute-start.9 = (f32[512,128]{1,0:T(8,128)S(1)}, f32[512,128]{1,0:T(8,128)}, u32[]{:S(2)}, u32[]{:S(2)}) collective-permute-start(f32[512,128]{1,0:T(8,128)S(1)} %bitcast_add_fusion.6), channel_id=1, source_target_pairs={{0,28},{4,0},{8,4},{12,8},{16,12},{20,16},{24,20},{28,24},{1,29},{... | collective-permute-start | bytes 786440 | tf_op jit(solution)/shard_map/ppermute | solution.py:56
  54.8 3.2 %collective-permute-done.2 = f32[512,128]{1,0:T(8,128)S(1)} collective-permute-done((f32[512,128]{1,0:T(8,128)S(1)}, f32[512,128]{1,0:T(8,128)S(1)}, u32[]{:S(2)}, u32[]{:S(2)}) %collective-permute-start.2) | collective-permute-done | bytes 262176 | tf_op jit(solution)/shard_map/ppermute | solution.py:55
  60.1 2.7 %collective-permute-start.10 = (f32[512,128]{1,0:T(8,128)S(1)}, f32[512,128]{1,0:T(8,128)}, u32[]{:S(2)}, u32[]{:S(2)}) collective-permute-start(f32[512,128]{1,0:T(8,128)S(1)} %bitcast_add_fusion.5), channel_id=1, source_target_pairs={{0,28},{4,0},{8,4},{12,8},{16,12},{20,16},{24,20},{28,24},{1,29},{... | collective-permute-start | bytes 786440 | tf_op jit(solution)/shard_map/ppermute | solution.py:56
  62.8 2.7 %collective-permute-done.3 = f32[512,128]{1,0:T(8,128)S(1)} collective-permute-done((f32[512,128]{1,0:T(8,128)S(1)}, f32[512,128]{1,0:T(8,128)S(1)}, u32[]{:S(2)}, u32[]{:S(2)}) %collective-permute-start.3) | collective-permute-done | bytes 262176 | tf_op jit(solution)/shard_map/ppermute | solution.py:55
  67.6 2.8 %collective-permute-start.11 = (f32[512,128]{1,0:T(8,128)S(1)}, f32[512,128]{1,0:T(8,128)}, u32[]{:S(2)}, u32[]{:S(2)}) collective-permute-start(f32[512,128]{1,0:T(8,128)S(1)} %bitcast_add_fusion.4), channel_id=1, source_target_pairs={{0,28},{4,0},{8,4},{12,8},{16,12},{20,16},{24,20},{28,24},{1,29},{... | collective-permute-start | bytes 786440 | tf_op jit(solution)/shard_map/ppermute | solution.py:56
  70.4 2.6 %collective-permute-done.4 = f32[512,128]{1,0:T(8,128)S(1)} collective-permute-done((f32[512,128]{1,0:T(8,128)S(1)}, f32[512,128]{1,0:T(8,128)S(1)}, u32[]{:S(2)}, u32[]{:S(2)}) %collective-permute-start.4) | collective-permute-done | bytes 262176 | tf_op jit(solution)/shard_map/ppermute | solution.py:55
  75.1 2.9 %collective-permute-start.12 = (f32[512,128]{1,0:T(8,128)S(1)}, f32[512,128]{1,0:T(8,128)}, u32[]{:S(2)}, u32[]{:S(2)}) collective-permute-start(f32[512,128]{1,0:T(8,128)S(1)} %bitcast_add_fusion.3), channel_id=1, source_target_pairs={{0,28},{4,0},{8,4},{12,8},{16,12},{20,16},{24,20},{28,24},{1,29},{... | collective-permute-start | bytes 786440 | tf_op jit(solution)/shard_map/ppermute | solution.py:56
  78.0 2.6 %collective-permute-done.5 = f32[512,128]{1,0:T(8,128)} collective-permute-done((f32[512,128]{1,0:T(8,128)S(1)}, f32[512,128]{1,0:T(8,128)}, u32[]{:S(2)}, u32[]{:S(2)}) %collective-permute-start.5) | collective-permute-done | bytes 262176 | tf_op jit(solution)/shard_map/ppermute | solution.py:55
  82.7 3.1 %collective-permute-start.13 = (f32[512,128]{1,0:T(8,128)S(1)}, f32[512,128]{1,0:T(8,128)}, u32[]{:S(2)}, u32[]{:S(2)}) collective-permute-start(f32[512,128]{1,0:T(8,128)S(1)} %bitcast_add_fusion.2), channel_id=1, source_target_pairs={{0,28},{4,0},{8,4},{12,8},{16,12},{20,16},{24,20},{28,24},{1,29},{... | collective-permute-start | bytes 786440 | tf_op jit(solution)/shard_map/ppermute | solution.py:56
  85.9 3.2 %collective-permute-done.6 = f32[512,128]{1,0:T(8,128)S(1)} collective-permute-done((f32[512,128]{1,0:T(8,128)S(1)}, f32[512,128]{1,0:T(8,128)S(1)}, u32[]{:S(2)}, u32[]{:S(2)}) %collective-permute-start.6) | collective-permute-done | bytes 262176 | tf_op jit(solution)/shard_map/ppermute | solution.py:55
  92.1 5.0 %all-to-all-start = ((f32[8,128,128]{2,1,0:T(8,128)}), f32[8,128,128]{2,1,0:T(8,128)S(1)}, u32[]{:S(2)}, u32[]{:S(2)}) async-start(f32[8,128,128]{2,1,0:T(8,128)} %bitcast.19), calls=%async_computation | async-start | bytes 1048576 | tf_op jit(solution)/shard_map/all_to_all | solution.py:99
  97.1 7.5 %all-to-all-done = f32[8,128,128]{2,1,0:T(8,128)S(1)} async-done(((f32[8,128,128]{2,1,0:T(8,128)}), f32[8,128,128]{2,1,0:T(8,128)S(1)}, u32[]{:S(2)}, u32[]{:S(2)}) %all-to-all-start) | async-done | bytes 524320 | tf_op jit(solution)/shard_map/all_to_all | solution.py:99
  104.7 1.5 convert_bitcast_fusion
  106.2 15.2 %all_to_all.15 = bf16[8,128,128]{2,1,0:T(8,128)(2,1)S(1)} all-to-all(bf16[8,128,128]{2,1,0:T(8,128)(2,1)S(1)} %broadcast_in_dim.44), channel_id=1, replica_groups=mesh['ylo'=2,'x'=4,'z'=8,'yhi'=2,'core'=2] {'z'}, dimensions={0} | all-to-all | bytes 524288 | tf_op jit(solution)/shard_map/all_to_all | solution.py:106
  121.4 1.8 broadcast_in_dim.45
  123.3 3.6 %all-to-all-start.2 = ((bf16[8,8,128,128]{3,2,1,0:T(8,128)(2,1)}), bf16[8,8,128,128]{3,2,1,0:T(8,128)(2,1)S(1)}, u32[]{:S(2)}, u32[]{:S(2)}) async-start(bf16[8,8,128,128]{3,2,1,0:T(8,128)(2,1)} %broadcast_in_dim.45), calls=%async_computation.2 | async-start | bytes 4194304 | tf_op jit(solution)/shard_map/all_to_all | solution.py:108
  126.9 16.2 %all-to-all-done.2 = bf16[8,8,128,128]{3,2,1,0:T(8,128)(2,1)S(1)} async-done(((bf16[8,8,128,128]{3,2,1,0:T(8,128)(2,1)}), bf16[8,8,128,128]{3,2,1,0:T(8,128)(2,1)S(1)}, u32[]{:S(2)}, u32[]{:S(2)}) %all-to-all-start.2) | async-done | bytes 2097184 | tf_op jit(solution)/shard_map/all_to_all | solution.py:108
  144.4 14.8 %shard_map.78 = f32[8,128,128]{2,1,0:T(8,128)} custom-call(s32[1152]{0:T(1024)} %get-tuple-element.13.index_ref, bf16[64,128,128]{2,1,0:T(8,128)(2,1)} %a_ref.1, bf16[64,128,128]{2,1,0:T(8,128)(2,1)} %bitcast.82), custom_call_target="tpu_custom_call" | custom-call | tf_op jit(solution)/shard_map/pallas_call | solution.py:31
  160.3 12.1 %collective-permute-start.14 = (f32[256,128]{1,0:T(8,128)S(1)}, f32[256,128]{1,0:T(8,128)S(1)}, u32[]{:S(2)}, u32[]{:S(2)}) collective-permute-start(f32[256,128]{1,0:T(8,128)S(1)} %dynamic-slice_bitcast_fusion.3), channel_id=1, source_target_pairs={{0,1},{1,0},{2,3},{3,2},{4,5},{5,4},{6,7},{7,6},{8,9},{9,8},{10,11... | collective-permute-start | bytes 393224 | tf_op jit(solution)/shard_map/ppermute | solution.py:55
  174.0 3.0 %collective-permute-start.16 = (f32[128,128]{1,0:T(8,128)S(1)}, f32[128,128]{1,0:T(8,128)S(1)}, u32[]{:S(2)}, u32[]{:S(2)}) collective-permute-start(f32[128,128]{1,0:T(8,128)S(1)} %dynamic-slice_bitcast_fusion.5), channel_id=1, source_target_pairs={{0,2},{2,0},{1,3},{3,1},{4,6},{6,4},{5,7},{7,5},{8,10},{10,8},{9,1... | collective-permute-start | bytes 196616 | tf_op jit(solution)/shard_map/ppermute | solution.py:55
  177.1 1.9 %collective-permute-done.16 = f32[128,128]{1,0:T(8,128)S(1)} collective-permute-done((f32[128,128]{1,0:T(8,128)S(1)}, f32[128,128]{1,0:T(8,128)S(1)}, u32[]{:S(2)}, u32[]{:S(2)}) %collective-permute-start.16) | collective-permute-done | bytes 65568 | tf_op jit(solution)/shard_map/ppermute | solution.py:55
  179.1 3.0 %collective-permute-start.18 = (f32[128,128]{1,0:T(8,128)S(1)}, f32[128,128]{1,0:T(8,128)S(1)}, u32[]{:S(2)}, u32[]{:S(2)}) collective-permute-start(f32[128,128]{1,0:T(8,128)S(1)} %bitcast_add_fusion.18), channel_id=1, source_target_pairs={{0,2},{2,0},{1,3},{3,1},{4,6},{6,4},{5,7},{7,5},{8,10},{10,8},{9,1... | collective-permute-start | bytes 196616 | tf_op jit(solution)/shard_map/ppermute | solution.py:72
  183.8 3.0 %collective-permute-done.19 = f32[128,128]{1,0:T(8,128)S(1)} collective-permute-done((f32[128,128]{1,0:T(8,128)S(1)}, f32[128,128]{1,0:T(8,128)S(1)}, u32[]{:S(2)}, u32[]{:S(2)}) %collective-permute-start.19) | collective-permute-done | bytes 65568 | tf_op jit(solution)/shard_map/ppermute | solution.py:73
  186.9 3.1 %collective-permute-start.20 = (f32[256,128]{1,0:T(8,128)S(1)}, f32[256,128]{1,0:T(8,128)S(1)}, u32[]{:S(2)}, u32[]{:S(2)}) collective-permute-start(f32[256,128]{1,0:T(8,128)S(1)} %get-tuple-element.9), channel_id=1, source_target_pairs={{0,1},{1,0},{2,3},{3,2},{4,5},{5,4},{6,7},{7,6},{8,9},{9,8},{10,11... | collective-permute-start | bytes 393224 | tf_op jit(solution)/shard_map/ppermute | solution.py:72
  (74 shorter events, 27.9 us)
Async XLA Ops:
  2.8 4.1 %copy-start.1 = (f32[1024,128]{1,0:T(8,128)S(1)}, f32[1024,128]{1,0:T(8,128)}, u32[]{:S(2)}) copy-start(f32[1024,128]{1,0:T(8,128)} %param.6) | copy-start | bytes 1572868
  28.7 12.4 %collective-permute-start = (f32[512,128]{1,0:T(8,128)S(1)}, f32[512,128]{1,0:T(8,128)S(1)}, u32[]{:S(2)}, u32[]{:S(2)}) collective-permute-start(f32[512,128]{1,0:T(8,128)S(1)} %dynamic-slice_bitcast_fusion.1), channel_id=1, source_target_pairs={{0,4},{4,8},{8,12},{12,16},{16,20},{20,24},{24,28},{28,0},{1,5},{5... | collective-permute-start | bytes 786440 | tf_op jit(solution)/shard_map/ppermute | solution.py:55
  31.2 11.0 %collective-permute-start.7 = (f32[512,128]{1,0:T(8,128)S(1)}, f32[512,128]{1,0:T(8,128)}, u32[]{:S(2)}, u32[]{:S(2)}) collective-permute-start(f32[512,128]{1,0:T(8,128)S(1)} %dynamic-slice_bitcast_fusion), channel_id=1, source_target_pairs={{0,28},{4,0},{8,4},{12,8},{16,12},{20,16},{24,20},{28,24},{1,29},{... | collective-permute-start | bytes 786440 | tf_op jit(solution)/shard_map/ppermute | solution.py:56
  42.1 7.9 %collective-permute-start.1 = (f32[512,128]{1,0:T(8,128)S(1)}, f32[512,128]{1,0:T(8,128)S(1)}, u32[]{:S(2)}, u32[]{:S(2)}) collective-permute-start(f32[512,128]{1,0:T(8,128)S(1)} %bitcast_add_fusion.14), channel_id=1, source_target_pairs={{0,4},{4,8},{8,12},{12,16},{16,20},{20,24},{24,28},{28,0},{1,5},{5... | collective-permute-start | bytes 786440 | tf_op jit(solution)/shard_map/ppermute | solution.py:55
  43.2 7.9 %collective-permute-start.8 = (f32[512,128]{1,0:T(8,128)S(1)}, f32[512,128]{1,0:T(8,128)}, u32[]{:S(2)}, u32[]{:S(2)}) collective-permute-start(f32[512,128]{1,0:T(8,128)S(1)} %bitcast_add_fusion.7), channel_id=1, source_target_pairs={{0,28},{4,0},{8,4},{12,8},{16,12},{20,16},{24,20},{28,24},{1,29},{... | collective-permute-start | bytes 786440 | tf_op jit(solution)/shard_map/ppermute | solution.py:56
  51.0 7.0 %collective-permute-start.2 = (f32[512,128]{1,0:T(8,128)S(1)}, f32[512,128]{1,0:T(8,128)S(1)}, u32[]{:S(2)}, u32[]{:S(2)}) collective-permute-start(f32[512,128]{1,0:T(8,128)S(1)} %bitcast_add_fusion.13), channel_id=1, source_target_pairs={{0,4},{4,8},{8,12},{12,16},{16,20},{20,24},{24,28},{28,0},{1,5},{5... | collective-permute-start | bytes 786440 | tf_op jit(solution)/shard_map/ppermute | solution.py:55
  52.1 7.0 %collective-permute-start.9 = (f32[512,128]{1,0:T(8,128)S(1)}, f32[512,128]{1,0:T(8,128)}, u32[]{:S(2)}, u32[]{:S(2)}) collective-permute-start(f32[512,128]{1,0:T(8,128)S(1)} %bitcast_add_fusion.6), channel_id=1, source_target_pairs={{0,28},{4,0},{8,4},{12,8},{16,12},{20,16},{24,20},{28,24},{1,29},{... | collective-permute-start | bytes 786440 | tf_op jit(solution)/shard_map/ppermute | solution.py:56
  59.0 6.5 %collective-permute-start.3 = (f32[512,128]{1,0:T(8,128)S(1)}, f32[512,128]{1,0:T(8,128)S(1)}, u32[]{:S(2)}, u32[]{:S(2)}) collective-permute-start(f32[512,128]{1,0:T(8,128)S(1)} %bitcast_add_fusion.12), channel_id=1, source_target_pairs={{0,4},{4,8},{8,12},{12,16},{16,20},{20,24},{24,28},{28,0},{1,5},{5... | collective-permute-start | bytes 786440 | tf_op jit(solution)/shard_map/ppermute | solution.py:55
  60.1 6.5 %collective-permute-start.10 = (f32[512,128]{1,0:T(8,128)S(1)}, f32[512,128]{1,0:T(8,128)}, u32[]{:S(2)}, u32[]{:S(2)}) collective-permute-start(f32[512,128]{1,0:T(8,128)S(1)} %bitcast_add_fusion.5), channel_id=1, source_target_pairs={{0,28},{4,0},{8,4},{12,8},{16,12},{20,16},{24,20},{28,24},{1,29},{... | collective-permute-start | bytes 786440 | tf_op jit(solution)/shard_map/ppermute | solution.py:56
  66.5 6.5 %collective-permute-start.4 = (f32[512,128]{1,0:T(8,128)S(1)}, f32[512,128]{1,0:T(8,128)S(1)}, u32[]{:S(2)}, u32[]{:S(2)}) collective-permute-start(f32[512,128]{1,0:T(8,128)S(1)} %bitcast_add_fusion.11), channel_id=1, source_target_pairs={{0,4},{4,8},{8,12},{12,16},{16,20},{20,24},{24,28},{28,0},{1,5},{5... | collective-permute-start | bytes 786440 | tf_op jit(solution)/shard_map/ppermute | solution.py:55
  67.6 6.5 %collective-permute-start.11 = (f32[512,128]{1,0:T(8,128)S(1)}, f32[512,128]{1,0:T(8,128)}, u32[]{:S(2)}, u32[]{:S(2)}) collective-permute-start(f32[512,128]{1,0:T(8,128)S(1)} %bitcast_add_fusion.4), channel_id=1, source_target_pairs={{0,28},{4,0},{8,4},{12,8},{16,12},{20,16},{24,20},{28,24},{1,29},{... | collective-permute-start | bytes 786440 | tf_op jit(solution)/shard_map/ppermute | solution.py:56
  74.0 6.6 %collective-permute-start.5 = (f32[512,128]{1,0:T(8,128)S(1)}, f32[512,128]{1,0:T(8,128)}, u32[]{:S(2)}, u32[]{:S(2)}) collective-permute-start(f32[512,128]{1,0:T(8,128)S(1)} %bitcast_add_fusion.10), channel_id=1, source_target_pairs={{0,4},{4,8},{8,12},{12,16},{16,20},{20,24},{24,28},{28,0},{1,5},{5... | collective-permute-start | bytes 786440 | tf_op jit(solution)/shard_map/ppermute | solution.py:55
  75.1 6.7 %collective-permute-start.12 = (f32[512,128]{1,0:T(8,128)S(1)}, f32[512,128]{1,0:T(8,128)}, u32[]{:S(2)}, u32[]{:S(2)}) collective-permute-start(f32[512,128]{1,0:T(8,128)S(1)} %bitcast_add_fusion.3), channel_id=1, source_target_pairs={{0,28},{4,0},{8,4},{12,8},{16,12},{20,16},{24,20},{28,24},{1,29},{... | collective-permute-start | bytes 786440 | tf_op jit(solution)/shard_map/ppermute | solution.py:56
  81.6 7.4 %collective-permute-start.6 = (f32[512,128]{1,0:T(8,128)S(1)}, f32[512,128]{1,0:T(8,128)S(1)}, u32[]{:S(2)}, u32[]{:S(2)}) collective-permute-start(f32[512,128]{1,0:T(8,128)S(1)} %bitcast_add_fusion.9), channel_id=1, source_target_pairs={{0,4},{4,8},{8,12},{12,16},{16,20},{20,24},{24,28},{28,0},{1,5},{5... | collective-permute-start | bytes 786440 | tf_op jit(solution)/shard_map/ppermute | solution.py:55
  82.7 7.5 %collective-permute-start.13 = (f32[512,128]{1,0:T(8,128)S(1)}, f32[512,128]{1,0:T(8,128)}, u32[]{:S(2)}, u32[]{:S(2)}) collective-permute-start(f32[512,128]{1,0:T(8,128)S(1)} %bitcast_add_fusion.2), channel_id=1, source_target_pairs={{0,28},{4,0},{8,4},{12,8},{16,12},{20,16},{24,20},{28,24},{1,29},{... | collective-permute-start | bytes 786440 | tf_op jit(solution)/shard_map/ppermute | solution.py:56
  92.1 12.6 %all-to-all-start = ((f32[8,128,128]{2,1,0:T(8,128)}), f32[8,128,128]{2,1,0:T(8,128)S(1)}, u32[]{:S(2)}, u32[]{:S(2)}) async-start(f32[8,128,128]{2,1,0:T(8,128)} %bitcast.19), calls=%async_computation | async-start | bytes 1048576 | tf_op jit(solution)/shard_map/all_to_all | solution.py:99
  123.3 19.8 %all-to-all-start.2 = ((bf16[8,8,128,128]{3,2,1,0:T(8,128)(2,1)}), bf16[8,8,128,128]{3,2,1,0:T(8,128)(2,1)S(1)}, u32[]{:S(2)}, u32[]{:S(2)}) async-start(bf16[8,8,128,128]{3,2,1,0:T(8,128)(2,1)} %broadcast_in_dim.45), calls=%async_computation.2 | async-start | bytes 4194304 | tf_op jit(solution)/shard_map/all_to_all | solution.py:108
  143.1 1.3 copy-start
  160.3 13.1 %collective-permute-start.14 = (f32[256,128]{1,0:T(8,128)S(1)}, f32[256,128]{1,0:T(8,128)S(1)}, u32[]{:S(2)}, u32[]{:S(2)}) collective-permute-start(f32[256,128]{1,0:T(8,128)S(1)} %dynamic-slice_bitcast_fusion.3), channel_id=1, source_target_pairs={{0,1},{1,0},{2,3},{3,2},{4,5},{5,4},{6,7},{7,6},{8,9},{9,8},{10,11... | collective-permute-start | bytes 393224 | tf_op jit(solution)/shard_map/ppermute | solution.py:55
  172.4 1.4 collective-permute-start.15
  174.0 5.1 %collective-permute-start.16 = (f32[128,128]{1,0:T(8,128)S(1)}, f32[128,128]{1,0:T(8,128)S(1)}, u32[]{:S(2)}, u32[]{:S(2)}) collective-permute-start(f32[128,128]{1,0:T(8,128)S(1)} %dynamic-slice_bitcast_fusion.5), channel_id=1, source_target_pairs={{0,2},{2,0},{1,3},{3,1},{4,6},{6,4},{5,7},{7,5},{8,10},{10,8},{9,1... | collective-permute-start | bytes 196616 | tf_op jit(solution)/shard_map/ppermute | solution.py:55
  177.0 5.1 %collective-permute-start.17 = (f32[128,128]{1,0:T(8,128)S(1)}, f32[128,128]{1,0:T(8,128)S(1)}, u32[]{:S(2)}, u32[]{:S(2)}) collective-permute-start(f32[128,128]{1,0:T(8,128)S(1)} %dynamic-slice_bitcast_fusion.4), channel_id=1, source_target_pairs={{0,2},{2,0},{1,3},{3,1},{4,6},{6,4},{5,7},{7,5},{8,10},{10,8},{9,1... | collective-permute-start | bytes 196616 | tf_op jit(solution)/shard_map/ppermute | solution.py:56
  179.1 4.7 %collective-permute-start.18 = (f32[128,128]{1,0:T(8,128)S(1)}, f32[128,128]{1,0:T(8,128)S(1)}, u32[]{:S(2)}, u32[]{:S(2)}) collective-permute-start(f32[128,128]{1,0:T(8,128)S(1)} %bitcast_add_fusion.18), channel_id=1, source_target_pairs={{0,2},{2,0},{1,3},{3,1},{4,6},{6,4},{5,7},{7,5},{8,10},{10,8},{9,1... | collective-permute-start | bytes 196616 | tf_op jit(solution)/shard_map/ppermute | solution.py:72
  182.1 4.7 %collective-permute-start.19 = (f32[128,128]{1,0:T(8,128)S(1)}, f32[128,128]{1,0:T(8,128)S(1)}, u32[]{:S(2)}, u32[]{:S(2)}) collective-permute-start(f32[128,128]{1,0:T(8,128)S(1)} %bitcast_add_fusion.17), channel_id=1, source_target_pairs={{0,2},{2,0},{1,3},{3,1},{4,6},{6,4},{5,7},{7,5},{8,10},{10,8},{9,1... | collective-permute-start | bytes 196616 | tf_op jit(solution)/shard_map/ppermute | solution.py:73
  186.9 4.1 %collective-permute-start.20 = (f32[256,128]{1,0:T(8,128)S(1)}, f32[256,128]{1,0:T(8,128)S(1)}, u32[]{:S(2)}, u32[]{:S(2)}) collective-permute-start(f32[256,128]{1,0:T(8,128)S(1)} %get-tuple-element.9), channel_id=1, source_target_pairs={{0,1},{1,0},{2,3},{3,2},{4,5},{5,4},{6,7},{7,6},{8,9},{9,8},{10,11... | collective-permute-start | bytes 393224 | tf_op jit(solution)/shard_map/ppermute | solution.py:72
  190.0 1.3 collective-permute-start.21

commit v4 on v3

--- a/solution.py
+++ b/solution.py
@@ -12,24 +12,29 @@
 PANEL_AXES = ("yhi", "core")
 
 
-def block_sum_kernel(index_ref, a_ref, b_ref, o_ref):
+def block_sum_kernel(index_ref, a_ref, b_ref, o_ref, *, b_transposed):
     o_ref[...] = jnp.zeros(o_ref.shape, o_ref.dtype)
     n_blocks = index_ref.shape[0] // 3
 
     def body(k, carry):
         a = a_ref[index_ref[k]]
         b = b_ref[index_ref[n_blocks + k]]
-        o_ref[index_ref[2 * n_blocks + k]] += jnp.dot(a, b, preferred_element_type=jnp.float32)
+        contract = ((1,), (1,) if b_transposed else (0,))
+        o_ref[index_ref[2 * n_blocks + k]] += lax.dot_general(
+            a, b, (contract, ((), ())), preferred_element_type=jnp.float32
+        )
         return carry
 
     lax.fori_loop(0, n_blocks, body, 0, unroll=8)
 
 
-def block_sums(index, a_tiles, b_tiles, n_out):
+def block_sums(index, a_tiles, b_tiles, n_out, b_transposed=False):
+    import functools
+
     tile = a_tiles.shape[1]
-    width = b_tiles.shape[2]
+    width = b_tiles.shape[1] if b_transposed else b_tiles.shape[2]
     return pl.pallas_call(
-        block_sum_kernel,
+        functools.partial(block_sum_kernel, b_transposed=b_transposed),
         grid_spec=pltpu.PrefetchScalarGridSpec(
             num_scalar_prefetch=1,
             grid=(1,),
@@ -44,9 +49,12 @@
 
 
 def ring_reduce_scatter(x, axis, n):
+    h = x.shape[1] // 2
+    return jnp.concatenate(ring_reduce_scatter_halves(x[:, :h], x[:, h:], axis, n), 0)
+
+
+def ring_reduce_scatter_halves(xl, xr, axis, n):
     i = lax.axis_index(axis)
-    h = x.shape[1] // 2
-    xl, xr = x[:, :h], x[:, h:]
     right = [(j, (j + 1) % n) for j in range(n)]
     left = [(j, (j - 1) % n) for j in range(n)]
     bl = lax.dynamic_index_in_dim(xl, (i - 1) % n, 0, keepdims=False)
@@ -56,7 +64,7 @@
         rr = lax.ppermute(br, axis, left)
         bl = rl + lax.dynamic_index_in_dim(xl, (i - s - 2) % n, 0, keepdims=False)
         br = rr + lax.dynamic_index_in_dim(xr, (i + s + 2) % n, 0, keepdims=False)
-    return jnp.concatenate([bl, br], 0)
+    return bl, br
 
 
 def ring_all_gather(x, axis, n):
@@ -81,35 +89,35 @@
     n_users = n_ylo * n_x * n_z
     tile_rows = weight_tiles.shape[1]
     width = user_emb0.shape[1]
-    user_tiles = user_emb0.astype(jnp.bfloat16).reshape(-1, tile_rows, width)
-    n_user_tiles = user_tiles.shape[0]
+    n_user_tiles = user_emb0.shape[0] // tile_rows
+    user_tiles_t = jnp.swapaxes(user_emb0.astype(jnp.bfloat16).reshape(-1, tile_rows, width), 1, 2)
     users_list = blk_user.reshape(-1)
     items_list = blk_item.reshape(-1)
     weights_list = blk_weight.reshape(-1)
-    weights_t = jnp.swapaxes(weight_tiles, 1, 2)
 
     item_ylo = items_list // (n_x * n_z)
     item_x = (items_list // n_z) % n_x
     item_z = items_list % n_z
-    item_slot = (item_z * n_ylo + item_ylo) * n_x + item_x
-    item_index = jnp.concatenate([weights_list, users_list, item_slot])
-    partial = block_sums(item_index, weights_t, user_tiles, n_users)
-    x = partial.reshape(n_z, n_ylo * n_x * tile_rows, width)
-    x = ring_reduce_scatter(x, "z", n_z)
-    x = lax.all_to_all(x.reshape(n_ylo * n_x, tile_rows, width), ("ylo", "x"), 0, 0, tiled=True)
-    own_sum = x.sum(0)
+    item_slot = (item_ylo * n_z + item_z) * n_x + item_x
+    item_index = jnp.concatenate([users_list, weights_list, item_slot])
+    partial_t = block_sums(item_index, user_tiles_t, weight_tiles, n_users)
+    halves = partial_t.reshape(n_ylo, n_z, n_x * tile_rows, width)
+    bl, br = ring_reduce_scatter_halves(halves[0], halves[1], "z", n_z)
+    x = jnp.concatenate([bl, br], 0).reshape(n_ylo * n_x, tile_rows, width)
+    x = lax.all_to_all(x, ("ylo", "x"), 0, 0, tiled=True)
+    own_sum = x.sum(0).T
 
     position = lax.axis_index(USER_AXES)
     own_base = lax.dynamic_slice_in_dim(item_base[0], position * tile_rows, tile_rows, 0)
     own_emb = (1.0 - teleport) * own_sum + teleport * own_base
-    own_bf = own_emb.astype(jnp.bfloat16)
-    t = lax.all_to_all(jnp.broadcast_to(own_bf[None], (n_z, tile_rows, width)), "z", 0, 0, tiled=True)
-    t = jnp.broadcast_to(t[None], (n_ylo * n_x, n_z, tile_rows, width))
+    own_bf_t = own_emb.astype(jnp.bfloat16).T
+    t = lax.all_to_all(jnp.broadcast_to(own_bf_t[None], (n_z, width, tile_rows)), "z", 0, 0, tiled=True)
+    t = jnp.broadcast_to(t[None], (n_ylo * n_x, n_z, width, tile_rows))
     t = lax.all_to_all(t, ("ylo", "x"), 0, 0, tiled=True)
-    item_tiles = t.reshape(n_users, tile_rows, width)
+    item_tiles_t = t.reshape(n_users, width, tile_rows)
 
     user_index = jnp.concatenate([weights_list, items_list, users_list])
-    user_part = block_sums(user_index, weight_tiles, item_tiles, n_user_tiles)
+    user_part = block_sums(user_index, weight_tiles, item_tiles_t, n_user_tiles, b_transposed=True)
     y = user_part.reshape(n_core, -1, width)
     y = ring_reduce_scatter(y, "core", n_core)
     y = ring_reduce_scatter(y.reshape(n_yhi, -1, width), "yhi", n_yhi)

time: 193 us -> 191 us (0.990)
  other arithmetic: 20.6 us -> 12.7 us
  waiting for transfers between devices: 55.7 us -> 60.9 us
  Pallas kernels: 30.3 us -> 34 us
    add x19, other arithmetic: 13.9 us -> 7.15 us  [the longest x9 6.87 us: ring_reduce_scatter_halves(): bl = rl + lax.dynamic_index_in_dim(xl, (i - s - 2) % n, 0, keepdims=False)]
    ppermute x18, waiting for transfers between devices: 27.5 us -> 33.6 us  [the longest x9 33.1 us: ring_reduce_scatter_halves(): rl = lax.ppermute(bl, axis, right)]
    pallas_call x2, Pallas kernels: 30.3 us -> 34 us  [block_sums(): pl.pallas_call(functools.partial(block_sum_kernel, b_transposed=b_transpo...]
    unnamed x5 -> x6, local copies, waits for them, and re-layouts: 5.47 us -> 2.15 us
  transfers between devices with their start and end apart: 24 -> 24, of which waited for: 17 -> 16; matrix products, arithmetic and copies ran while one was open for 7% -> 5% of each run, Pallas kernels for 0% -> 0%
where the time goes in v4:
time: 191 us; the launch traced here: 190 us
  waiting for transfers between devices  60.9 us (32%)
  starting transfers between devices  55.3 us (29%)
  Pallas kernels  34 us (18%)
  blocking collectives  14 us (7%)
  other arithmetic  12.7 us (7%)
  local copies, waits for them, and re-layouts  12 us (6%)
    pallas_call x2, Pallas kernels, block_sums(): pl.pallas_call(functools.partial(block_sum_kernel, b_transposed=b_transpo...  34 us
    ppermute x9, waiting for transfers between devices, ring_reduce_scatter_halves(): rl = lax.ppermute(bl, axis, right)  33.1 us
    ppermute x9, starting transfers between devices, ring_reduce_scatter_halves(): rr = lax.ppermute(br, axis, left)  20.9 us
    ppermute x9, starting transfers between devices, ring_reduce_scatter_halves(): rl = lax.ppermute(bl, axis, right)  18 us
    all_to_all x1, waiting for transfers between devices, per_device(): t = lax.all_to_all(t, ('ylo', 'x'), 0, 0, tiled=True)  16.2 us
    all_to_all x1, blocking collectives, per_device(): lax.all_to_all(jnp.broadcast_to(own_bf_t[None], (n_z, width, tile_rows)),...  14 us
    add x9, other arithmetic, ring_reduce_scatter_halves(): bl = rl + lax.dynamic_index_in_dim(xl, (i - s - 2) % n, 0, keepdims=False)  6.87 us
    all_to_all x1, waiting for transfers between devices, per_device(): x = lax.all_to_all(x, ('ylo', 'x'), 0, 0, tiled=True)  6.6 us
  transfers between devices with their start and end apart: 24, of which 16 were waited for; matrix products, arithmetic and copies ran while one was open for 5% of the time, Pallas kernels for 0%

profile of v4, /device:TPU:1, one launch (start us, length us, event | category | flops | bytes accessed | tf_op | source)
XLA Modules:
  0.0 190.0 jit_solution(16183676438135955886)
XLA Ops:
  5.3 15.6 %shard_map.77 = f32[64,128,128]{2,1,0:T(8,128)} custom-call(s32[1152]{0:T(1024)} %get-tuple-element.14.index_ref, bf16[8,128,128]{2,1,0:T(8,128)(2,1)} %bitcast.112, bf16[64,128,128]{2,1,0:T(8,128)(2,1)} %a_ref.1), custom_call_target="tpu_custom_call" | custom-call | tf_op jit(solution)/shard_map/pallas_call | solution.py:36
  20.9 4.1 %fusion.9 = (f32[32,128,128]{2,1,0:T(8,128)}, f32[32,128,128]{2,1,0:T(8,128)S(1)}) fusion(f32[64,128,128]{2,1,0:T(8,128)} %shard_map.77), kind=kLoop, calls=%fused_computation.62 | loop fusion | bytes 8388608 | tf_op jit(solution)/shard_map/slice | solution.py:105
  25.9 2.6 %collective-permute-start = (f32[512,128]{1,0:T(8,128)S(1)}, f32[512,128]{1,0:T(8,128)S(1)}, u32[]{:S(2)}, u32[]{:S(2)}) collective-permute-start(f32[512,128]{1,0:T(8,128)S(1)} %dynamic-slice_bitcast_fusion.1), channel_id=1, source_target_pairs={{0,4},{4,8},{8,12},{12,16},{16,20},{20,24},{24,28},{28,0},{1,5},{5... | collective-permute-start | bytes 786440 | tf_op jit(solution)/shard_map/ppermute | solution.py:63
  28.5 4.0 %collective-permute-start.7 = (f32[512,128]{1,0:T(8,128)S(1)}, f32[512,128]{1,0:T(8,128)S(1)}, u32[]{:S(2)}, u32[]{:S(2)}) collective-permute-start(f32[512,128]{1,0:T(8,128)S(1)} %dynamic-slice_bitcast_fusion), channel_id=1, source_target_pairs={{0,28},{4,0},{8,4},{12,8},{16,12},{20,16},{24,20},{28,24},{1,29},{... | collective-permute-start | bytes 786440 | tf_op jit(solution)/shard_map/ppermute | solution.py:64
  32.5 5.8 %collective-permute-done = f32[512,128]{1,0:T(8,128)S(1)} collective-permute-done((f32[512,128]{1,0:T(8,128)S(1)}, f32[512,128]{1,0:T(8,128)S(1)}, u32[]{:S(2)}, u32[]{:S(2)}) %collective-permute-start) | collective-permute-done | bytes 262176 | tf_op jit(solution)/shard_map/ppermute | solution.py:63
  39.5 2.7 %collective-permute-start.8 = (f32[512,128]{1,0:T(8,128)S(1)}, f32[512,128]{1,0:T(8,128)S(1)}, u32[]{:S(2)}, u32[]{:S(2)}) collective-permute-start(f32[512,128]{1,0:T(8,128)S(1)} %bitcast_add_fusion.7), channel_id=1, source_target_pairs={{0,28},{4,0},{8,4},{12,8},{16,12},{20,16},{24,20},{28,24},{1,29},{... | collective-permute-start | bytes 786440 | tf_op jit(solution)/shard_map/ppermute | solution.py:64
  42.2 5.0 %collective-permute-done.1 = f32[512,128]{1,0:T(8,128)S(1)} collective-permute-done((f32[512,128]{1,0:T(8,128)S(1)}, f32[512,128]{1,0:T(8,128)S(1)}, u32[]{:S(2)}, u32[]{:S(2)}) %collective-permute-start.1) | collective-permute-done | bytes 262176 | tf_op jit(solution)/shard_map/ppermute | solution.py:63
  48.3 2.7 %collective-permute-start.9 = (f32[512,128]{1,0:T(8,128)S(1)}, f32[512,128]{1,0:T(8,128)S(1)}, u32[]{:S(2)}, u32[]{:S(2)}) collective-permute-start(f32[512,128]{1,0:T(8,128)S(1)} %bitcast_add_fusion.6), channel_id=1, source_target_pairs={{0,28},{4,0},{8,4},{12,8},{16,12},{20,16},{24,20},{28,24},{1,29},{... | collective-permute-start | bytes 786440 | tf_op jit(solution)/shard_map/ppermute | solution.py:64
  51.0 4.1 %collective-permute-done.2 = f32[512,128]{1,0:T(8,128)S(1)} collective-permute-done((f32[512,128]{1,0:T(8,128)S(1)}, f32[512,128]{1,0:T(8,128)S(1)}, u32[]{:S(2)}, u32[]{:S(2)}) %collective-permute-start.2) | collective-permute-done | bytes 262176 | tf_op jit(solution)/shard_map/ppermute | solution.py:63
  56.3 2.7 %collective-permute-start.10 = (f32[512,128]{1,0:T(8,128)S(1)}, f32[512,128]{1,0:T(8,128)S(1)}, u32[]{:S(2)}, u32[]{:S(2)}) collective-permute-start(f32[512,128]{1,0:T(8,128)S(1)} %bitcast_add_fusion.5), channel_id=1, source_target_pairs={{0,28},{4,0},{8,4},{12,8},{16,12},{20,16},{24,20},{28,24},{1,29},{... | collective-permute-start | bytes 786440 | tf_op jit(solution)/shard_map/ppermute | solution.py:64
  59.0 3.6 %collective-permute-done.3 = f32[512,128]{1,0:T(8,128)S(1)} collective-permute-done((f32[512,128]{1,0:T(8,128)S(1)}, f32[512,128]{1,0:T(8,128)S(1)}, u32[]{:S(2)}, u32[]{:S(2)}) %collective-permute-start.3) | collective-permute-done | bytes 262176 | tf_op jit(solution)/shard_map/ppermute | solution.py:63
  63.8 2.7 %collective-permute-start.11 = (f32[512,128]{1,0:T(8,128)S(1)}, f32[512,128]{1,0:T(8,128)S(1)}, u32[]{:S(2)}, u32[]{:S(2)}) collective-permute-start(f32[512,128]{1,0:T(8,128)S(1)} %bitcast_add_fusion.4), channel_id=1, source_target_pairs={{0,28},{4,0},{8,4},{12,8},{16,12},{20,16},{24,20},{28,24},{1,29},{... | collective-permute-start | bytes 786440 | tf_op jit(solution)/shard_map/ppermute | solution.py:64
  66.5 3.6 %collective-permute-done.4 = f32[512,128]{1,0:T(8,128)S(1)} collective-permute-done((f32[512,128]{1,0:T(8,128)S(1)}, f32[512,128]{1,0:T(8,128)S(1)}, u32[]{:S(2)}, u32[]{:S(2)}) %collective-permute-start.4) | collective-permute-done | bytes 262176 | tf_op jit(solution)/shard_map/ppermute | solution.py:63
  71.3 2.7 %collective-permute-start.12 = (f32[512,128]{1,0:T(8,128)S(1)}, f32[512,128]{1,0:T(8,128)S(1)}, u32[]{:S(2)}, u32[]{:S(2)}) collective-permute-start(f32[512,128]{1,0:T(8,128)S(1)} %bitcast_add_fusion.3), channel_id=1, source_target_pairs={{0,28},{4,0},{8,4},{12,8},{16,12},{20,16},{24,20},{28,24},{1,29},{... | collective-permute-start | bytes 786440 | tf_op jit(solution)/shard_map/ppermute | solution.py:64
  74.0 3.6 %collective-permute-done.5 = f32[512,128]{1,0:T(8,128)S(1)} collective-permute-done((f32[512,128]{1,0:T(8,128)S(1)}, f32[512,128]{1,0:T(8,128)S(1)}, u32[]{:S(2)}, u32[]{:S(2)}) %collective-permute-start.5) | collective-permute-done | bytes 262176 | tf_op jit(solution)/shard_map/ppermute | solution.py:63
  78.8 2.9 %collective-permute-start.13 = (f32[512,128]{1,0:T(8,128)S(1)}, f32[512,128]{1,0:T(8,128)S(1)}, u32[]{:S(2)}, u32[]{:S(2)}) collective-permute-start(f32[512,128]{1,0:T(8,128)S(1)} %bitcast_add_fusion.2), channel_id=1, source_target_pairs={{0,28},{4,0},{8,4},{12,8},{16,12},{20,16},{24,20},{28,24},{1,29},{... | collective-permute-start | bytes 786440 | tf_op jit(solution)/shard_map/ppermute | solution.py:64
  81.7 4.6 %collective-permute-done.6 = f32[512,128]{1,0:T(8,128)S(1)} collective-permute-done((f32[512,128]{1,0:T(8,128)S(1)}, f32[512,128]{1,0:T(8,128)S(1)}, u32[]{:S(2)}, u32[]{:S(2)}) %collective-permute-start.6) | collective-permute-done | bytes 262176 | tf_op jit(solution)/shard_map/ppermute | solution.py:63
  88.1 5.2 %all-to-all-start = ((f32[8,128,128]{2,1,0:T(8,128)}), f32[8,128,128]{2,1,0:T(8,128)S(1)}, u32[]{:S(2)}, u32[]{:S(2)}) async-start(f32[8,128,128]{2,1,0:T(8,128)} %bitcast.20), calls=%async_computation | async-start | bytes 1048576 | tf_op jit(solution)/shard_map/all_to_all | solution.py:107
  94.2 6.6 %all-to-all-done = f32[8,128,128]{2,1,0:T(8,128)S(1)} async-done(((f32[8,128,128]{2,1,0:T(8,128)}), f32[8,128,128]{2,1,0:T(8,128)S(1)}, u32[]{:S(2)}, u32[]{:S(2)}) %all-to-all-start) | async-done | bytes 524320 | tf_op jit(solution)/shard_map/all_to_all | solution.py:107
  100.9 14.0 %all_to_all.15 = bf16[8,128,128]{2,1,0:T(8,128)(2,1)S(1)} all-to-all(bf16[8,128,128]{2,1,0:T(8,128)(2,1)S(1)} %broadcast_in_dim.43), channel_id=1, replica_groups=mesh['ylo'=2,'x'=4,'z'=8,'yhi'=2,'core'=2] {'z'}, dimensions={0} | all-to-all | bytes 524288 | tf_op jit(solution)/shard_map/all_to_all | solution.py:114
  115.0 1.8 broadcast_in_dim.44
  116.8 3.6 %all-to-all-start.2 = ((bf16[8,8,128,128]{3,2,1,0:T(8,128)(2,1)}), bf16[8,8,128,128]{3,2,1,0:T(8,128)(2,1)S(1)}, u32[]{:S(2)}, u32[]{:S(2)}) async-start(bf16[8,8,128,128]{3,2,1,0:T(8,128)(2,1)} %broadcast_in_dim.44), calls=%async_computation.2 | async-start | bytes 4194304 | tf_op jit(solution)/shard_map/all_to_all | solution.py:116
  120.5 16.2 %all-to-all-done.2 = bf16[8,8,128,128]{3,2,1,0:T(8,128)(2,1)S(1)} async-done(((bf16[8,8,128,128]{3,2,1,0:T(8,128)(2,1)}), bf16[8,8,128,128]{3,2,1,0:T(8,128)(2,1)S(1)}, u32[]{:S(2)}, u32[]{:S(2)}) %all-to-all-start.2) | async-done | bytes 2097184 | tf_op jit(solution)/shard_map/all_to_all | solution.py:116
  136.6 1.3 copy-done
  138.0 18.5 %shard_map.78 = f32[8,128,128]{2,1,0:T(8,128)} custom-call(s32[1152]{0:T(1024)} %get-tuple-element.15.index_ref, bf16[64,128,128]{2,1,0:T(8,128)(2,1)} %a_ref.1, bf16[64,128,128]{2,1,0:T(8,128)(2,1)} %bitcast.109), custom_call_target="tpu_custom_call" | custom-call | tf_op jit(solution)/shard_map/pallas_call | solution.py:36
  157.5 11.9 %collective-permute-start.14 = (f32[256,128]{1,0:T(8,128)S(1)}, f32[256,128]{1,0:T(8,128)S(1)}, u32[]{:S(2)}, u32[]{:S(2)}) collective-permute-start(f32[256,128]{1,0:T(8,128)S(1)} %dynamic-slice_bitcast_fusion.3), channel_id=1, source_target_pairs={{0,1},{1,0},{2,3},{3,2},{4,5},{5,4},{6,7},{7,6},{8,9},{9,8},{10,11... | collective-permute-start | bytes 393224 | tf_op jit(solution)/shard_map/ppermute | solution.py:63
  170.9 3.1 %collective-permute-start.16 = (f32[128,128]{1,0:T(8,128)S(1)}, f32[128,128]{1,0:T(8,128)S(1)}, u32[]{:S(2)}, u32[]{:S(2)}) collective-permute-start(f32[128,128]{1,0:T(8,128)S(1)} %dynamic-slice_bitcast_fusion.5), channel_id=1, source_target_pairs={{0,2},{2,0},{1,3},{3,1},{4,6},{6,4},{5,7},{7,5},{8,10},{10,8},{9,1... | collective-permute-start | bytes 196616 | tf_op jit(solution)/shard_map/ppermute | solution.py:63
  174.1 2.0 %collective-permute-done.16 = f32[128,128]{1,0:T(8,128)S(1)} collective-permute-done((f32[128,128]{1,0:T(8,128)S(1)}, f32[128,128]{1,0:T(8,128)S(1)}, u32[]{:S(2)}, u32[]{:S(2)}) %collective-permute-start.16) | collective-permute-done | bytes 65568 | tf_op jit(solution)/shard_map/ppermute | solution.py:63
  176.1 3.0 %collective-permute-start.18 = (f32[128,128]{1,0:T(8,128)S(1)}, f32[128,128]{1,0:T(8,128)S(1)}, u32[]{:S(2)}, u32[]{:S(2)}) collective-permute-start(f32[128,128]{1,0:T(8,128)S(1)} %bitcast_add_fusion.18), channel_id=1, source_target_pairs={{0,2},{2,0},{1,3},{3,1},{4,6},{6,4},{5,7},{7,5},{8,10},{10,8},{9,1... | collective-permute-start | bytes 196616 | tf_op jit(solution)/shard_map/ppermute | solution.py:80
  179.2 1.4 collective-permute-start.19
  180.8 3.0 %collective-permute-done.19 = f32[128,128]{1,0:T(8,128)S(1)} collective-permute-done((f32[128,128]{1,0:T(8,128)S(1)}, f32[128,128]{1,0:T(8,128)S(1)}, u32[]{:S(2)}, u32[]{:S(2)}) %collective-permute-start.19) | collective-permute-done | bytes 65568 | tf_op jit(solution)/shard_map/ppermute | solution.py:81
  183.9 3.1 %collective-permute-start.20 = (f32[256,128]{1,0:T(8,128)S(1)}, f32[256,128]{1,0:T(8,128)S(1)}, u32[]{:S(2)}, u32[]{:S(2)}) collective-permute-start(f32[256,128]{1,0:T(8,128)S(1)} %get-tuple-element.9), channel_id=1, source_target_pairs={{0,1},{1,0},{2,3},{3,2},{4,5},{5,4},{6,7},{7,6},{8,9},{9,8},{10,11... | collective-permute-start | bytes 393224 | tf_op jit(solution)/shard_map/ppermute | solution.py:80
  (77 shorter events, 21.1 us)
Async XLA Ops:
  25.9 12.4 %collective-permute-start = (f32[512,128]{1,0:T(8,128)S(1)}, f32[512,128]{1,0:T(8,128)S(1)}, u32[]{:S(2)}, u32[]{:S(2)}) collective-permute-start(f32[512,128]{1,0:T(8,128)S(1)} %dynamic-slice_bitcast_fusion.1), channel_id=1, source_target_pairs={{0,4},{4,8},{8,12},{12,16},{16,20},{20,24},{24,28},{28,0},{1,5},{5... | collective-permute-start | bytes 786440 | tf_op jit(solution)/shard_map/ppermute | solution.py:63
  28.5 10.9 %collective-permute-start.7 = (f32[512,128]{1,0:T(8,128)S(1)}, f32[512,128]{1,0:T(8,128)S(1)}, u32[]{:S(2)}, u32[]{:S(2)}) collective-permute-start(f32[512,128]{1,0:T(8,128)S(1)} %dynamic-slice_bitcast_fusion), channel_id=1, source_target_pairs={{0,28},{4,0},{8,4},{12,8},{16,12},{20,16},{24,20},{28,24},{1,29},{... | collective-permute-start | bytes 786440 | tf_op jit(solution)/shard_map/ppermute | solution.py:64
  39.3 7.8 %collective-permute-start.1 = (f32[512,128]{1,0:T(8,128)S(1)}, f32[512,128]{1,0:T(8,128)S(1)}, u32[]{:S(2)}, u32[]{:S(2)}) collective-permute-start(f32[512,128]{1,0:T(8,128)S(1)} %bitcast_add_fusion.14), channel_id=1, source_target_pairs={{0,4},{4,8},{8,12},{12,16},{16,20},{20,24},{24,28},{28,0},{1,5},{5... | collective-permute-start | bytes 786440 | tf_op jit(solution)/shard_map/ppermute | solution.py:63
  39.5 8.8 %collective-permute-start.8 = (f32[512,128]{1,0:T(8,128)S(1)}, f32[512,128]{1,0:T(8,128)S(1)}, u32[]{:S(2)}, u32[]{:S(2)}) collective-permute-start(f32[512,128]{1,0:T(8,128)S(1)} %bitcast_add_fusion.7), channel_id=1, source_target_pairs={{0,28},{4,0},{8,4},{12,8},{16,12},{20,16},{24,20},{28,24},{1,29},{... | collective-permute-start | bytes 786440 | tf_op jit(solution)/shard_map/ppermute | solution.py:64
  48.2 7.0 %collective-permute-start.2 = (f32[512,128]{1,0:T(8,128)S(1)}, f32[512,128]{1,0:T(8,128)S(1)}, u32[]{:S(2)}, u32[]{:S(2)}) collective-permute-start(f32[512,128]{1,0:T(8,128)S(1)} %bitcast_add_fusion.13), channel_id=1, source_target_pairs={{0,4},{4,8},{8,12},{12,16},{16,20},{20,24},{24,28},{28,0},{1,5},{5... | collective-permute-start | bytes 786440 | tf_op jit(solution)/shard_map/ppermute | solution.py:63
  48.3 7.9 %collective-permute-start.9 = (f32[512,128]{1,0:T(8,128)S(1)}, f32[512,128]{1,0:T(8,128)S(1)}, u32[]{:S(2)}, u32[]{:S(2)}) collective-permute-start(f32[512,128]{1,0:T(8,128)S(1)} %bitcast_add_fusion.6), channel_id=1, source_target_pairs={{0,28},{4,0},{8,4},{12,8},{16,12},{20,16},{24,20},{28,24},{1,29},{... | collective-permute-start | bytes 786440 | tf_op jit(solution)/shard_map/ppermute | solution.py:64
  56.1 6.5 %collective-permute-start.3 = (f32[512,128]{1,0:T(8,128)S(1)}, f32[512,128]{1,0:T(8,128)S(1)}, u32[]{:S(2)}, u32[]{:S(2)}) collective-permute-start(f32[512,128]{1,0:T(8,128)S(1)} %bitcast_add_fusion.12), channel_id=1, source_target_pairs={{0,4},{4,8},{8,12},{12,16},{16,20},{20,24},{24,28},{28,0},{1,5},{5... | collective-permute-start | bytes 786440 | tf_op jit(solution)/shard_map/ppermute | solution.py:63
  56.3 7.4 %collective-permute-start.10 = (f32[512,128]{1,0:T(8,128)S(1)}, f32[512,128]{1,0:T(8,128)S(1)}, u32[]{:S(2)}, u32[]{:S(2)}) collective-permute-start(f32[512,128]{1,0:T(8,128)S(1)} %bitcast_add_fusion.5), channel_id=1, source_target_pairs={{0,28},{4,0},{8,4},{12,8},{16,12},{20,16},{24,20},{28,24},{1,29},{... | collective-permute-start | bytes 786440 | tf_op jit(solution)/shard_map/ppermute | solution.py:64
  63.6 6.5 %collective-permute-start.4 = (f32[512,128]{1,0:T(8,128)S(1)}, f32[512,128]{1,0:T(8,128)S(1)}, u32[]{:S(2)}, u32[]{:S(2)}) collective-permute-start(f32[512,128]{1,0:T(8,128)S(1)} %bitcast_add_fusion.11), channel_id=1, source_target_pairs={{0,4},{4,8},{8,12},{12,16},{16,20},{20,24},{24,28},{28,0},{1,5},{5... | collective-permute-start | bytes 786440 | tf_op jit(solution)/shard_map/ppermute | solution.py:63
  63.8 7.4 %collective-permute-start.11 = (f32[512,128]{1,0:T(8,128)S(1)}, f32[512,128]{1,0:T(8,128)S(1)}, u32[]{:S(2)}, u32[]{:S(2)}) collective-permute-start(f32[512,128]{1,0:T(8,128)S(1)} %bitcast_add_fusion.4), channel_id=1, source_target_pairs={{0,28},{4,0},{8,4},{12,8},{16,12},{20,16},{24,20},{28,24},{1,29},{... | collective-permute-start | bytes 786440 | tf_op jit(solution)/shard_map/ppermute | solution.py:64
  71.1 6.5 %collective-permute-start.5 = (f32[512,128]{1,0:T(8,128)S(1)}, f32[512,128]{1,0:T(8,128)S(1)}, u32[]{:S(2)}, u32[]{:S(2)}) collective-permute-start(f32[512,128]{1,0:T(8,128)S(1)} %bitcast_add_fusion.10), channel_id=1, source_target_pairs={{0,4},{4,8},{8,12},{12,16},{16,20},{20,24},{24,28},{28,0},{1,5},{5... | collective-permute-start | bytes 786440 | tf_op jit(solution)/shard_map/ppermute | solution.py:63
  71.3 7.4 %collective-permute-start.12 = (f32[512,128]{1,0:T(8,128)S(1)}, f32[512,128]{1,0:T(8,128)S(1)}, u32[]{:S(2)}, u32[]{:S(2)}) collective-permute-start(f32[512,128]{1,0:T(8,128)S(1)} %bitcast_add_fusion.3), channel_id=1, source_target_pairs={{0,28},{4,0},{8,4},{12,8},{16,12},{20,16},{24,20},{28,24},{1,29},{... | collective-permute-start | bytes 786440 | tf_op jit(solution)/shard_map/ppermute | solution.py:64
  78.6 7.6 %collective-permute-start.6 = (f32[512,128]{1,0:T(8,128)S(1)}, f32[512,128]{1,0:T(8,128)S(1)}, u32[]{:S(2)}, u32[]{:S(2)}) collective-permute-start(f32[512,128]{1,0:T(8,128)S(1)} %bitcast_add_fusion.9), channel_id=1, source_target_pairs={{0,4},{4,8},{8,12},{12,16},{16,20},{20,24},{24,28},{28,0},{1,5},{5... | collective-permute-start | bytes 786440 | tf_op jit(solution)/shard_map/ppermute | solution.py:63
  78.8 8.4 %collective-permute-start.13 = (f32[512,128]{1,0:T(8,128)S(1)}, f32[512,128]{1,0:T(8,128)S(1)}, u32[]{:S(2)}, u32[]{:S(2)}) collective-permute-start(f32[512,128]{1,0:T(8,128)S(1)} %bitcast_add_fusion.2), channel_id=1, source_target_pairs={{0,28},{4,0},{8,4},{12,8},{16,12},{20,16},{24,20},{28,24},{1,29},{... | collective-permute-start | bytes 786440 | tf_op jit(solution)/shard_map/ppermute | solution.py:64
  88.1 12.8 %all-to-all-start = ((f32[8,128,128]{2,1,0:T(8,128)}), f32[8,128,128]{2,1,0:T(8,128)S(1)}, u32[]{:S(2)}, u32[]{:S(2)}) async-start(f32[8,128,128]{2,1,0:T(8,128)} %bitcast.20), calls=%async_computation | async-start | bytes 1048576 | tf_op jit(solution)/shard_map/all_to_all | solution.py:107
  116.8 19.8 %all-to-all-start.2 = ((bf16[8,8,128,128]{3,2,1,0:T(8,128)(2,1)}), bf16[8,8,128,128]{3,2,1,0:T(8,128)(2,1)S(1)}, u32[]{:S(2)}, u32[]{:S(2)}) async-start(bf16[8,8,128,128]{3,2,1,0:T(8,128)(2,1)} %broadcast_in_dim.44), calls=%async_computation.2 | async-start | bytes 4194304 | tf_op jit(solution)/shard_map/all_to_all | solution.py:116
  136.6 1.3 copy-start
  157.5 12.9 %collective-permute-start.14 = (f32[256,128]{1,0:T(8,128)S(1)}, f32[256,128]{1,0:T(8,128)S(1)}, u32[]{:S(2)}, u32[]{:S(2)}) collective-permute-start(f32[256,128]{1,0:T(8,128)S(1)} %dynamic-slice_bitcast_fusion.3), channel_id=1, source_target_pairs={{0,1},{1,0},{2,3},{3,2},{4,5},{5,4},{6,7},{7,6},{8,9},{9,8},{10,11... | collective-permute-start | bytes 393224 | tf_op jit(solution)/shard_map/ppermute | solution.py:63
  169.4 1.4 collective-permute-start.15
  170.9 5.2 %collective-permute-start.16 = (f32[128,128]{1,0:T(8,128)S(1)}, f32[128,128]{1,0:T(8,128)S(1)}, u32[]{:S(2)}, u32[]{:S(2)}) collective-permute-start(f32[128,128]{1,0:T(8,128)S(1)} %dynamic-slice_bitcast_fusion.5), channel_id=1, source_target_pairs={{0,2},{2,0},{1,3},{3,1},{4,6},{6,4},{5,7},{7,5},{8,10},{10,8},{9,1... | collective-permute-start | bytes 196616 | tf_op jit(solution)/shard_map/ppermute | solution.py:63
  174.0 5.1 %collective-permute-start.17 = (f32[128,128]{1,0:T(8,128)S(1)}, f32[128,128]{1,0:T(8,128)S(1)}, u32[]{:S(2)}, u32[]{:S(2)}) collective-permute-start(f32[128,128]{1,0:T(8,128)S(1)} %dynamic-slice_bitcast_fusion.4), channel_id=1, source_target_pairs={{0,2},{2,0},{1,3},{3,1},{4,6},{6,4},{5,7},{7,5},{8,10},{10,8},{9,1... | collective-permute-start | bytes 196616 | tf_op jit(solution)/shard_map/ppermute | solution.py:64
  176.1 13.1 %copy-start.1 = (f32[1024,128]{1,0:T(8,128)S(1)}, f32[1024,128]{1,0:T(8,128)}, u32[]{:S(2)}) copy-start(f32[1024,128]{1,0:T(8,128)} %param.6) | copy-start | bytes 1572868
  176.1 4.7 %collective-permute-start.18 = (f32[128,128]{1,0:T(8,128)S(1)}, f32[128,128]{1,0:T(8,128)S(1)}, u32[]{:S(2)}, u32[]{:S(2)}) collective-permute-start(f32[128,128]{1,0:T(8,128)S(1)} %bitcast_add_fusion.18), channel_id=1, source_target_pairs={{0,2},{2,0},{1,3},{3,1},{4,6},{6,4},{5,7},{7,5},{8,10},{10,8},{9,1... | collective-permute-start | bytes 196616 | tf_op jit(solution)/shard_map/ppermute | solution.py:80
  179.2 4.7 %collective-permute-start.19 = (f32[128,128]{1,0:T(8,128)S(1)}, f32[128,128]{1,0:T(8,128)S(1)}, u32[]{:S(2)}, u32[]{:S(2)}) collective-permute-start(f32[128,128]{1,0:T(8,128)S(1)} %bitcast_add_fusion.17), channel_id=1, source_target_pairs={{0,2},{2,0},{1,3},{3,1},{4,6},{6,4},{5,7},{7,5},{8,10},{10,8},{9,1... | collective-permute-start | bytes 196616 | tf_op jit(solution)/shard_map/ppermute | solution.py:81
  183.9 4.1 %collective-permute-start.20 = (f32[256,128]{1,0:T(8,128)S(1)}, f32[256,128]{1,0:T(8,128)S(1)}, u32[]{:S(2)}, u32[]{:S(2)}) collective-permute-start(f32[256,128]{1,0:T(8,128)S(1)} %get-tuple-element.9), channel_id=1, source_target_pairs={{0,1},{1,0},{2,3},{3,2},{4,5},{5,4},{6,7},{7,6},{8,9},{9,8},{10,11... | collective-permute-start | bytes 393224 | tf_op jit(solution)/shard_map/ppermute | solution.py:80
  187.8 1.3 collective-permute-start.21

commit v5 on v4

--- a/solution.py
+++ b/solution.py
@@ -101,11 +101,16 @@
     item_slot = (item_ylo * n_z + item_z) * n_x + item_x
     item_index = jnp.concatenate([users_list, weights_list, item_slot])
     partial_t = block_sums(item_index, user_tiles_t, weight_tiles, n_users)
-    halves = partial_t.reshape(n_ylo, n_z, n_x * tile_rows, width)
-    bl, br = ring_reduce_scatter_halves(halves[0], halves[1], "z", n_z)
-    x = jnp.concatenate([bl, br], 0).reshape(n_ylo * n_x, tile_rows, width)
-    x = lax.all_to_all(x, ("ylo", "x"), 0, 0, tiled=True)
-    own_sum = x.sum(0).T
+    half = tile_rows // 2
+    pt = partial_t.reshape(n_ylo, n_z, n_x, tile_rows, width)
+    late = pt[..., half:, :].transpose(0, 2, 1, 3, 4).reshape(n_ylo * n_x, n_z, half, width)
+    late = lax.all_to_all(late, ("ylo", "x"), 0, 0, tiled=True).sum(0)
+    early = pt[..., :half, :].reshape(n_ylo, n_z, n_x * half, width)
+    bl, br = ring_reduce_scatter_halves(early[0], early[1], "z", n_z)
+    early = jnp.concatenate([bl, br], 0).reshape(n_ylo * n_x, half, width)
+    early = lax.all_to_all(early, ("ylo", "x"), 0, 0, tiled=True).sum(0)
+    late = lax.all_to_all(late, "z", 0, 0, tiled=True).sum(0)
+    own_sum = jnp.concatenate([early, late], 0).T
 
     position = lax.axis_index(USER_AXES)
     own_base = lax.dynamic_slice_in_dim(item_base[0], position * tile_rows, tile_rows, 0)

time: 191 us -> 191 us (level)
  starting transfers between devices: 55.3 us -> 67.2 us
  waiting for transfers between devices: 60.9 us -> 52.7 us
  other arithmetic: 12.7 us -> 10.4 us
    ppermute x9, waiting for transfers between devices: 33.1 us -> 18.1 us  [ring_reduce_scatter_halves(): rl = lax.ppermute(bl, axis, right)]
    all_to_all x1 -> x3, starting transfers between devices: 5.22 us -> 16.2 us  [the longest x1 6.14 us: per_device(): late = lax.all_to_all(late, 'z', 0, 0, tiled=True).sum(0)]
    all_to_all x1 -> x3, waiting for transfers between devices: 6.6 us -> 13.7 us  [the longest x1 8.37 us: per_device(): late = lax.all_to_all(late, 'z', 0, 0, tiled=True).sum(0)]
    add x9, other arithmetic: 6.87 us -> 2.94 us  [ring_reduce_scatter_halves(): bl = rl + lax.dynamic_index_in_dim(xl, (i - s - 2) % n, 0, keepdims=False)]
    slice x1 -> x2, local copies, waits for them, and re-layouts: 4.06 us -> 3.42 us  [the longest x1 1.73 us: per_device(): pt[..., half:, :].transpose(0, 2, 1, 3, 4)]
  transfers between devices with their start and end apart: 24 -> 26, of which waited for: 16 -> 16; matrix products, arithmetic and copies ran while one was open for 5% -> 6% of each run, Pallas kernels for 0% -> 0%
where the time goes in v5:
time: 191 us; the launch traced here: 190 us
  starting transfers between devices  67.2 us (35%)
  waiting for transfers between devices  52.7 us (28%)
  Pallas kernels  34 us (18%)
  blocking collectives  12.7 us (7%)
  local copies, waits for them, and re-layouts  11.9 us (6%)
  other arithmetic  10.4 us (5%)
    pallas_call x2, Pallas kernels, block_sums(): pl.pallas_call(functools.partial(block_sum_kernel, b_transposed=b_transpo...  34 us
    ppermute x9, starting transfers between devices, ring_reduce_scatter_halves(): rr = lax.ppermute(br, axis, left)  21.7 us
    ppermute x9, starting transfers between devices, ring_reduce_scatter_halves(): rl = lax.ppermute(bl, axis, right)  18.7 us
    ppermute x9, waiting for transfers between devices, ring_reduce_scatter_halves(): rl = lax.ppermute(bl, axis, right)  18.1 us
    all_to_all x1, waiting for transfers between devices, per_device(): t = lax.all_to_all(t, ('ylo', 'x'), 0, 0, tiled=True)  16 us
    all_to_all x1, blocking collectives, per_device(): lax.all_to_all(jnp.broadcast_to(own_bf_t[None], (n_z, width, tile_rows)),...  12.7 us
    all_to_all x1, waiting for transfers between devices, per_device(): late = lax.all_to_all(late, 'z', 0, 0, tiled=True).sum(0)  8.37 us
    all_to_all x1, starting transfers between devices, per_device(): late = lax.all_to_all(late, 'z', 0, 0, tiled=True).sum(0)  6.14 us
  transfers between devices with their start and end apart: 26, of which 16 were waited for; matrix products, arithmetic and copies ran while one was open for 6% of the time, Pallas kernels for 0%

profile of v5, /device:TPU:1, one launch (start us, length us, event | category | flops | bytes accessed | tf_op | source)
XLA Modules:
  0.0 190.0 jit_solution(8362653983827231641)
XLA Ops:
  5.3 15.6 %shard_map.77 = f32[64,128,128]{2,1,0:T(8,128)} custom-call(s32[1152]{0:T(1024)} %get-tuple-element.16.index_ref, bf16[8,128,128]{2,1,0:T(8,128)(2,1)} %bitcast.121, bf16[64,128,128]{2,1,0:T(8,128)(2,1)} %a_ref.1), custom_call_target="tpu_custom_call" | custom-call | tf_op jit(solution)/shard_map/pallas_call | solution.py:36
  20.9 1.7 fusion.11
  22.6 2.5 %collective-permute-start = (f32[256,128]{1,0:T(8,128)S(1)}, f32[256,128]{1,0:T(8,128)S(1)}, u32[]{:S(2)}, u32[]{:S(2)}) collective-permute-start(f32[256,128]{1,0:T(8,128)S(1)} %dynamic-slice_bitcast_fusion.3), channel_id=1, source_target_pairs={{0,4},{4,8},{8,12},{12,16},{16,20},{20,24},{24,28},{28,0},{1,5},{5... | collective-permute-start | bytes 393224 | tf_op jit(solution)/shard_map/ppermute | solution.py:63
  25.1 4.1 %collective-permute-start.7 = (f32[256,128]{1,0:T(8,128)S(1)}, f32[256,128]{1,0:T(8,128)}, u32[]{:S(2)}, u32[]{:S(2)}) collective-permute-start(f32[256,128]{1,0:T(8,128)S(1)} %dynamic-slice_bitcast_fusion.2), channel_id=1, source_target_pairs={{0,28},{4,0},{8,4},{12,8},{16,12},{20,16},{24,20},{28,24},{1,29},{... | collective-permute-start | bytes 393224 | tf_op jit(solution)/shard_map/ppermute | solution.py:64
  29.3 1.7 slice.51
  32.5 5.0 %all-to-all-start.1 = ((f32[8,8,64,128]{3,2,1,0:T(8,128)}), f32[8,8,64,128]{3,2,1,0:T(8,128)S(1)}, u32[]{:S(2)}, u32[]{:S(2)}) async-start(f32[8,8,64,128]{3,2,1,0:T(8,128)} %bitcast.101), calls=%async_computation.1 | async-start | bytes 4194304 | tf_op jit(solution)/shard_map/all_to_all | solution.py:107
  39.5 2.7 %collective-permute-start.8 = (f32[256,128]{1,0:T(8,128)S(1)}, f32[256,128]{1,0:T(8,128)S(1)}, u32[]{:S(2)}, u32[]{:S(2)}) collective-permute-start(f32[256,128]{1,0:T(8,128)S(1)} %bitcast_add_fusion.9), channel_id=1, source_target_pairs={{0,28},{4,0},{8,4},{12,8},{16,12},{20,16},{24,20},{28,24},{1,29},{... | collective-permute-start | bytes 393224 | tf_op jit(solution)/shard_map/ppermute | solution.py:64
  44.9 2.7 %collective-permute-start.9 = (f32[256,128]{1,0:T(8,128)S(1)}, f32[256,128]{1,0:T(8,128)S(1)}, u32[]{:S(2)}, u32[]{:S(2)}) collective-permute-start(f32[256,128]{1,0:T(8,128)S(1)} %bitcast_add_fusion.8), channel_id=1, source_target_pairs={{0,28},{4,0},{8,4},{12,8},{16,12},{20,16},{24,20},{28,24},{1,29},{... | collective-permute-start | bytes 393224 | tf_op jit(solution)/shard_map/ppermute | solution.py:64
  47.7 2.5 %collective-permute-done.2 = f32[256,128]{1,0:T(8,128)S(1)} collective-permute-done((f32[256,128]{1,0:T(8,128)S(1)}, f32[256,128]{1,0:T(8,128)S(1)}, u32[]{:S(2)}, u32[]{:S(2)}) %collective-permute-start.2) | collective-permute-done | bytes 131104 | tf_op jit(solution)/shard_map/ppermute | solution.py:63
  51.3 2.7 %collective-permute-start.10 = (f32[256,128]{1,0:T(8,128)S(1)}, f32[256,128]{1,0:T(8,128)S(1)}, u32[]{:S(2)}, u32[]{:S(2)}) collective-permute-start(f32[256,128]{1,0:T(8,128)S(1)} %bitcast_add_fusion.7), channel_id=1, source_target_pairs={{0,28},{4,0},{8,4},{12,8},{16,12},{20,16},{24,20},{28,24},{1,29},{... | collective-permute-start | bytes 393224 | tf_op jit(solution)/shard_map/ppermute | solution.py:64
  54.0 2.5 %collective-permute-done.3 = f32[256,128]{1,0:T(8,128)S(1)} collective-permute-done((f32[256,128]{1,0:T(8,128)S(1)}, f32[256,128]{1,0:T(8,128)S(1)}, u32[]{:S(2)}, u32[]{:S(2)}) %collective-permute-start.3) | collective-permute-done | bytes 131104 | tf_op jit(solution)/shard_map/ppermute | solution.py:63
  56.7 2.7 %collective-permute-start.11 = (f32[256,128]{1,0:T(8,128)S(1)}, f32[256,128]{1,0:T(8,128)S(1)}, u32[]{:S(2)}, u32[]{:S(2)}) collective-permute-start(f32[256,128]{1,0:T(8,128)S(1)} %bitcast_add_fusion.6), channel_id=1, source_target_pairs={{0,28},{4,0},{8,4},{12,8},{16,12},{20,16},{24,20},{28,24},{1,29},{... | collective-permute-start | bytes 393224 | tf_op jit(solution)/shard_map/ppermute | solution.py:64
  59.4 2.5 %collective-permute-done.4 = f32[256,128]{1,0:T(8,128)S(1)} collective-permute-done((f32[256,128]{1,0:T(8,128)S(1)}, f32[256,128]{1,0:T(8,128)S(1)}, u32[]{:S(2)}, u32[]{:S(2)}) %collective-permute-start.4) | collective-permute-done | bytes 131104 | tf_op jit(solution)/shard_map/ppermute | solution.py:63
  62.1 2.7 %collective-permute-start.12 = (f32[256,128]{1,0:T(8,128)S(1)}, f32[256,128]{1,0:T(8,128)S(1)}, u32[]{:S(2)}, u32[]{:S(2)}) collective-permute-start(f32[256,128]{1,0:T(8,128)S(1)} %bitcast_add_fusion.5), channel_id=1, source_target_pairs={{0,28},{4,0},{8,4},{12,8},{16,12},{20,16},{24,20},{28,24},{1,29},{... | collective-permute-start | bytes 393224 | tf_op jit(solution)/shard_map/ppermute | solution.py:64
  64.8 2.5 %collective-permute-done.5 = f32[256,128]{1,0:T(8,128)S(1)} collective-permute-done((f32[256,128]{1,0:T(8,128)S(1)}, f32[256,128]{1,0:T(8,128)S(1)}, u32[]{:S(2)}, u32[]{:S(2)}) %collective-permute-start.5) | collective-permute-done | bytes 131104 | tf_op jit(solution)/shard_map/ppermute | solution.py:63
  67.5 3.2 %collective-permute-start.13 = (f32[256,128]{1,0:T(8,128)S(1)}, f32[256,128]{1,0:T(8,128)S(1)}, u32[]{:S(2)}, u32[]{:S(2)}) collective-permute-start(f32[256,128]{1,0:T(8,128)S(1)} %bitcast_add_fusion.4), channel_id=1, source_target_pairs={{0,28},{4,0},{8,4},{12,8},{16,12},{20,16},{24,20},{28,24},{1,29},{... | collective-permute-start | bytes 393224 | tf_op jit(solution)/shard_map/ppermute | solution.py:64
  70.7 3.5 %collective-permute-done.6 = f32[256,128]{1,0:T(8,128)S(1)} collective-permute-done((f32[256,128]{1,0:T(8,128)S(1)}, f32[256,128]{1,0:T(8,128)S(1)}, u32[]{:S(2)}, u32[]{:S(2)}) %collective-permute-start.6) | collective-permute-done | bytes 131104 | tf_op jit(solution)/shard_map/ppermute | solution.py:63
  75.0 5.0 %all-to-all-start = ((f32[8,64,128]{2,1,0:T(8,128)}), f32[8,64,128]{2,1,0:T(8,128)S(1)}, u32[]{:S(2)}, u32[]{:S(2)}) async-start(f32[8,64,128]{2,1,0:T(8,128)} %bitcast.21), calls=%async_computation | async-start | bytes 524288 | tf_op jit(solution)/shard_map/all_to_all | solution.py:111
  80.8 5.3 %all-to-all-done = f32[8,64,128]{2,1,0:T(8,128)S(1)} async-done(((f32[8,64,128]{2,1,0:T(8,128)}), f32[8,64,128]{2,1,0:T(8,128)S(1)}, u32[]{:S(2)}, u32[]{:S(2)}) %all-to-all-start) | async-done | bytes 262176 | tf_op jit(solution)/shard_map/all_to_all | solution.py:111
  86.1 6.1 %all-to-all-start.2 = ((f32[8,64,128]{2,1,0:T(8,128)}), f32[8,64,128]{2,1,0:T(8,128)S(1)}, u32[]{:S(2)}, u32[]{:S(2)}) async-start(f32[8,64,128]{2,1,0:T(8,128)} %reduce_sum.28), calls=%async_computation.2 | async-start | bytes 524288 | tf_op jit(solution)/shard_map/all_to_all | solution.py:112
  93.2 8.4 %all-to-all-done.2 = f32[8,64,128]{2,1,0:T(8,128)S(1)} async-done(((f32[8,64,128]{2,1,0:T(8,128)}), f32[8,64,128]{2,1,0:T(8,128)S(1)}, u32[]{:S(2)}, u32[]{:S(2)}) %all-to-all-start.2) | async-done | bytes 262176 | tf_op jit(solution)/shard_map/all_to_all | solution.py:112
  101.7 12.7 %all_to_all.25 = bf16[8,128,128]{2,1,0:T(8,128)(2,1)S(1)} all-to-all(bf16[8,128,128]{2,1,0:T(8,128)(2,1)S(1)} %broadcast_in_dim.43), channel_id=1, replica_groups=mesh['ylo'=2,'x'=4,'z'=8,'yhi'=2,'core'=2] {'z'}, dimensions={0} | all-to-all | bytes 524288 | tf_op jit(solution)/shard_map/all_to_all | solution.py:119
  114.4 1.8 broadcast_in_dim.44
  116.2 3.6 %all-to-all-start.4 = ((bf16[8,8,128,128]{3,2,1,0:T(8,128)(2,1)}), bf16[8,8,128,128]{3,2,1,0:T(8,128)(2,1)S(1)}, u32[]{:S(2)}, u32[]{:S(2)}) async-start(bf16[8,8,128,128]{3,2,1,0:T(8,128)(2,1)} %broadcast_in_dim.44), calls=%async_computation.4 | async-start | bytes 4194304 | tf_op jit(solution)/shard_map/all_to_all | solution.py:121
  119.8 16.0 %all-to-all-done.4 = bf16[8,8,128,128]{3,2,1,0:T(8,128)(2,1)S(1)} async-done(((bf16[8,8,128,128]{3,2,1,0:T(8,128)(2,1)}), bf16[8,8,128,128]{3,2,1,0:T(8,128)(2,1)S(1)}, u32[]{:S(2)}, u32[]{:S(2)}) %all-to-all-start.4) | async-done | bytes 2097184 | tf_op jit(solution)/shard_map/all_to_all | solution.py:121
  137.1 18.5 %shard_map.78 = f32[8,128,128]{2,1,0:T(8,128)} custom-call(s32[1152]{0:T(1024)} %get-tuple-element.17.index_ref, bf16[64,128,128]{2,1,0:T(8,128)(2,1)} %a_ref.1, bf16[64,128,128]{2,1,0:T(8,128)(2,1)} %bitcast.102), custom_call_target="tpu_custom_call" | custom-call | tf_op jit(solution)/shard_map/pallas_call | solution.py:36
  156.7 13.2 %collective-permute-start.14 = (f32[256,128]{1,0:T(8,128)S(1)}, f32[256,128]{1,0:T(8,128)S(1)}, u32[]{:S(2)}, u32[]{:S(2)}) collective-permute-start(f32[256,128]{1,0:T(8,128)S(1)} %dynamic-slice_bitcast_fusion.1), channel_id=1, source_target_pairs={{0,1},{1,0},{2,3},{3,2},{4,5},{5,4},{6,7},{7,6},{8,9},{9,8},{10,11... | collective-permute-start | bytes 393224 | tf_op jit(solution)/shard_map/ppermute | solution.py:63
  171.5 2.5 %collective-permute-start.16 = (f32[128,128]{1,0:T(8,128)S(1)}, f32[128,128]{1,0:T(8,128)S(1)}, u32[]{:S(2)}, u32[]{:S(2)}) collective-permute-start(f32[128,128]{1,0:T(8,128)S(1)} %dynamic-slice_bitcast_fusion.5), channel_id=1, source_target_pairs={{0,2},{2,0},{1,3},{3,1},{4,6},{6,4},{5,7},{7,5},{8,10},{10,8},{9,1... | collective-permute-start | bytes 196616 | tf_op jit(solution)/shard_map/ppermute | solution.py:63
  174.5 2.0 %collective-permute-done.16 = f32[128,128]{1,0:T(8,128)S(1)} collective-permute-done((f32[128,128]{1,0:T(8,128)S(1)}, f32[128,128]{1,0:T(8,128)S(1)}, u32[]{:S(2)}, u32[]{:S(2)}) %collective-permute-start.16) | collective-permute-done | bytes 65568 | tf_op jit(solution)/shard_map/ppermute | solution.py:63
  176.6 2.5 %collective-permute-start.18 = (f32[128,128]{1,0:T(8,128)S(1)}, f32[128,128]{1,0:T(8,128)S(1)}, u32[]{:S(2)}, u32[]{:S(2)}) collective-permute-start(f32[128,128]{1,0:T(8,128)S(1)} %bitcast_add_fusion.18), channel_id=1, source_target_pairs={{0,2},{2,0},{1,3},{3,1},{4,6},{6,4},{5,7},{7,5},{8,10},{10,8},{9,1... | collective-permute-start | bytes 196616 | tf_op jit(solution)/shard_map/ppermute | solution.py:80
  181.3 2.5 %collective-permute-done.19 = f32[128,128]{1,0:T(8,128)S(1)} collective-permute-done((f32[128,128]{1,0:T(8,128)S(1)}, f32[128,128]{1,0:T(8,128)S(1)}, u32[]{:S(2)}, u32[]{:S(2)}) %collective-permute-start.19) | collective-permute-done | bytes 65568 | tf_op jit(solution)/shard_map/ppermute | solution.py:81
  183.9 3.1 %collective-permute-start.20 = (f32[256,128]{1,0:T(8,128)S(1)}, f32[256,128]{1,0:T(8,128)S(1)}, u32[]{:S(2)}, u32[]{:S(2)}) collective-permute-start(f32[256,128]{1,0:T(8,128)S(1)} %get-tuple-element.11), channel_id=1, source_target_pairs={{0,1},{1,0},{2,3},{3,2},{4,5},{5,4},{6,7},{7,6},{8,9},{9,8},{10,11... | collective-permute-start | bytes 393224 | tf_op jit(solution)/shard_map/ppermute | solution.py:80
  (89 shorter events, 24.6 us)
Async XLA Ops:
  22.6 8.4 %copy-start.1 = (f32[1,8,4,64,128]{4,3,2,1,0:T(8,128)}, f32[1,8,4,64,128]{4,3,2,1,0:T(8,128)S(1)}, u32[]{:S(2)}) copy-start(f32[1,8,4,64,128]{4,3,2,1,0:T(8,128)S(1)} %get-tuple-element.6) | copy-start | bytes 3145732
  22.6 14.9 %collective-permute-start = (f32[256,128]{1,0:T(8,128)S(1)}, f32[256,128]{1,0:T(8,128)S(1)}, u32[]{:S(2)}, u32[]{:S(2)}) collective-permute-start(f32[256,128]{1,0:T(8,128)S(1)} %dynamic-slice_bitcast_fusion.3), channel_id=1, source_target_pairs={{0,4},{4,8},{8,12},{12,16},{16,20},{20,24},{24,28},{28,0},{1,5},{5... | collective-permute-start | bytes 393224 | tf_op jit(solution)/shard_map/ppermute | solution.py:63
  25.1 13.5 %collective-permute-start.7 = (f32[256,128]{1,0:T(8,128)S(1)}, f32[256,128]{1,0:T(8,128)}, u32[]{:S(2)}, u32[]{:S(2)}) collective-permute-start(f32[256,128]{1,0:T(8,128)S(1)} %dynamic-slice_bitcast_fusion.2), channel_id=1, source_target_pairs={{0,28},{4,0},{8,4},{12,8},{16,12},{20,16},{24,20},{28,24},{1,29},{... | collective-permute-start | bytes 393224 | tf_op jit(solution)/shard_map/ppermute | solution.py:64
  32.5 42.5 %all-to-all-start.1 = ((f32[8,8,64,128]{3,2,1,0:T(8,128)}), f32[8,8,64,128]{3,2,1,0:T(8,128)S(1)}, u32[]{:S(2)}, u32[]{:S(2)}) async-start(f32[8,8,64,128]{3,2,1,0:T(8,128)} %bitcast.101), calls=%async_computation.1 | async-start | bytes 4194304 | tf_op jit(solution)/shard_map/all_to_all | solution.py:107
  37.5 19.1 %copy-start.2 = (f32[1,8,4,64,128]{4,3,2,1,0:T(8,128)S(1)}, f32[1,8,4,64,128]{4,3,2,1,0:T(8,128)}, u32[]{:S(2)}) copy-start(f32[1,8,4,64,128]{4,3,2,1,0:T(8,128)} %copy-done.1) | copy-start | bytes 3145732
  38.5 5.4 %collective-permute-start.1 = (f32[256,128]{1,0:T(8,128)S(1)}, f32[256,128]{1,0:T(8,128)S(1)}, u32[]{:S(2)}, u32[]{:S(2)}) collective-permute-start(f32[256,128]{1,0:T(8,128)S(1)} %bitcast_add_fusion.16), channel_id=1, source_target_pairs={{0,4},{4,8},{8,12},{12,16},{16,20},{20,24},{24,28},{28,0},{1,5},{5... | collective-permute-start | bytes 393224 | tf_op jit(solution)/shard_map/ppermute | solution.py:63
  39.5 5.4 %collective-permute-start.8 = (f32[256,128]{1,0:T(8,128)S(1)}, f32[256,128]{1,0:T(8,128)S(1)}, u32[]{:S(2)}, u32[]{:S(2)}) collective-permute-start(f32[256,128]{1,0:T(8,128)S(1)} %bitcast_add_fusion.9), channel_id=1, source_target_pairs={{0,28},{4,0},{8,4},{12,8},{16,12},{20,16},{24,20},{28,24},{1,29},{... | collective-permute-start | bytes 393224 | tf_op jit(solution)/shard_map/ppermute | solution.py:64
  44.8 5.4 %collective-permute-start.2 = (f32[256,128]{1,0:T(8,128)S(1)}, f32[256,128]{1,0:T(8,128)S(1)}, u32[]{:S(2)}, u32[]{:S(2)}) collective-permute-start(f32[256,128]{1,0:T(8,128)S(1)} %bitcast_add_fusion.15), channel_id=1, source_target_pairs={{0,4},{4,8},{8,12},{12,16},{16,20},{20,24},{24,28},{28,0},{1,5},{5... | collective-permute-start | bytes 393224 | tf_op jit(solution)/shard_map/ppermute | solution.py:63
  44.9 6.3 %collective-permute-start.9 = (f32[256,128]{1,0:T(8,128)S(1)}, f32[256,128]{1,0:T(8,128)S(1)}, u32[]{:S(2)}, u32[]{:S(2)}) collective-permute-start(f32[256,128]{1,0:T(8,128)S(1)} %bitcast_add_fusion.8), channel_id=1, source_target_pairs={{0,28},{4,0},{8,4},{12,8},{16,12},{20,16},{24,20},{28,24},{1,29},{... | collective-permute-start | bytes 393224 | tf_op jit(solution)/shard_map/ppermute | solution.py:64
  51.1 5.4 %collective-permute-start.3 = (f32[256,128]{1,0:T(8,128)S(1)}, f32[256,128]{1,0:T(8,128)S(1)}, u32[]{:S(2)}, u32[]{:S(2)}) collective-permute-start(f32[256,128]{1,0:T(8,128)S(1)} %bitcast_add_fusion.14), channel_id=1, source_target_pairs={{0,4},{4,8},{8,12},{12,16},{16,20},{20,24},{24,28},{28,0},{1,5},{5... | collective-permute-start | bytes 393224 | tf_op jit(solution)/shard_map/ppermute | solution.py:63
  51.3 5.4 %collective-permute-start.10 = (f32[256,128]{1,0:T(8,128)S(1)}, f32[256,128]{1,0:T(8,128)S(1)}, u32[]{:S(2)}, u32[]{:S(2)}) collective-permute-start(f32[256,128]{1,0:T(8,128)S(1)} %bitcast_add_fusion.7), channel_id=1, source_target_pairs={{0,28},{4,0},{8,4},{12,8},{16,12},{20,16},{24,20},{28,24},{1,29},{... | collective-permute-start | bytes 393224 | tf_op jit(solution)/shard_map/ppermute | solution.py:64
  56.6 5.4 %collective-permute-start.4 = (f32[256,128]{1,0:T(8,128)S(1)}, f32[256,128]{1,0:T(8,128)S(1)}, u32[]{:S(2)}, u32[]{:S(2)}) collective-permute-start(f32[256,128]{1,0:T(8,128)S(1)} %bitcast_add_fusion.13), channel_id=1, source_target_pairs={{0,4},{4,8},{8,12},{12,16},{16,20},{20,24},{24,28},{28,0},{1,5},{5... | collective-permute-start | bytes 393224 | tf_op jit(solution)/shard_map/ppermute | solution.py:63
  56.7 5.4 %collective-permute-start.11 = (f32[256,128]{1,0:T(8,128)S(1)}, f32[256,128]{1,0:T(8,128)S(1)}, u32[]{:S(2)}, u32[]{:S(2)}) collective-permute-start(f32[256,128]{1,0:T(8,128)S(1)} %bitcast_add_fusion.6), channel_id=1, source_target_pairs={{0,28},{4,0},{8,4},{12,8},{16,12},{20,16},{24,20},{28,24},{1,29},{... | collective-permute-start | bytes 393224 | tf_op jit(solution)/shard_map/ppermute | solution.py:64
  62.0 5.4 %collective-permute-start.5 = (f32[256,128]{1,0:T(8,128)S(1)}, f32[256,128]{1,0:T(8,128)S(1)}, u32[]{:S(2)}, u32[]{:S(2)}) collective-permute-start(f32[256,128]{1,0:T(8,128)S(1)} %bitcast_add_fusion.12), channel_id=1, source_target_pairs={{0,4},{4,8},{8,12},{12,16},{16,20},{20,24},{24,28},{28,0},{1,5},{5... | collective-permute-start | bytes 393224 | tf_op jit(solution)/shard_map/ppermute | solution.py:63
  62.1 5.4 %collective-permute-start.12 = (f32[256,128]{1,0:T(8,128)S(1)}, f32[256,128]{1,0:T(8,128)S(1)}, u32[]{:S(2)}, u32[]{:S(2)}) collective-permute-start(f32[256,128]{1,0:T(8,128)S(1)} %bitcast_add_fusion.5), channel_id=1, source_target_pairs={{0,28},{4,0},{8,4},{12,8},{16,12},{20,16},{24,20},{28,24},{1,29},{... | collective-permute-start | bytes 393224 | tf_op jit(solution)/shard_map/ppermute | solution.py:64
  67.4 6.8 %collective-permute-start.6 = (f32[256,128]{1,0:T(8,128)S(1)}, f32[256,128]{1,0:T(8,128)S(1)}, u32[]{:S(2)}, u32[]{:S(2)}) collective-permute-start(f32[256,128]{1,0:T(8,128)S(1)} %bitcast_add_fusion.11), channel_id=1, source_target_pairs={{0,4},{4,8},{8,12},{12,16},{16,20},{20,24},{24,28},{28,0},{1,5},{5... | collective-permute-start | bytes 393224 | tf_op jit(solution)/shard_map/ppermute | solution.py:63
  67.5 6.7 %collective-permute-start.13 = (f32[256,128]{1,0:T(8,128)S(1)}, f32[256,128]{1,0:T(8,128)S(1)}, u32[]{:S(2)}, u32[]{:S(2)}) collective-permute-start(f32[256,128]{1,0:T(8,128)S(1)} %bitcast_add_fusion.4), channel_id=1, source_target_pairs={{0,28},{4,0},{8,4},{12,8},{16,12},{20,16},{24,20},{28,24},{1,29},{... | collective-permute-start | bytes 393224 | tf_op jit(solution)/shard_map/ppermute | solution.py:64
  75.0 11.2 %all-to-all-start = ((f32[8,64,128]{2,1,0:T(8,128)}), f32[8,64,128]{2,1,0:T(8,128)S(1)}, u32[]{:S(2)}, u32[]{:S(2)}) async-start(f32[8,64,128]{2,1,0:T(8,128)} %bitcast.21), calls=%async_computation | async-start | bytes 524288 | tf_op jit(solution)/shard_map/all_to_all | solution.py:111
  86.1 15.5 %all-to-all-start.2 = ((f32[8,64,128]{2,1,0:T(8,128)}), f32[8,64,128]{2,1,0:T(8,128)S(1)}, u32[]{:S(2)}, u32[]{:S(2)}) async-start(f32[8,64,128]{2,1,0:T(8,128)} %reduce_sum.28), calls=%async_computation.2 | async-start | bytes 524288 | tf_op jit(solution)/shard_map/all_to_all | solution.py:112
  116.2 19.6 %all-to-all-start.4 = ((bf16[8,8,128,128]{3,2,1,0:T(8,128)(2,1)}), bf16[8,8,128,128]{3,2,1,0:T(8,128)(2,1)S(1)}, u32[]{:S(2)}, u32[]{:S(2)}) async-start(bf16[8,8,128,128]{3,2,1,0:T(8,128)(2,1)} %broadcast_in_dim.44), calls=%async_computation.4 | async-start | bytes 4194304 | tf_op jit(solution)/shard_map/all_to_all | solution.py:121
  135.8 1.3 copy-start
  156.7 14.2 %collective-permute-start.14 = (f32[256,128]{1,0:T(8,128)S(1)}, f32[256,128]{1,0:T(8,128)S(1)}, u32[]{:S(2)}, u32[]{:S(2)}) collective-permute-start(f32[256,128]{1,0:T(8,128)S(1)} %dynamic-slice_bitcast_fusion.1), channel_id=1, source_target_pairs={{0,1},{1,0},{2,3},{3,2},{4,5},{5,4},{6,7},{7,6},{8,9},{9,8},{10,11... | collective-permute-start | bytes 393224 | tf_op jit(solution)/shard_map/ppermute | solution.py:63
  170.0 1.4 collective-permute-start.15
  171.5 5.1 %collective-permute-start.16 = (f32[128,128]{1,0:T(8,128)S(1)}, f32[128,128]{1,0:T(8,128)S(1)}, u32[]{:S(2)}, u32[]{:S(2)}) collective-permute-start(f32[128,128]{1,0:T(8,128)S(1)} %dynamic-slice_bitcast_fusion.5), channel_id=1, source_target_pairs={{0,2},{2,0},{1,3},{3,1},{4,6},{6,4},{5,7},{7,5},{8,10},{10,8},{9,1... | collective-permute-start | bytes 196616 | tf_op jit(solution)/shard_map/ppermute | solution.py:63
  174.0 5.1 %collective-permute-start.17 = (f32[128,128]{1,0:T(8,128)S(1)}, f32[128,128]{1,0:T(8,128)S(1)}, u32[]{:S(2)}, u32[]{:S(2)}) collective-permute-start(f32[128,128]{1,0:T(8,128)S(1)} %dynamic-slice_bitcast_fusion.4), channel_id=1, source_target_pairs={{0,2},{2,0},{1,3},{3,1},{4,6},{6,4},{5,7},{7,5},{8,10},{10,8},{9,1... | collective-permute-start | bytes 196616 | tf_op jit(solution)/shard_map/ppermute | solution.py:64
  176.6 12.5 %copy-start.3 = (f32[1024,128]{1,0:T(8,128)S(1)}, f32[1024,128]{1,0:T(8,128)}, u32[]{:S(2)}) copy-start(f32[1024,128]{1,0:T(8,128)} %param.6) | copy-start | bytes 1572868
  176.6 4.7 %collective-permute-start.18 = (f32[128,128]{1,0:T(8,128)S(1)}, f32[128,128]{1,0:T(8,128)S(1)}, u32[]{:S(2)}, u32[]{:S(2)}) collective-permute-start(f32[128,128]{1,0:T(8,128)S(1)} %bitcast_add_fusion.18), channel_id=1, source_target_pairs={{0,2},{2,0},{1,3},{3,1},{4,6},{6,4},{5,7},{7,5},{8,10},{10,8},{9,1... | collective-permute-start | bytes 196616 | tf_op jit(solution)/shard_map/ppermute | solution.py:80
  179.1 4.7 %collective-permute-start.19 = (f32[128,128]{1,0:T(8,128)S(1)}, f32[128,128]{1,0:T(8,128)S(1)}, u32[]{:S(2)}, u32[]{:S(2)}) collective-permute-start(f32[128,128]{1,0:T(8,128)S(1)} %bitcast_add_fusion.17), channel_id=1, source_target_pairs={{0,2},{2,0},{1,3},{3,1},{4,6},{6,4},{5,7},{7,5},{8,10},{10,8},{9,1... | collective-permute-start | bytes 196616 | tf_op jit(solution)/shard_map/ppermute | solution.py:81
  183.9 4.1 %collective-permute-start.20 = (f32[256,128]{1,0:T(8,128)S(1)}, f32[256,128]{1,0:T(8,128)S(1)}, u32[]{:S(2)}, u32[]{:S(2)}) collective-permute-start(f32[256,128]{1,0:T(8,128)S(1)} %get-tuple-element.11), channel_id=1, source_target_pairs={{0,1},{1,0},{2,3},{3,2},{4,5},{5,4},{6,7},{7,6},{8,9},{9,8},{10,11... | collective-permute-start | bytes 393224 | tf_op jit(solution)/shard_map/ppermute | solution.py:80
  187.7 1.3 collective-permute-start.21

commit v6 on v4

--- a/solution.py
+++ b/solution.py
@@ -25,7 +25,7 @@
         )
         return carry
 
-    lax.fori_loop(0, n_blocks, body, 0, unroll=8)
+    lax.fori_loop(0, n_blocks, body, 0, unroll=16)
 
 
 def block_sums(index, a_tiles, b_tiles, n_out, b_transposed=False):

time: 191 us -> 184 us (0.963)
  Pallas kernels: 34 us -> 27.6 us
    pallas_call x2, Pallas kernels: 34 us -> 27.6 us  [block_sums(): pl.pallas_call(functools.partial(block_sum_kernel, b_transposed=b_transpo...]
where the time goes in v6:
time: 184 us
  waiting for transfers between devices  61.1 us (33%)
  starting transfers between devices  54.6 us (30%)
  Pallas kernels  27.6 us (15%)
  blocking collectives  14.4 us (8%)
  other arithmetic  12.7 us (7%)
  local copies, waits for them, and re-layouts  12 us (7%)
    ppermute x9, waiting for transfers between devices, ring_reduce_scatter_halves(): rl = lax.ppermute(bl, axis, right)  33.3 us
    pallas_call x2, Pallas kernels, block_sums(): pl.pallas_call(functools.partial(block_sum_kernel, b_transposed=b_transpo...  27.6 us
    ppermute x9, starting transfers between devices, ring_reduce_scatter_halves(): rr = lax.ppermute(br, axis, left)  21.1 us
    ppermute x9, starting transfers between devices, ring_reduce_scatter_halves(): rl = lax.ppermute(bl, axis, right)  17.7 us
    all_to_all x1, waiting for transfers between devices, per_device(): t = lax.all_to_all(t, ('ylo', 'x'), 0, 0, tiled=True)  16.2 us
    all_to_all x1, blocking collectives, per_device(): lax.all_to_all(jnp.broadcast_to(own_bf_t[None], (n_z, width, tile_rows)),...  14.4 us
    add x9, other arithmetic, ring_reduce_scatter_halves(): bl = rl + lax.dynamic_index_in_dim(xl, (i - s - 2) % n, 0, keepdims=False)  6.87 us
    all_to_all x1, waiting for transfers between devices, per_device(): x = lax.all_to_all(x, ('ylo', 'x'), 0, 0, tiled=True)  6.6 us
  transfers between devices with their start and end apart: 24, of which 16 were waited for; matrix products, arithmetic and copies ran while one was open for 5% of the time, Pallas kernels for 0%

profile of v6, /device:TPU:1, one launch (start us, length us, event | category | flops | bytes accessed | tf_op | source)
XLA Modules:
  0.0 183.5 jit_solution(5262099142200919553)
XLA Ops:
  5.3 11.9 %shard_map.77 = f32[64,128,128]{2,1,0:T(8,128)} custom-call(s32[1152]{0:T(1024)} %get-tuple-element.14.index_ref, bf16[8,128,128]{2,1,0:T(8,128)(2,1)} %bitcast.112, bf16[64,128,128]{2,1,0:T(8,128)(2,1)} %a_ref.1), custom_call_target="tpu_custom_call" | custom-call | tf_op jit(solution)/shard_map/pallas_call | solution.py:36
  17.2 4.1 %fusion.9 = (f32[32,128,128]{2,1,0:T(8,128)}, f32[32,128,128]{2,1,0:T(8,128)S(1)}) fusion(f32[64,128,128]{2,1,0:T(8,128)} %shard_map.77), kind=kLoop, calls=%fused_computation.62 | loop fusion | bytes 8388608 | tf_op jit(solution)/shard_map/slice | solution.py:105
  22.3 2.5 %collective-permute-start = (f32[512,128]{1,0:T(8,128)S(1)}, f32[512,128]{1,0:T(8,128)S(1)}, u32[]{:S(2)}, u32[]{:S(2)}) collective-permute-start(f32[512,128]{1,0:T(8,128)S(1)} %dynamic-slice_bitcast_fusion.1), channel_id=1, source_target_pairs={{0,4},{4,8},{8,12},{12,16},{16,20},{20,24},{24,28},{28,0},{1,5},{5... | collective-permute-start | bytes 786440 | tf_op jit(solution)/shard_map/ppermute | solution.py:63
  24.8 4.1 %collective-permute-start.7 = (f32[512,128]{1,0:T(8,128)S(1)}, f32[512,128]{1,0:T(8,128)S(1)}, u32[]{:S(2)}, u32[]{:S(2)}) collective-permute-start(f32[512,128]{1,0:T(8,128)S(1)} %dynamic-slice_bitcast_fusion), channel_id=1, source_target_pairs={{0,28},{4,0},{8,4},{12,8},{16,12},{20,16},{24,20},{28,24},{1,29},{... | collective-permute-start | bytes 786440 | tf_op jit(solution)/shard_map/ppermute | solution.py:64
  28.9 5.9 %collective-permute-done = f32[512,128]{1,0:T(8,128)S(1)} collective-permute-done((f32[512,128]{1,0:T(8,128)S(1)}, f32[512,128]{1,0:T(8,128)S(1)}, u32[]{:S(2)}, u32[]{:S(2)}) %collective-permute-start) | collective-permute-done | bytes 262176 | tf_op jit(solution)/shard_map/ppermute | solution.py:63
  35.8 2.7 %collective-permute-start.8 = (f32[512,128]{1,0:T(8,128)S(1)}, f32[512,128]{1,0:T(8,128)S(1)}, u32[]{:S(2)}, u32[]{:S(2)}) collective-permute-start(f32[512,128]{1,0:T(8,128)S(1)} %bitcast_add_fusion.7), channel_id=1, source_target_pairs={{0,28},{4,0},{8,4},{12,8},{16,12},{20,16},{24,20},{28,24},{1,29},{... | collective-permute-start | bytes 786440 | tf_op jit(solution)/shard_map/ppermute | solution.py:64
  38.6 5.0 %collective-permute-done.1 = f32[512,128]{1,0:T(8,128)S(1)} collective-permute-done((f32[512,128]{1,0:T(8,128)S(1)}, f32[512,128]{1,0:T(8,128)S(1)}, u32[]{:S(2)}, u32[]{:S(2)}) %collective-permute-start.1) | collective-permute-done | bytes 262176 | tf_op jit(solution)/shard_map/ppermute | solution.py:63
  44.7 2.7 %collective-permute-start.9 = (f32[512,128]{1,0:T(8,128)S(1)}, f32[512,128]{1,0:T(8,128)S(1)}, u32[]{:S(2)}, u32[]{:S(2)}) collective-permute-start(f32[512,128]{1,0:T(8,128)S(1)} %bitcast_add_fusion.6), channel_id=1, source_target_pairs={{0,28},{4,0},{8,4},{12,8},{16,12},{20,16},{24,20},{28,24},{1,29},{... | collective-permute-start | bytes 786440 | tf_op jit(solution)/shard_map/ppermute | solution.py:64
  47.5 4.2 %collective-permute-done.2 = f32[512,128]{1,0:T(8,128)S(1)} collective-permute-done((f32[512,128]{1,0:T(8,128)S(1)}, f32[512,128]{1,0:T(8,128)S(1)}, u32[]{:S(2)}, u32[]{:S(2)}) %collective-permute-start.2) | collective-permute-done | bytes 262176 | tf_op jit(solution)/shard_map/ppermute | solution.py:63
  52.8 2.7 %collective-permute-start.10 = (f32[512,128]{1,0:T(8,128)S(1)}, f32[512,128]{1,0:T(8,128)S(1)}, u32[]{:S(2)}, u32[]{:S(2)}) collective-permute-start(f32[512,128]{1,0:T(8,128)S(1)} %bitcast_add_fusion.5), channel_id=1, source_target_pairs={{0,28},{4,0},{8,4},{12,8},{16,12},{20,16},{24,20},{28,24},{1,29},{... | collective-permute-start | bytes 786440 | tf_op jit(solution)/shard_map/ppermute | solution.py:64
  55.5 3.6 %collective-permute-done.3 = f32[512,128]{1,0:T(8,128)S(1)} collective-permute-done((f32[512,128]{1,0:T(8,128)S(1)}, f32[512,128]{1,0:T(8,128)S(1)}, u32[]{:S(2)}, u32[]{:S(2)}) %collective-permute-start.3) | collective-permute-done | bytes 262176 | tf_op jit(solution)/shard_map/ppermute | solution.py:63
  60.3 2.7 %collective-permute-start.11 = (f32[512,128]{1,0:T(8,128)S(1)}, f32[512,128]{1,0:T(8,128)S(1)}, u32[]{:S(2)}, u32[]{:S(2)}) collective-permute-start(f32[512,128]{1,0:T(8,128)S(1)} %bitcast_add_fusion.4), channel_id=1, source_target_pairs={{0,28},{4,0},{8,4},{12,8},{16,12},{20,16},{24,20},{28,24},{1,29},{... | collective-permute-start | bytes 786440 | tf_op jit(solution)/shard_map/ppermute | solution.py:64
  63.0 3.6 %collective-permute-done.4 = f32[512,128]{1,0:T(8,128)S(1)} collective-permute-done((f32[512,128]{1,0:T(8,128)S(1)}, f32[512,128]{1,0:T(8,128)S(1)}, u32[]{:S(2)}, u32[]{:S(2)}) %collective-permute-start.4) | collective-permute-done | bytes 262176 | tf_op jit(solution)/shard_map/ppermute | solution.py:63
  67.7 2.7 %collective-permute-start.12 = (f32[512,128]{1,0:T(8,128)S(1)}, f32[512,128]{1,0:T(8,128)S(1)}, u32[]{:S(2)}, u32[]{:S(2)}) collective-permute-start(f32[512,128]{1,0:T(8,128)S(1)} %bitcast_add_fusion.3), channel_id=1, source_target_pairs={{0,28},{4,0},{8,4},{12,8},{16,12},{20,16},{24,20},{28,24},{1,29},{... | collective-permute-start | bytes 786440 | tf_op jit(solution)/shard_map/ppermute | solution.py:64
  70.5 3.6 %collective-permute-done.5 = f32[512,128]{1,0:T(8,128)S(1)} collective-permute-done((f32[512,128]{1,0:T(8,128)S(1)}, f32[512,128]{1,0:T(8,128)S(1)}, u32[]{:S(2)}, u32[]{:S(2)}) %collective-permute-start.5) | collective-permute-done | bytes 262176 | tf_op jit(solution)/shard_map/ppermute | solution.py:63
  75.2 2.9 %collective-permute-start.13 = (f32[512,128]{1,0:T(8,128)S(1)}, f32[512,128]{1,0:T(8,128)S(1)}, u32[]{:S(2)}, u32[]{:S(2)}) collective-permute-start(f32[512,128]{1,0:T(8,128)S(1)} %bitcast_add_fusion.2), channel_id=1, source_target_pairs={{0,28},{4,0},{8,4},{12,8},{16,12},{20,16},{24,20},{28,24},{1,29},{... | collective-permute-start | bytes 786440 | tf_op jit(solution)/shard_map/ppermute | solution.py:64
  78.1 4.5 %collective-permute-done.6 = f32[512,128]{1,0:T(8,128)S(1)} collective-permute-done((f32[512,128]{1,0:T(8,128)S(1)}, f32[512,128]{1,0:T(8,128)S(1)}, u32[]{:S(2)}, u32[]{:S(2)}) %collective-permute-start.6) | collective-permute-done | bytes 262176 | tf_op jit(solution)/shard_map/ppermute | solution.py:63
  84.5 5.0 %all-to-all-start = ((f32[8,128,128]{2,1,0:T(8,128)}), f32[8,128,128]{2,1,0:T(8,128)S(1)}, u32[]{:S(2)}, u32[]{:S(2)}) async-start(f32[8,128,128]{2,1,0:T(8,128)} %bitcast.20), calls=%async_computation | async-start | bytes 1048576 | tf_op jit(solution)/shard_map/all_to_all | solution.py:107
  90.4 6.6 %all-to-all-done = f32[8,128,128]{2,1,0:T(8,128)S(1)} async-done(((f32[8,128,128]{2,1,0:T(8,128)}), f32[8,128,128]{2,1,0:T(8,128)S(1)}, u32[]{:S(2)}, u32[]{:S(2)}) %all-to-all-start) | async-done | bytes 524320 | tf_op jit(solution)/shard_map/all_to_all | solution.py:107
  97.1 14.4 %all_to_all.15 = bf16[8,128,128]{2,1,0:T(8,128)(2,1)S(1)} all-to-all(bf16[8,128,128]{2,1,0:T(8,128)(2,1)S(1)} %broadcast_in_dim.43), channel_id=1, replica_groups=mesh['ylo'=2,'x'=4,'z'=8,'yhi'=2,'core'=2] {'z'}, dimensions={0} | all-to-all | bytes 524288 | tf_op jit(solution)/shard_map/all_to_all | solution.py:114
  111.5 1.8 broadcast_in_dim.44
  113.4 3.6 %all-to-all-start.2 = ((bf16[8,8,128,128]{3,2,1,0:T(8,128)(2,1)}), bf16[8,8,128,128]{3,2,1,0:T(8,128)(2,1)S(1)}, u32[]{:S(2)}, u32[]{:S(2)}) async-start(bf16[8,8,128,128]{3,2,1,0:T(8,128)(2,1)} %broadcast_in_dim.44), calls=%async_computation.2 | async-start | bytes 4194304 | tf_op jit(solution)/shard_map/all_to_all | solution.py:116
  117.0 16.2 %all-to-all-done.2 = bf16[8,8,128,128]{3,2,1,0:T(8,128)(2,1)S(1)} async-done(((bf16[8,8,128,128]{3,2,1,0:T(8,128)(2,1)}), bf16[8,8,128,128]{3,2,1,0:T(8,128)(2,1)S(1)}, u32[]{:S(2)}, u32[]{:S(2)}) %all-to-all-start.2) | async-done | bytes 2097184 | tf_op jit(solution)/shard_map/all_to_all | solution.py:116
  133.2 1.3 copy-done
  134.5 15.7 %shard_map.78 = f32[8,128,128]{2,1,0:T(8,128)} custom-call(s32[1152]{0:T(1024)} %get-tuple-element.15.index_ref, bf16[64,128,128]{2,1,0:T(8,128)(2,1)} %a_ref.1, bf16[64,128,128]{2,1,0:T(8,128)(2,1)} %bitcast.109), custom_call_target="tpu_custom_call" | custom-call | tf_op jit(solution)/shard_map/pallas_call | solution.py:36
  151.3 11.9 %collective-permute-start.14 = (f32[256,128]{1,0:T(8,128)S(1)}, f32[256,128]{1,0:T(8,128)S(1)}, u32[]{:S(2)}, u32[]{:S(2)}) collective-permute-start(f32[256,128]{1,0:T(8,128)S(1)} %dynamic-slice_bitcast_fusion.3), channel_id=1, source_target_pairs={{0,1},{1,0},{2,3},{3,2},{4,5},{5,4},{6,7},{7,6},{8,9},{9,8},{10,11... | collective-permute-start | bytes 393224 | tf_op jit(solution)/shard_map/ppermute | solution.py:63
  164.8 2.7 %collective-permute-start.16 = (f32[128,128]{1,0:T(8,128)S(1)}, f32[128,128]{1,0:T(8,128)S(1)}, u32[]{:S(2)}, u32[]{:S(2)}) collective-permute-start(f32[128,128]{1,0:T(8,128)S(1)} %dynamic-slice_bitcast_fusion.5), channel_id=1, source_target_pairs={{0,2},{2,0},{1,3},{3,1},{4,6},{6,4},{5,7},{7,5},{8,10},{10,8},{9,1... | collective-permute-start | bytes 196616 | tf_op jit(solution)/shard_map/ppermute | solution.py:63
  167.8 2.0 %collective-permute-done.16 = f32[128,128]{1,0:T(8,128)S(1)} collective-permute-done((f32[128,128]{1,0:T(8,128)S(1)}, f32[128,128]{1,0:T(8,128)S(1)}, u32[]{:S(2)}, u32[]{:S(2)}) %collective-permute-start.16) | collective-permute-done | bytes 65568 | tf_op jit(solution)/shard_map/ppermute | solution.py:63
  169.9 2.7 %collective-permute-start.18 = (f32[128,128]{1,0:T(8,128)S(1)}, f32[128,128]{1,0:T(8,128)S(1)}, u32[]{:S(2)}, u32[]{:S(2)}) collective-permute-start(f32[128,128]{1,0:T(8,128)S(1)} %bitcast_add_fusion.18), channel_id=1, source_target_pairs={{0,2},{2,0},{1,3},{3,1},{4,6},{6,4},{5,7},{7,5},{8,10},{10,8},{9,1... | collective-permute-start | bytes 196616 | tf_op jit(solution)/shard_map/ppermute | solution.py:80
  172.6 1.4 collective-permute-start.19
  174.6 2.7 %collective-permute-done.19 = f32[128,128]{1,0:T(8,128)S(1)} collective-permute-done((f32[128,128]{1,0:T(8,128)S(1)}, f32[128,128]{1,0:T(8,128)S(1)}, u32[]{:S(2)}, u32[]{:S(2)}) %collective-permute-start.19) | collective-permute-done | bytes 65568 | tf_op jit(solution)/shard_map/ppermute | solution.py:81
  177.4 3.1 %collective-permute-start.20 = (f32[256,128]{1,0:T(8,128)S(1)}, f32[256,128]{1,0:T(8,128)S(1)}, u32[]{:S(2)}, u32[]{:S(2)}) collective-permute-start(f32[256,128]{1,0:T(8,128)S(1)} %get-tuple-element.9), channel_id=1, source_target_pairs={{0,1},{1,0},{2,3},{3,2},{4,5},{5,4},{6,7},{7,6},{8,9},{9,8},{10,11... | collective-permute-start | bytes 393224 | tf_op jit(solution)/shard_map/ppermute | solution.py:80
  (77 shorter events, 21.6 us)
Async XLA Ops:
  22.3 12.5 %collective-permute-start = (f32[512,128]{1,0:T(8,128)S(1)}, f32[512,128]{1,0:T(8,128)S(1)}, u32[]{:S(2)}, u32[]{:S(2)}) collective-permute-start(f32[512,128]{1,0:T(8,128)S(1)} %dynamic-slice_bitcast_fusion.1), channel_id=1, source_target_pairs={{0,4},{4,8},{8,12},{12,16},{16,20},{20,24},{24,28},{28,0},{1,5},{5... | collective-permute-start | bytes 786440 | tf_op jit(solution)/shard_map/ppermute | solution.py:63
  24.8 11.0 %collective-permute-start.7 = (f32[512,128]{1,0:T(8,128)S(1)}, f32[512,128]{1,0:T(8,128)S(1)}, u32[]{:S(2)}, u32[]{:S(2)}) collective-permute-start(f32[512,128]{1,0:T(8,128)S(1)} %dynamic-slice_bitcast_fusion), channel_id=1, source_target_pairs={{0,28},{4,0},{8,4},{12,8},{16,12},{20,16},{24,20},{28,24},{1,29},{... | collective-permute-start | bytes 786440 | tf_op jit(solution)/shard_map/ppermute | solution.py:64
  35.7 7.9 %collective-permute-start.1 = (f32[512,128]{1,0:T(8,128)S(1)}, f32[512,128]{1,0:T(8,128)S(1)}, u32[]{:S(2)}, u32[]{:S(2)}) collective-permute-start(f32[512,128]{1,0:T(8,128)S(1)} %bitcast_add_fusion.14), channel_id=1, source_target_pairs={{0,4},{4,8},{8,12},{12,16},{16,20},{20,24},{24,28},{28,0},{1,5},{5... | collective-permute-start | bytes 786440 | tf_op jit(solution)/shard_map/ppermute | solution.py:63
  35.8 8.8 %collective-permute-start.8 = (f32[512,128]{1,0:T(8,128)S(1)}, f32[512,128]{1,0:T(8,128)S(1)}, u32[]{:S(2)}, u32[]{:S(2)}) collective-permute-start(f32[512,128]{1,0:T(8,128)S(1)} %bitcast_add_fusion.7), channel_id=1, source_target_pairs={{0,28},{4,0},{8,4},{12,8},{16,12},{20,16},{24,20},{28,24},{1,29},{... | collective-permute-start | bytes 786440 | tf_op jit(solution)/shard_map/ppermute | solution.py:64
  44.6 7.0 %collective-permute-start.2 = (f32[512,128]{1,0:T(8,128)S(1)}, f32[512,128]{1,0:T(8,128)S(1)}, u32[]{:S(2)}, u32[]{:S(2)}) collective-permute-start(f32[512,128]{1,0:T(8,128)S(1)} %bitcast_add_fusion.13), channel_id=1, source_target_pairs={{0,4},{4,8},{8,12},{12,16},{16,20},{20,24},{24,28},{28,0},{1,5},{5... | collective-permute-start | bytes 786440 | tf_op jit(solution)/shard_map/ppermute | solution.py:63
  44.7 8.0 %collective-permute-start.9 = (f32[512,128]{1,0:T(8,128)S(1)}, f32[512,128]{1,0:T(8,128)S(1)}, u32[]{:S(2)}, u32[]{:S(2)}) collective-permute-start(f32[512,128]{1,0:T(8,128)S(1)} %bitcast_add_fusion.6), channel_id=1, source_target_pairs={{0,28},{4,0},{8,4},{12,8},{16,12},{20,16},{24,20},{28,24},{1,29},{... | collective-permute-start | bytes 786440 | tf_op jit(solution)/shard_map/ppermute | solution.py:64
  52.6 6.5 %collective-permute-start.3 = (f32[512,128]{1,0:T(8,128)S(1)}, f32[512,128]{1,0:T(8,128)S(1)}, u32[]{:S(2)}, u32[]{:S(2)}) collective-permute-start(f32[512,128]{1,0:T(8,128)S(1)} %bitcast_add_fusion.12), channel_id=1, source_target_pairs={{0,4},{4,8},{8,12},{12,16},{16,20},{20,24},{24,28},{28,0},{1,5},{5... | collective-permute-start | bytes 786440 | tf_op jit(solution)/shard_map/ppermute | solution.py:63
  52.8 7.4 %collective-permute-start.10 = (f32[512,128]{1,0:T(8,128)S(1)}, f32[512,128]{1,0:T(8,128)S(1)}, u32[]{:S(2)}, u32[]{:S(2)}) collective-permute-start(f32[512,128]{1,0:T(8,128)S(1)} %bitcast_add_fusion.5), channel_id=1, source_target_pairs={{0,28},{4,0},{8,4},{12,8},{16,12},{20,16},{24,20},{28,24},{1,29},{... | collective-permute-start | bytes 786440 | tf_op jit(solution)/shard_map/ppermute | solution.py:64
  60.1 6.5 %collective-permute-start.4 = (f32[512,128]{1,0:T(8,128)S(1)}, f32[512,128]{1,0:T(8,128)S(1)}, u32[]{:S(2)}, u32[]{:S(2)}) collective-permute-start(f32[512,128]{1,0:T(8,128)S(1)} %bitcast_add_fusion.11), channel_id=1, source_target_pairs={{0,4},{4,8},{8,12},{12,16},{16,20},{20,24},{24,28},{28,0},{1,5},{5... | collective-permute-start | bytes 786440 | tf_op jit(solution)/shard_map/ppermute | solution.py:63
  60.3 7.4 %collective-permute-start.11 = (f32[512,128]{1,0:T(8,128)S(1)}, f32[512,128]{1,0:T(8,128)S(1)}, u32[]{:S(2)}, u32[]{:S(2)}) collective-permute-start(f32[512,128]{1,0:T(8,128)S(1)} %bitcast_add_fusion.4), channel_id=1, source_target_pairs={{0,28},{4,0},{8,4},{12,8},{16,12},{20,16},{24,20},{28,24},{1,29},{... | collective-permute-start | bytes 786440 | tf_op jit(solution)/shard_map/ppermute | solution.py:64
  67.6 6.5 %collective-permute-start.5 = (f32[512,128]{1,0:T(8,128)S(1)}, f32[512,128]{1,0:T(8,128)S(1)}, u32[]{:S(2)}, u32[]{:S(2)}) collective-permute-start(f32[512,128]{1,0:T(8,128)S(1)} %bitcast_add_fusion.10), channel_id=1, source_target_pairs={{0,4},{4,8},{8,12},{12,16},{16,20},{20,24},{24,28},{28,0},{1,5},{5... | collective-permute-start | bytes 786440 | tf_op jit(solution)/shard_map/ppermute | solution.py:63
  67.7 7.4 %collective-permute-start.12 = (f32[512,128]{1,0:T(8,128)S(1)}, f32[512,128]{1,0:T(8,128)S(1)}, u32[]{:S(2)}, u32[]{:S(2)}) collective-permute-start(f32[512,128]{1,0:T(8,128)S(1)} %bitcast_add_fusion.3), channel_id=1, source_target_pairs={{0,28},{4,0},{8,4},{12,8},{16,12},{20,16},{24,20},{28,24},{1,29},{... | collective-permute-start | bytes 786440 | tf_op jit(solution)/shard_map/ppermute | solution.py:64
  75.1 7.5 %collective-permute-start.6 = (f32[512,128]{1,0:T(8,128)S(1)}, f32[512,128]{1,0:T(8,128)S(1)}, u32[]{:S(2)}, u32[]{:S(2)}) collective-permute-start(f32[512,128]{1,0:T(8,128)S(1)} %bitcast_add_fusion.9), channel_id=1, source_target_pairs={{0,4},{4,8},{8,12},{12,16},{16,20},{20,24},{24,28},{28,0},{1,5},{5... | collective-permute-start | bytes 786440 | tf_op jit(solution)/shard_map/ppermute | solution.py:63
  75.2 8.4 %collective-permute-start.13 = (f32[512,128]{1,0:T(8,128)S(1)}, f32[512,128]{1,0:T(8,128)S(1)}, u32[]{:S(2)}, u32[]{:S(2)}) collective-permute-start(f32[512,128]{1,0:T(8,128)S(1)} %bitcast_add_fusion.2), channel_id=1, source_target_pairs={{0,28},{4,0},{8,4},{12,8},{16,12},{20,16},{24,20},{28,24},{1,29},{... | collective-permute-start | bytes 786440 | tf_op jit(solution)/shard_map/ppermute | solution.py:64
  84.5 12.5 %all-to-all-start = ((f32[8,128,128]{2,1,0:T(8,128)}), f32[8,128,128]{2,1,0:T(8,128)S(1)}, u32[]{:S(2)}, u32[]{:S(2)}) async-start(f32[8,128,128]{2,1,0:T(8,128)} %bitcast.20), calls=%async_computation | async-start | bytes 1048576 | tf_op jit(solution)/shard_map/all_to_all | solution.py:107
  113.4 19.8 %all-to-all-start.2 = ((bf16[8,8,128,128]{3,2,1,0:T(8,128)(2,1)}), bf16[8,8,128,128]{3,2,1,0:T(8,128)(2,1)S(1)}, u32[]{:S(2)}, u32[]{:S(2)}) async-start(bf16[8,8,128,128]{3,2,1,0:T(8,128)(2,1)} %broadcast_in_dim.44), calls=%async_computation.2 | async-start | bytes 4194304 | tf_op jit(solution)/shard_map/all_to_all | solution.py:116
  133.2 1.3 copy-start
  151.3 12.9 %collective-permute-start.14 = (f32[256,128]{1,0:T(8,128)S(1)}, f32[256,128]{1,0:T(8,128)S(1)}, u32[]{:S(2)}, u32[]{:S(2)}) collective-permute-start(f32[256,128]{1,0:T(8,128)S(1)} %dynamic-slice_bitcast_fusion.3), channel_id=1, source_target_pairs={{0,1},{1,0},{2,3},{3,2},{4,5},{5,4},{6,7},{7,6},{8,9},{9,8},{10,11... | collective-permute-start | bytes 393224 | tf_op jit(solution)/shard_map/ppermute | solution.py:63
  163.2 1.4 collective-permute-start.15
  164.8 5.1 %collective-permute-start.16 = (f32[128,128]{1,0:T(8,128)S(1)}, f32[128,128]{1,0:T(8,128)S(1)}, u32[]{:S(2)}, u32[]{:S(2)}) collective-permute-start(f32[128,128]{1,0:T(8,128)S(1)} %dynamic-slice_bitcast_fusion.5), channel_id=1, source_target_pairs={{0,2},{2,0},{1,3},{3,1},{4,6},{6,4},{5,7},{7,5},{8,10},{10,8},{9,1... | collective-permute-start | bytes 196616 | tf_op jit(solution)/shard_map/ppermute | solution.py:63
  167.5 5.1 %collective-permute-start.17 = (f32[128,128]{1,0:T(8,128)S(1)}, f32[128,128]{1,0:T(8,128)S(1)}, u32[]{:S(2)}, u32[]{:S(2)}) collective-permute-start(f32[128,128]{1,0:T(8,128)S(1)} %dynamic-slice_bitcast_fusion.4), channel_id=1, source_target_pairs={{0,2},{2,0},{1,3},{3,1},{4,6},{6,4},{5,7},{7,5},{8,10},{10,8},{9,1... | collective-permute-start | bytes 196616 | tf_op jit(solution)/shard_map/ppermute | solution.py:64
  169.9 12.8 %copy-start.1 = (f32[1024,128]{1,0:T(8,128)S(1)}, f32[1024,128]{1,0:T(8,128)}, u32[]{:S(2)}) copy-start(f32[1024,128]{1,0:T(8,128)} %param.6) | copy-start | bytes 1572868
  169.9 4.7 %collective-permute-start.18 = (f32[128,128]{1,0:T(8,128)S(1)}, f32[128,128]{1,0:T(8,128)S(1)}, u32[]{:S(2)}, u32[]{:S(2)}) collective-permute-start(f32[128,128]{1,0:T(8,128)S(1)} %bitcast_add_fusion.18), channel_id=1, source_target_pairs={{0,2},{2,0},{1,3},{3,1},{4,6},{6,4},{5,7},{7,5},{8,10},{10,8},{9,1... | collective-permute-start | bytes 196616 | tf_op jit(solution)/shard_map/ppermute | solution.py:80
  172.6 4.7 %collective-permute-start.19 = (f32[128,128]{1,0:T(8,128)S(1)}, f32[128,128]{1,0:T(8,128)S(1)}, u32[]{:S(2)}, u32[]{:S(2)}) collective-permute-start(f32[128,128]{1,0:T(8,128)S(1)} %bitcast_add_fusion.17), channel_id=1, source_target_pairs={{0,2},{2,0},{1,3},{3,1},{4,6},{6,4},{5,7},{7,5},{8,10},{10,8},{9,1... | collective-permute-start | bytes 196616 | tf_op jit(solution)/shard_map/ppermute | solution.py:81
  177.4 4.1 %collective-permute-start.20 = (f32[256,128]{1,0:T(8,128)S(1)}, f32[256,128]{1,0:T(8,128)S(1)}, u32[]{:S(2)}, u32[]{:S(2)}) collective-permute-start(f32[256,128]{1,0:T(8,128)S(1)} %get-tuple-element.9), channel_id=1, source_target_pairs={{0,1},{1,0},{2,3},{3,2},{4,5},{5,4},{6,7},{7,6},{8,9},{9,8},{10,11... | collective-permute-start | bytes 393224 | tf_op jit(solution)/shard_map/ppermute | solution.py:80
  181.2 1.3 collective-permute-start.21

commit v7 on v6

--- a/solution.py
+++ b/solution.py
@@ -25,7 +25,7 @@
         )
         return carry
 
-    lax.fori_loop(0, n_blocks, body, 0, unroll=16)
+    lax.fori_loop(0, n_blocks, body, 0, unroll=32)
 
 
 def block_sums(index, a_tiles, b_tiles, n_out, b_transposed=False):
@@ -110,14 +110,14 @@
     position = lax.axis_index(USER_AXES)
     own_base = lax.dynamic_slice_in_dim(item_base[0], position * tile_rows, tile_rows, 0)
     own_emb = (1.0 - teleport) * own_sum + teleport * own_base
-    own_bf_t = own_emb.astype(jnp.bfloat16).T
-    t = lax.all_to_all(jnp.broadcast_to(own_bf_t[None], (n_z, width, tile_rows)), "z", 0, 0, tiled=True)
-    t = jnp.broadcast_to(t[None], (n_ylo * n_x, n_z, width, tile_rows))
+    own_bf = own_emb.astype(jnp.bfloat16)
+    t = lax.all_to_all(jnp.broadcast_to(own_bf[None], (n_z, tile_rows, width)), "z", 0, 0, tiled=True)
+    t = jnp.broadcast_to(t[None], (n_ylo * n_x, n_z, tile_rows, width))
     t = lax.all_to_all(t, ("ylo", "x"), 0, 0, tiled=True)
-    item_tiles_t = t.reshape(n_users, width, tile_rows)
+    item_tiles = t.reshape(n_users, tile_rows, width)
 
     user_index = jnp.concatenate([weights_list, items_list, users_list])
-    user_part = block_sums(user_index, weight_tiles, item_tiles_t, n_user_tiles, b_transposed=True)
+    user_part = block_sums(user_index, weight_tiles, item_tiles, n_user_tiles)
     y = user_part.reshape(n_core, -1, width)
     y = ring_reduce_scatter(y, "core", n_core)
     y = ring_reduce_scatter(y.reshape(n_yhi, -1, width), "yhi", n_yhi)

time: 184 us -> 176 us (0.957)
  Pallas kernels: 27.6 us -> 19.7 us
    pallas_call x2, Pallas kernels: 27.6 us -> 19.7 us  [block_sums(): pl.pallas_call(functools.partial(block_sum_kernel, b_transposed=b_transpo...]
where the time goes in v7:
time: 176 us
  waiting for transfers between devices  61 us (35%)
  starting transfers between devices  54.7 us (31%)
  Pallas kernels  19.7 us (11%)
  blocking collectives  14.4 us (8%)
  other arithmetic  12.7 us (7%)
  local copies, waits for them, and re-layouts  12 us (7%)
    ppermute x9, waiting for transfers between devices, ring_reduce_scatter_halves(): rl = lax.ppermute(bl, axis, right)  33.3 us
    ppermute x9, starting transfers between devices, ring_reduce_scatter_halves(): rr = lax.ppermute(br, axis, left)  21.2 us
    pallas_call x2, Pallas kernels, block_sums(): pl.pallas_call(functools.partial(block_sum_kernel, b_transposed=b_transpo...  19.7 us
    ppermute x9, starting transfers between devices, ring_reduce_scatter_halves(): rl = lax.ppermute(bl, axis, right)  17.7 us
    all_to_all x1, waiting for transfers between devices, per_device(): t = lax.all_to_all(t, ('ylo', 'x'), 0, 0, tiled=True)  16.2 us
    all_to_all x1, blocking collectives, per_device(): lax.all_to_all(jnp.broadcast_to(own_bf[None], (n_z, tile_rows, width)), '...  14.4 us
    add x9, other arithmetic, ring_reduce_scatter_halves(): bl = rl + lax.dynamic_index_in_dim(xl, (i - s - 2) % n, 0, keepdims=False)  6.87 us
    all_to_all x1, waiting for transfers between devices, per_device(): x = lax.all_to_all(x, ('ylo', 'x'), 0, 0, tiled=True)  6.6 us
  transfers between devices with their start and end apart: 24, of which 16 were waited for; matrix products, arithmetic and copies ran while one was open for 5% of the time, Pallas kernels for 0%

profile of v7, /device:TPU:1, one launch (start us, length us, event | category | flops | bytes accessed | tf_op | source)
XLA Modules:
  0.0 175.7 jit_solution(17273301376447290953)
XLA Ops:
  5.3 10.3 %shard_map.77 = f32[64,128,128]{2,1,0:T(8,128)} custom-call(s32[1152]{0:T(1024)} %get-tuple-element.14.index_ref, bf16[8,128,128]{2,1,0:T(8,128)(2,1)} %bitcast.110, bf16[64,128,128]{2,1,0:T(8,128)(2,1)} %a_ref.1), custom_call_target="tpu_custom_call" | custom-call | tf_op jit(solution)/shard_map/pallas_call | solution.py:36
  15.6 4.0 %fusion.10 = (f32[32,128,128]{2,1,0:T(8,128)}, f32[32,128,128]{2,1,0:T(8,128)S(1)}) fusion(f32[64,128,128]{2,1,0:T(8,128)} %shard_map.77), kind=kLoop, calls=%fused_computation.62 | loop fusion | bytes 8388608 | tf_op jit(solution)/shard_map/slice | solution.py:105
  20.5 2.5 %collective-permute-start = (f32[512,128]{1,0:T(8,128)S(1)}, f32[512,128]{1,0:T(8,128)S(1)}, u32[]{:S(2)}, u32[]{:S(2)}) collective-permute-start(f32[512,128]{1,0:T(8,128)S(1)} %dynamic-slice_bitcast_fusion.1), channel_id=1, source_target_pairs={{0,4},{4,8},{8,12},{12,16},{16,20},{20,24},{24,28},{28,0},{1,5},{5... | collective-permute-start | bytes 786440 | tf_op jit(solution)/shard_map/ppermute | solution.py:63
  23.1 4.1 %collective-permute-start.7 = (f32[512,128]{1,0:T(8,128)S(1)}, f32[512,128]{1,0:T(8,128)S(1)}, u32[]{:S(2)}, u32[]{:S(2)}) collective-permute-start(f32[512,128]{1,0:T(8,128)S(1)} %dynamic-slice_bitcast_fusion), channel_id=1, source_target_pairs={{0,28},{4,0},{8,4},{12,8},{16,12},{20,16},{24,20},{28,24},{1,29},{... | collective-permute-start | bytes 786440 | tf_op jit(solution)/shard_map/ppermute | solution.py:64
  27.1 5.9 %collective-permute-done = f32[512,128]{1,0:T(8,128)S(1)} collective-permute-done((f32[512,128]{1,0:T(8,128)S(1)}, f32[512,128]{1,0:T(8,128)S(1)}, u32[]{:S(2)}, u32[]{:S(2)}) %collective-permute-start) | collective-permute-done | bytes 262176 | tf_op jit(solution)/shard_map/ppermute | solution.py:63
  34.1 2.7 %collective-permute-start.8 = (f32[512,128]{1,0:T(8,128)S(1)}, f32[512,128]{1,0:T(8,128)S(1)}, u32[]{:S(2)}, u32[]{:S(2)}) collective-permute-start(f32[512,128]{1,0:T(8,128)S(1)} %bitcast_add_fusion.7), channel_id=1, source_target_pairs={{0,28},{4,0},{8,4},{12,8},{16,12},{20,16},{24,20},{28,24},{1,29},{... | collective-permute-start | bytes 786440 | tf_op jit(solution)/shard_map/ppermute | solution.py:64
  36.8 5.0 %collective-permute-done.1 = f32[512,128]{1,0:T(8,128)S(1)} collective-permute-done((f32[512,128]{1,0:T(8,128)S(1)}, f32[512,128]{1,0:T(8,128)S(1)}, u32[]{:S(2)}, u32[]{:S(2)}) %collective-permute-start.1) | collective-permute-done | bytes 262176 | tf_op jit(solution)/shard_map/ppermute | solution.py:63
  43.0 2.7 %collective-permute-start.9 = (f32[512,128]{1,0:T(8,128)S(1)}, f32[512,128]{1,0:T(8,128)S(1)}, u32[]{:S(2)}, u32[]{:S(2)}) collective-permute-start(f32[512,128]{1,0:T(8,128)S(1)} %bitcast_add_fusion.6), channel_id=1, source_target_pairs={{0,28},{4,0},{8,4},{12,8},{16,12},{20,16},{24,20},{28,24},{1,29},{... | collective-permute-start | bytes 786440 | tf_op jit(solution)/shard_map/ppermute | solution.py:64
  45.7 4.2 %collective-permute-done.2 = f32[512,128]{1,0:T(8,128)S(1)} collective-permute-done((f32[512,128]{1,0:T(8,128)S(1)}, f32[512,128]{1,0:T(8,128)S(1)}, u32[]{:S(2)}, u32[]{:S(2)}) %collective-permute-start.2) | collective-permute-done | bytes 262176 | tf_op jit(solution)/shard_map/ppermute | solution.py:63
  51.0 2.7 %collective-permute-start.10 = (f32[512,128]{1,0:T(8,128)S(1)}, f32[512,128]{1,0:T(8,128)S(1)}, u32[]{:S(2)}, u32[]{:S(2)}) collective-permute-start(f32[512,128]{1,0:T(8,128)S(1)} %bitcast_add_fusion.5), channel_id=1, source_target_pairs={{0,28},{4,0},{8,4},{12,8},{16,12},{20,16},{24,20},{28,24},{1,29},{... | collective-permute-start | bytes 786440 | tf_op jit(solution)/shard_map/ppermute | solution.py:64
  53.7 3.6 %collective-permute-done.3 = f32[512,128]{1,0:T(8,128)S(1)} collective-permute-done((f32[512,128]{1,0:T(8,128)S(1)}, f32[512,128]{1,0:T(8,128)S(1)}, u32[]{:S(2)}, u32[]{:S(2)}) %collective-permute-start.3) | collective-permute-done | bytes 262176 | tf_op jit(solution)/shard_map/ppermute | solution.py:63
  58.5 2.7 %collective-permute-start.11 = (f32[512,128]{1,0:T(8,128)S(1)}, f32[512,128]{1,0:T(8,128)S(1)}, u32[]{:S(2)}, u32[]{:S(2)}) collective-permute-start(f32[512,128]{1,0:T(8,128)S(1)} %bitcast_add_fusion.4), channel_id=1, source_target_pairs={{0,28},{4,0},{8,4},{12,8},{16,12},{20,16},{24,20},{28,24},{1,29},{... | collective-permute-start | bytes 786440 | tf_op jit(solution)/shard_map/ppermute | solution.py:64
  61.2 3.6 %collective-permute-done.4 = f32[512,128]{1,0:T(8,128)S(1)} collective-permute-done((f32[512,128]{1,0:T(8,128)S(1)}, f32[512,128]{1,0:T(8,128)S(1)}, u32[]{:S(2)}, u32[]{:S(2)}) %collective-permute-start.4) | collective-permute-done | bytes 262176 | tf_op jit(solution)/shard_map/ppermute | solution.py:63
  66.0 2.7 %collective-permute-start.12 = (f32[512,128]{1,0:T(8,128)S(1)}, f32[512,128]{1,0:T(8,128)S(1)}, u32[]{:S(2)}, u32[]{:S(2)}) collective-permute-start(f32[512,128]{1,0:T(8,128)S(1)} %bitcast_add_fusion.3), channel_id=1, source_target_pairs={{0,28},{4,0},{8,4},{12,8},{16,12},{20,16},{24,20},{28,24},{1,29},{... | collective-permute-start | bytes 786440 | tf_op jit(solution)/shard_map/ppermute | solution.py:64
  68.7 3.6 %collective-permute-done.5 = f32[512,128]{1,0:T(8,128)S(1)} collective-permute-done((f32[512,128]{1,0:T(8,128)S(1)}, f32[512,128]{1,0:T(8,128)S(1)}, u32[]{:S(2)}, u32[]{:S(2)}) %collective-permute-start.5) | collective-permute-done | bytes 262176 | tf_op jit(solution)/shard_map/ppermute | solution.py:63
  73.5 2.9 %collective-permute-start.13 = (f32[512,128]{1,0:T(8,128)S(1)}, f32[512,128]{1,0:T(8,128)S(1)}, u32[]{:S(2)}, u32[]{:S(2)}) collective-permute-start(f32[512,128]{1,0:T(8,128)S(1)} %bitcast_add_fusion.2), channel_id=1, source_target_pairs={{0,28},{4,0},{8,4},{12,8},{16,12},{20,16},{24,20},{28,24},{1,29},{... | collective-permute-start | bytes 786440 | tf_op jit(solution)/shard_map/ppermute | solution.py:64
  76.4 4.5 %collective-permute-done.6 = f32[512,128]{1,0:T(8,128)S(1)} collective-permute-done((f32[512,128]{1,0:T(8,128)S(1)}, f32[512,128]{1,0:T(8,128)S(1)}, u32[]{:S(2)}, u32[]{:S(2)}) %collective-permute-start.6) | collective-permute-done | bytes 262176 | tf_op jit(solution)/shard_map/ppermute | solution.py:63
  82.8 5.0 %all-to-all-start = ((f32[8,128,128]{2,1,0:T(8,128)}), f32[8,128,128]{2,1,0:T(8,128)S(1)}, u32[]{:S(2)}, u32[]{:S(2)}) async-start(f32[8,128,128]{2,1,0:T(8,128)} %bitcast.20), calls=%async_computation | async-start | bytes 1048576 | tf_op jit(solution)/shard_map/all_to_all | solution.py:107
  88.7 6.6 %all-to-all-done = f32[8,128,128]{2,1,0:T(8,128)S(1)} async-done(((f32[8,128,128]{2,1,0:T(8,128)}), f32[8,128,128]{2,1,0:T(8,128)S(1)}, u32[]{:S(2)}, u32[]{:S(2)}) %all-to-all-start) | async-done | bytes 524320 | tf_op jit(solution)/shard_map/all_to_all | solution.py:107
  95.5 14.4 %all_to_all.15 = bf16[8,128,128]{2,1,0:T(8,128)(2,1)S(1)} all-to-all(bf16[8,128,128]{2,1,0:T(8,128)(2,1)S(1)} %broadcast_in_dim.43), channel_id=1, replica_groups=mesh['ylo'=2,'x'=4,'z'=8,'yhi'=2,'core'=2] {'z'}, dimensions={0} | all-to-all | bytes 524288 | tf_op jit(solution)/shard_map/all_to_all | solution.py:114
  109.9 1.8 %broadcast_in_dim.44 = bf16[8,8,128,128]{3,2,1,0:T(8,128)(2,1)} broadcast(bf16[8,128,128]{2,1,0:T(8,128)(2,1)S(1)} %all_to_all.15), dimensions={1,2,3} | broadcast | bytes 2359296 | tf_op jit(solution)/shard_map/broadcast_in_dim | solution.py:115
  111.8 3.6 %all-to-all-start.2 = ((bf16[8,8,128,128]{3,2,1,0:T(8,128)(2,1)}), bf16[8,8,128,128]{3,2,1,0:T(8,128)(2,1)S(1)}, u32[]{:S(2)}, u32[]{:S(2)}) async-start(bf16[8,8,128,128]{3,2,1,0:T(8,128)(2,1)} %broadcast_in_dim.44), calls=%async_computation.2 | async-start | bytes 4194304 | tf_op jit(solution)/shard_map/all_to_all | solution.py:116
  115.4 16.2 %all-to-all-done.2 = bf16[8,8,128,128]{3,2,1,0:T(8,128)(2,1)S(1)} async-done(((bf16[8,8,128,128]{3,2,1,0:T(8,128)(2,1)}), bf16[8,8,128,128]{3,2,1,0:T(8,128)(2,1)S(1)}, u32[]{:S(2)}, u32[]{:S(2)}) %all-to-all-start.2) | async-done | bytes 2097184 | tf_op jit(solution)/shard_map/all_to_all | solution.py:116
  131.6 1.3 copy-done
  132.9 9.4 %shard_map.78 = f32[8,128,128]{2,1,0:T(8,128)} custom-call(s32[1152]{0:T(1024)} %get-tuple-element.15.index_ref, bf16[64,128,128]{2,1,0:T(8,128)(2,1)} %a_ref.1, bf16[64,128,128]{2,1,0:T(8,128)(2,1)} %bitcast.107), custom_call_target="tpu_custom_call" | custom-call | tf_op jit(solution)/shard_map/pallas_call | solution.py:36
  143.4 12.0 %collective-permute-start.14 = (f32[256,128]{1,0:T(8,128)S(1)}, f32[256,128]{1,0:T(8,128)S(1)}, u32[]{:S(2)}, u32[]{:S(2)}) collective-permute-start(f32[256,128]{1,0:T(8,128)S(1)} %dynamic-slice_bitcast_fusion.3), channel_id=1, source_target_pairs={{0,1},{1,0},{2,3},{3,2},{4,5},{5,4},{6,7},{7,6},{8,9},{9,8},{10,11... | collective-permute-start | bytes 393224 | tf_op jit(solution)/shard_map/ppermute | solution.py:63
  157.0 2.7 %collective-permute-start.16 = (f32[128,128]{1,0:T(8,128)S(1)}, f32[128,128]{1,0:T(8,128)S(1)}, u32[]{:S(2)}, u32[]{:S(2)}) collective-permute-start(f32[128,128]{1,0:T(8,128)S(1)} %dynamic-slice_bitcast_fusion.5), channel_id=1, source_target_pairs={{0,2},{2,0},{1,3},{3,1},{4,6},{6,4},{5,7},{7,5},{8,10},{10,8},{9,1... | collective-permute-start | bytes 196616 | tf_op jit(solution)/shard_map/ppermute | solution.py:63
  160.1 2.0 %collective-permute-done.16 = f32[128,128]{1,0:T(8,128)S(1)} collective-permute-done((f32[128,128]{1,0:T(8,128)S(1)}, f32[128,128]{1,0:T(8,128)S(1)}, u32[]{:S(2)}, u32[]{:S(2)}) %collective-permute-start.16) | collective-permute-done | bytes 65568 | tf_op jit(solution)/shard_map/ppermute | solution.py:63
  162.1 2.7 %collective-permute-start.18 = (f32[128,128]{1,0:T(8,128)S(1)}, f32[128,128]{1,0:T(8,128)S(1)}, u32[]{:S(2)}, u32[]{:S(2)}) collective-permute-start(f32[128,128]{1,0:T(8,128)S(1)} %bitcast_add_fusion.18), channel_id=1, source_target_pairs={{0,2},{2,0},{1,3},{3,1},{4,6},{6,4},{5,7},{7,5},{8,10},{10,8},{9,1... | collective-permute-start | bytes 196616 | tf_op jit(solution)/shard_map/ppermute | solution.py:80
  164.8 1.4 collective-permute-start.19
  166.8 2.7 %collective-permute-done.19 = f32[128,128]{1,0:T(8,128)S(1)} collective-permute-done((f32[128,128]{1,0:T(8,128)S(1)}, f32[128,128]{1,0:T(8,128)S(1)}, u32[]{:S(2)}, u32[]{:S(2)}) %collective-permute-start.19) | collective-permute-done | bytes 65568 | tf_op jit(solution)/shard_map/ppermute | solution.py:81
  169.5 3.1 %collective-permute-start.20 = (f32[256,128]{1,0:T(8,128)S(1)}, f32[256,128]{1,0:T(8,128)S(1)}, u32[]{:S(2)}, u32[]{:S(2)}) collective-permute-start(f32[256,128]{1,0:T(8,128)S(1)} %get-tuple-element.9), channel_id=1, source_target_pairs={{0,1},{1,0},{2,3},{3,2},{4,5},{5,4},{6,7},{7,6},{8,9},{9,8},{10,11... | collective-permute-start | bytes 393224 | tf_op jit(solution)/shard_map/ppermute | solution.py:80
  (78 shorter events, 21.9 us)
Async XLA Ops:
  20.5 12.5 %collective-permute-start = (f32[512,128]{1,0:T(8,128)S(1)}, f32[512,128]{1,0:T(8,128)S(1)}, u32[]{:S(2)}, u32[]{:S(2)}) collective-permute-start(f32[512,128]{1,0:T(8,128)S(1)} %dynamic-slice_bitcast_fusion.1), channel_id=1, source_target_pairs={{0,4},{4,8},{8,12},{12,16},{16,20},{20,24},{24,28},{28,0},{1,5},{5... | collective-permute-start | bytes 786440 | tf_op jit(solution)/shard_map/ppermute | solution.py:63
  23.1 11.0 %collective-permute-start.7 = (f32[512,128]{1,0:T(8,128)S(1)}, f32[512,128]{1,0:T(8,128)S(1)}, u32[]{:S(2)}, u32[]{:S(2)}) collective-permute-start(f32[512,128]{1,0:T(8,128)S(1)} %dynamic-slice_bitcast_fusion), channel_id=1, source_target_pairs={{0,28},{4,0},{8,4},{12,8},{16,12},{20,16},{24,20},{28,24},{1,29},{... | collective-permute-start | bytes 786440 | tf_op jit(solution)/shard_map/ppermute | solution.py:64
  34.0 7.9 %collective-permute-start.1 = (f32[512,128]{1,0:T(8,128)S(1)}, f32[512,128]{1,0:T(8,128)S(1)}, u32[]{:S(2)}, u32[]{:S(2)}) collective-permute-start(f32[512,128]{1,0:T(8,128)S(1)} %bitcast_add_fusion.14), channel_id=1, source_target_pairs={{0,4},{4,8},{8,12},{12,16},{16,20},{20,24},{24,28},{28,0},{1,5},{5... | collective-permute-start | bytes 786440 | tf_op jit(solution)/shard_map/ppermute | solution.py:63
  34.1 8.8 %collective-permute-start.8 = (f32[512,128]{1,0:T(8,128)S(1)}, f32[512,128]{1,0:T(8,128)S(1)}, u32[]{:S(2)}, u32[]{:S(2)}) collective-permute-start(f32[512,128]{1,0:T(8,128)S(1)} %bitcast_add_fusion.7), channel_id=1, source_target_pairs={{0,28},{4,0},{8,4},{12,8},{16,12},{20,16},{24,20},{28,24},{1,29},{... | collective-permute-start | bytes 786440 | tf_op jit(solution)/shard_map/ppermute | solution.py:64
  42.8 7.0 %collective-permute-start.2 = (f32[512,128]{1,0:T(8,128)S(1)}, f32[512,128]{1,0:T(8,128)S(1)}, u32[]{:S(2)}, u32[]{:S(2)}) collective-permute-start(f32[512,128]{1,0:T(8,128)S(1)} %bitcast_add_fusion.13), channel_id=1, source_target_pairs={{0,4},{4,8},{8,12},{12,16},{16,20},{20,24},{24,28},{28,0},{1,5},{5... | collective-permute-start | bytes 786440 | tf_op jit(solution)/shard_map/ppermute | solution.py:63
  43.0 8.0 %collective-permute-start.9 = (f32[512,128]{1,0:T(8,128)S(1)}, f32[512,128]{1,0:T(8,128)S(1)}, u32[]{:S(2)}, u32[]{:S(2)}) collective-permute-start(f32[512,128]{1,0:T(8,128)S(1)} %bitcast_add_fusion.6), channel_id=1, source_target_pairs={{0,28},{4,0},{8,4},{12,8},{16,12},{20,16},{24,20},{28,24},{1,29},{... | collective-permute-start | bytes 786440 | tf_op jit(solution)/shard_map/ppermute | solution.py:64
  50.9 6.5 %collective-permute-start.3 = (f32[512,128]{1,0:T(8,128)S(1)}, f32[512,128]{1,0:T(8,128)S(1)}, u32[]{:S(2)}, u32[]{:S(2)}) collective-permute-start(f32[512,128]{1,0:T(8,128)S(1)} %bitcast_add_fusion.12), channel_id=1, source_target_pairs={{0,4},{4,8},{8,12},{12,16},{16,20},{20,24},{24,28},{28,0},{1,5},{5... | collective-permute-start | bytes 786440 | tf_op jit(solution)/shard_map/ppermute | solution.py:63
  51.0 7.4 %collective-permute-start.10 = (f32[512,128]{1,0:T(8,128)S(1)}, f32[512,128]{1,0:T(8,128)S(1)}, u32[]{:S(2)}, u32[]{:S(2)}) collective-permute-start(f32[512,128]{1,0:T(8,128)S(1)} %bitcast_add_fusion.5), channel_id=1, source_target_pairs={{0,28},{4,0},{8,4},{12,8},{16,12},{20,16},{24,20},{28,24},{1,29},{... | collective-permute-start | bytes 786440 | tf_op jit(solution)/shard_map/ppermute | solution.py:64
  58.4 6.5 %collective-permute-start.4 = (f32[512,128]{1,0:T(8,128)S(1)}, f32[512,128]{1,0:T(8,128)S(1)}, u32[]{:S(2)}, u32[]{:S(2)}) collective-permute-start(f32[512,128]{1,0:T(8,128)S(1)} %bitcast_add_fusion.11), channel_id=1, source_target_pairs={{0,4},{4,8},{8,12},{12,16},{16,20},{20,24},{24,28},{28,0},{1,5},{5... | collective-permute-start | bytes 786440 | tf_op jit(solution)/shard_map/ppermute | solution.py:63
  58.5 7.4 %collective-permute-start.11 = (f32[512,128]{1,0:T(8,128)S(1)}, f32[512,128]{1,0:T(8,128)S(1)}, u32[]{:S(2)}, u32[]{:S(2)}) collective-permute-start(f32[512,128]{1,0:T(8,128)S(1)} %bitcast_add_fusion.4), channel_id=1, source_target_pairs={{0,28},{4,0},{8,4},{12,8},{16,12},{20,16},{24,20},{28,24},{1,29},{... | collective-permute-start | bytes 786440 | tf_op jit(solution)/shard_map/ppermute | solution.py:64
  65.8 6.5 %collective-permute-start.5 = (f32[512,128]{1,0:T(8,128)S(1)}, f32[512,128]{1,0:T(8,128)S(1)}, u32[]{:S(2)}, u32[]{:S(2)}) collective-permute-start(f32[512,128]{1,0:T(8,128)S(1)} %bitcast_add_fusion.10), channel_id=1, source_target_pairs={{0,4},{4,8},{8,12},{12,16},{16,20},{20,24},{24,28},{28,0},{1,5},{5... | collective-permute-start | bytes 786440 | tf_op jit(solution)/shard_map/ppermute | solution.py:63
  66.0 7.4 %collective-permute-start.12 = (f32[512,128]{1,0:T(8,128)S(1)}, f32[512,128]{1,0:T(8,128)S(1)}, u32[]{:S(2)}, u32[]{:S(2)}) collective-permute-start(f32[512,128]{1,0:T(8,128)S(1)} %bitcast_add_fusion.3), channel_id=1, source_target_pairs={{0,28},{4,0},{8,4},{12,8},{16,12},{20,16},{24,20},{28,24},{1,29},{... | collective-permute-start | bytes 786440 | tf_op jit(solution)/shard_map/ppermute | solution.py:64
  73.3 7.6 %collective-permute-start.6 = (f32[512,128]{1,0:T(8,128)S(1)}, f32[512,128]{1,0:T(8,128)S(1)}, u32[]{:S(2)}, u32[]{:S(2)}) collective-permute-start(f32[512,128]{1,0:T(8,128)S(1)} %bitcast_add_fusion.9), channel_id=1, source_target_pairs={{0,4},{4,8},{8,12},{12,16},{16,20},{20,24},{24,28},{28,0},{1,5},{5... | collective-permute-start | bytes 786440 | tf_op jit(solution)/shard_map/ppermute | solution.py:63
  73.5 8.4 %collective-permute-start.13 = (f32[512,128]{1,0:T(8,128)S(1)}, f32[512,128]{1,0:T(8,128)S(1)}, u32[]{:S(2)}, u32[]{:S(2)}) collective-permute-start(f32[512,128]{1,0:T(8,128)S(1)} %bitcast_add_fusion.2), channel_id=1, source_target_pairs={{0,28},{4,0},{8,4},{12,8},{16,12},{20,16},{24,20},{28,24},{1,29},{... | collective-permute-start | bytes 786440 | tf_op jit(solution)/shard_map/ppermute | solution.py:64
  82.8 12.6 %all-to-all-start = ((f32[8,128,128]{2,1,0:T(8,128)}), f32[8,128,128]{2,1,0:T(8,128)S(1)}, u32[]{:S(2)}, u32[]{:S(2)}) async-start(f32[8,128,128]{2,1,0:T(8,128)} %bitcast.20), calls=%async_computation | async-start | bytes 1048576 | tf_op jit(solution)/shard_map/all_to_all | solution.py:107
  111.8 19.8 %all-to-all-start.2 = ((bf16[8,8,128,128]{3,2,1,0:T(8,128)(2,1)}), bf16[8,8,128,128]{3,2,1,0:T(8,128)(2,1)S(1)}, u32[]{:S(2)}, u32[]{:S(2)}) async-start(bf16[8,8,128,128]{3,2,1,0:T(8,128)(2,1)} %broadcast_in_dim.44), calls=%async_computation.2 | async-start | bytes 4194304 | tf_op jit(solution)/shard_map/all_to_all | solution.py:116
  131.6 1.3 copy-start
  143.4 13.0 %collective-permute-start.14 = (f32[256,128]{1,0:T(8,128)S(1)}, f32[256,128]{1,0:T(8,128)S(1)}, u32[]{:S(2)}, u32[]{:S(2)}) collective-permute-start(f32[256,128]{1,0:T(8,128)S(1)} %dynamic-slice_bitcast_fusion.3), channel_id=1, source_target_pairs={{0,1},{1,0},{2,3},{3,2},{4,5},{5,4},{6,7},{7,6},{8,9},{9,8},{10,11... | collective-permute-start | bytes 393224 | tf_op jit(solution)/shard_map/ppermute | solution.py:63
  155.5 1.4 collective-permute-start.15
  157.0 5.1 %collective-permute-start.16 = (f32[128,128]{1,0:T(8,128)S(1)}, f32[128,128]{1,0:T(8,128)S(1)}, u32[]{:S(2)}, u32[]{:S(2)}) collective-permute-start(f32[128,128]{1,0:T(8,128)S(1)} %dynamic-slice_bitcast_fusion.5), channel_id=1, source_target_pairs={{0,2},{2,0},{1,3},{3,1},{4,6},{6,4},{5,7},{7,5},{8,10},{10,8},{9,1... | collective-permute-start | bytes 196616 | tf_op jit(solution)/shard_map/ppermute | solution.py:63
  159.6 5.1 %collective-permute-start.17 = (f32[128,128]{1,0:T(8,128)S(1)}, f32[128,128]{1,0:T(8,128)S(1)}, u32[]{:S(2)}, u32[]{:S(2)}) collective-permute-start(f32[128,128]{1,0:T(8,128)S(1)} %dynamic-slice_bitcast_fusion.4), channel_id=1, source_target_pairs={{0,2},{2,0},{1,3},{3,1},{4,6},{6,4},{5,7},{7,5},{8,10},{10,8},{9,1... | collective-permute-start | bytes 196616 | tf_op jit(solution)/shard_map/ppermute | solution.py:64
  162.1 12.7 %copy-start.1 = (f32[1024,128]{1,0:T(8,128)S(1)}, f32[1024,128]{1,0:T(8,128)}, u32[]{:S(2)}) copy-start(f32[1024,128]{1,0:T(8,128)} %param.6) | copy-start | bytes 1572868
  162.1 4.7 %collective-permute-start.18 = (f32[128,128]{1,0:T(8,128)S(1)}, f32[128,128]{1,0:T(8,128)S(1)}, u32[]{:S(2)}, u32[]{:S(2)}) collective-permute-start(f32[128,128]{1,0:T(8,128)S(1)} %bitcast_add_fusion.18), channel_id=1, source_target_pairs={{0,2},{2,0},{1,3},{3,1},{4,6},{6,4},{5,7},{7,5},{8,10},{10,8},{9,1... | collective-permute-start | bytes 196616 | tf_op jit(solution)/shard_map/ppermute | solution.py:80
  164.8 4.7 %collective-permute-start.19 = (f32[128,128]{1,0:T(8,128)S(1)}, f32[128,128]{1,0:T(8,128)S(1)}, u32[]{:S(2)}, u32[]{:S(2)}) collective-permute-start(f32[128,128]{1,0:T(8,128)S(1)} %bitcast_add_fusion.17), channel_id=1, source_target_pairs={{0,2},{2,0},{1,3},{3,1},{4,6},{6,4},{5,7},{7,5},{8,10},{10,8},{9,1... | collective-permute-start | bytes 196616 | tf_op jit(solution)/shard_map/ppermute | solution.py:81
  169.5 4.1 %collective-permute-start.20 = (f32[256,128]{1,0:T(8,128)S(1)}, f32[256,128]{1,0:T(8,128)S(1)}, u32[]{:S(2)}, u32[]{:S(2)}) collective-permute-start(f32[256,128]{1,0:T(8,128)S(1)} %get-tuple-element.9), channel_id=1, source_target_pairs={{0,1},{1,0},{2,3},{3,2},{4,5},{5,4},{6,7},{7,6},{8,9},{9,8},{10,11... | collective-permute-start | bytes 393224 | tf_op jit(solution)/shard_map/ppermute | solution.py:80
  173.4 1.3 collective-permute-start.21

commit v8 on v7

--- a/solution.py
+++ b/solution.py
@@ -55,15 +55,26 @@
 
 def ring_reduce_scatter_halves(xl, xr, axis, n):
     i = lax.axis_index(axis)
+    if xr is None:
+        both = xl
+
+        def chunk(side, j):
+            return both[side, j]
+
+    else:
+
+        def chunk(side, j):
+            return lax.dynamic_index_in_dim((xl, xr)[side], j, 0, keepdims=False)
+
     right = [(j, (j + 1) % n) for j in range(n)]
     left = [(j, (j - 1) % n) for j in range(n)]
-    bl = lax.dynamic_index_in_dim(xl, (i - 1) % n, 0, keepdims=False)
-    br = lax.dynamic_index_in_dim(xr, (i + 1) % n, 0, keepdims=False)
+    bl = chunk(0, (i - 1) % n)
+    br = chunk(1, (i + 1) % n)
     for s in range(n - 1):
         rl = lax.ppermute(bl, axis, right)
         rr = lax.ppermute(br, axis, left)
-        bl = rl + lax.dynamic_index_in_dim(xl, (i - s - 2) % n, 0, keepdims=False)
-        br = rr + lax.dynamic_index_in_dim(xr, (i + s + 2) % n, 0, keepdims=False)
+        bl = rl + chunk(0, (i - s - 2) % n)
+        br = rr + chunk(1, (i + s + 2) % n)
     return bl, br
 
 
@@ -102,7 +113,7 @@
     item_index = jnp.concatenate([users_list, weights_list, item_slot])
     partial_t = block_sums(item_index, user_tiles_t, weight_tiles, n_users)
     halves = partial_t.reshape(n_ylo, n_z, n_x * tile_rows, width)
-    bl, br = ring_reduce_scatter_halves(halves[0], halves[1], "z", n_z)
+    bl, br = ring_reduce_scatter_halves(halves, None, "z", n_z)
     x = jnp.concatenate([bl, br], 0).reshape(n_ylo * n_x, tile_rows, width)
     x = lax.all_to_all(x, ("ylo", "x"), 0, 0, tiled=True)
     own_sum = x.sum(0).T

time: 176 us -> 178 us (1.011)
  waiting for transfers between devices: 61 us -> 69.5 us
  starting transfers between devices: 54.7 us -> 50.6 us
  local copies, waits for them, and re-layouts: 12 us -> 8.24 us
    ppermute x9, waiting for transfers between devices: 0.46 us -> 17.5 us  [ring_reduce_scatter_halves(): rr = lax.ppermute(br, axis, left)]
    ppermute x9, starting transfers between devices: 21.2 us -> 11.4 us  [ring_reduce_scatter_halves(): rr = lax.ppermute(br, axis, left)]
    ppermute x9, waiting for transfers between devices: 33.3 us -> 24.9 us  [ring_reduce_scatter_halves(): rl = lax.ppermute(bl, axis, right)]
    ppermute x9, starting transfers between devices: 17.7 us -> 23.4 us  [ring_reduce_scatter_halves(): rl = lax.ppermute(bl, axis, right)]
    slice x1 -> x0, local copies, waits for them, and re-layouts: 3.95 us -> none  [per_device(): bl, br = ring_reduce_scatter_halves(halves[0], halves[1], 'z', n_z)]
    add x18 -> x11, other arithmetic: 7.13 us -> 7.64 us  [the longest x9 7.61 us: ring_reduce_scatter_halves(): bl = rl + chunk(0, (i - s - 2) % n)]
  transfers between devices with their start and end apart: 24 -> 24, of which waited for: 16 -> 20; matrix products, arithmetic and copies ran while one was open for 5% -> 1% of each run, Pallas kernels for 0% -> 0%
where the time goes in v8:
time: 178 us; the launch traced here: 177 us
  waiting for transfers between devices  69.5 us (39%)
  starting transfers between devices  50.6 us (28%)
  Pallas kernels  19.8 us (11%)
  blocking collectives  14.4 us (8%)
  other arithmetic  13.3 us (7%)
  local copies, waits for them, and re-layouts  8.24 us (5%)
    ppermute x9, waiting for transfers between devices, ring_reduce_scatter_halves(): rl = lax.ppermute(bl, axis, right)  24.9 us
    ppermute x9, starting transfers between devices, ring_reduce_scatter_halves(): rl = lax.ppermute(bl, axis, right)  23.4 us
    pallas_call x2, Pallas kernels, block_sums(): pl.pallas_call(functools.partial(block_sum_kernel, b_transposed=b_transpo...  19.8 us
    ppermute x9, waiting for transfers between devices, ring_reduce_scatter_halves(): rr = lax.ppermute(br, axis, left)  17.5 us
    all_to_all x1, waiting for transfers between devices, per_device(): t = lax.all_to_all(t, ('ylo', 'x'), 0, 0, tiled=True)  16 us
    all_to_all x1, blocking collectives, per_device(): lax.all_to_all(jnp.broadcast_to(own_bf[None], (n_z, tile_rows, width)), '...  14.4 us
    ppermute x9, starting transfers between devices, ring_reduce_scatter_halves(): rr = lax.ppermute(br, axis, left)  11.4 us
    add x9, other arithmetic, ring_reduce_scatter_halves(): bl = rl + chunk(0, (i - s - 2) % n)  7.61 us
  transfers between devices with their start and end apart: 24, of which 20 were waited for; matrix products, arithmetic and copies ran while one was open for 1% of the time, Pallas kernels for 0%

profile of v8, /device:TPU:1, one launch (start us, length us, event | category | flops | bytes accessed | tf_op | source)
XLA Modules:
  0.0 176.8 jit_solution(3011204930757727169)
XLA Ops:
  5.3 10.3 %shard_map.77 = f32[64,128,128]{2,1,0:T(8,128)} custom-call(s32[1152]{0:T(1024)} %get-tuple-element.28.index_ref, bf16[8,128,128]{2,1,0:T(8,128)(2,1)} %bitcast.101, bf16[64,128,128]{2,1,0:T(8,128)(2,1)} %a_ref.1), custom_call_target="tpu_custom_call" | custom-call | tf_op jit(solution)/shard_map/pallas_call | solution.py:36
  16.7 2.5 %collective-permute-start = (f32[512,128]{1,0:T(8,128)S(1)}, f32[512,128]{1,0:T(8,128)S(1)}, u32[]{:S(2)}, u32[]{:S(2)}) collective-permute-start(f32[512,128]{1,0:T(8,128)S(1)} %get-tuple-element.18), channel_id=1, source_target_pairs={{0,4},{4,8},{8,12},{12,16},{16,20},{20,24},{24,28},{28,0},{1,5},{5... | collective-permute-start | bytes 786440 | tf_op jit(solution)/shard_map/ppermute | solution.py:74
  19.2 4.0 %collective-permute-start.7 = (f32[512,128]{1,0:T(8,128)S(1)}, f32[512,128]{1,0:T(8,128)S(1)}, u32[]{:S(2)}, u32[]{:S(2)}) collective-permute-start(f32[512,128]{1,0:T(8,128)S(1)} %get-tuple-element.19), channel_id=1, source_target_pairs={{0,28},{4,0},{8,4},{12,8},{16,12},{20,16},{24,20},{28,24},{1,29},{... | collective-permute-start | bytes 786440 | tf_op jit(solution)/shard_map/ppermute | solution.py:75
  23.3 5.9 %collective-permute-done = f32[512,128]{1,0:T(8,128)S(1)} collective-permute-done((f32[512,128]{1,0:T(8,128)S(1)}, f32[512,128]{1,0:T(8,128)S(1)}, u32[]{:S(2)}, u32[]{:S(2)}) %collective-permute-start) | collective-permute-done | bytes 262176 | tf_op jit(solution)/shard_map/ppermute | solution.py:74
  30.4 2.7 %collective-permute-start.8 = (f32[512,128]{1,0:T(8,128)S(1)}, f32[512,128]{1,0:T(8,128)S(1)}, u32[]{:S(2)}, u32[]{:S(2)}) collective-permute-start(f32[512,128]{1,0:T(8,128)S(1)} %get-tuple-element.17), channel_id=1, source_target_pairs={{0,28},{4,0},{8,4},{12,8},{16,12},{20,16},{24,20},{28,24},{1,29},{... | collective-permute-start | bytes 786440 | tf_op jit(solution)/shard_map/ppermute | solution.py:75
  33.1 5.2 %collective-permute-done.1 = f32[512,128]{1,0:T(8,128)S(1)} collective-permute-done((f32[512,128]{1,0:T(8,128)S(1)}, f32[512,128]{1,0:T(8,128)S(1)}, u32[]{:S(2)}, u32[]{:S(2)}) %collective-permute-start.1) | collective-permute-done | bytes 262176 | tf_op jit(solution)/shard_map/ppermute | solution.py:74
  40.4 1.7 collective-permute-start.9
  42.1 4.3 %collective-permute-done.2 = f32[512,128]{1,0:T(8,128)S(1)} collective-permute-done((f32[512,128]{1,0:T(8,128)S(1)}, f32[512,128]{1,0:T(8,128)S(1)}, u32[]{:S(2)}, u32[]{:S(2)}) %collective-permute-start.2) | collective-permute-done | bytes 262176 | tf_op jit(solution)/shard_map/ppermute | solution.py:74
  47.5 2.2 %collective-permute-start.10 = (f32[512,128]{1,0:T(8,128)S(1)}, f32[512,128]{1,0:T(8,128)S(1)}, u32[]{:S(2)}, u32[]{:S(2)}) collective-permute-start(f32[512,128]{1,0:T(8,128)S(1)} %get-tuple-element.13), channel_id=1, source_target_pairs={{0,28},{4,0},{8,4},{12,8},{16,12},{20,16},{24,20},{28,24},{1,29},{... | collective-permute-start | bytes 786440 | tf_op jit(solution)/shard_map/ppermute | solution.py:75
  49.7 3.3 %collective-permute-done.10 = f32[512,128]{1,0:T(8,128)S(1)} collective-permute-done((f32[512,128]{1,0:T(8,128)S(1)}, f32[512,128]{1,0:T(8,128)S(1)}, u32[]{:S(2)}, u32[]{:S(2)}) %collective-permute-start.10) | collective-permute-done | bytes 262176 | tf_op jit(solution)/shard_map/ppermute | solution.py:75
  53.0 3.1 %collective-permute-done.3 = f32[512,128]{1,0:T(8,128)S(1)} collective-permute-done((f32[512,128]{1,0:T(8,128)S(1)}, f32[512,128]{1,0:T(8,128)S(1)}, u32[]{:S(2)}, u32[]{:S(2)}) %collective-permute-start.3) | collective-permute-done | bytes 262176 | tf_op jit(solution)/shard_map/ppermute | solution.py:74
  57.3 1.5 collective-permute-start.4
  58.7 3.8 %collective-permute-done.11 = f32[512,128]{1,0:T(8,128)S(1)} collective-permute-done((f32[512,128]{1,0:T(8,128)S(1)}, f32[512,128]{1,0:T(8,128)S(1)}, u32[]{:S(2)}, u32[]{:S(2)}) %collective-permute-start.11) | collective-permute-done | bytes 262176 | tf_op jit(solution)/shard_map/ppermute | solution.py:75
  65.0 1.5 collective-permute-start.5
  66.4 4.3 %collective-permute-done.12 = f32[512,128]{1,0:T(8,128)S(1)} collective-permute-done((f32[512,128]{1,0:T(8,128)S(1)}, f32[512,128]{1,0:T(8,128)S(1)}, u32[]{:S(2)}, u32[]{:S(2)}) %collective-permute-start.12) | collective-permute-done | bytes 262176 | tf_op jit(solution)/shard_map/ppermute | solution.py:75
  73.2 1.5 collective-permute-start.6
  74.6 5.7 %collective-permute-done.13 = f32[512,128]{1,0:T(8,128)S(1)} collective-permute-done((f32[512,128]{1,0:T(8,128)S(1)}, f32[512,128]{1,0:T(8,128)S(1)}, u32[]{:S(2)}, u32[]{:S(2)}) %collective-permute-start.13) | collective-permute-done | bytes 262176 | tf_op jit(solution)/shard_map/ppermute | solution.py:75
  83.3 5.0 %all-to-all-start = ((f32[8,128,128]{2,1,0:T(8,128)}), f32[8,128,128]{2,1,0:T(8,128)S(1)}, u32[]{:S(2)}, u32[]{:S(2)}) async-start(f32[8,128,128]{2,1,0:T(8,128)} %bitcast.19), calls=%async_computation | async-start | bytes 1048576 | tf_op jit(solution)/shard_map/all_to_all | solution.py:118
  89.2 6.6 %all-to-all-done = f32[8,128,128]{2,1,0:T(8,128)S(1)} async-done(((f32[8,128,128]{2,1,0:T(8,128)}), f32[8,128,128]{2,1,0:T(8,128)S(1)}, u32[]{:S(2)}, u32[]{:S(2)}) %all-to-all-start) | async-done | bytes 524320 | tf_op jit(solution)/shard_map/all_to_all | solution.py:118
  96.1 14.4 %all_to_all.15 = bf16[8,128,128]{2,1,0:T(8,128)(2,1)S(1)} all-to-all(bf16[8,128,128]{2,1,0:T(8,128)(2,1)S(1)} %broadcast_in_dim.43), channel_id=1, replica_groups=mesh['ylo'=2,'x'=4,'z'=8,'yhi'=2,'core'=2] {'z'}, dimensions={0} | all-to-all | bytes 524288 | tf_op jit(solution)/shard_map/all_to_all | solution.py:125
  110.5 1.8 %broadcast_in_dim.44 = bf16[8,8,128,128]{3,2,1,0:T(8,128)(2,1)} broadcast(bf16[8,128,128]{2,1,0:T(8,128)(2,1)S(1)} %all_to_all.15), dimensions={1,2,3} | broadcast | bytes 2359296 | tf_op jit(solution)/shard_map/broadcast_in_dim | solution.py:126
  112.3 3.6 %all-to-all-start.2 = ((bf16[8,8,128,128]{3,2,1,0:T(8,128)(2,1)}), bf16[8,8,128,128]{3,2,1,0:T(8,128)(2,1)S(1)}, u32[]{:S(2)}, u32[]{:S(2)}) async-start(bf16[8,8,128,128]{3,2,1,0:T(8,128)(2,1)} %broadcast_in_dim.44), calls=%async_computation.2 | async-start | bytes 4194304 | tf_op jit(solution)/shard_map/all_to_all | solution.py:127
  116.0 16.0 %all-to-all-done.2 = bf16[8,8,128,128]{3,2,1,0:T(8,128)(2,1)S(1)} async-done(((bf16[8,8,128,128]{3,2,1,0:T(8,128)(2,1)}), bf16[8,8,128,128]{3,2,1,0:T(8,128)(2,1)S(1)}, u32[]{:S(2)}, u32[]{:S(2)}) %all-to-all-start.2) | async-done | bytes 2097184 | tf_op jit(solution)/shard_map/all_to_all | solution.py:127
  132.0 1.3 copy-done
  133.3 9.5 %shard_map.78 = f32[8,128,128]{2,1,0:T(8,128)} custom-call(s32[1152]{0:T(1024)} %get-tuple-element.29.index_ref, bf16[64,128,128]{2,1,0:T(8,128)(2,1)} %a_ref.1, bf16[64,128,128]{2,1,0:T(8,128)(2,1)} %bitcast.98), custom_call_target="tpu_custom_call" | custom-call | tf_op jit(solution)/shard_map/pallas_call | solution.py:36
  143.9 12.7 %collective-permute-start.14 = (f32[256,128]{1,0:T(8,128)S(1)}, f32[256,128]{1,0:T(8,128)S(1)}, u32[]{:S(2)}, u32[]{:S(2)}) collective-permute-start(f32[256,128]{1,0:T(8,128)S(1)} %dynamic-slice_bitcast_fusion.3), channel_id=1, source_target_pairs={{0,1},{1,0},{2,3},{3,2},{4,5},{5,4},{6,7},{7,6},{8,9},{9,8},{10,11... | collective-permute-start | bytes 393224 | tf_op jit(solution)/shard_map/ppermute | solution.py:74
  158.1 2.7 %collective-permute-start.16 = (f32[128,128]{1,0:T(8,128)S(1)}, f32[128,128]{1,0:T(8,128)S(1)}, u32[]{:S(2)}, u32[]{:S(2)}) collective-permute-start(f32[128,128]{1,0:T(8,128)S(1)} %dynamic-slice_bitcast_fusion.5), channel_id=1, source_target_pairs={{0,2},{2,0},{1,3},{3,1},{4,6},{6,4},{5,7},{7,5},{8,10},{10,8},{9,1... | collective-permute-start | bytes 196616 | tf_op jit(solution)/shard_map/ppermute | solution.py:74
  161.2 2.0 %collective-permute-done.16 = f32[128,128]{1,0:T(8,128)S(1)} collective-permute-done((f32[128,128]{1,0:T(8,128)S(1)}, f32[128,128]{1,0:T(8,128)S(1)}, u32[]{:S(2)}, u32[]{:S(2)}) %collective-permute-start.16) | collective-permute-done | bytes 65568 | tf_op jit(solution)/shard_map/ppermute | solution.py:74
  163.2 2.7 %collective-permute-start.18 = (f32[128,128]{1,0:T(8,128)S(1)}, f32[128,128]{1,0:T(8,128)S(1)}, u32[]{:S(2)}, u32[]{:S(2)}) collective-permute-start(f32[128,128]{1,0:T(8,128)S(1)} %bitcast_add_fusion.18), channel_id=1, source_target_pairs={{0,2},{2,0},{1,3},{3,1},{4,6},{6,4},{5,7},{7,5},{8,10},{10,8},{9,1... | collective-permute-start | bytes 196616 | tf_op jit(solution)/shard_map/ppermute | solution.py:91
  166.0 1.4 collective-permute-start.19
  168.0 2.7 %collective-permute-done.19 = f32[128,128]{1,0:T(8,128)S(1)} collective-permute-done((f32[128,128]{1,0:T(8,128)S(1)}, f32[128,128]{1,0:T(8,128)S(1)}, u32[]{:S(2)}, u32[]{:S(2)}) %collective-permute-start.19) | collective-permute-done | bytes 65568 | tf_op jit(solution)/shard_map/ppermute | solution.py:92
  170.7 3.1 %collective-permute-start.20 = (f32[256,128]{1,0:T(8,128)S(1)}, f32[256,128]{1,0:T(8,128)S(1)}, u32[]{:S(2)}, u32[]{:S(2)}) collective-permute-start(f32[256,128]{1,0:T(8,128)S(1)} %get-tuple-element.23), channel_id=1, source_target_pairs={{0,1},{1,0},{2,3},{3,2},{4,5},{5,4},{6,7},{7,6},{8,9},{9,8},{10,11... | collective-permute-start | bytes 393224 | tf_op jit(solution)/shard_map/ppermute | solution.py:91
  (69 shorter events, 27.0 us)
Async XLA Ops:
  16.7 12.5 %collective-permute-start = (f32[512,128]{1,0:T(8,128)S(1)}, f32[512,128]{1,0:T(8,128)S(1)}, u32[]{:S(2)}, u32[]{:S(2)}) collective-permute-start(f32[512,128]{1,0:T(8,128)S(1)} %get-tuple-element.18), channel_id=1, source_target_pairs={{0,4},{4,8},{8,12},{12,16},{16,20},{20,24},{24,28},{28,0},{1,5},{5... | collective-permute-start | bytes 786440 | tf_op jit(solution)/shard_map/ppermute | solution.py:74
  19.2 10.0 %collective-permute-start.7 = (f32[512,128]{1,0:T(8,128)S(1)}, f32[512,128]{1,0:T(8,128)S(1)}, u32[]{:S(2)}, u32[]{:S(2)}) collective-permute-start(f32[512,128]{1,0:T(8,128)S(1)} %get-tuple-element.19), channel_id=1, source_target_pairs={{0,28},{4,0},{8,4},{12,8},{16,12},{20,16},{24,20},{28,24},{1,29},{... | collective-permute-start | bytes 786440 | tf_op jit(solution)/shard_map/ppermute | solution.py:75
  30.3 7.9 %collective-permute-start.1 = (f32[512,128]{1,0:T(8,128)S(1)}, f32[512,128]{1,0:T(8,128)S(1)}, u32[]{:S(2)}, u32[]{:S(2)}) collective-permute-start(f32[512,128]{1,0:T(8,128)S(1)} %get-tuple-element.16), channel_id=1, source_target_pairs={{0,4},{4,8},{8,12},{12,16},{16,20},{20,24},{24,28},{28,0},{1,5},{5... | collective-permute-start | bytes 786440 | tf_op jit(solution)/shard_map/ppermute | solution.py:74
  30.4 7.8 %collective-permute-start.8 = (f32[512,128]{1,0:T(8,128)S(1)}, f32[512,128]{1,0:T(8,128)S(1)}, u32[]{:S(2)}, u32[]{:S(2)}) collective-permute-start(f32[512,128]{1,0:T(8,128)S(1)} %get-tuple-element.17), channel_id=1, source_target_pairs={{0,28},{4,0},{8,4},{12,8},{16,12},{20,16},{24,20},{28,24},{1,29},{... | collective-permute-start | bytes 786440 | tf_op jit(solution)/shard_map/ppermute | solution.py:75
  39.3 7.1 %collective-permute-start.2 = (f32[512,128]{1,0:T(8,128)S(1)}, f32[512,128]{1,0:T(8,128)S(1)}, u32[]{:S(2)}, u32[]{:S(2)}) collective-permute-start(f32[512,128]{1,0:T(8,128)S(1)} %get-tuple-element.14), channel_id=1, source_target_pairs={{0,4},{4,8},{8,12},{12,16},{16,20},{20,24},{24,28},{28,0},{1,5},{5... | collective-permute-start | bytes 786440 | tf_op jit(solution)/shard_map/ppermute | solution.py:74
  40.4 6.0 %collective-permute-start.9 = (f32[512,128]{1,0:T(8,128)S(1)}, f32[512,128]{1,0:T(8,128)S(1)}, u32[]{:S(2)}, u32[]{:S(2)}) collective-permute-start(f32[512,128]{1,0:T(8,128)S(1)} %get-tuple-element.15), channel_id=1, source_target_pairs={{0,28},{4,0},{8,4},{12,8},{16,12},{20,16},{24,20},{28,24},{1,29},{... | collective-permute-start | bytes 786440 | tf_op jit(solution)/shard_map/ppermute | solution.py:75
  47.5 5.5 %collective-permute-start.10 = (f32[512,128]{1,0:T(8,128)S(1)}, f32[512,128]{1,0:T(8,128)S(1)}, u32[]{:S(2)}, u32[]{:S(2)}) collective-permute-start(f32[512,128]{1,0:T(8,128)S(1)} %get-tuple-element.13), channel_id=1, source_target_pairs={{0,28},{4,0},{8,4},{12,8},{16,12},{20,16},{24,20},{28,24},{1,29},{... | collective-permute-start | bytes 786440 | tf_op jit(solution)/shard_map/ppermute | solution.py:75
  49.7 6.4 %collective-permute-start.3 = (f32[512,128]{1,0:T(8,128)S(1)}, f32[512,128]{1,0:T(8,128)S(1)}, u32[]{:S(2)}, u32[]{:S(2)}) collective-permute-start(f32[512,128]{1,0:T(8,128)S(1)} %get-tuple-element.12), channel_id=1, source_target_pairs={{0,4},{4,8},{8,12},{12,16},{16,20},{20,24},{24,28},{28,0},{1,5},{5... | collective-permute-start | bytes 786440 | tf_op jit(solution)/shard_map/ppermute | solution.py:74
  57.2 5.3 %collective-permute-start.11 = (f32[512,128]{1,0:T(8,128)S(1)}, f32[512,128]{1,0:T(8,128)S(1)}, u32[]{:S(2)}, u32[]{:S(2)}) collective-permute-start(f32[512,128]{1,0:T(8,128)S(1)} %get-tuple-element.11), channel_id=1, source_target_pairs={{0,28},{4,0},{8,4},{12,8},{16,12},{20,16},{24,20},{28,24},{1,29},{... | collective-permute-start | bytes 786440 | tf_op jit(solution)/shard_map/ppermute | solution.py:75
  57.3 6.5 %collective-permute-start.4 = (f32[512,128]{1,0:T(8,128)S(1)}, f32[512,128]{1,0:T(8,128)S(1)}, u32[]{:S(2)}, u32[]{:S(2)}) collective-permute-start(f32[512,128]{1,0:T(8,128)S(1)} %get-tuple-element.10), channel_id=1, source_target_pairs={{0,4},{4,8},{8,12},{12,16},{16,20},{20,24},{24,28},{28,0},{1,5},{5... | collective-permute-start | bytes 786440 | tf_op jit(solution)/shard_map/ppermute | solution.py:74
  64.9 5.8 %collective-permute-start.12 = (f32[512,128]{1,0:T(8,128)S(1)}, f32[512,128]{1,0:T(8,128)S(1)}, u32[]{:S(2)}, u32[]{:S(2)}) collective-permute-start(f32[512,128]{1,0:T(8,128)S(1)} %get-tuple-element.9), channel_id=1, source_target_pairs={{0,28},{4,0},{8,4},{12,8},{16,12},{20,16},{24,20},{28,24},{1,29},{... | collective-permute-start | bytes 786440 | tf_op jit(solution)/shard_map/ppermute | solution.py:75
  65.0 7.0 %collective-permute-start.5 = (f32[512,128]{1,0:T(8,128)S(1)}, f32[512,128]{1,0:T(8,128)S(1)}, u32[]{:S(2)}, u32[]{:S(2)}) collective-permute-start(f32[512,128]{1,0:T(8,128)S(1)} %get-tuple-element.8), channel_id=1, source_target_pairs={{0,4},{4,8},{8,12},{12,16},{16,20},{20,24},{24,28},{28,0},{1,5},{5... | collective-permute-start | bytes 786440 | tf_op jit(solution)/shard_map/ppermute | solution.py:74
  73.1 7.3 %collective-permute-start.13 = (f32[512,128]{1,0:T(8,128)S(1)}, f32[512,128]{1,0:T(8,128)S(1)}, u32[]{:S(2)}, u32[]{:S(2)}) collective-permute-start(f32[512,128]{1,0:T(8,128)S(1)} %get-tuple-element.7), channel_id=1, source_target_pairs={{0,28},{4,0},{8,4},{12,8},{16,12},{20,16},{24,20},{28,24},{1,29},{... | collective-permute-start | bytes 786440 | tf_op jit(solution)/shard_map/ppermute | solution.py:75
  73.2 8.2 %collective-permute-start.6 = (f32[512,128]{1,0:T(8,128)S(1)}, f32[512,128]{1,0:T(8,128)S(1)}, u32[]{:S(2)}, u32[]{:S(2)}) collective-permute-start(f32[512,128]{1,0:T(8,128)S(1)} %get-tuple-element.6), channel_id=1, source_target_pairs={{0,4},{4,8},{8,12},{12,16},{16,20},{20,24},{24,28},{28,0},{1,5},{5... | collective-permute-start | bytes 786440 | tf_op jit(solution)/shard_map/ppermute | solution.py:74
  83.3 12.6 %all-to-all-start = ((f32[8,128,128]{2,1,0:T(8,128)}), f32[8,128,128]{2,1,0:T(8,128)S(1)}, u32[]{:S(2)}, u32[]{:S(2)}) async-start(f32[8,128,128]{2,1,0:T(8,128)} %bitcast.19), calls=%async_computation | async-start | bytes 1048576 | tf_op jit(solution)/shard_map/all_to_all | solution.py:118
  112.3 19.6 %all-to-all-start.2 = ((bf16[8,8,128,128]{3,2,1,0:T(8,128)(2,1)}), bf16[8,8,128,128]{3,2,1,0:T(8,128)(2,1)S(1)}, u32[]{:S(2)}, u32[]{:S(2)}) async-start(bf16[8,8,128,128]{3,2,1,0:T(8,128)(2,1)} %broadcast_in_dim.44), calls=%async_computation.2 | async-start | bytes 4194304 | tf_op jit(solution)/shard_map/all_to_all | solution.py:127
  132.0 1.3 copy-start
  142.8 33.2 %copy-start.1 = (f32[1024,128]{1,0:T(8,128)S(1)}, f32[1024,128]{1,0:T(8,128)}, u32[]{:S(2)}) copy-start(f32[1024,128]{1,0:T(8,128)} %param.6) | copy-start | bytes 1572868
  143.9 13.7 %collective-permute-start.14 = (f32[256,128]{1,0:T(8,128)S(1)}, f32[256,128]{1,0:T(8,128)S(1)}, u32[]{:S(2)}, u32[]{:S(2)}) collective-permute-start(f32[256,128]{1,0:T(8,128)S(1)} %dynamic-slice_bitcast_fusion.3), channel_id=1, source_target_pairs={{0,1},{1,0},{2,3},{3,2},{4,5},{5,4},{6,7},{7,6},{8,9},{9,8},{10,11... | collective-permute-start | bytes 393224 | tf_op jit(solution)/shard_map/ppermute | solution.py:74
  156.6 1.4 collective-permute-start.15
  158.1 5.1 %collective-permute-start.16 = (f32[128,128]{1,0:T(8,128)S(1)}, f32[128,128]{1,0:T(8,128)S(1)}, u32[]{:S(2)}, u32[]{:S(2)}) collective-permute-start(f32[128,128]{1,0:T(8,128)S(1)} %dynamic-slice_bitcast_fusion.5), channel_id=1, source_target_pairs={{0,2},{2,0},{1,3},{3,1},{4,6},{6,4},{5,7},{7,5},{8,10},{10,8},{9,1... | collective-permute-start | bytes 196616 | tf_op jit(solution)/shard_map/ppermute | solution.py:74
  160.8 5.1 %collective-permute-start.17 = (f32[128,128]{1,0:T(8,128)S(1)}, f32[128,128]{1,0:T(8,128)S(1)}, u32[]{:S(2)}, u32[]{:S(2)}) collective-permute-start(f32[128,128]{1,0:T(8,128)S(1)} %dynamic-slice_bitcast_fusion.4), channel_id=1, source_target_pairs={{0,2},{2,0},{1,3},{3,1},{4,6},{6,4},{5,7},{7,5},{8,10},{10,8},{9,1... | collective-permute-start | bytes 196616 | tf_op jit(solution)/shard_map/ppermute | solution.py:75
  163.2 4.7 %collective-permute-start.18 = (f32[128,128]{1,0:T(8,128)S(1)}, f32[128,128]{1,0:T(8,128)S(1)}, u32[]{:S(2)}, u32[]{:S(2)}) collective-permute-start(f32[128,128]{1,0:T(8,128)S(1)} %bitcast_add_fusion.18), channel_id=1, source_target_pairs={{0,2},{2,0},{1,3},{3,1},{4,6},{6,4},{5,7},{7,5},{8,10},{10,8},{9,1... | collective-permute-start | bytes 196616 | tf_op jit(solution)/shard_map/ppermute | solution.py:91
  166.0 4.7 %collective-permute-start.19 = (f32[128,128]{1,0:T(8,128)S(1)}, f32[128,128]{1,0:T(8,128)S(1)}, u32[]{:S(2)}, u32[]{:S(2)}) collective-permute-start(f32[128,128]{1,0:T(8,128)S(1)} %bitcast_add_fusion.17), channel_id=1, source_target_pairs={{0,2},{2,0},{1,3},{3,1},{4,6},{6,4},{5,7},{7,5},{8,10},{10,8},{9,1... | collective-permute-start | bytes 196616 | tf_op jit(solution)/shard_map/ppermute | solution.py:92
  170.7 4.1 %collective-permute-start.20 = (f32[256,128]{1,0:T(8,128)S(1)}, f32[256,128]{1,0:T(8,128)S(1)}, u32[]{:S(2)}, u32[]{:S(2)}) collective-permute-start(f32[256,128]{1,0:T(8,128)S(1)} %get-tuple-element.23), channel_id=1, source_target_pairs={{0,1},{1,0},{2,3},{3,2},{4,5},{5,4},{6,7},{7,6},{8,9},{9,8},{10,11... | collective-permute-start | bytes 393224 | tf_op jit(solution)/shard_map/ppermute | solution.py:91
  174.6 1.3 collective-permute-start.21

commit v9 on v7

--- a/solution.py
+++ b/solution.py
@@ -111,12 +111,15 @@
     own_base = lax.dynamic_slice_in_dim(item_base[0], position * tile_rows, tile_rows, 0)
     own_emb = (1.0 - teleport) * own_sum + teleport * own_base
     own_bf = own_emb.astype(jnp.bfloat16)
-    t = lax.all_to_all(jnp.broadcast_to(own_bf[None], (n_z, tile_rows, width)), "z", 0, 0, tiled=True)
-    t = jnp.broadcast_to(t[None], (n_ylo * n_x, n_z, tile_rows, width))
-    t = lax.all_to_all(t, ("ylo", "x"), 0, 0, tiled=True)
+    t = lax.all_to_all(
+        jnp.broadcast_to(own_bf[None], (n_ylo * n_x, tile_rows, width)), ("ylo", "x"), 0, 0, tiled=True
+    )
+    t = jnp.broadcast_to(t[None], (n_z, n_ylo * n_x, tile_rows, width))
+    t = lax.all_to_all(t, "z", 0, 0, tiled=True)
     item_tiles = t.reshape(n_users, tile_rows, width)
+    gathered_slot = (item_z * n_ylo + item_ylo) * n_x + item_x
 
-    user_index = jnp.concatenate([weights_list, items_list, users_list])
+    user_index = jnp.concatenate([weights_list, gathered_slot, users_list])
     user_part = block_sums(user_index, weight_tiles, item_tiles, n_user_tiles)
     y = user_part.reshape(n_core, -1, width)
     y = ring_reduce_scatter(y, "core", n_core)

time: 176 us -> 198 us (1.12)
  waiting for transfers between devices: 61 us -> 88.1 us
  blocking collectives: 14.4 us -> 9.55 us
    all_to_all x1, waiting for transfers between devices: 16.2 us -> 43.1 us  [per_device(): t = lax.all_to_all(t, 'z', 0, 0, tiled=True)]
    all_to_all x1, blocking collectives: 14.4 us -> 9.55 us  [per_device(): lax.all_to_all(jnp.broadcast_to(own_bf[None], (n_ylo * n_x, tile_rows, wi...]
    ppermute x9, starting transfers between devices: 17.7 us -> 15 us  [ring_reduce_scatter_halves(): rl = lax.ppermute(bl, axis, right)]
    all_to_all x1, starting transfers between devices: 3.6 us -> 5.73 us  [per_device(): t = lax.all_to_all(t, 'z', 0, 0, tiled=True)]
where the time goes in v9:
time: 198 us; the launch traced here: 197 us
  waiting for transfers between devices  88.1 us (44%)
  starting transfers between devices  54 us (27%)
  Pallas kernels  19.7 us (10%)
  other arithmetic  12.7 us (6%)
  local copies, waits for them, and re-layouts  12 us (6%)
  blocking collectives  9.55 us (5%)
    all_to_all x1, waiting for transfers between devices, per_device(): t = lax.all_to_all(t, 'z', 0, 0, tiled=True)  43.1 us
    ppermute x9, waiting for transfers between devices, ring_reduce_scatter_halves(): rl = lax.ppermute(bl, axis, right)  33.3 us
    ppermute x9, starting transfers between devices, ring_reduce_scatter_halves(): rr = lax.ppermute(br, axis, left)  21.2 us
    pallas_call x2, Pallas kernels, block_sums(): pl.pallas_call(functools.partial(block_sum_kernel, b_transposed=b_transpo...  19.7 us
    ppermute x9, starting transfers between devices, ring_reduce_scatter_halves(): rl = lax.ppermute(bl, axis, right)  15 us
    all_to_all x1, blocking collectives, per_device(): lax.all_to_all(jnp.broadcast_to(own_bf[None], (n_ylo * n_x, tile_rows, wi...  9.55 us
    add x9, other arithmetic, ring_reduce_scatter_halves(): bl = rl + lax.dynamic_index_in_dim(xl, (i - s - 2) % n, 0, keepdims=False)  6.87 us
    all_to_all x1, waiting for transfers between devices, per_device(): x = lax.all_to_all(x, ('ylo', 'x'), 0, 0, tiled=True)  6.6 us
  transfers between devices with their start and end apart: 24, of which 16 were waited for; matrix products, arithmetic and copies ran while one was open for 5% of the time, Pallas kernels for 0%

profile of v9, /device:TPU:1, one launch (start us, length us, event | category | flops | bytes accessed | tf_op | source)
XLA Modules:
  0.0 197.2 jit_solution(8821253664949065861)
XLA Ops:
  5.3 10.3 %shard_map.77 = f32[64,128,128]{2,1,0:T(8,128)} custom-call(s32[1152]{0:T(1024)} %get-tuple-element.14.index_ref, bf16[8,128,128]{2,1,0:T(8,128)(2,1)} %bitcast.110, bf16[64,128,128]{2,1,0:T(8,128)(2,1)} %a_ref.1), custom_call_target="tpu_custom_call" | custom-call | tf_op jit(solution)/shard_map/pallas_call | solution.py:36
  15.6 3.9 %fusion.5 = (f32[32,128,128]{2,1,0:T(8,128)}, f32[32,128,128]{2,1,0:T(8,128)S(1)}) fusion(f32[64,128,128]{2,1,0:T(8,128)} %shard_map.77), kind=kLoop, calls=%fused_computation.60 | loop fusion | bytes 8388608 | tf_op jit(solution)/shard_map/slice | solution.py:105
  20.5 2.5 %collective-permute-start = (f32[512,128]{1,0:T(8,128)S(1)}, f32[512,128]{1,0:T(8,128)S(1)}, u32[]{:S(2)}, u32[]{:S(2)}) collective-permute-start(f32[512,128]{1,0:T(8,128)S(1)} %dynamic-slice_bitcast_fusion.1), channel_id=1, source_target_pairs={{0,4},{4,8},{8,12},{12,16},{16,20},{20,24},{24,28},{28,0},{1,5},{5... | collective-permute-start | bytes 786440 | tf_op jit(solution)/shard_map/ppermute | solution.py:63
  23.1 4.1 %collective-permute-start.7 = (f32[512,128]{1,0:T(8,128)S(1)}, f32[512,128]{1,0:T(8,128)S(1)}, u32[]{:S(2)}, u32[]{:S(2)}) collective-permute-start(f32[512,128]{1,0:T(8,128)S(1)} %dynamic-slice_bitcast_fusion), channel_id=1, source_target_pairs={{0,28},{4,0},{8,4},{12,8},{16,12},{20,16},{24,20},{28,24},{1,29},{... | collective-permute-start | bytes 786440 | tf_op jit(solution)/shard_map/ppermute | solution.py:64
  27.1 5.9 %collective-permute-done = f32[512,128]{1,0:T(8,128)S(1)} collective-permute-done((f32[512,128]{1,0:T(8,128)S(1)}, f32[512,128]{1,0:T(8,128)S(1)}, u32[]{:S(2)}, u32[]{:S(2)}) %collective-permute-start) | collective-permute-done | bytes 262176 | tf_op jit(solution)/shard_map/ppermute | solution.py:63
  34.2 2.7 %collective-permute-start.8 = (f32[512,128]{1,0:T(8,128)S(1)}, f32[512,128]{1,0:T(8,128)S(1)}, u32[]{:S(2)}, u32[]{:S(2)}) collective-permute-start(f32[512,128]{1,0:T(8,128)S(1)} %bitcast_add_fusion.7), channel_id=1, source_target_pairs={{0,28},{4,0},{8,4},{12,8},{16,12},{20,16},{24,20},{28,24},{1,29},{... | collective-permute-start | bytes 786440 | tf_op jit(solution)/shard_map/ppermute | solution.py:64
  36.9 5.1 %collective-permute-done.1 = f32[512,128]{1,0:T(8,128)S(1)} collective-permute-done((f32[512,128]{1,0:T(8,128)S(1)}, f32[512,128]{1,0:T(8,128)S(1)}, u32[]{:S(2)}, u32[]{:S(2)}) %collective-permute-start.1) | collective-permute-done | bytes 262176 | tf_op jit(solution)/shard_map/ppermute | solution.py:63
  43.1 2.7 %collective-permute-start.9 = (f32[512,128]{1,0:T(8,128)S(1)}, f32[512,128]{1,0:T(8,128)S(1)}, u32[]{:S(2)}, u32[]{:S(2)}) collective-permute-start(f32[512,128]{1,0:T(8,128)S(1)} %bitcast_add_fusion.6), channel_id=1, source_target_pairs={{0,28},{4,0},{8,4},{12,8},{16,12},{20,16},{24,20},{28,24},{1,29},{... | collective-permute-start | bytes 786440 | tf_op jit(solution)/shard_map/ppermute | solution.py:64
  45.8 4.2 %collective-permute-done.2 = f32[512,128]{1,0:T(8,128)S(1)} collective-permute-done((f32[512,128]{1,0:T(8,128)S(1)}, f32[512,128]{1,0:T(8,128)S(1)}, u32[]{:S(2)}, u32[]{:S(2)}) %collective-permute-start.2) | collective-permute-done | bytes 262176 | tf_op jit(solution)/shard_map/ppermute | solution.py:63
  51.1 2.7 %collective-permute-start.10 = (f32[512,128]{1,0:T(8,128)S(1)}, f32[512,128]{1,0:T(8,128)S(1)}, u32[]{:S(2)}, u32[]{:S(2)}) collective-permute-start(f32[512,128]{1,0:T(8,128)S(1)} %bitcast_add_fusion.5), channel_id=1, source_target_pairs={{0,28},{4,0},{8,4},{12,8},{16,12},{20,16},{24,20},{28,24},{1,29},{... | collective-permute-start | bytes 786440 | tf_op jit(solution)/shard_map/ppermute | solution.py:64
  53.8 3.6 %collective-permute-done.3 = f32[512,128]{1,0:T(8,128)S(1)} collective-permute-done((f32[512,128]{1,0:T(8,128)S(1)}, f32[512,128]{1,0:T(8,128)S(1)}, u32[]{:S(2)}, u32[]{:S(2)}) %collective-permute-start.3) | collective-permute-done | bytes 262176 | tf_op jit(solution)/shard_map/ppermute | solution.py:63
  58.6 2.7 %collective-permute-start.11 = (f32[512,128]{1,0:T(8,128)S(1)}, f32[512,128]{1,0:T(8,128)S(1)}, u32[]{:S(2)}, u32[]{:S(2)}) collective-permute-start(f32[512,128]{1,0:T(8,128)S(1)} %bitcast_add_fusion.4), channel_id=1, source_target_pairs={{0,28},{4,0},{8,4},{12,8},{16,12},{20,16},{24,20},{28,24},{1,29},{... | collective-permute-start | bytes 786440 | tf_op jit(solution)/shard_map/ppermute | solution.py:64
  61.3 3.6 %collective-permute-done.4 = f32[512,128]{1,0:T(8,128)S(1)} collective-permute-done((f32[512,128]{1,0:T(8,128)S(1)}, f32[512,128]{1,0:T(8,128)S(1)}, u32[]{:S(2)}, u32[]{:S(2)}) %collective-permute-start.4) | collective-permute-done | bytes 262176 | tf_op jit(solution)/shard_map/ppermute | solution.py:63
  66.1 2.7 %collective-permute-start.12 = (f32[512,128]{1,0:T(8,128)S(1)}, f32[512,128]{1,0:T(8,128)S(1)}, u32[]{:S(2)}, u32[]{:S(2)}) collective-permute-start(f32[512,128]{1,0:T(8,128)S(1)} %bitcast_add_fusion.3), channel_id=1, source_target_pairs={{0,28},{4,0},{8,4},{12,8},{16,12},{20,16},{24,20},{28,24},{1,29},{... | collective-permute-start | bytes 786440 | tf_op jit(solution)/shard_map/ppermute | solution.py:64
  68.8 3.6 %collective-permute-done.5 = f32[512,128]{1,0:T(8,128)S(1)} collective-permute-done((f32[512,128]{1,0:T(8,128)S(1)}, f32[512,128]{1,0:T(8,128)S(1)}, u32[]{:S(2)}, u32[]{:S(2)}) %collective-permute-start.5) | collective-permute-done | bytes 262176 | tf_op jit(solution)/shard_map/ppermute | solution.py:63
  73.6 2.9 %collective-permute-start.13 = (f32[512,128]{1,0:T(8,128)S(1)}, f32[512,128]{1,0:T(8,128)S(1)}, u32[]{:S(2)}, u32[]{:S(2)}) collective-permute-start(f32[512,128]{1,0:T(8,128)S(1)} %bitcast_add_fusion.2), channel_id=1, source_target_pairs={{0,28},{4,0},{8,4},{12,8},{16,12},{20,16},{24,20},{28,24},{1,29},{... | collective-permute-start | bytes 786440 | tf_op jit(solution)/shard_map/ppermute | solution.py:64
  76.5 4.5 %collective-permute-done.6 = f32[512,128]{1,0:T(8,128)S(1)} collective-permute-done((f32[512,128]{1,0:T(8,128)S(1)}, f32[512,128]{1,0:T(8,128)S(1)}, u32[]{:S(2)}, u32[]{:S(2)}) %collective-permute-start.6) | collective-permute-done | bytes 262176 | tf_op jit(solution)/shard_map/ppermute | solution.py:63
  82.8 5.0 %all-to-all-start = ((f32[8,128,128]{2,1,0:T(8,128)}), f32[8,128,128]{2,1,0:T(8,128)S(1)}, u32[]{:S(2)}, u32[]{:S(2)}) async-start(f32[8,128,128]{2,1,0:T(8,128)} %bitcast.20), calls=%async_computation | async-start | bytes 1048576 | tf_op jit(solution)/shard_map/all_to_all | solution.py:107
  88.7 6.6 %all-to-all-done = f32[8,128,128]{2,1,0:T(8,128)S(1)} async-done(((f32[8,128,128]{2,1,0:T(8,128)}), f32[8,128,128]{2,1,0:T(8,128)S(1)}, u32[]{:S(2)}, u32[]{:S(2)}) %all-to-all-start) | async-done | bytes 524320 | tf_op jit(solution)/shard_map/all_to_all | solution.py:107
  95.6 9.5 %all_to_all.15 = bf16[8,128,128]{2,1,0:T(8,128)(2,1)S(1)} all-to-all(bf16[8,128,128]{2,1,0:T(8,128)(2,1)S(1)} %broadcast_in_dim.43), channel_id=1, replica_groups=mesh['ylo'=2,'x'=4,'z'=8,'yhi'=2,'core'=2] {'ylo','x'}, dimensions={0} | all-to-all | bytes 524288 | tf_op jit(solution)/shard_map/all_to_all | solution.py:114
  105.1 1.8 broadcast_in_dim.44
  106.9 5.7 %all-to-all-start.2 = ((bf16[8,8,128,128]{3,2,1,0:T(8,128)(2,1)}), bf16[8,8,128,128]{3,2,1,0:T(8,128)(2,1)S(1)}, u32[]{:S(2)}, u32[]{:S(2)}) async-start(bf16[8,8,128,128]{3,2,1,0:T(8,128)(2,1)} %broadcast_in_dim.44), calls=%async_computation.2 | async-start | bytes 4194304 | tf_op jit(solution)/shard_map/all_to_all | solution.py:118
  112.7 43.1 %all-to-all-done.2 = bf16[8,8,128,128]{3,2,1,0:T(8,128)(2,1)S(1)} async-done(((bf16[8,8,128,128]{3,2,1,0:T(8,128)(2,1)}), bf16[8,8,128,128]{3,2,1,0:T(8,128)(2,1)S(1)}, u32[]{:S(2)}, u32[]{:S(2)}) %all-to-all-start.2) | async-done | bytes 2097184 | tf_op jit(solution)/shard_map/all_to_all | solution.py:118
  155.8 1.3 copy-done
  157.1 9.4 %shard_map.78 = f32[8,128,128]{2,1,0:T(8,128)} custom-call(s32[1152]{0:T(1024)} %get-tuple-element.15.index_ref, bf16[64,128,128]{2,1,0:T(8,128)(2,1)} %a_ref.1, bf16[64,128,128]{2,1,0:T(8,128)(2,1)} %bitcast.107), custom_call_target="tpu_custom_call" | custom-call | tf_op jit(solution)/shard_map/pallas_call | solution.py:36
  167.7 9.2 %collective-permute-start.14 = (f32[256,128]{1,0:T(8,128)S(1)}, f32[256,128]{1,0:T(8,128)S(1)}, u32[]{:S(2)}, u32[]{:S(2)}) collective-permute-start(f32[256,128]{1,0:T(8,128)S(1)} %dynamic-slice_bitcast_fusion.3), channel_id=1, source_target_pairs={{0,1},{1,0},{2,3},{3,2},{4,5},{5,4},{6,7},{7,6},{8,9},{9,8},{10,11... | collective-permute-start | bytes 393224 | tf_op jit(solution)/shard_map/ppermute | solution.py:63
  178.4 2.7 %collective-permute-start.16 = (f32[128,128]{1,0:T(8,128)S(1)}, f32[128,128]{1,0:T(8,128)S(1)}, u32[]{:S(2)}, u32[]{:S(2)}) collective-permute-start(f32[128,128]{1,0:T(8,128)S(1)} %dynamic-slice_bitcast_fusion.5), channel_id=1, source_target_pairs={{0,2},{2,0},{1,3},{3,1},{4,6},{6,4},{5,7},{7,5},{8,10},{10,8},{9,1... | collective-permute-start | bytes 196616 | tf_op jit(solution)/shard_map/ppermute | solution.py:63
  181.5 2.0 %collective-permute-done.16 = f32[128,128]{1,0:T(8,128)S(1)} collective-permute-done((f32[128,128]{1,0:T(8,128)S(1)}, f32[128,128]{1,0:T(8,128)S(1)}, u32[]{:S(2)}, u32[]{:S(2)}) %collective-permute-start.16) | collective-permute-done | bytes 65568 | tf_op jit(solution)/shard_map/ppermute | solution.py:63
  183.5 2.7 %collective-permute-start.18 = (f32[128,128]{1,0:T(8,128)S(1)}, f32[128,128]{1,0:T(8,128)S(1)}, u32[]{:S(2)}, u32[]{:S(2)}) collective-permute-start(f32[128,128]{1,0:T(8,128)S(1)} %bitcast_add_fusion.18), channel_id=1, source_target_pairs={{0,2},{2,0},{1,3},{3,1},{4,6},{6,4},{5,7},{7,5},{8,10},{10,8},{9,1... | collective-permute-start | bytes 196616 | tf_op jit(solution)/shard_map/ppermute | solution.py:80
  186.3 1.4 collective-permute-start.19
  188.3 2.7 %collective-permute-done.19 = f32[128,128]{1,0:T(8,128)S(1)} collective-permute-done((f32[128,128]{1,0:T(8,128)S(1)}, f32[128,128]{1,0:T(8,128)S(1)}, u32[]{:S(2)}, u32[]{:S(2)}) %collective-permute-start.19) | collective-permute-done | bytes 65568 | tf_op jit(solution)/shard_map/ppermute | solution.py:81
  191.0 3.1 %collective-permute-start.20 = (f32[256,128]{1,0:T(8,128)S(1)}, f32[256,128]{1,0:T(8,128)S(1)}, u32[]{:S(2)}, u32[]{:S(2)}) collective-permute-start(f32[256,128]{1,0:T(8,128)S(1)} %get-tuple-element.9), channel_id=1, source_target_pairs={{0,1},{1,0},{2,3},{3,2},{4,5},{5,4},{6,7},{7,6},{8,9},{9,8},{10,11... | collective-permute-start | bytes 393224 | tf_op jit(solution)/shard_map/ppermute | solution.py:80
  (78 shorter events, 21.8 us)
Async XLA Ops:
  20.5 12.5 %collective-permute-start = (f32[512,128]{1,0:T(8,128)S(1)}, f32[512,128]{1,0:T(8,128)S(1)}, u32[]{:S(2)}, u32[]{:S(2)}) collective-permute-start(f32[512,128]{1,0:T(8,128)S(1)} %dynamic-slice_bitcast_fusion.1), channel_id=1, source_target_pairs={{0,4},{4,8},{8,12},{12,16},{16,20},{20,24},{24,28},{28,0},{1,5},{5... | collective-permute-start | bytes 786440 | tf_op jit(solution)/shard_map/ppermute | solution.py:63
  23.1 11.1 %collective-permute-start.7 = (f32[512,128]{1,0:T(8,128)S(1)}, f32[512,128]{1,0:T(8,128)S(1)}, u32[]{:S(2)}, u32[]{:S(2)}) collective-permute-start(f32[512,128]{1,0:T(8,128)S(1)} %dynamic-slice_bitcast_fusion), channel_id=1, source_target_pairs={{0,28},{4,0},{8,4},{12,8},{16,12},{20,16},{24,20},{28,24},{1,29},{... | collective-permute-start | bytes 786440 | tf_op jit(solution)/shard_map/ppermute | solution.py:64
  34.0 7.9 %collective-permute-start.1 = (f32[512,128]{1,0:T(8,128)S(1)}, f32[512,128]{1,0:T(8,128)S(1)}, u32[]{:S(2)}, u32[]{:S(2)}) collective-permute-start(f32[512,128]{1,0:T(8,128)S(1)} %bitcast_add_fusion.14), channel_id=1, source_target_pairs={{0,4},{4,8},{8,12},{12,16},{16,20},{20,24},{24,28},{28,0},{1,5},{5... | collective-permute-start | bytes 786440 | tf_op jit(solution)/shard_map/ppermute | solution.py:63
  34.2 8.9 %collective-permute-start.8 = (f32[512,128]{1,0:T(8,128)S(1)}, f32[512,128]{1,0:T(8,128)S(1)}, u32[]{:S(2)}, u32[]{:S(2)}) collective-permute-start(f32[512,128]{1,0:T(8,128)S(1)} %bitcast_add_fusion.7), channel_id=1, source_target_pairs={{0,28},{4,0},{8,4},{12,8},{16,12},{20,16},{24,20},{28,24},{1,29},{... | collective-permute-start | bytes 786440 | tf_op jit(solution)/shard_map/ppermute | solution.py:64
  42.9 7.1 %collective-permute-start.2 = (f32[512,128]{1,0:T(8,128)S(1)}, f32[512,128]{1,0:T(8,128)S(1)}, u32[]{:S(2)}, u32[]{:S(2)}) collective-permute-start(f32[512,128]{1,0:T(8,128)S(1)} %bitcast_add_fusion.13), channel_id=1, source_target_pairs={{0,4},{4,8},{8,12},{12,16},{16,20},{20,24},{24,28},{28,0},{1,5},{5... | collective-permute-start | bytes 786440 | tf_op jit(solution)/shard_map/ppermute | solution.py:63
  43.1 8.0 %collective-permute-start.9 = (f32[512,128]{1,0:T(8,128)S(1)}, f32[512,128]{1,0:T(8,128)S(1)}, u32[]{:S(2)}, u32[]{:S(2)}) collective-permute-start(f32[512,128]{1,0:T(8,128)S(1)} %bitcast_add_fusion.6), channel_id=1, source_target_pairs={{0,28},{4,0},{8,4},{12,8},{16,12},{20,16},{24,20},{28,24},{1,29},{... | collective-permute-start | bytes 786440 | tf_op jit(solution)/shard_map/ppermute | solution.py:64
  51.0 6.5 %collective-permute-start.3 = (f32[512,128]{1,0:T(8,128)S(1)}, f32[512,128]{1,0:T(8,128)S(1)}, u32[]{:S(2)}, u32[]{:S(2)}) collective-permute-start(f32[512,128]{1,0:T(8,128)S(1)} %bitcast_add_fusion.12), channel_id=1, source_target_pairs={{0,4},{4,8},{8,12},{12,16},{16,20},{20,24},{24,28},{28,0},{1,5},{5... | collective-permute-start | bytes 786440 | tf_op jit(solution)/shard_map/ppermute | solution.py:63
  51.1 7.4 %collective-permute-start.10 = (f32[512,128]{1,0:T(8,128)S(1)}, f32[512,128]{1,0:T(8,128)S(1)}, u32[]{:S(2)}, u32[]{:S(2)}) collective-permute-start(f32[512,128]{1,0:T(8,128)S(1)} %bitcast_add_fusion.5), channel_id=1, source_target_pairs={{0,28},{4,0},{8,4},{12,8},{16,12},{20,16},{24,20},{28,24},{1,29},{... | collective-permute-start | bytes 786440 | tf_op jit(solution)/shard_map/ppermute | solution.py:64
  58.5 6.5 %collective-permute-start.4 = (f32[512,128]{1,0:T(8,128)S(1)}, f32[512,128]{1,0:T(8,128)S(1)}, u32[]{:S(2)}, u32[]{:S(2)}) collective-permute-start(f32[512,128]{1,0:T(8,128)S(1)} %bitcast_add_fusion.11), channel_id=1, source_target_pairs={{0,4},{4,8},{8,12},{12,16},{16,20},{20,24},{24,28},{28,0},{1,5},{5... | collective-permute-start | bytes 786440 | tf_op jit(solution)/shard_map/ppermute | solution.py:63
  58.6 7.4 %collective-permute-start.11 = (f32[512,128]{1,0:T(8,128)S(1)}, f32[512,128]{1,0:T(8,128)S(1)}, u32[]{:S(2)}, u32[]{:S(2)}) collective-permute-start(f32[512,128]{1,0:T(8,128)S(1)} %bitcast_add_fusion.4), channel_id=1, source_target_pairs={{0,28},{4,0},{8,4},{12,8},{16,12},{20,16},{24,20},{28,24},{1,29},{... | collective-permute-start | bytes 786440 | tf_op jit(solution)/shard_map/ppermute | solution.py:64
  66.0 6.5 %collective-permute-start.5 = (f32[512,128]{1,0:T(8,128)S(1)}, f32[512,128]{1,0:T(8,128)S(1)}, u32[]{:S(2)}, u32[]{:S(2)}) collective-permute-start(f32[512,128]{1,0:T(8,128)S(1)} %bitcast_add_fusion.10), channel_id=1, source_target_pairs={{0,4},{4,8},{8,12},{12,16},{16,20},{20,24},{24,28},{28,0},{1,5},{5... | collective-permute-start | bytes 786440 | tf_op jit(solution)/shard_map/ppermute | solution.py:63
  66.1 7.4 %collective-permute-start.12 = (f32[512,128]{1,0:T(8,128)S(1)}, f32[512,128]{1,0:T(8,128)S(1)}, u32[]{:S(2)}, u32[]{:S(2)}) collective-permute-start(f32[512,128]{1,0:T(8,128)S(1)} %bitcast_add_fusion.3), channel_id=1, source_target_pairs={{0,28},{4,0},{8,4},{12,8},{16,12},{20,16},{24,20},{28,24},{1,29},{... | collective-permute-start | bytes 786440 | tf_op jit(solution)/shard_map/ppermute | solution.py:64
  73.4 7.5 %collective-permute-start.6 = (f32[512,128]{1,0:T(8,128)S(1)}, f32[512,128]{1,0:T(8,128)S(1)}, u32[]{:S(2)}, u32[]{:S(2)}) collective-permute-start(f32[512,128]{1,0:T(8,128)S(1)} %bitcast_add_fusion.9), channel_id=1, source_target_pairs={{0,4},{4,8},{8,12},{12,16},{16,20},{20,24},{24,28},{28,0},{1,5},{5... | collective-permute-start | bytes 786440 | tf_op jit(solution)/shard_map/ppermute | solution.py:63
  73.6 8.4 %collective-permute-start.13 = (f32[512,128]{1,0:T(8,128)S(1)}, f32[512,128]{1,0:T(8,128)S(1)}, u32[]{:S(2)}, u32[]{:S(2)}) collective-permute-start(f32[512,128]{1,0:T(8,128)S(1)} %bitcast_add_fusion.2), channel_id=1, source_target_pairs={{0,28},{4,0},{8,4},{12,8},{16,12},{20,16},{24,20},{28,24},{1,29},{... | collective-permute-start | bytes 786440 | tf_op jit(solution)/shard_map/ppermute | solution.py:64
  82.8 12.5 %all-to-all-start = ((f32[8,128,128]{2,1,0:T(8,128)}), f32[8,128,128]{2,1,0:T(8,128)S(1)}, u32[]{:S(2)}, u32[]{:S(2)}) async-start(f32[8,128,128]{2,1,0:T(8,128)} %bitcast.20), calls=%async_computation | async-start | bytes 1048576 | tf_op jit(solution)/shard_map/all_to_all | solution.py:107
  106.9 48.8 %all-to-all-start.2 = ((bf16[8,8,128,128]{3,2,1,0:T(8,128)(2,1)}), bf16[8,8,128,128]{3,2,1,0:T(8,128)(2,1)S(1)}, u32[]{:S(2)}, u32[]{:S(2)}) async-start(bf16[8,8,128,128]{3,2,1,0:T(8,128)(2,1)} %broadcast_in_dim.44), calls=%async_computation.2 | async-start | bytes 4194304 | tf_op jit(solution)/shard_map/all_to_all | solution.py:118
  155.8 1.3 copy-start
  167.7 10.2 %collective-permute-start.14 = (f32[256,128]{1,0:T(8,128)S(1)}, f32[256,128]{1,0:T(8,128)S(1)}, u32[]{:S(2)}, u32[]{:S(2)}) collective-permute-start(f32[256,128]{1,0:T(8,128)S(1)} %dynamic-slice_bitcast_fusion.3), channel_id=1, source_target_pairs={{0,1},{1,0},{2,3},{3,2},{4,5},{5,4},{6,7},{7,6},{8,9},{9,8},{10,11... | collective-permute-start | bytes 393224 | tf_op jit(solution)/shard_map/ppermute | solution.py:63
  176.9 1.4 collective-permute-start.15
  178.4 5.1 %collective-permute-start.16 = (f32[128,128]{1,0:T(8,128)S(1)}, f32[128,128]{1,0:T(8,128)S(1)}, u32[]{:S(2)}, u32[]{:S(2)}) collective-permute-start(f32[128,128]{1,0:T(8,128)S(1)} %dynamic-slice_bitcast_fusion.5), channel_id=1, source_target_pairs={{0,2},{2,0},{1,3},{3,1},{4,6},{6,4},{5,7},{7,5},{8,10},{10,8},{9,1... | collective-permute-start | bytes 196616 | tf_op jit(solution)/shard_map/ppermute | solution.py:63
  181.1 5.1 %collective-permute-start.17 = (f32[128,128]{1,0:T(8,128)S(1)}, f32[128,128]{1,0:T(8,128)S(1)}, u32[]{:S(2)}, u32[]{:S(2)}) collective-permute-start(f32[128,128]{1,0:T(8,128)S(1)} %dynamic-slice_bitcast_fusion.4), channel_id=1, source_target_pairs={{0,2},{2,0},{1,3},{3,1},{4,6},{6,4},{5,7},{7,5},{8,10},{10,8},{9,1... | collective-permute-start | bytes 196616 | tf_op jit(solution)/shard_map/ppermute | solution.py:64
  183.5 12.8 %copy-start.1 = (f32[1024,128]{1,0:T(8,128)S(1)}, f32[1024,128]{1,0:T(8,128)}, u32[]{:S(2)}) copy-start(f32[1024,128]{1,0:T(8,128)} %param.6) | copy-start | bytes 1572868
  183.5 4.7 %collective-permute-start.18 = (f32[128,128]{1,0:T(8,128)S(1)}, f32[128,128]{1,0:T(8,128)S(1)}, u32[]{:S(2)}, u32[]{:S(2)}) collective-permute-start(f32[128,128]{1,0:T(8,128)S(1)} %bitcast_add_fusion.18), channel_id=1, source_target_pairs={{0,2},{2,0},{1,3},{3,1},{4,6},{6,4},{5,7},{7,5},{8,10},{10,8},{9,1... | collective-permute-start | bytes 196616 | tf_op jit(solution)/shard_map/ppermute | solution.py:80
  186.3 4.7 %collective-permute-start.19 = (f32[128,128]{1,0:T(8,128)S(1)}, f32[128,128]{1,0:T(8,128)S(1)}, u32[]{:S(2)}, u32[]{:S(2)}) collective-permute-start(f32[128,128]{1,0:T(8,128)S(1)} %bitcast_add_fusion.17), channel_id=1, source_target_pairs={{0,2},{2,0},{1,3},{3,1},{4,6},{6,4},{5,7},{7,5},{8,10},{10,8},{9,1... | collective-permute-start | bytes 196616 | tf_op jit(solution)/shard_map/ppermute | solution.py:81
  191.0 4.1 %collective-permute-start.20 = (f32[256,128]{1,0:T(8,128)S(1)}, f32[256,128]{1,0:T(8,128)S(1)}, u32[]{:S(2)}, u32[]{:S(2)}) collective-permute-start(f32[256,128]{1,0:T(8,128)S(1)} %get-tuple-element.9), channel_id=1, source_target_pairs={{0,1},{1,0},{2,3},{3,2},{4,5},{5,4},{6,7},{7,6},{8,9},{9,8},{10,11... | collective-permute-start | bytes 393224 | tf_op jit(solution)/shard_map/ppermute | solution.py:80
  194.9 1.3 collective-permute-start.21

commit v10 on v7

--- a/solution.py
+++ b/solution.py
@@ -25,7 +25,7 @@
         )
         return carry
 
-    lax.fori_loop(0, n_blocks, body, 0, unroll=32)
+    lax.fori_loop(0, n_blocks, body, 0, unroll=64)
 
 
 def block_sums(index, a_tiles, b_tiles, n_out, b_transposed=False):

time: 176 us -> 175 us (level)
  no operation moved by 1% of the time
where the time goes in v10:
time: 175 us; the launch traced here: 174 us
  waiting for transfers between devices  61.1 us (35%)
  starting transfers between devices  54.7 us (31%)
  Pallas kernels  18.3 us (10%)
  blocking collectives  14.3 us (8%)
  other arithmetic  12.7 us (7%)
  local copies, waits for them, and re-layouts  12 us (7%)
    ppermute x9, waiting for transfers between devices, ring_reduce_scatter_halves(): rl = lax.ppermute(bl, axis, right)  33.3 us
    ppermute x9, starting transfers between devices, ring_reduce_scatter_halves(): rr = lax.ppermute(br, axis, left)  21 us
    pallas_call x2, Pallas kernels, block_sums(): pl.pallas_call(functools.partial(block_sum_kernel, b_transposed=b_transpo...  18.3 us
    ppermute x9, starting transfers between devices, ring_reduce_scatter_halves(): rl = lax.ppermute(bl, axis, right)  17.9 us
    all_to_all x1, waiting for transfers between devices, per_device(): t = lax.all_to_all(t, ('ylo', 'x'), 0, 0, tiled=True)  16.2 us
    all_to_all x1, blocking collectives, per_device(): lax.all_to_all(jnp.broadcast_to(own_bf[None], (n_z, tile_rows, width)), '...  14.3 us
    add x9, other arithmetic, ring_reduce_scatter_halves(): bl = rl + lax.dynamic_index_in_dim(xl, (i - s - 2) % n, 0, keepdims=False)  6.87 us
    all_to_all x1, waiting for transfers between devices, per_device(): x = lax.all_to_all(x, ('ylo', 'x'), 0, 0, tiled=True)  6.6 us
  transfers between devices with their start and end apart: 24, of which 16 were waited for; matrix products, arithmetic and copies ran while one was open for 5% of the time, Pallas kernels for 0%

profile of v10, /device:TPU:1, one launch (start us, length us, event | category | flops | bytes accessed | tf_op | source)
XLA Modules:
  0.0 174.2 jit_solution(12155369790393306516)
XLA Ops:
  5.3 9.6 %shard_map.77 = f32[64,128,128]{2,1,0:T(8,128)} custom-call(s32[1152]{0:T(1024)} %get-tuple-element.14.index_ref, bf16[8,128,128]{2,1,0:T(8,128)(2,1)} %bitcast.110, bf16[64,128,128]{2,1,0:T(8,128)(2,1)} %a_ref.1), custom_call_target="tpu_custom_call" | custom-call | tf_op jit(solution)/shard_map/pallas_call | solution.py:36
  14.9 4.0 %fusion.10 = (f32[32,128,128]{2,1,0:T(8,128)}, f32[32,128,128]{2,1,0:T(8,128)S(1)}) fusion(f32[64,128,128]{2,1,0:T(8,128)} %shard_map.77), kind=kLoop, calls=%fused_computation.62 | loop fusion | bytes 8388608 | tf_op jit(solution)/shard_map/slice | solution.py:105
  19.8 2.5 %collective-permute-start = (f32[512,128]{1,0:T(8,128)S(1)}, f32[512,128]{1,0:T(8,128)S(1)}, u32[]{:S(2)}, u32[]{:S(2)}) collective-permute-start(f32[512,128]{1,0:T(8,128)S(1)} %dynamic-slice_bitcast_fusion.1), channel_id=1, source_target_pairs={{0,4},{4,8},{8,12},{12,16},{16,20},{20,24},{24,28},{28,0},{1,5},{5... | collective-permute-start | bytes 786440 | tf_op jit(solution)/shard_map/ppermute | solution.py:63
  22.4 4.1 %collective-permute-start.7 = (f32[512,128]{1,0:T(8,128)S(1)}, f32[512,128]{1,0:T(8,128)S(1)}, u32[]{:S(2)}, u32[]{:S(2)}) collective-permute-start(f32[512,128]{1,0:T(8,128)S(1)} %dynamic-slice_bitcast_fusion), channel_id=1, source_target_pairs={{0,28},{4,0},{8,4},{12,8},{16,12},{20,16},{24,20},{28,24},{1,29},{... | collective-permute-start | bytes 786440 | tf_op jit(solution)/shard_map/ppermute | solution.py:64
  26.4 5.9 %collective-permute-done = f32[512,128]{1,0:T(8,128)S(1)} collective-permute-done((f32[512,128]{1,0:T(8,128)S(1)}, f32[512,128]{1,0:T(8,128)S(1)}, u32[]{:S(2)}, u32[]{:S(2)}) %collective-permute-start) | collective-permute-done | bytes 262176 | tf_op jit(solution)/shard_map/ppermute | solution.py:63
  33.4 2.7 %collective-permute-start.8 = (f32[512,128]{1,0:T(8,128)S(1)}, f32[512,128]{1,0:T(8,128)S(1)}, u32[]{:S(2)}, u32[]{:S(2)}) collective-permute-start(f32[512,128]{1,0:T(8,128)S(1)} %bitcast_add_fusion.7), channel_id=1, source_target_pairs={{0,28},{4,0},{8,4},{12,8},{16,12},{20,16},{24,20},{28,24},{1,29},{... | collective-permute-start | bytes 786440 | tf_op jit(solution)/shard_map/ppermute | solution.py:64
  36.1 5.0 %collective-permute-done.1 = f32[512,128]{1,0:T(8,128)S(1)} collective-permute-done((f32[512,128]{1,0:T(8,128)S(1)}, f32[512,128]{1,0:T(8,128)S(1)}, u32[]{:S(2)}, u32[]{:S(2)}) %collective-permute-start.1) | collective-permute-done | bytes 262176 | tf_op jit(solution)/shard_map/ppermute | solution.py:63
  42.3 2.7 %collective-permute-start.9 = (f32[512,128]{1,0:T(8,128)S(1)}, f32[512,128]{1,0:T(8,128)S(1)}, u32[]{:S(2)}, u32[]{:S(2)}) collective-permute-start(f32[512,128]{1,0:T(8,128)S(1)} %bitcast_add_fusion.6), channel_id=1, source_target_pairs={{0,28},{4,0},{8,4},{12,8},{16,12},{20,16},{24,20},{28,24},{1,29},{... | collective-permute-start | bytes 786440 | tf_op jit(solution)/shard_map/ppermute | solution.py:64
  45.0 4.2 %collective-permute-done.2 = f32[512,128]{1,0:T(8,128)S(1)} collective-permute-done((f32[512,128]{1,0:T(8,128)S(1)}, f32[512,128]{1,0:T(8,128)S(1)}, u32[]{:S(2)}, u32[]{:S(2)}) %collective-permute-start.2) | collective-permute-done | bytes 262176 | tf_op jit(solution)/shard_map/ppermute | solution.py:63
  50.3 2.7 %collective-permute-start.10 = (f32[512,128]{1,0:T(8,128)S(1)}, f32[512,128]{1,0:T(8,128)S(1)}, u32[]{:S(2)}, u32[]{:S(2)}) collective-permute-start(f32[512,128]{1,0:T(8,128)S(1)} %bitcast_add_fusion.5), channel_id=1, source_target_pairs={{0,28},{4,0},{8,4},{12,8},{16,12},{20,16},{24,20},{28,24},{1,29},{... | collective-permute-start | bytes 786440 | tf_op jit(solution)/shard_map/ppermute | solution.py:64
  53.0 3.6 %collective-permute-done.3 = f32[512,128]{1,0:T(8,128)S(1)} collective-permute-done((f32[512,128]{1,0:T(8,128)S(1)}, f32[512,128]{1,0:T(8,128)S(1)}, u32[]{:S(2)}, u32[]{:S(2)}) %collective-permute-start.3) | collective-permute-done | bytes 262176 | tf_op jit(solution)/shard_map/ppermute | solution.py:63
  57.8 2.7 %collective-permute-start.11 = (f32[512,128]{1,0:T(8,128)S(1)}, f32[512,128]{1,0:T(8,128)S(1)}, u32[]{:S(2)}, u32[]{:S(2)}) collective-permute-start(f32[512,128]{1,0:T(8,128)S(1)} %bitcast_add_fusion.4), channel_id=1, source_target_pairs={{0,28},{4,0},{8,4},{12,8},{16,12},{20,16},{24,20},{28,24},{1,29},{... | collective-permute-start | bytes 786440 | tf_op jit(solution)/shard_map/ppermute | solution.py:64
  60.5 3.6 %collective-permute-done.4 = f32[512,128]{1,0:T(8,128)S(1)} collective-permute-done((f32[512,128]{1,0:T(8,128)S(1)}, f32[512,128]{1,0:T(8,128)S(1)}, u32[]{:S(2)}, u32[]{:S(2)}) %collective-permute-start.4) | collective-permute-done | bytes 262176 | tf_op jit(solution)/shard_map/ppermute | solution.py:63
  65.3 2.7 %collective-permute-start.12 = (f32[512,128]{1,0:T(8,128)S(1)}, f32[512,128]{1,0:T(8,128)S(1)}, u32[]{:S(2)}, u32[]{:S(2)}) collective-permute-start(f32[512,128]{1,0:T(8,128)S(1)} %bitcast_add_fusion.3), channel_id=1, source_target_pairs={{0,28},{4,0},{8,4},{12,8},{16,12},{20,16},{24,20},{28,24},{1,29},{... | collective-permute-start | bytes 786440 | tf_op jit(solution)/shard_map/ppermute | solution.py:64
  68.0 3.6 %collective-permute-done.5 = f32[512,128]{1,0:T(8,128)S(1)} collective-permute-done((f32[512,128]{1,0:T(8,128)S(1)}, f32[512,128]{1,0:T(8,128)S(1)}, u32[]{:S(2)}, u32[]{:S(2)}) %collective-permute-start.5) | collective-permute-done | bytes 262176 | tf_op jit(solution)/shard_map/ppermute | solution.py:63
  73.0 2.7 %collective-permute-start.13 = (f32[512,128]{1,0:T(8,128)S(1)}, f32[512,128]{1,0:T(8,128)S(1)}, u32[]{:S(2)}, u32[]{:S(2)}) collective-permute-start(f32[512,128]{1,0:T(8,128)S(1)} %bitcast_add_fusion.2), channel_id=1, source_target_pairs={{0,28},{4,0},{8,4},{12,8},{16,12},{20,16},{24,20},{28,24},{1,29},{... | collective-permute-start | bytes 786440 | tf_op jit(solution)/shard_map/ppermute | solution.py:64
  75.7 4.5 %collective-permute-done.6 = f32[512,128]{1,0:T(8,128)S(1)} collective-permute-done((f32[512,128]{1,0:T(8,128)S(1)}, f32[512,128]{1,0:T(8,128)S(1)}, u32[]{:S(2)}, u32[]{:S(2)}) %collective-permute-start.6) | collective-permute-done | bytes 262176 | tf_op jit(solution)/shard_map/ppermute | solution.py:63
  82.1 5.0 %all-to-all-start = ((f32[8,128,128]{2,1,0:T(8,128)}), f32[8,128,128]{2,1,0:T(8,128)S(1)}, u32[]{:S(2)}, u32[]{:S(2)}) async-start(f32[8,128,128]{2,1,0:T(8,128)} %bitcast.20), calls=%async_computation | async-start | bytes 1048576 | tf_op jit(solution)/shard_map/all_to_all | solution.py:107
  88.0 6.6 %all-to-all-done = f32[8,128,128]{2,1,0:T(8,128)S(1)} async-done(((f32[8,128,128]{2,1,0:T(8,128)}), f32[8,128,128]{2,1,0:T(8,128)S(1)}, u32[]{:S(2)}, u32[]{:S(2)}) %all-to-all-start) | async-done | bytes 524320 | tf_op jit(solution)/shard_map/all_to_all | solution.py:107
  94.9 14.3 %all_to_all.15 = bf16[8,128,128]{2,1,0:T(8,128)(2,1)S(1)} all-to-all(bf16[8,128,128]{2,1,0:T(8,128)(2,1)S(1)} %broadcast_in_dim.43), channel_id=1, replica_groups=mesh['ylo'=2,'x'=4,'z'=8,'yhi'=2,'core'=2] {'z'}, dimensions={0} | all-to-all | bytes 524288 | tf_op jit(solution)/shard_map/all_to_all | solution.py:114
  109.2 1.8 %broadcast_in_dim.44 = bf16[8,8,128,128]{3,2,1,0:T(8,128)(2,1)} broadcast(bf16[8,128,128]{2,1,0:T(8,128)(2,1)S(1)} %all_to_all.15), dimensions={1,2,3} | broadcast | bytes 2359296 | tf_op jit(solution)/shard_map/broadcast_in_dim | solution.py:115
  111.1 3.6 %all-to-all-start.2 = ((bf16[8,8,128,128]{3,2,1,0:T(8,128)(2,1)}), bf16[8,8,128,128]{3,2,1,0:T(8,128)(2,1)S(1)}, u32[]{:S(2)}, u32[]{:S(2)}) async-start(bf16[8,8,128,128]{3,2,1,0:T(8,128)(2,1)} %broadcast_in_dim.44), calls=%async_computation.2 | async-start | bytes 4194304 | tf_op jit(solution)/shard_map/all_to_all | solution.py:116
  114.7 16.2 %all-to-all-done.2 = bf16[8,8,128,128]{3,2,1,0:T(8,128)(2,1)S(1)} async-done(((bf16[8,8,128,128]{3,2,1,0:T(8,128)(2,1)}), bf16[8,8,128,128]{3,2,1,0:T(8,128)(2,1)S(1)}, u32[]{:S(2)}, u32[]{:S(2)}) %all-to-all-start.2) | async-done | bytes 2097184 | tf_op jit(solution)/shard_map/all_to_all | solution.py:116
  130.9 1.3 copy-done
  132.2 8.7 %shard_map.78 = f32[8,128,128]{2,1,0:T(8,128)} custom-call(s32[1152]{0:T(1024)} %get-tuple-element.15.index_ref, bf16[64,128,128]{2,1,0:T(8,128)(2,1)} %a_ref.1, bf16[64,128,128]{2,1,0:T(8,128)(2,1)} %bitcast.107), custom_call_target="tpu_custom_call" | custom-call | tf_op jit(solution)/shard_map/pallas_call | solution.py:36
  142.0 11.9 %collective-permute-start.14 = (f32[256,128]{1,0:T(8,128)S(1)}, f32[256,128]{1,0:T(8,128)S(1)}, u32[]{:S(2)}, u32[]{:S(2)}) collective-permute-start(f32[256,128]{1,0:T(8,128)S(1)} %dynamic-slice_bitcast_fusion.3), channel_id=1, source_target_pairs={{0,1},{1,0},{2,3},{3,2},{4,5},{5,4},{6,7},{7,6},{8,9},{9,8},{10,11... | collective-permute-start | bytes 393224 | tf_op jit(solution)/shard_map/ppermute | solution.py:63
  155.5 2.7 %collective-permute-start.16 = (f32[128,128]{1,0:T(8,128)S(1)}, f32[128,128]{1,0:T(8,128)S(1)}, u32[]{:S(2)}, u32[]{:S(2)}) collective-permute-start(f32[128,128]{1,0:T(8,128)S(1)} %dynamic-slice_bitcast_fusion.5), channel_id=1, source_target_pairs={{0,2},{2,0},{1,3},{3,1},{4,6},{6,4},{5,7},{7,5},{8,10},{10,8},{9,1... | collective-permute-start | bytes 196616 | tf_op jit(solution)/shard_map/ppermute | solution.py:63
  158.6 2.0 %collective-permute-done.16 = f32[128,128]{1,0:T(8,128)S(1)} collective-permute-done((f32[128,128]{1,0:T(8,128)S(1)}, f32[128,128]{1,0:T(8,128)S(1)}, u32[]{:S(2)}, u32[]{:S(2)}) %collective-permute-start.16) | collective-permute-done | bytes 65568 | tf_op jit(solution)/shard_map/ppermute | solution.py:63
  160.6 2.7 %collective-permute-start.18 = (f32[128,128]{1,0:T(8,128)S(1)}, f32[128,128]{1,0:T(8,128)S(1)}, u32[]{:S(2)}, u32[]{:S(2)}) collective-permute-start(f32[128,128]{1,0:T(8,128)S(1)} %bitcast_add_fusion.18), channel_id=1, source_target_pairs={{0,2},{2,0},{1,3},{3,1},{4,6},{6,4},{5,7},{7,5},{8,10},{10,8},{9,1... | collective-permute-start | bytes 196616 | tf_op jit(solution)/shard_map/ppermute | solution.py:80
  163.3 1.4 collective-permute-start.19
  165.3 2.7 %collective-permute-done.19 = f32[128,128]{1,0:T(8,128)S(1)} collective-permute-done((f32[128,128]{1,0:T(8,128)S(1)}, f32[128,128]{1,0:T(8,128)S(1)}, u32[]{:S(2)}, u32[]{:S(2)}) %collective-permute-start.19) | collective-permute-done | bytes 65568 | tf_op jit(solution)/shard_map/ppermute | solution.py:81
  168.1 3.1 %collective-permute-start.20 = (f32[256,128]{1,0:T(8,128)S(1)}, f32[256,128]{1,0:T(8,128)S(1)}, u32[]{:S(2)}, u32[]{:S(2)}) collective-permute-start(f32[256,128]{1,0:T(8,128)S(1)} %get-tuple-element.9), channel_id=1, source_target_pairs={{0,1},{1,0},{2,3},{3,2},{4,5},{5,4},{6,7},{7,6},{8,9},{9,8},{10,11... | collective-permute-start | bytes 393224 | tf_op jit(solution)/shard_map/ppermute | solution.py:80
  (78 shorter events, 22.0 us)
Async XLA Ops:
  19.8 12.5 %collective-permute-start = (f32[512,128]{1,0:T(8,128)S(1)}, f32[512,128]{1,0:T(8,128)S(1)}, u32[]{:S(2)}, u32[]{:S(2)}) collective-permute-start(f32[512,128]{1,0:T(8,128)S(1)} %dynamic-slice_bitcast_fusion.1), channel_id=1, source_target_pairs={{0,4},{4,8},{8,12},{12,16},{16,20},{20,24},{24,28},{28,0},{1,5},{5... | collective-permute-start | bytes 786440 | tf_op jit(solution)/shard_map/ppermute | solution.py:63
  22.4 11.0 %collective-permute-start.7 = (f32[512,128]{1,0:T(8,128)S(1)}, f32[512,128]{1,0:T(8,128)S(1)}, u32[]{:S(2)}, u32[]{:S(2)}) collective-permute-start(f32[512,128]{1,0:T(8,128)S(1)} %dynamic-slice_bitcast_fusion), channel_id=1, source_target_pairs={{0,28},{4,0},{8,4},{12,8},{16,12},{20,16},{24,20},{28,24},{1,29},{... | collective-permute-start | bytes 786440 | tf_op jit(solution)/shard_map/ppermute | solution.py:64
  33.3 7.9 %collective-permute-start.1 = (f32[512,128]{1,0:T(8,128)S(1)}, f32[512,128]{1,0:T(8,128)S(1)}, u32[]{:S(2)}, u32[]{:S(2)}) collective-permute-start(f32[512,128]{1,0:T(8,128)S(1)} %bitcast_add_fusion.14), channel_id=1, source_target_pairs={{0,4},{4,8},{8,12},{12,16},{16,20},{20,24},{24,28},{28,0},{1,5},{5... | collective-permute-start | bytes 786440 | tf_op jit(solution)/shard_map/ppermute | solution.py:63
  33.4 8.8 %collective-permute-start.8 = (f32[512,128]{1,0:T(8,128)S(1)}, f32[512,128]{1,0:T(8,128)S(1)}, u32[]{:S(2)}, u32[]{:S(2)}) collective-permute-start(f32[512,128]{1,0:T(8,128)S(1)} %bitcast_add_fusion.7), channel_id=1, source_target_pairs={{0,28},{4,0},{8,4},{12,8},{16,12},{20,16},{24,20},{28,24},{1,29},{... | collective-permute-start | bytes 786440 | tf_op jit(solution)/shard_map/ppermute | solution.py:64
  42.2 7.0 %collective-permute-start.2 = (f32[512,128]{1,0:T(8,128)S(1)}, f32[512,128]{1,0:T(8,128)S(1)}, u32[]{:S(2)}, u32[]{:S(2)}) collective-permute-start(f32[512,128]{1,0:T(8,128)S(1)} %bitcast_add_fusion.13), channel_id=1, source_target_pairs={{0,4},{4,8},{8,12},{12,16},{16,20},{20,24},{24,28},{28,0},{1,5},{5... | collective-permute-start | bytes 786440 | tf_op jit(solution)/shard_map/ppermute | solution.py:63
  42.3 8.0 %collective-permute-start.9 = (f32[512,128]{1,0:T(8,128)S(1)}, f32[512,128]{1,0:T(8,128)S(1)}, u32[]{:S(2)}, u32[]{:S(2)}) collective-permute-start(f32[512,128]{1,0:T(8,128)S(1)} %bitcast_add_fusion.6), channel_id=1, source_target_pairs={{0,28},{4,0},{8,4},{12,8},{16,12},{20,16},{24,20},{28,24},{1,29},{... | collective-permute-start | bytes 786440 | tf_op jit(solution)/shard_map/ppermute | solution.py:64
  50.2 6.5 %collective-permute-start.3 = (f32[512,128]{1,0:T(8,128)S(1)}, f32[512,128]{1,0:T(8,128)S(1)}, u32[]{:S(2)}, u32[]{:S(2)}) collective-permute-start(f32[512,128]{1,0:T(8,128)S(1)} %bitcast_add_fusion.12), channel_id=1, source_target_pairs={{0,4},{4,8},{8,12},{12,16},{16,20},{20,24},{24,28},{28,0},{1,5},{5... | collective-permute-start | bytes 786440 | tf_op jit(solution)/shard_map/ppermute | solution.py:63
  50.3 7.4 %collective-permute-start.10 = (f32[512,128]{1,0:T(8,128)S(1)}, f32[512,128]{1,0:T(8,128)S(1)}, u32[]{:S(2)}, u32[]{:S(2)}) collective-permute-start(f32[512,128]{1,0:T(8,128)S(1)} %bitcast_add_fusion.5), channel_id=1, source_target_pairs={{0,28},{4,0},{8,4},{12,8},{16,12},{20,16},{24,20},{28,24},{1,29},{... | collective-permute-start | bytes 786440 | tf_op jit(solution)/shard_map/ppermute | solution.py:64
  57.7 6.5 %collective-permute-start.4 = (f32[512,128]{1,0:T(8,128)S(1)}, f32[512,128]{1,0:T(8,128)S(1)}, u32[]{:S(2)}, u32[]{:S(2)}) collective-permute-start(f32[512,128]{1,0:T(8,128)S(1)} %bitcast_add_fusion.11), channel_id=1, source_target_pairs={{0,4},{4,8},{8,12},{12,16},{16,20},{20,24},{24,28},{28,0},{1,5},{5... | collective-permute-start | bytes 786440 | tf_op jit(solution)/shard_map/ppermute | solution.py:63
  57.8 7.4 %collective-permute-start.11 = (f32[512,128]{1,0:T(8,128)S(1)}, f32[512,128]{1,0:T(8,128)S(1)}, u32[]{:S(2)}, u32[]{:S(2)}) collective-permute-start(f32[512,128]{1,0:T(8,128)S(1)} %bitcast_add_fusion.4), channel_id=1, source_target_pairs={{0,28},{4,0},{8,4},{12,8},{16,12},{20,16},{24,20},{28,24},{1,29},{... | collective-permute-start | bytes 786440 | tf_op jit(solution)/shard_map/ppermute | solution.py:64
  65.2 6.5 %collective-permute-start.5 = (f32[512,128]{1,0:T(8,128)S(1)}, f32[512,128]{1,0:T(8,128)S(1)}, u32[]{:S(2)}, u32[]{:S(2)}) collective-permute-start(f32[512,128]{1,0:T(8,128)S(1)} %bitcast_add_fusion.10), channel_id=1, source_target_pairs={{0,4},{4,8},{8,12},{12,16},{16,20},{20,24},{24,28},{28,0},{1,5},{5... | collective-permute-start | bytes 786440 | tf_op jit(solution)/shard_map/ppermute | solution.py:63
  65.3 7.6 %collective-permute-start.12 = (f32[512,128]{1,0:T(8,128)S(1)}, f32[512,128]{1,0:T(8,128)S(1)}, u32[]{:S(2)}, u32[]{:S(2)}) collective-permute-start(f32[512,128]{1,0:T(8,128)S(1)} %bitcast_add_fusion.3), channel_id=1, source_target_pairs={{0,28},{4,0},{8,4},{12,8},{16,12},{20,16},{24,20},{28,24},{1,29},{... | collective-permute-start | bytes 786440 | tf_op jit(solution)/shard_map/ppermute | solution.py:64
  72.7 7.5 %collective-permute-start.6 = (f32[512,128]{1,0:T(8,128)S(1)}, f32[512,128]{1,0:T(8,128)S(1)}, u32[]{:S(2)}, u32[]{:S(2)}) collective-permute-start(f32[512,128]{1,0:T(8,128)S(1)} %bitcast_add_fusion.9), channel_id=1, source_target_pairs={{0,4},{4,8},{8,12},{12,16},{16,20},{20,24},{24,28},{28,0},{1,5},{5... | collective-permute-start | bytes 786440 | tf_op jit(solution)/shard_map/ppermute | solution.py:63
  73.0 8.2 %collective-permute-start.13 = (f32[512,128]{1,0:T(8,128)S(1)}, f32[512,128]{1,0:T(8,128)S(1)}, u32[]{:S(2)}, u32[]{:S(2)}) collective-permute-start(f32[512,128]{1,0:T(8,128)S(1)} %bitcast_add_fusion.2), channel_id=1, source_target_pairs={{0,28},{4,0},{8,4},{12,8},{16,12},{20,16},{24,20},{28,24},{1,29},{... | collective-permute-start | bytes 786440 | tf_op jit(solution)/shard_map/ppermute | solution.py:64
  82.1 12.6 %all-to-all-start = ((f32[8,128,128]{2,1,0:T(8,128)}), f32[8,128,128]{2,1,0:T(8,128)S(1)}, u32[]{:S(2)}, u32[]{:S(2)}) async-start(f32[8,128,128]{2,1,0:T(8,128)} %bitcast.20), calls=%async_computation | async-start | bytes 1048576 | tf_op jit(solution)/shard_map/all_to_all | solution.py:107
  111.1 19.8 %all-to-all-start.2 = ((bf16[8,8,128,128]{3,2,1,0:T(8,128)(2,1)}), bf16[8,8,128,128]{3,2,1,0:T(8,128)(2,1)S(1)}, u32[]{:S(2)}, u32[]{:S(2)}) async-start(bf16[8,8,128,128]{3,2,1,0:T(8,128)(2,1)} %broadcast_in_dim.44), calls=%async_computation.2 | async-start | bytes 4194304 | tf_op jit(solution)/shard_map/all_to_all | solution.py:116
  130.9 1.3 copy-start
  142.0 12.9 %collective-permute-start.14 = (f32[256,128]{1,0:T(8,128)S(1)}, f32[256,128]{1,0:T(8,128)S(1)}, u32[]{:S(2)}, u32[]{:S(2)}) collective-permute-start(f32[256,128]{1,0:T(8,128)S(1)} %dynamic-slice_bitcast_fusion.3), channel_id=1, source_target_pairs={{0,1},{1,0},{2,3},{3,2},{4,5},{5,4},{6,7},{7,6},{8,9},{9,8},{10,11... | collective-permute-start | bytes 393224 | tf_op jit(solution)/shard_map/ppermute | solution.py:63
  154.0 1.4 collective-permute-start.15
  155.5 5.1 %collective-permute-start.16 = (f32[128,128]{1,0:T(8,128)S(1)}, f32[128,128]{1,0:T(8,128)S(1)}, u32[]{:S(2)}, u32[]{:S(2)}) collective-permute-start(f32[128,128]{1,0:T(8,128)S(1)} %dynamic-slice_bitcast_fusion.5), channel_id=1, source_target_pairs={{0,2},{2,0},{1,3},{3,1},{4,6},{6,4},{5,7},{7,5},{8,10},{10,8},{9,1... | collective-permute-start | bytes 196616 | tf_op jit(solution)/shard_map/ppermute | solution.py:63
  158.2 5.1 %collective-permute-start.17 = (f32[128,128]{1,0:T(8,128)S(1)}, f32[128,128]{1,0:T(8,128)S(1)}, u32[]{:S(2)}, u32[]{:S(2)}) collective-permute-start(f32[128,128]{1,0:T(8,128)S(1)} %dynamic-slice_bitcast_fusion.4), channel_id=1, source_target_pairs={{0,2},{2,0},{1,3},{3,1},{4,6},{6,4},{5,7},{7,5},{8,10},{10,8},{9,1... | collective-permute-start | bytes 196616 | tf_op jit(solution)/shard_map/ppermute | solution.py:64
  160.6 12.7 %copy-start.1 = (f32[1024,128]{1,0:T(8,128)S(1)}, f32[1024,128]{1,0:T(8,128)}, u32[]{:S(2)}) copy-start(f32[1024,128]{1,0:T(8,128)} %param.6) | copy-start | bytes 1572868
  160.6 4.7 %collective-permute-start.18 = (f32[128,128]{1,0:T(8,128)S(1)}, f32[128,128]{1,0:T(8,128)S(1)}, u32[]{:S(2)}, u32[]{:S(2)}) collective-permute-start(f32[128,128]{1,0:T(8,128)S(1)} %bitcast_add_fusion.18), channel_id=1, source_target_pairs={{0,2},{2,0},{1,3},{3,1},{4,6},{6,4},{5,7},{7,5},{8,10},{10,8},{9,1... | collective-permute-start | bytes 196616 | tf_op jit(solution)/shard_map/ppermute | solution.py:80
  163.3 4.7 %collective-permute-start.19 = (f32[128,128]{1,0:T(8,128)S(1)}, f32[128,128]{1,0:T(8,128)S(1)}, u32[]{:S(2)}, u32[]{:S(2)}) collective-permute-start(f32[128,128]{1,0:T(8,128)S(1)} %bitcast_add_fusion.17), channel_id=1, source_target_pairs={{0,2},{2,0},{1,3},{3,1},{4,6},{6,4},{5,7},{7,5},{8,10},{10,8},{9,1... | collective-permute-start | bytes 196616 | tf_op jit(solution)/shard_map/ppermute | solution.py:81
  168.1 4.1 %collective-permute-start.20 = (f32[256,128]{1,0:T(8,128)S(1)}, f32[256,128]{1,0:T(8,128)S(1)}, u32[]{:S(2)}, u32[]{:S(2)}) collective-permute-start(f32[256,128]{1,0:T(8,128)S(1)} %get-tuple-element.9), channel_id=1, source_target_pairs={{0,1},{1,0},{2,3},{3,2},{4,5},{5,4},{6,7},{7,6},{8,9},{9,8},{10,11... | collective-permute-start | bytes 393224 | tf_op jit(solution)/shard_map/ppermute | solution.py:80
  171.9 1.3 collective-permute-start.21

commit v11 on v10

--- a/solution.py
+++ b/solution.py
@@ -25,7 +25,7 @@
         )
         return carry
 
-    lax.fori_loop(0, n_blocks, body, 0, unroll=64)
+    lax.fori_loop(0, n_blocks, body, 0, unroll=128)
 
 
 def block_sums(index, a_tiles, b_tiles, n_out, b_transposed=False):

time: 175 us -> 174 us (level)
  no operation moved by 1% of the time
where the time goes in v11:
time: 174 us
  waiting for transfers between devices  61.1 us (35%)
  starting transfers between devices  54.6 us (31%)
  Pallas kernels  17.7 us (10%)
  blocking collectives  14.4 us (8%)
  other arithmetic  12.7 us (7%)
  local copies, waits for them, and re-layouts  12 us (7%)
    ppermute x9, waiting for transfers between devices, ring_reduce_scatter_halves(): rl = lax.ppermute(bl, axis, right)  33.3 us
    ppermute x9, starting transfers between devices, ring_reduce_scatter_halves(): rr = lax.ppermute(br, axis, left)  21.1 us
    ppermute x9, starting transfers between devices, ring_reduce_scatter_halves(): rl = lax.ppermute(bl, axis, right)  17.7 us
    pallas_call x2, Pallas kernels, block_sums(): pl.pallas_call(functools.partial(block_sum_kernel, b_transposed=b_transpo...  17.7 us
    all_to_all x1, waiting for transfers between devices, per_device(): t = lax.all_to_all(t, ('ylo', 'x'), 0, 0, tiled=True)  16.2 us
    all_to_all x1, blocking collectives, per_device(): lax.all_to_all(jnp.broadcast_to(own_bf[None], (n_z, tile_rows, width)), '...  14.4 us
    add x9, other arithmetic, ring_reduce_scatter_halves(): bl = rl + lax.dynamic_index_in_dim(xl, (i - s - 2) % n, 0, keepdims=False)  6.87 us
    all_to_all x1, waiting for transfers between devices, per_device(): x = lax.all_to_all(x, ('ylo', 'x'), 0, 0, tiled=True)  6.6 us
  transfers between devices with their start and end apart: 24, of which 16 were waited for; matrix products, arithmetic and copies ran while one was open for 5% of the time, Pallas kernels for 0%

profile of v11, /device:TPU:1, one launch (start us, length us, event | category | flops | bytes accessed | tf_op | source)
XLA Modules:
  0.0 173.6 jit_solution(14637143377090416259)
XLA Ops:
  5.3 9.3 %shard_map.77 = f32[64,128,128]{2,1,0:T(8,128)} custom-call(s32[1152]{0:T(1024)} %get-tuple-element.14.index_ref, bf16[8,128,128]{2,1,0:T(8,128)(2,1)} %bitcast.110, bf16[64,128,128]{2,1,0:T(8,128)(2,1)} %a_ref.1), custom_call_target="tpu_custom_call" | custom-call | tf_op jit(solution)/shard_map/pallas_call | solution.py:36
  14.6 4.0 %fusion.10 = (f32[32,128,128]{2,1,0:T(8,128)}, f32[32,128,128]{2,1,0:T(8,128)S(1)}) fusion(f32[64,128,128]{2,1,0:T(8,128)} %shard_map.77), kind=kLoop, calls=%fused_computation.62 | loop fusion | bytes 8388608 | tf_op jit(solution)/shard_map/slice | solution.py:105
  19.5 2.5 %collective-permute-start = (f32[512,128]{1,0:T(8,128)S(1)}, f32[512,128]{1,0:T(8,128)S(1)}, u32[]{:S(2)}, u32[]{:S(2)}) collective-permute-start(f32[512,128]{1,0:T(8,128)S(1)} %dynamic-slice_bitcast_fusion.1), channel_id=1, source_target_pairs={{0,4},{4,8},{8,12},{12,16},{16,20},{20,24},{24,28},{28,0},{1,5},{5... | collective-permute-start | bytes 786440 | tf_op jit(solution)/shard_map/ppermute | solution.py:63
  22.0 4.1 %collective-permute-start.7 = (f32[512,128]{1,0:T(8,128)S(1)}, f32[512,128]{1,0:T(8,128)S(1)}, u32[]{:S(2)}, u32[]{:S(2)}) collective-permute-start(f32[512,128]{1,0:T(8,128)S(1)} %dynamic-slice_bitcast_fusion), channel_id=1, source_target_pairs={{0,28},{4,0},{8,4},{12,8},{16,12},{20,16},{24,20},{28,24},{1,29},{... | collective-permute-start | bytes 786440 | tf_op jit(solution)/shard_map/ppermute | solution.py:64
  26.1 5.9 %collective-permute-done = f32[512,128]{1,0:T(8,128)S(1)} collective-permute-done((f32[512,128]{1,0:T(8,128)S(1)}, f32[512,128]{1,0:T(8,128)S(1)}, u32[]{:S(2)}, u32[]{:S(2)}) %collective-permute-start) | collective-permute-done | bytes 262176 | tf_op jit(solution)/shard_map/ppermute | solution.py:63
  33.1 2.7 %collective-permute-start.8 = (f32[512,128]{1,0:T(8,128)S(1)}, f32[512,128]{1,0:T(8,128)S(1)}, u32[]{:S(2)}, u32[]{:S(2)}) collective-permute-start(f32[512,128]{1,0:T(8,128)S(1)} %bitcast_add_fusion.7), channel_id=1, source_target_pairs={{0,28},{4,0},{8,4},{12,8},{16,12},{20,16},{24,20},{28,24},{1,29},{... | collective-permute-start | bytes 786440 | tf_op jit(solution)/shard_map/ppermute | solution.py:64
  35.8 5.0 %collective-permute-done.1 = f32[512,128]{1,0:T(8,128)S(1)} collective-permute-done((f32[512,128]{1,0:T(8,128)S(1)}, f32[512,128]{1,0:T(8,128)S(1)}, u32[]{:S(2)}, u32[]{:S(2)}) %collective-permute-start.1) | collective-permute-done | bytes 262176 | tf_op jit(solution)/shard_map/ppermute | solution.py:63
  42.0 2.7 %collective-permute-start.9 = (f32[512,128]{1,0:T(8,128)S(1)}, f32[512,128]{1,0:T(8,128)S(1)}, u32[]{:S(2)}, u32[]{:S(2)}) collective-permute-start(f32[512,128]{1,0:T(8,128)S(1)} %bitcast_add_fusion.6), channel_id=1, source_target_pairs={{0,28},{4,0},{8,4},{12,8},{16,12},{20,16},{24,20},{28,24},{1,29},{... | collective-permute-start | bytes 786440 | tf_op jit(solution)/shard_map/ppermute | solution.py:64
  44.7 4.2 %collective-permute-done.2 = f32[512,128]{1,0:T(8,128)S(1)} collective-permute-done((f32[512,128]{1,0:T(8,128)S(1)}, f32[512,128]{1,0:T(8,128)S(1)}, u32[]{:S(2)}, u32[]{:S(2)}) %collective-permute-start.2) | collective-permute-done | bytes 262176 | tf_op jit(solution)/shard_map/ppermute | solution.py:63
  50.0 2.7 %collective-permute-start.10 = (f32[512,128]{1,0:T(8,128)S(1)}, f32[512,128]{1,0:T(8,128)S(1)}, u32[]{:S(2)}, u32[]{:S(2)}) collective-permute-start(f32[512,128]{1,0:T(8,128)S(1)} %bitcast_add_fusion.5), channel_id=1, source_target_pairs={{0,28},{4,0},{8,4},{12,8},{16,12},{20,16},{24,20},{28,24},{1,29},{... | collective-permute-start | bytes 786440 | tf_op jit(solution)/shard_map/ppermute | solution.py:64
  52.7 3.6 %collective-permute-done.3 = f32[512,128]{1,0:T(8,128)S(1)} collective-permute-done((f32[512,128]{1,0:T(8,128)S(1)}, f32[512,128]{1,0:T(8,128)S(1)}, u32[]{:S(2)}, u32[]{:S(2)}) %collective-permute-start.3) | collective-permute-done | bytes 262176 | tf_op jit(solution)/shard_map/ppermute | solution.py:63
  57.5 2.7 %collective-permute-start.11 = (f32[512,128]{1,0:T(8,128)S(1)}, f32[512,128]{1,0:T(8,128)S(1)}, u32[]{:S(2)}, u32[]{:S(2)}) collective-permute-start(f32[512,128]{1,0:T(8,128)S(1)} %bitcast_add_fusion.4), channel_id=1, source_target_pairs={{0,28},{4,0},{8,4},{12,8},{16,12},{20,16},{24,20},{28,24},{1,29},{... | collective-permute-start | bytes 786440 | tf_op jit(solution)/shard_map/ppermute | solution.py:64
  60.2 3.6 %collective-permute-done.4 = f32[512,128]{1,0:T(8,128)S(1)} collective-permute-done((f32[512,128]{1,0:T(8,128)S(1)}, f32[512,128]{1,0:T(8,128)S(1)}, u32[]{:S(2)}, u32[]{:S(2)}) %collective-permute-start.4) | collective-permute-done | bytes 262176 | tf_op jit(solution)/shard_map/ppermute | solution.py:63
  65.0 2.9 %collective-permute-start.12 = (f32[512,128]{1,0:T(8,128)S(1)}, f32[512,128]{1,0:T(8,128)S(1)}, u32[]{:S(2)}, u32[]{:S(2)}) collective-permute-start(f32[512,128]{1,0:T(8,128)S(1)} %bitcast_add_fusion.3), channel_id=1, source_target_pairs={{0,28},{4,0},{8,4},{12,8},{16,12},{20,16},{24,20},{28,24},{1,29},{... | collective-permute-start | bytes 786440 | tf_op jit(solution)/shard_map/ppermute | solution.py:64
  67.9 3.5 %collective-permute-done.5 = f32[512,128]{1,0:T(8,128)S(1)} collective-permute-done((f32[512,128]{1,0:T(8,128)S(1)}, f32[512,128]{1,0:T(8,128)S(1)}, u32[]{:S(2)}, u32[]{:S(2)}) %collective-permute-start.5) | collective-permute-done | bytes 262176 | tf_op jit(solution)/shard_map/ppermute | solution.py:63
  72.5 2.7 %collective-permute-start.13 = (f32[512,128]{1,0:T(8,128)S(1)}, f32[512,128]{1,0:T(8,128)S(1)}, u32[]{:S(2)}, u32[]{:S(2)}) collective-permute-start(f32[512,128]{1,0:T(8,128)S(1)} %bitcast_add_fusion.2), channel_id=1, source_target_pairs={{0,28},{4,0},{8,4},{12,8},{16,12},{20,16},{24,20},{28,24},{1,29},{... | collective-permute-start | bytes 786440 | tf_op jit(solution)/shard_map/ppermute | solution.py:64
  75.2 4.7 %collective-permute-done.6 = f32[512,128]{1,0:T(8,128)S(1)} collective-permute-done((f32[512,128]{1,0:T(8,128)S(1)}, f32[512,128]{1,0:T(8,128)S(1)}, u32[]{:S(2)}, u32[]{:S(2)}) %collective-permute-start.6) | collective-permute-done | bytes 262176 | tf_op jit(solution)/shard_map/ppermute | solution.py:63
  81.7 5.0 %all-to-all-start = ((f32[8,128,128]{2,1,0:T(8,128)}), f32[8,128,128]{2,1,0:T(8,128)S(1)}, u32[]{:S(2)}, u32[]{:S(2)}) async-start(f32[8,128,128]{2,1,0:T(8,128)} %bitcast.20), calls=%async_computation | async-start | bytes 1048576 | tf_op jit(solution)/shard_map/all_to_all | solution.py:107
  87.7 6.6 %all-to-all-done = f32[8,128,128]{2,1,0:T(8,128)S(1)} async-done(((f32[8,128,128]{2,1,0:T(8,128)}), f32[8,128,128]{2,1,0:T(8,128)S(1)}, u32[]{:S(2)}, u32[]{:S(2)}) %all-to-all-start) | async-done | bytes 524320 | tf_op jit(solution)/shard_map/all_to_all | solution.py:107
  94.5 14.4 %all_to_all.15 = bf16[8,128,128]{2,1,0:T(8,128)(2,1)S(1)} all-to-all(bf16[8,128,128]{2,1,0:T(8,128)(2,1)S(1)} %broadcast_in_dim.43), channel_id=1, replica_groups=mesh['ylo'=2,'x'=4,'z'=8,'yhi'=2,'core'=2] {'z'}, dimensions={0} | all-to-all | bytes 524288 | tf_op jit(solution)/shard_map/all_to_all | solution.py:114
  108.9 1.8 %broadcast_in_dim.44 = bf16[8,8,128,128]{3,2,1,0:T(8,128)(2,1)} broadcast(bf16[8,128,128]{2,1,0:T(8,128)(2,1)S(1)} %all_to_all.15), dimensions={1,2,3} | broadcast | bytes 2359296 | tf_op jit(solution)/shard_map/broadcast_in_dim | solution.py:115
  110.7 3.6 %all-to-all-start.2 = ((bf16[8,8,128,128]{3,2,1,0:T(8,128)(2,1)}), bf16[8,8,128,128]{3,2,1,0:T(8,128)(2,1)S(1)}, u32[]{:S(2)}, u32[]{:S(2)}) async-start(bf16[8,8,128,128]{3,2,1,0:T(8,128)(2,1)} %broadcast_in_dim.44), calls=%async_computation.2 | async-start | bytes 4194304 | tf_op jit(solution)/shard_map/all_to_all | solution.py:116
  114.4 16.2 %all-to-all-done.2 = bf16[8,8,128,128]{3,2,1,0:T(8,128)(2,1)S(1)} async-done(((bf16[8,8,128,128]{3,2,1,0:T(8,128)(2,1)}), bf16[8,8,128,128]{3,2,1,0:T(8,128)(2,1)S(1)}, u32[]{:S(2)}, u32[]{:S(2)}) %all-to-all-start.2) | async-done | bytes 2097184 | tf_op jit(solution)/shard_map/all_to_all | solution.py:116
  130.5 1.3 copy-done
  131.9 8.4 %shard_map.78 = f32[8,128,128]{2,1,0:T(8,128)} custom-call(s32[1152]{0:T(1024)} %get-tuple-element.15.index_ref, bf16[64,128,128]{2,1,0:T(8,128)(2,1)} %a_ref.1, bf16[64,128,128]{2,1,0:T(8,128)(2,1)} %bitcast.107), custom_call_target="tpu_custom_call" | custom-call | tf_op jit(solution)/shard_map/pallas_call | solution.py:36
  141.4 11.9 %collective-permute-start.14 = (f32[256,128]{1,0:T(8,128)S(1)}, f32[256,128]{1,0:T(8,128)S(1)}, u32[]{:S(2)}, u32[]{:S(2)}) collective-permute-start(f32[256,128]{1,0:T(8,128)S(1)} %dynamic-slice_bitcast_fusion.3), channel_id=1, source_target_pairs={{0,1},{1,0},{2,3},{3,2},{4,5},{5,4},{6,7},{7,6},{8,9},{9,8},{10,11... | collective-permute-start | bytes 393224 | tf_op jit(solution)/shard_map/ppermute | solution.py:63
  154.8 2.7 %collective-permute-start.16 = (f32[128,128]{1,0:T(8,128)S(1)}, f32[128,128]{1,0:T(8,128)S(1)}, u32[]{:S(2)}, u32[]{:S(2)}) collective-permute-start(f32[128,128]{1,0:T(8,128)S(1)} %dynamic-slice_bitcast_fusion.5), channel_id=1, source_target_pairs={{0,2},{2,0},{1,3},{3,1},{4,6},{6,4},{5,7},{7,5},{8,10},{10,8},{9,1... | collective-permute-start | bytes 196616 | tf_op jit(solution)/shard_map/ppermute | solution.py:63
  157.9 2.0 %collective-permute-done.16 = f32[128,128]{1,0:T(8,128)S(1)} collective-permute-done((f32[128,128]{1,0:T(8,128)S(1)}, f32[128,128]{1,0:T(8,128)S(1)}, u32[]{:S(2)}, u32[]{:S(2)}) %collective-permute-start.16) | collective-permute-done | bytes 65568 | tf_op jit(solution)/shard_map/ppermute | solution.py:63
  160.0 2.7 %collective-permute-start.18 = (f32[128,128]{1,0:T(8,128)S(1)}, f32[128,128]{1,0:T(8,128)S(1)}, u32[]{:S(2)}, u32[]{:S(2)}) collective-permute-start(f32[128,128]{1,0:T(8,128)S(1)} %bitcast_add_fusion.18), channel_id=1, source_target_pairs={{0,2},{2,0},{1,3},{3,1},{4,6},{6,4},{5,7},{7,5},{8,10},{10,8},{9,1... | collective-permute-start | bytes 196616 | tf_op jit(solution)/shard_map/ppermute | solution.py:80
  162.7 1.4 collective-permute-start.19
  164.7 2.7 %collective-permute-done.19 = f32[128,128]{1,0:T(8,128)S(1)} collective-permute-done((f32[128,128]{1,0:T(8,128)S(1)}, f32[128,128]{1,0:T(8,128)S(1)}, u32[]{:S(2)}, u32[]{:S(2)}) %collective-permute-start.19) | collective-permute-done | bytes 65568 | tf_op jit(solution)/shard_map/ppermute | solution.py:81
  167.4 3.1 %collective-permute-start.20 = (f32[256,128]{1,0:T(8,128)S(1)}, f32[256,128]{1,0:T(8,128)S(1)}, u32[]{:S(2)}, u32[]{:S(2)}) collective-permute-start(f32[256,128]{1,0:T(8,128)S(1)} %get-tuple-element.9), channel_id=1, source_target_pairs={{0,1},{1,0},{2,3},{3,2},{4,5},{5,4},{6,7},{7,6},{8,9},{9,8},{10,11... | collective-permute-start | bytes 393224 | tf_op jit(solution)/shard_map/ppermute | solution.py:80
  (78 shorter events, 21.8 us)
Async XLA Ops:
  19.5 12.5 %collective-permute-start = (f32[512,128]{1,0:T(8,128)S(1)}, f32[512,128]{1,0:T(8,128)S(1)}, u32[]{:S(2)}, u32[]{:S(2)}) collective-permute-start(f32[512,128]{1,0:T(8,128)S(1)} %dynamic-slice_bitcast_fusion.1), channel_id=1, source_target_pairs={{0,4},{4,8},{8,12},{12,16},{16,20},{20,24},{24,28},{28,0},{1,5},{5... | collective-permute-start | bytes 786440 | tf_op jit(solution)/shard_map/ppermute | solution.py:63
  22.0 11.0 %collective-permute-start.7 = (f32[512,128]{1,0:T(8,128)S(1)}, f32[512,128]{1,0:T(8,128)S(1)}, u32[]{:S(2)}, u32[]{:S(2)}) collective-permute-start(f32[512,128]{1,0:T(8,128)S(1)} %dynamic-slice_bitcast_fusion), channel_id=1, source_target_pairs={{0,28},{4,0},{8,4},{12,8},{16,12},{20,16},{24,20},{28,24},{1,29},{... | collective-permute-start | bytes 786440 | tf_op jit(solution)/shard_map/ppermute | solution.py:64
  32.9 7.9 %collective-permute-start.1 = (f32[512,128]{1,0:T(8,128)S(1)}, f32[512,128]{1,0:T(8,128)S(1)}, u32[]{:S(2)}, u32[]{:S(2)}) collective-permute-start(f32[512,128]{1,0:T(8,128)S(1)} %bitcast_add_fusion.14), channel_id=1, source_target_pairs={{0,4},{4,8},{8,12},{12,16},{16,20},{20,24},{24,28},{28,0},{1,5},{5... | collective-permute-start | bytes 786440 | tf_op jit(solution)/shard_map/ppermute | solution.py:63
  33.1 8.8 %collective-permute-start.8 = (f32[512,128]{1,0:T(8,128)S(1)}, f32[512,128]{1,0:T(8,128)S(1)}, u32[]{:S(2)}, u32[]{:S(2)}) collective-permute-start(f32[512,128]{1,0:T(8,128)S(1)} %bitcast_add_fusion.7), channel_id=1, source_target_pairs={{0,28},{4,0},{8,4},{12,8},{16,12},{20,16},{24,20},{28,24},{1,29},{... | collective-permute-start | bytes 786440 | tf_op jit(solution)/shard_map/ppermute | solution.py:64
  41.8 7.0 %collective-permute-start.2 = (f32[512,128]{1,0:T(8,128)S(1)}, f32[512,128]{1,0:T(8,128)S(1)}, u32[]{:S(2)}, u32[]{:S(2)}) collective-permute-start(f32[512,128]{1,0:T(8,128)S(1)} %bitcast_add_fusion.13), channel_id=1, source_target_pairs={{0,4},{4,8},{8,12},{12,16},{16,20},{20,24},{24,28},{28,0},{1,5},{5... | collective-permute-start | bytes 786440 | tf_op jit(solution)/shard_map/ppermute | solution.py:63
  42.0 8.0 %collective-permute-start.9 = (f32[512,128]{1,0:T(8,128)S(1)}, f32[512,128]{1,0:T(8,128)S(1)}, u32[]{:S(2)}, u32[]{:S(2)}) collective-permute-start(f32[512,128]{1,0:T(8,128)S(1)} %bitcast_add_fusion.6), channel_id=1, source_target_pairs={{0,28},{4,0},{8,4},{12,8},{16,12},{20,16},{24,20},{28,24},{1,29},{... | collective-permute-start | bytes 786440 | tf_op jit(solution)/shard_map/ppermute | solution.py:64
  49.9 6.5 %collective-permute-start.3 = (f32[512,128]{1,0:T(8,128)S(1)}, f32[512,128]{1,0:T(8,128)S(1)}, u32[]{:S(2)}, u32[]{:S(2)}) collective-permute-start(f32[512,128]{1,0:T(8,128)S(1)} %bitcast_add_fusion.12), channel_id=1, source_target_pairs={{0,4},{4,8},{8,12},{12,16},{16,20},{20,24},{24,28},{28,0},{1,5},{5... | collective-permute-start | bytes 786440 | tf_op jit(solution)/shard_map/ppermute | solution.py:63
  50.0 7.4 %collective-permute-start.10 = (f32[512,128]{1,0:T(8,128)S(1)}, f32[512,128]{1,0:T(8,128)S(1)}, u32[]{:S(2)}, u32[]{:S(2)}) collective-permute-start(f32[512,128]{1,0:T(8,128)S(1)} %bitcast_add_fusion.5), channel_id=1, source_target_pairs={{0,28},{4,0},{8,4},{12,8},{16,12},{20,16},{24,20},{28,24},{1,29},{... | collective-permute-start | bytes 786440 | tf_op jit(solution)/shard_map/ppermute | solution.py:64
  57.3 6.5 %collective-permute-start.4 = (f32[512,128]{1,0:T(8,128)S(1)}, f32[512,128]{1,0:T(8,128)S(1)}, u32[]{:S(2)}, u32[]{:S(2)}) collective-permute-start(f32[512,128]{1,0:T(8,128)S(1)} %bitcast_add_fusion.11), channel_id=1, source_target_pairs={{0,4},{4,8},{8,12},{12,16},{16,20},{20,24},{24,28},{28,0},{1,5},{5... | collective-permute-start | bytes 786440 | tf_op jit(solution)/shard_map/ppermute | solution.py:63
  57.5 7.4 %collective-permute-start.11 = (f32[512,128]{1,0:T(8,128)S(1)}, f32[512,128]{1,0:T(8,128)S(1)}, u32[]{:S(2)}, u32[]{:S(2)}) collective-permute-start(f32[512,128]{1,0:T(8,128)S(1)} %bitcast_add_fusion.4), channel_id=1, source_target_pairs={{0,28},{4,0},{8,4},{12,8},{16,12},{20,16},{24,20},{28,24},{1,29},{... | collective-permute-start | bytes 786440 | tf_op jit(solution)/shard_map/ppermute | solution.py:64
  64.8 6.5 %collective-permute-start.5 = (f32[512,128]{1,0:T(8,128)S(1)}, f32[512,128]{1,0:T(8,128)S(1)}, u32[]{:S(2)}, u32[]{:S(2)}) collective-permute-start(f32[512,128]{1,0:T(8,128)S(1)} %bitcast_add_fusion.10), channel_id=1, source_target_pairs={{0,4},{4,8},{8,12},{12,16},{16,20},{20,24},{24,28},{28,0},{1,5},{5... | collective-permute-start | bytes 786440 | tf_op jit(solution)/shard_map/ppermute | solution.py:63
  65.0 7.4 %collective-permute-start.12 = (f32[512,128]{1,0:T(8,128)S(1)}, f32[512,128]{1,0:T(8,128)S(1)}, u32[]{:S(2)}, u32[]{:S(2)}) collective-permute-start(f32[512,128]{1,0:T(8,128)S(1)} %bitcast_add_fusion.3), channel_id=1, source_target_pairs={{0,28},{4,0},{8,4},{12,8},{16,12},{20,16},{24,20},{28,24},{1,29},{... | collective-permute-start | bytes 786440 | tf_op jit(solution)/shard_map/ppermute | solution.py:64
  72.3 7.5 %collective-permute-start.6 = (f32[512,128]{1,0:T(8,128)S(1)}, f32[512,128]{1,0:T(8,128)S(1)}, u32[]{:S(2)}, u32[]{:S(2)}) collective-permute-start(f32[512,128]{1,0:T(8,128)S(1)} %bitcast_add_fusion.9), channel_id=1, source_target_pairs={{0,4},{4,8},{8,12},{12,16},{16,20},{20,24},{24,28},{28,0},{1,5},{5... | collective-permute-start | bytes 786440 | tf_op jit(solution)/shard_map/ppermute | solution.py:63
  72.5 8.4 %collective-permute-start.13 = (f32[512,128]{1,0:T(8,128)S(1)}, f32[512,128]{1,0:T(8,128)S(1)}, u32[]{:S(2)}, u32[]{:S(2)}) collective-permute-start(f32[512,128]{1,0:T(8,128)S(1)} %bitcast_add_fusion.2), channel_id=1, source_target_pairs={{0,28},{4,0},{8,4},{12,8},{16,12},{20,16},{24,20},{28,24},{1,29},{... | collective-permute-start | bytes 786440 | tf_op jit(solution)/shard_map/ppermute | solution.py:64
  81.7 12.5 %all-to-all-start = ((f32[8,128,128]{2,1,0:T(8,128)}), f32[8,128,128]{2,1,0:T(8,128)S(1)}, u32[]{:S(2)}, u32[]{:S(2)}) async-start(f32[8,128,128]{2,1,0:T(8,128)} %bitcast.20), calls=%async_computation | async-start | bytes 1048576 | tf_op jit(solution)/shard_map/all_to_all | solution.py:107
  110.7 19.8 %all-to-all-start.2 = ((bf16[8,8,128,128]{3,2,1,0:T(8,128)(2,1)}), bf16[8,8,128,128]{3,2,1,0:T(8,128)(2,1)S(1)}, u32[]{:S(2)}, u32[]{:S(2)}) async-start(bf16[8,8,128,128]{3,2,1,0:T(8,128)(2,1)} %broadcast_in_dim.44), calls=%async_computation.2 | async-start | bytes 4194304 | tf_op jit(solution)/shard_map/all_to_all | solution.py:116
  130.5 1.3 copy-start
  141.4 12.9 %collective-permute-start.14 = (f32[256,128]{1,0:T(8,128)S(1)}, f32[256,128]{1,0:T(8,128)S(1)}, u32[]{:S(2)}, u32[]{:S(2)}) collective-permute-start(f32[256,128]{1,0:T(8,128)S(1)} %dynamic-slice_bitcast_fusion.3), channel_id=1, source_target_pairs={{0,1},{1,0},{2,3},{3,2},{4,5},{5,4},{6,7},{7,6},{8,9},{9,8},{10,11... | collective-permute-start | bytes 393224 | tf_op jit(solution)/shard_map/ppermute | solution.py:63
  153.3 1.4 collective-permute-start.15
  154.8 5.1 %collective-permute-start.16 = (f32[128,128]{1,0:T(8,128)S(1)}, f32[128,128]{1,0:T(8,128)S(1)}, u32[]{:S(2)}, u32[]{:S(2)}) collective-permute-start(f32[128,128]{1,0:T(8,128)S(1)} %dynamic-slice_bitcast_fusion.5), channel_id=1, source_target_pairs={{0,2},{2,0},{1,3},{3,1},{4,6},{6,4},{5,7},{7,5},{8,10},{10,8},{9,1... | collective-permute-start | bytes 196616 | tf_op jit(solution)/shard_map/ppermute | solution.py:63
  157.6 5.1 %collective-permute-start.17 = (f32[128,128]{1,0:T(8,128)S(1)}, f32[128,128]{1,0:T(8,128)S(1)}, u32[]{:S(2)}, u32[]{:S(2)}) collective-permute-start(f32[128,128]{1,0:T(8,128)S(1)} %dynamic-slice_bitcast_fusion.4), channel_id=1, source_target_pairs={{0,2},{2,0},{1,3},{3,1},{4,6},{6,4},{5,7},{7,5},{8,10},{10,8},{9,1... | collective-permute-start | bytes 196616 | tf_op jit(solution)/shard_map/ppermute | solution.py:64
  160.0 12.8 %copy-start.1 = (f32[1024,128]{1,0:T(8,128)S(1)}, f32[1024,128]{1,0:T(8,128)}, u32[]{:S(2)}) copy-start(f32[1024,128]{1,0:T(8,128)} %param.6) | copy-start | bytes 1572868
  160.0 4.7 %collective-permute-start.18 = (f32[128,128]{1,0:T(8,128)S(1)}, f32[128,128]{1,0:T(8,128)S(1)}, u32[]{:S(2)}, u32[]{:S(2)}) collective-permute-start(f32[128,128]{1,0:T(8,128)S(1)} %bitcast_add_fusion.18), channel_id=1, source_target_pairs={{0,2},{2,0},{1,3},{3,1},{4,6},{6,4},{5,7},{7,5},{8,10},{10,8},{9,1... | collective-permute-start | bytes 196616 | tf_op jit(solution)/shard_map/ppermute | solution.py:80
  162.7 4.7 %collective-permute-start.19 = (f32[128,128]{1,0:T(8,128)S(1)}, f32[128,128]{1,0:T(8,128)S(1)}, u32[]{:S(2)}, u32[]{:S(2)}) collective-permute-start(f32[128,128]{1,0:T(8,128)S(1)} %bitcast_add_fusion.17), channel_id=1, source_target_pairs={{0,2},{2,0},{1,3},{3,1},{4,6},{6,4},{5,7},{7,5},{8,10},{10,8},{9,1... | collective-permute-start | bytes 196616 | tf_op jit(solution)/shard_map/ppermute | solution.py:81
  167.4 4.1 %collective-permute-start.20 = (f32[256,128]{1,0:T(8,128)S(1)}, f32[256,128]{1,0:T(8,128)S(1)}, u32[]{:S(2)}, u32[]{:S(2)}) collective-permute-start(f32[256,128]{1,0:T(8,128)S(1)} %get-tuple-element.9), channel_id=1, source_target_pairs={{0,1},{1,0},{2,3},{3,2},{4,5},{5,4},{6,7},{7,6},{8,9},{9,8},{10,11... | collective-permute-start | bytes 393224 | tf_op jit(solution)/shard_map/ppermute | solution.py:80
  171.3 1.3 collective-permute-start.21

commit v12 on v10

--- a/solution.py
+++ b/solution.py
@@ -120,8 +120,7 @@
     user_part = block_sums(user_index, weight_tiles, item_tiles, n_user_tiles)
     y = user_part.reshape(n_core, -1, width)
     y = ring_reduce_scatter(y, "core", n_core)
-    y = ring_reduce_scatter(y.reshape(n_yhi, -1, width), "yhi", n_yhi)
-    y = ring_all_gather(y, "yhi", n_yhi).reshape(-1, width)
+    y = y + lax.ppermute(y, "yhi", [(j, (j + 1) % n_yhi) for j in range(n_yhi)])
     y = ring_all_gather(y, "core", n_core).reshape(-1, width)
     user_out = (1.0 - teleport) * y + teleport * user_emb0
     return (user_out, own_emb[None])

time: 175 us -> 170 us (0.971)
  starting transfers between devices: 54.7 us -> 48.1 us
    ppermute x0 -> x1, waiting for transfers between devices: none -> 6.6 us  [per_device(): y = y + lax.ppermute(y, 'yhi', [(j, (j + 1) % n_yhi) for j in range(n_yhi)])]
    ppermute x2 -> x1, starting transfers between devices: 5.82 us -> 1.09 us  [ring_all_gather(): bl = lax.ppermute(bl, axis, right)]
    ppermute x0 -> x1, starting transfers between devices: none -> 2.71 us  [per_device(): y = y + lax.ppermute(y, 'yhi', [(j, (j + 1) % n_yhi) for j in range(n_yhi)])]
    ppermute x2 -> x1, waiting for transfers between devices: 3.78 us -> 1.08 us  [ring_all_gather(): br = lax.ppermute(br, axis, left)]
    ppermute x9 -> x8, starting transfers between devices: 17.9 us -> 15.2 us  [ring_reduce_scatter_halves(): rl = lax.ppermute(bl, axis, right)]
    ppermute x9 -> x8, waiting for transfers between devices: 33.3 us -> 31.3 us  [ring_reduce_scatter_halves(): rl = lax.ppermute(bl, axis, right)]
    ppermute x9 -> x8, starting transfers between devices: 21 us -> 20.6 us  [ring_reduce_scatter_halves(): rr = lax.ppermute(br, axis, left)]
    add x9 -> x8, other arithmetic: 6.87 us -> 6.86 us  [ring_reduce_scatter_halves(): bl = rl + lax.dynamic_index_in_dim(xl, (i - s - 2) % n, 0, keepdims=False)]
  transfers between devices with their start and end apart: 24 -> 21, of which waited for: 16 -> 14; matrix products, arithmetic and copies ran while one was open for 5% -> 5% of each run, Pallas kernels for 0% -> 0%
where the time goes in v12:
time: 170 us; the launch traced here: 169 us
  waiting for transfers between devices  62.5 us (37%)
  starting transfers between devices  48.1 us (28%)
  Pallas kernels  18.3 us (11%)
  blocking collectives  14.4 us (8%)
  other arithmetic  12.7 us (7%)
  local copies, waits for them, and re-layouts  12.1 us (7%)
    ppermute x8, waiting for transfers between devices, ring_reduce_scatter_halves(): rl = lax.ppermute(bl, axis, right)  31.3 us
    ppermute x8, starting transfers between devices, ring_reduce_scatter_halves(): rr = lax.ppermute(br, axis, left)  20.6 us
    pallas_call x2, Pallas kernels, block_sums(): pl.pallas_call(functools.partial(block_sum_kernel, b_transposed=b_transpo...  18.3 us
    all_to_all x1, waiting for transfers between devices, per_device(): t = lax.all_to_all(t, ('ylo', 'x'), 0, 0, tiled=True)  16.2 us
    ppermute x8, starting transfers between devices, ring_reduce_scatter_halves(): rl = lax.ppermute(bl, axis, right)  15.2 us
    all_to_all x1, blocking collectives, per_device(): lax.all_to_all(jnp.broadcast_to(own_bf[None], (n_z, tile_rows, width)), '...  14.4 us
    add x8, other arithmetic, ring_reduce_scatter_halves(): bl = rl + lax.dynamic_index_in_dim(xl, (i - s - 2) % n, 0, keepdims=False)  6.86 us
    all_to_all x1, waiting for transfers between devices, per_device(): x = lax.all_to_all(x, ('ylo', 'x'), 0, 0, tiled=True)  6.6 us
  transfers between devices with their start and end apart: 21, of which 14 were waited for; matrix products, arithmetic and copies ran while one was open for 5% of the time, Pallas kernels for 0%

profile of v12, /device:TPU:1, one launch (start us, length us, event | category | flops | bytes accessed | tf_op | source)
XLA Modules:
  0.0 169.2 jit_solution(5153095868605702235)
XLA Ops:
  2.8 1.1 convert_element_type.6
  5.3 9.6 %shard_map.77 = f32[64,128,128]{2,1,0:T(8,128)} custom-call(s32[1152]{0:T(1024)} %get-tuple-element.14.index_ref, bf16[8,128,128]{2,1,0:T(8,128)(2,1)} %bitcast.87, bf16[64,128,128]{2,1,0:T(8,128)(2,1)} %a_ref.1), custom_call_target="tpu_custom_call" | custom-call | tf_op jit(solution)/shard_map/pallas_call | solution.py:36
  14.9 4.1 %fusion.11 = (f32[32,128,128]{2,1,0:T(8,128)}, f32[32,128,128]{2,1,0:T(8,128)S(1)}) fusion(f32[64,128,128]{2,1,0:T(8,128)} %shard_map.77), kind=kLoop, calls=%fused_computation.53 | loop fusion | bytes 8388608 | tf_op jit(solution)/shard_map/slice | solution.py:105
  19.9 2.5 %collective-permute-start = (f32[512,128]{1,0:T(8,128)S(1)}, f32[512,128]{1,0:T(8,128)S(1)}, u32[]{:S(2)}, u32[]{:S(2)}) collective-permute-start(f32[512,128]{1,0:T(8,128)S(1)} %dynamic-slice_bitcast_fusion.1), channel_id=1, source_target_pairs={{0,4},{4,8},{8,12},{12,16},{16,20},{20,24},{24,28},{28,0},{1,5},{5... | collective-permute-start | bytes 786440 | tf_op jit(solution)/shard_map/ppermute | solution.py:63
  22.5 4.1 %collective-permute-start.7 = (f32[512,128]{1,0:T(8,128)S(1)}, f32[512,128]{1,0:T(8,128)S(1)}, u32[]{:S(2)}, u32[]{:S(2)}) collective-permute-start(f32[512,128]{1,0:T(8,128)S(1)} %dynamic-slice_bitcast_fusion), channel_id=1, source_target_pairs={{0,28},{4,0},{8,4},{12,8},{16,12},{20,16},{24,20},{28,24},{1,29},{... | collective-permute-start | bytes 786440 | tf_op jit(solution)/shard_map/ppermute | solution.py:64
  26.6 5.9 %collective-permute-done = f32[512,128]{1,0:T(8,128)S(1)} collective-permute-done((f32[512,128]{1,0:T(8,128)S(1)}, f32[512,128]{1,0:T(8,128)S(1)}, u32[]{:S(2)}, u32[]{:S(2)}) %collective-permute-start) | collective-permute-done | bytes 262176 | tf_op jit(solution)/shard_map/ppermute | solution.py:63
  33.6 2.7 %collective-permute-start.8 = (f32[512,128]{1,0:T(8,128)S(1)}, f32[512,128]{1,0:T(8,128)S(1)}, u32[]{:S(2)}, u32[]{:S(2)}) collective-permute-start(f32[512,128]{1,0:T(8,128)S(1)} %bitcast_add_fusion.7), channel_id=1, source_target_pairs={{0,28},{4,0},{8,4},{12,8},{16,12},{20,16},{24,20},{28,24},{1,29},{... | collective-permute-start | bytes 786440 | tf_op jit(solution)/shard_map/ppermute | solution.py:64
  36.3 5.0 %collective-permute-done.1 = f32[512,128]{1,0:T(8,128)S(1)} collective-permute-done((f32[512,128]{1,0:T(8,128)S(1)}, f32[512,128]{1,0:T(8,128)S(1)}, u32[]{:S(2)}, u32[]{:S(2)}) %collective-permute-start.1) | collective-permute-done | bytes 262176 | tf_op jit(solution)/shard_map/ppermute | solution.py:63
  42.4 2.7 %collective-permute-start.9 = (f32[512,128]{1,0:T(8,128)S(1)}, f32[512,128]{1,0:T(8,128)S(1)}, u32[]{:S(2)}, u32[]{:S(2)}) collective-permute-start(f32[512,128]{1,0:T(8,128)S(1)} %bitcast_add_fusion.6), channel_id=1, source_target_pairs={{0,28},{4,0},{8,4},{12,8},{16,12},{20,16},{24,20},{28,24},{1,29},{... | collective-permute-start | bytes 786440 | tf_op jit(solution)/shard_map/ppermute | solution.py:64
  45.2 4.2 %collective-permute-done.2 = f32[512,128]{1,0:T(8,128)S(1)} collective-permute-done((f32[512,128]{1,0:T(8,128)S(1)}, f32[512,128]{1,0:T(8,128)S(1)}, u32[]{:S(2)}, u32[]{:S(2)}) %collective-permute-start.2) | collective-permute-done | bytes 262176 | tf_op jit(solution)/shard_map/ppermute | solution.py:63
  50.5 2.7 %collective-permute-start.10 = (f32[512,128]{1,0:T(8,128)S(1)}, f32[512,128]{1,0:T(8,128)S(1)}, u32[]{:S(2)}, u32[]{:S(2)}) collective-permute-start(f32[512,128]{1,0:T(8,128)S(1)} %bitcast_add_fusion.5), channel_id=1, source_target_pairs={{0,28},{4,0},{8,4},{12,8},{16,12},{20,16},{24,20},{28,24},{1,29},{... | collective-permute-start | bytes 786440 | tf_op jit(solution)/shard_map/ppermute | solution.py:64
  53.2 3.6 %collective-permute-done.3 = f32[512,128]{1,0:T(8,128)S(1)} collective-permute-done((f32[512,128]{1,0:T(8,128)S(1)}, f32[512,128]{1,0:T(8,128)S(1)}, u32[]{:S(2)}, u32[]{:S(2)}) %collective-permute-start.3) | collective-permute-done | bytes 262176 | tf_op jit(solution)/shard_map/ppermute | solution.py:63
  58.0 2.7 %collective-permute-start.11 = (f32[512,128]{1,0:T(8,128)S(1)}, f32[512,128]{1,0:T(8,128)S(1)}, u32[]{:S(2)}, u32[]{:S(2)}) collective-permute-start(f32[512,128]{1,0:T(8,128)S(1)} %bitcast_add_fusion.4), channel_id=1, source_target_pairs={{0,28},{4,0},{8,4},{12,8},{16,12},{20,16},{24,20},{28,24},{1,29},{... | collective-permute-start | bytes 786440 | tf_op jit(solution)/shard_map/ppermute | solution.py:64
  60.7 3.6 %collective-permute-done.4 = f32[512,128]{1,0:T(8,128)S(1)} collective-permute-done((f32[512,128]{1,0:T(8,128)S(1)}, f32[512,128]{1,0:T(8,128)S(1)}, u32[]{:S(2)}, u32[]{:S(2)}) %collective-permute-start.4) | collective-permute-done | bytes 262176 | tf_op jit(solution)/shard_map/ppermute | solution.py:63
  65.5 2.7 %collective-permute-start.12 = (f32[512,128]{1,0:T(8,128)S(1)}, f32[512,128]{1,0:T(8,128)S(1)}, u32[]{:S(2)}, u32[]{:S(2)}) collective-permute-start(f32[512,128]{1,0:T(8,128)S(1)} %bitcast_add_fusion.3), channel_id=1, source_target_pairs={{0,28},{4,0},{8,4},{12,8},{16,12},{20,16},{24,20},{28,24},{1,29},{... | collective-permute-start | bytes 786440 | tf_op jit(solution)/shard_map/ppermute | solution.py:64
  68.2 3.6 %collective-permute-done.5 = f32[512,128]{1,0:T(8,128)S(1)} collective-permute-done((f32[512,128]{1,0:T(8,128)S(1)}, f32[512,128]{1,0:T(8,128)S(1)}, u32[]{:S(2)}, u32[]{:S(2)}) %collective-permute-start.5) | collective-permute-done | bytes 262176 | tf_op jit(solution)/shard_map/ppermute | solution.py:63
  73.1 2.7 %collective-permute-start.13 = (f32[512,128]{1,0:T(8,128)S(1)}, f32[512,128]{1,0:T(8,128)S(1)}, u32[]{:S(2)}, u32[]{:S(2)}) collective-permute-start(f32[512,128]{1,0:T(8,128)S(1)} %bitcast_add_fusion.2), channel_id=1, source_target_pairs={{0,28},{4,0},{8,4},{12,8},{16,12},{20,16},{24,20},{28,24},{1,29},{... | collective-permute-start | bytes 786440 | tf_op jit(solution)/shard_map/ppermute | solution.py:64
  75.8 4.5 %collective-permute-done.6 = f32[512,128]{1,0:T(8,128)S(1)} collective-permute-done((f32[512,128]{1,0:T(8,128)S(1)}, f32[512,128]{1,0:T(8,128)S(1)}, u32[]{:S(2)}, u32[]{:S(2)}) %collective-permute-start.6) | collective-permute-done | bytes 262176 | tf_op jit(solution)/shard_map/ppermute | solution.py:63
  82.2 5.0 %all-to-all-start = ((f32[8,128,128]{2,1,0:T(8,128)}), f32[8,128,128]{2,1,0:T(8,128)S(1)}, u32[]{:S(2)}, u32[]{:S(2)}) async-start(f32[8,128,128]{2,1,0:T(8,128)} %bitcast.20), calls=%async_computation | async-start | bytes 1048576 | tf_op jit(solution)/shard_map/all_to_all | solution.py:107
  88.2 6.6 %all-to-all-done = f32[8,128,128]{2,1,0:T(8,128)S(1)} async-done(((f32[8,128,128]{2,1,0:T(8,128)}), f32[8,128,128]{2,1,0:T(8,128)S(1)}, u32[]{:S(2)}, u32[]{:S(2)}) %all-to-all-start) | async-done | bytes 524320 | tf_op jit(solution)/shard_map/all_to_all | solution.py:107
  95.0 14.4 %all_to_all.15 = bf16[8,128,128]{2,1,0:T(8,128)(2,1)S(1)} all-to-all(bf16[8,128,128]{2,1,0:T(8,128)(2,1)S(1)} %broadcast_in_dim.29), channel_id=1, replica_groups=mesh['ylo'=2,'x'=4,'z'=8,'yhi'=2,'core'=2] {'z'}, dimensions={0} | all-to-all | bytes 524288 | tf_op jit(solution)/shard_map/all_to_all | solution.py:114
  109.4 1.8 %broadcast_in_dim.30 = bf16[8,8,128,128]{3,2,1,0:T(8,128)(2,1)} broadcast(bf16[8,128,128]{2,1,0:T(8,128)(2,1)S(1)} %all_to_all.15), dimensions={1,2,3} | broadcast | bytes 2359296 | tf_op jit(solution)/shard_map/broadcast_in_dim | solution.py:115
  111.2 3.6 %all-to-all-start.2 = ((bf16[8,8,128,128]{3,2,1,0:T(8,128)(2,1)}), bf16[8,8,128,128]{3,2,1,0:T(8,128)(2,1)S(1)}, u32[]{:S(2)}, u32[]{:S(2)}) async-start(bf16[8,8,128,128]{3,2,1,0:T(8,128)(2,1)} %broadcast_in_dim.30), calls=%async_computation.2 | async-start | bytes 4194304 | tf_op jit(solution)/shard_map/all_to_all | solution.py:116
  114.8 16.2 %all-to-all-done.2 = bf16[8,8,128,128]{3,2,1,0:T(8,128)(2,1)S(1)} async-done(((bf16[8,8,128,128]{3,2,1,0:T(8,128)(2,1)}), bf16[8,8,128,128]{3,2,1,0:T(8,128)(2,1)S(1)}, u32[]{:S(2)}, u32[]{:S(2)}) %all-to-all-start.2) | async-done | bytes 2097184 | tf_op jit(solution)/shard_map/all_to_all | solution.py:116
  131.0 1.3 copy-done
  132.4 8.7 %shard_map.78 = f32[8,128,128]{2,1,0:T(8,128)} custom-call(s32[1152]{0:T(1024)} %get-tuple-element.15.index_ref, bf16[64,128,128]{2,1,0:T(8,128)(2,1)} %a_ref.1, bf16[64,128,128]{2,1,0:T(8,128)(2,1)} %bitcast.85), custom_call_target="tpu_custom_call" | custom-call | tf_op jit(solution)/shard_map/pallas_call | solution.py:36
  141.1 1.1 fusion.12
  142.2 11.9 %collective-permute-start.14 = (f32[256,128]{1,0:T(8,128)S(1)}, f32[256,128]{1,0:T(8,128)S(1)}, u32[]{:S(2)}, u32[]{:S(2)}) collective-permute-start(f32[256,128]{1,0:T(8,128)S(1)} %dynamic-slice_bitcast_fusion.3), channel_id=1, source_target_pairs={{0,1},{1,0},{2,3},{3,2},{4,5},{5,4},{6,7},{7,6},{8,9},{9,8},{10,11... | collective-permute-start | bytes 393224 | tf_op jit(solution)/shard_map/ppermute | solution.py:63
  155.6 2.7 %collective-permute-start.16 = (f32[512,128]{1,0:T(8,128)S(1)}, f32[512,128]{1,0:T(8,128)S(1)}, u32[]{:S(2)}, u32[]{:S(2)}) collective-permute-start(f32[512,128]{1,0:T(8,128)S(1)} %pad_maximum_fusion.1), channel_id=1, source_target_pairs={{0,2},{2,0},{1,3},{3,1},{4,6},{6,4},{5,7},{7,5},{8,10},{10,8},{9,1... | collective-permute-start | bytes 786440 | tf_op jit(solution)/shard_map/ppermute | solution.py:123
  158.3 6.6 %collective-permute-done.16 = f32[512,128]{1,0:T(8,128)S(1)} collective-permute-done((f32[512,128]{1,0:T(8,128)S(1)}, f32[512,128]{1,0:T(8,128)S(1)}, u32[]{:S(2)}, u32[]{:S(2)}) %collective-permute-start.16) | collective-permute-done | bytes 262176 | tf_op jit(solution)/shard_map/ppermute | solution.py:123
  165.1 1.1 collective-permute-start.17
  167.1 1.1 collective-permute-done.18
  (63 shorter events, 17.8 us)
Async XLA Ops:
  19.9 12.5 %collective-permute-start = (f32[512,128]{1,0:T(8,128)S(1)}, f32[512,128]{1,0:T(8,128)S(1)}, u32[]{:S(2)}, u32[]{:S(2)}) collective-permute-start(f32[512,128]{1,0:T(8,128)S(1)} %dynamic-slice_bitcast_fusion.1), channel_id=1, source_target_pairs={{0,4},{4,8},{8,12},{12,16},{16,20},{20,24},{24,28},{28,0},{1,5},{5... | collective-permute-start | bytes 786440 | tf_op jit(solution)/shard_map/ppermute | solution.py:63
  22.5 11.0 %collective-permute-start.7 = (f32[512,128]{1,0:T(8,128)S(1)}, f32[512,128]{1,0:T(8,128)S(1)}, u32[]{:S(2)}, u32[]{:S(2)}) collective-permute-start(f32[512,128]{1,0:T(8,128)S(1)} %dynamic-slice_bitcast_fusion), channel_id=1, source_target_pairs={{0,28},{4,0},{8,4},{12,8},{16,12},{20,16},{24,20},{28,24},{1,29},{... | collective-permute-start | bytes 786440 | tf_op jit(solution)/shard_map/ppermute | solution.py:64
  33.4 7.9 %collective-permute-start.1 = (f32[512,128]{1,0:T(8,128)S(1)}, f32[512,128]{1,0:T(8,128)S(1)}, u32[]{:S(2)}, u32[]{:S(2)}) collective-permute-start(f32[512,128]{1,0:T(8,128)S(1)} %bitcast_add_fusion.14), channel_id=1, source_target_pairs={{0,4},{4,8},{8,12},{12,16},{16,20},{20,24},{24,28},{28,0},{1,5},{5... | collective-permute-start | bytes 786440 | tf_op jit(solution)/shard_map/ppermute | solution.py:63
  33.6 8.8 %collective-permute-start.8 = (f32[512,128]{1,0:T(8,128)S(1)}, f32[512,128]{1,0:T(8,128)S(1)}, u32[]{:S(2)}, u32[]{:S(2)}) collective-permute-start(f32[512,128]{1,0:T(8,128)S(1)} %bitcast_add_fusion.7), channel_id=1, source_target_pairs={{0,28},{4,0},{8,4},{12,8},{16,12},{20,16},{24,20},{28,24},{1,29},{... | collective-permute-start | bytes 786440 | tf_op jit(solution)/shard_map/ppermute | solution.py:64
  42.3 7.0 %collective-permute-start.2 = (f32[512,128]{1,0:T(8,128)S(1)}, f32[512,128]{1,0:T(8,128)S(1)}, u32[]{:S(2)}, u32[]{:S(2)}) collective-permute-start(f32[512,128]{1,0:T(8,128)S(1)} %bitcast_add_fusion.13), channel_id=1, source_target_pairs={{0,4},{4,8},{8,12},{12,16},{16,20},{20,24},{24,28},{28,0},{1,5},{5... | collective-permute-start | bytes 786440 | tf_op jit(solution)/shard_map/ppermute | solution.py:63
  42.4 8.0 %collective-permute-start.9 = (f32[512,128]{1,0:T(8,128)S(1)}, f32[512,128]{1,0:T(8,128)S(1)}, u32[]{:S(2)}, u32[]{:S(2)}) collective-permute-start(f32[512,128]{1,0:T(8,128)S(1)} %bitcast_add_fusion.6), channel_id=1, source_target_pairs={{0,28},{4,0},{8,4},{12,8},{16,12},{20,16},{24,20},{28,24},{1,29},{... | collective-permute-start | bytes 786440 | tf_op jit(solution)/shard_map/ppermute | solution.py:64
  50.3 6.5 %collective-permute-start.3 = (f32[512,128]{1,0:T(8,128)S(1)}, f32[512,128]{1,0:T(8,128)S(1)}, u32[]{:S(2)}, u32[]{:S(2)}) collective-permute-start(f32[512,128]{1,0:T(8,128)S(1)} %bitcast_add_fusion.12), channel_id=1, source_target_pairs={{0,4},{4,8},{8,12},{12,16},{16,20},{20,24},{24,28},{28,0},{1,5},{5... | collective-permute-start | bytes 786440 | tf_op jit(solution)/shard_map/ppermute | solution.py:63
  50.5 7.4 %collective-permute-start.10 = (f32[512,128]{1,0:T(8,128)S(1)}, f32[512,128]{1,0:T(8,128)S(1)}, u32[]{:S(2)}, u32[]{:S(2)}) collective-permute-start(f32[512,128]{1,0:T(8,128)S(1)} %bitcast_add_fusion.5), channel_id=1, source_target_pairs={{0,28},{4,0},{8,4},{12,8},{16,12},{20,16},{24,20},{28,24},{1,29},{... | collective-permute-start | bytes 786440 | tf_op jit(solution)/shard_map/ppermute | solution.py:64
  57.8 6.5 %collective-permute-start.4 = (f32[512,128]{1,0:T(8,128)S(1)}, f32[512,128]{1,0:T(8,128)S(1)}, u32[]{:S(2)}, u32[]{:S(2)}) collective-permute-start(f32[512,128]{1,0:T(8,128)S(1)} %bitcast_add_fusion.11), channel_id=1, source_target_pairs={{0,4},{4,8},{8,12},{12,16},{16,20},{20,24},{24,28},{28,0},{1,5},{5... | collective-permute-start | bytes 786440 | tf_op jit(solution)/shard_map/ppermute | solution.py:63
  58.0 7.4 %collective-permute-start.11 = (f32[512,128]{1,0:T(8,128)S(1)}, f32[512,128]{1,0:T(8,128)S(1)}, u32[]{:S(2)}, u32[]{:S(2)}) collective-permute-start(f32[512,128]{1,0:T(8,128)S(1)} %bitcast_add_fusion.4), channel_id=1, source_target_pairs={{0,28},{4,0},{8,4},{12,8},{16,12},{20,16},{24,20},{28,24},{1,29},{... | collective-permute-start | bytes 786440 | tf_op jit(solution)/shard_map/ppermute | solution.py:64
  65.3 6.5 %collective-permute-start.5 = (f32[512,128]{1,0:T(8,128)S(1)}, f32[512,128]{1,0:T(8,128)S(1)}, u32[]{:S(2)}, u32[]{:S(2)}) collective-permute-start(f32[512,128]{1,0:T(8,128)S(1)} %bitcast_add_fusion.10), channel_id=1, source_target_pairs={{0,4},{4,8},{8,12},{12,16},{16,20},{20,24},{24,28},{28,0},{1,5},{5... | collective-permute-start | bytes 786440 | tf_op jit(solution)/shard_map/ppermute | solution.py:63
  65.5 7.6 %collective-permute-start.12 = (f32[512,128]{1,0:T(8,128)S(1)}, f32[512,128]{1,0:T(8,128)S(1)}, u32[]{:S(2)}, u32[]{:S(2)}) collective-permute-start(f32[512,128]{1,0:T(8,128)S(1)} %bitcast_add_fusion.3), channel_id=1, source_target_pairs={{0,28},{4,0},{8,4},{12,8},{16,12},{20,16},{24,20},{28,24},{1,29},{... | collective-permute-start | bytes 786440 | tf_op jit(solution)/shard_map/ppermute | solution.py:64
  72.8 7.5 %collective-permute-start.6 = (f32[512,128]{1,0:T(8,128)S(1)}, f32[512,128]{1,0:T(8,128)S(1)}, u32[]{:S(2)}, u32[]{:S(2)}) collective-permute-start(f32[512,128]{1,0:T(8,128)S(1)} %bitcast_add_fusion.9), channel_id=1, source_target_pairs={{0,4},{4,8},{8,12},{12,16},{16,20},{20,24},{24,28},{28,0},{1,5},{5... | collective-permute-start | bytes 786440 | tf_op jit(solution)/shard_map/ppermute | solution.py:63
  73.1 8.2 %collective-permute-start.13 = (f32[512,128]{1,0:T(8,128)S(1)}, f32[512,128]{1,0:T(8,128)S(1)}, u32[]{:S(2)}, u32[]{:S(2)}) collective-permute-start(f32[512,128]{1,0:T(8,128)S(1)} %bitcast_add_fusion.2), channel_id=1, source_target_pairs={{0,28},{4,0},{8,4},{12,8},{16,12},{20,16},{24,20},{28,24},{1,29},{... | collective-permute-start | bytes 786440 | tf_op jit(solution)/shard_map/ppermute | solution.py:64
  82.2 12.5 %all-to-all-start = ((f32[8,128,128]{2,1,0:T(8,128)}), f32[8,128,128]{2,1,0:T(8,128)S(1)}, u32[]{:S(2)}, u32[]{:S(2)}) async-start(f32[8,128,128]{2,1,0:T(8,128)} %bitcast.20), calls=%async_computation | async-start | bytes 1048576 | tf_op jit(solution)/shard_map/all_to_all | solution.py:107
  111.2 19.8 %all-to-all-start.2 = ((bf16[8,8,128,128]{3,2,1,0:T(8,128)(2,1)}), bf16[8,8,128,128]{3,2,1,0:T(8,128)(2,1)S(1)}, u32[]{:S(2)}, u32[]{:S(2)}) async-start(bf16[8,8,128,128]{3,2,1,0:T(8,128)(2,1)} %broadcast_in_dim.30), calls=%async_computation.2 | async-start | bytes 4194304 | tf_op jit(solution)/shard_map/all_to_all | solution.py:116
  131.0 1.3 copy-start
  142.2 12.9 %collective-permute-start.14 = (f32[256,128]{1,0:T(8,128)S(1)}, f32[256,128]{1,0:T(8,128)S(1)}, u32[]{:S(2)}, u32[]{:S(2)}) collective-permute-start(f32[256,128]{1,0:T(8,128)S(1)} %dynamic-slice_bitcast_fusion.3), channel_id=1, source_target_pairs={{0,1},{1,0},{2,3},{3,2},{4,5},{5,4},{6,7},{7,6},{8,9},{9,8},{10,11... | collective-permute-start | bytes 393224 | tf_op jit(solution)/shard_map/ppermute | solution.py:63
  154.1 1.4 collective-permute-start.15
  155.6 12.7 %copy-start.1 = (f32[1024,128]{1,0:T(8,128)S(1)}, f32[1024,128]{1,0:T(8,128)}, u32[]{:S(2)}) copy-start(f32[1024,128]{1,0:T(8,128)} %param.6) | copy-start | bytes 1572868
  155.6 9.3 %collective-permute-start.16 = (f32[512,128]{1,0:T(8,128)S(1)}, f32[512,128]{1,0:T(8,128)S(1)}, u32[]{:S(2)}, u32[]{:S(2)}) collective-permute-start(f32[512,128]{1,0:T(8,128)S(1)} %pad_maximum_fusion.1), channel_id=1, source_target_pairs={{0,2},{2,0},{1,3},{3,1},{4,6},{6,4},{5,7},{7,5},{8,10},{10,8},{9,1... | collective-permute-start | bytes 786440 | tf_op jit(solution)/shard_map/ppermute | solution.py:123
  165.1 2.1 %collective-permute-start.17 = (f32[256,128]{1,0:T(8,128)S(1)}, f32[256,128]{1,0:T(8,128)S(1)}, u32[]{:S(2)}, u32[]{:S(2)}) collective-permute-start(f32[256,128]{1,0:T(8,128)S(1)} %get-tuple-element.11), channel_id=1, source_target_pairs={{0,1},{1,0},{2,3},{3,2},{4,5},{5,4},{6,7},{7,6},{8,9},{9,8},{10,11... | collective-permute-start | bytes 393224 | tf_op jit(solution)/shard_map/ppermute | solution.py:80
  166.9 1.3 collective-permute-start.18

commit v13 on v12

--- a/solution.py
+++ b/solution.py
@@ -118,10 +118,9 @@
 
     user_index = jnp.concatenate([weights_list, items_list, users_list])
     user_part = block_sums(user_index, weight_tiles, item_tiles, n_user_tiles)
-    y = user_part.reshape(n_core, -1, width)
-    y = ring_reduce_scatter(y, "core", n_core)
+    y = user_part.reshape(-1, width)
+    y = y + lax.ppermute(y, "core", [(j, (j + 1) % n_core) for j in range(n_core)])
     y = y + lax.ppermute(y, "yhi", [(j, (j + 1) % n_yhi) for j in range(n_yhi)])
-    y = ring_all_gather(y, "core", n_core).reshape(-1, width)
     user_out = (1.0 - teleport) * y + teleport * user_emb0
     return (user_out, own_emb[None])
 

time: 170 us -> 169 us (level)
  blocking collectives: 14.4 us -> 33.9 us
  waiting for transfers between devices: 62.5 us -> 50.1 us
  starting transfers between devices: 48.1 us -> 43.1 us
  local copies, waits for them, and re-layouts: 12.1 us -> 8.2 us
    all_to_all x0 -> x1, blocking collectives: none -> 19.5 us  [per_device(): t = lax.all_to_all(t, ('ylo', 'x'), 0, 0, tiled=True)]
    all_to_all x1 -> x0, waiting for transfers between devices: 16.2 us -> none  [per_device(): t = lax.all_to_all(t, ('ylo', 'x'), 0, 0, tiled=True)]
    ppermute x8 -> x7, starting transfers between devices: 15.2 us -> 3.21 us  [ring_reduce_scatter_halves(): rl = lax.ppermute(bl, axis, right)]
    ppermute x2 -> x1, starting transfers between devices: 1.11 us -> 11.7 us  [per_device(): lax.ppermute(y, 'core', [(j, (j + 1) % n_core) for j in range(n_core)])]
    ppermute x1, waiting for transfers between devices: 6.6 us -> 11.3 us  [per_device(): y = y + lax.ppermute(y, 'yhi', [(j, (j + 1) % n_yhi) for j in range(n_yhi)])]
    all_to_all x1 -> x0, starting transfers between devices: 3.6 us -> none  [per_device(): t = lax.all_to_all(t, ('ylo', 'x'), 0, 0, tiled=True)]
    ppermute x8 -> x7, waiting for transfers between devices: 31.3 us -> 30.5 us  [ring_reduce_scatter_halves(): rl = lax.ppermute(bl, axis, right)]
    ppermute x8 -> x7, starting transfers between devices: 20.6 us -> 20.4 us  [ring_reduce_scatter_halves(): rr = lax.ppermute(br, axis, left)]
  transfers between devices with their start and end apart: 21 -> 17, of which waited for: 14 -> 10; matrix products, arithmetic and copies ran while one was open for 5% -> 5% of each run, Pallas kernels for 0% -> 0%
where the time goes in v13:
time: 169 us; the launch traced here: 168 us
  waiting for transfers between devices  50.1 us (30%)
  starting transfers between devices  43.1 us (26%)
  blocking collectives  33.9 us (20%)
  Pallas kernels  18.5 us (11%)
  other arithmetic  13.7 us (8%)
  local copies, waits for them, and re-layouts  8.2 us (5%)
    ppermute x7, waiting for transfers between devices, ring_reduce_scatter_halves(): rl = lax.ppermute(bl, axis, right)  30.5 us
    ppermute x7, starting transfers between devices, ring_reduce_scatter_halves(): rr = lax.ppermute(br, axis, left)  20.4 us
    all_to_all x1, blocking collectives, per_device(): t = lax.all_to_all(t, ('ylo', 'x'), 0, 0, tiled=True)  19.5 us
    pallas_call x2, Pallas kernels, block_sums(): pl.pallas_call(functools.partial(block_sum_kernel, b_transposed=b_transpo...  18.5 us
    all_to_all x1, blocking collectives, per_device(): lax.all_to_all(jnp.broadcast_to(own_bf[None], (n_z, tile_rows, width)), '...  14.4 us
    ppermute x1, starting transfers between devices, per_device(): lax.ppermute(y, 'core', [(j, (j + 1) % n_core) for j in range(n_core)])  11.7 us
    ppermute x1, waiting for transfers between devices, per_device(): y = y + lax.ppermute(y, 'yhi', [(j, (j + 1) % n_yhi) for j in range(n_yhi)])  11.3 us
    add x7, other arithmetic, ring_reduce_scatter_halves(): bl = rl + lax.dynamic_index_in_dim(xl, (i - s - 2) % n, 0, keepdims=False)  6.85 us
  transfers between devices with their start and end apart: 17, of which 10 were waited for; matrix products, arithmetic and copies ran while one was open for 5% of the time, Pallas kernels for 0%

profile of v13, /device:TPU:1, one launch (start us, length us, event | category | flops | bytes accessed | tf_op | source)
XLA Modules:
  0.0 168.4 jit_solution(3470963964887011307)
XLA Ops:
  2.8 1.1 convert_element_type.6
  5.3 9.6 %shard_map.77 = f32[64,128,128]{2,1,0:T(8,128)} custom-call(s32[1152]{0:T(1024)} %get-tuple-element.8.index_ref, bf16[8,128,128]{2,1,0:T(8,128)(2,1)} %bitcast.72, bf16[64,128,128]{2,1,0:T(8,128)(2,1)} %a_ref.1), custom_call_target="tpu_custom_call" | custom-call | tf_op jit(solution)/shard_map/pallas_call | solution.py:36
  14.9 4.0 %fusion.9 = (f32[32,128,128]{2,1,0:T(8,128)}, f32[32,128,128]{2,1,0:T(8,128)S(1)}) fusion(f32[64,128,128]{2,1,0:T(8,128)} %shard_map.77), kind=kLoop, calls=%fused_computation.44 | loop fusion | bytes 8388608 | tf_op jit(solution)/shard_map/slice | solution.py:105
  19.9 2.5 %collective-permute-start = (f32[512,128]{1,0:T(8,128)S(1)}, f32[512,128]{1,0:T(8,128)S(1)}, u32[]{:S(2)}, u32[]{:S(2)}) collective-permute-start(f32[512,128]{1,0:T(8,128)S(1)} %dynamic-slice_bitcast_fusion.1), channel_id=1, source_target_pairs={{0,4},{4,8},{8,12},{12,16},{16,20},{20,24},{24,28},{28,0},{1,5},{5... | collective-permute-start | bytes 786440 | tf_op jit(solution)/shard_map/ppermute | solution.py:63
  22.5 4.1 %collective-permute-start.7 = (f32[512,128]{1,0:T(8,128)S(1)}, f32[512,128]{1,0:T(8,128)S(1)}, u32[]{:S(2)}, u32[]{:S(2)}) collective-permute-start(f32[512,128]{1,0:T(8,128)S(1)} %dynamic-slice_bitcast_fusion), channel_id=1, source_target_pairs={{0,28},{4,0},{8,4},{12,8},{16,12},{20,16},{24,20},{28,24},{1,29},{... | collective-permute-start | bytes 786440 | tf_op jit(solution)/shard_map/ppermute | solution.py:64
  26.5 5.9 %collective-permute-done = f32[512,128]{1,0:T(8,128)S(1)} collective-permute-done((f32[512,128]{1,0:T(8,128)S(1)}, f32[512,128]{1,0:T(8,128)S(1)}, u32[]{:S(2)}, u32[]{:S(2)}) %collective-permute-start) | collective-permute-done | bytes 262176 | tf_op jit(solution)/shard_map/ppermute | solution.py:63
  32.4 1.0 bitcast_add_fusion.13
  33.5 2.7 %collective-permute-start.8 = (f32[512,128]{1,0:T(8,128)S(1)}, f32[512,128]{1,0:T(8,128)S(1)}, u32[]{:S(2)}, u32[]{:S(2)}) collective-permute-start(f32[512,128]{1,0:T(8,128)S(1)} %bitcast_add_fusion.6), channel_id=1, source_target_pairs={{0,28},{4,0},{8,4},{12,8},{16,12},{20,16},{24,20},{28,24},{1,29},{... | collective-permute-start | bytes 786440 | tf_op jit(solution)/shard_map/ppermute | solution.py:64
  36.2 5.0 %collective-permute-done.1 = f32[512,128]{1,0:T(8,128)S(1)} collective-permute-done((f32[512,128]{1,0:T(8,128)S(1)}, f32[512,128]{1,0:T(8,128)S(1)}, u32[]{:S(2)}, u32[]{:S(2)}) %collective-permute-start.1) | collective-permute-done | bytes 262176 | tf_op jit(solution)/shard_map/ppermute | solution.py:63
  41.3 1.0 bitcast_add_fusion.12
  42.4 2.7 %collective-permute-start.9 = (f32[512,128]{1,0:T(8,128)S(1)}, f32[512,128]{1,0:T(8,128)S(1)}, u32[]{:S(2)}, u32[]{:S(2)}) collective-permute-start(f32[512,128]{1,0:T(8,128)S(1)} %bitcast_add_fusion.5), channel_id=1, source_target_pairs={{0,28},{4,0},{8,4},{12,8},{16,12},{20,16},{24,20},{28,24},{1,29},{... | collective-permute-start | bytes 786440 | tf_op jit(solution)/shard_map/ppermute | solution.py:64
  45.1 4.2 %collective-permute-done.2 = f32[512,128]{1,0:T(8,128)S(1)} collective-permute-done((f32[512,128]{1,0:T(8,128)S(1)}, f32[512,128]{1,0:T(8,128)S(1)}, u32[]{:S(2)}, u32[]{:S(2)}) %collective-permute-start.2) | collective-permute-done | bytes 262176 | tf_op jit(solution)/shard_map/ppermute | solution.py:63
  49.3 1.0 bitcast_add_fusion.11
  50.4 2.7 %collective-permute-start.10 = (f32[512,128]{1,0:T(8,128)S(1)}, f32[512,128]{1,0:T(8,128)S(1)}, u32[]{:S(2)}, u32[]{:S(2)}) collective-permute-start(f32[512,128]{1,0:T(8,128)S(1)} %bitcast_add_fusion.4), channel_id=1, source_target_pairs={{0,28},{4,0},{8,4},{12,8},{16,12},{20,16},{24,20},{28,24},{1,29},{... | collective-permute-start | bytes 786440 | tf_op jit(solution)/shard_map/ppermute | solution.py:64
  53.1 3.6 %collective-permute-done.3 = f32[512,128]{1,0:T(8,128)S(1)} collective-permute-done((f32[512,128]{1,0:T(8,128)S(1)}, f32[512,128]{1,0:T(8,128)S(1)}, u32[]{:S(2)}, u32[]{:S(2)}) %collective-permute-start.3) | collective-permute-done | bytes 262176 | tf_op jit(solution)/shard_map/ppermute | solution.py:63
  56.8 1.0 bitcast_add_fusion.10
  57.9 2.7 %collective-permute-start.11 = (f32[512,128]{1,0:T(8,128)S(1)}, f32[512,128]{1,0:T(8,128)S(1)}, u32[]{:S(2)}, u32[]{:S(2)}) collective-permute-start(f32[512,128]{1,0:T(8,128)S(1)} %bitcast_add_fusion.3), channel_id=1, source_target_pairs={{0,28},{4,0},{8,4},{12,8},{16,12},{20,16},{24,20},{28,24},{1,29},{... | collective-permute-start | bytes 786440 | tf_op jit(solution)/shard_map/ppermute | solution.py:64
  60.6 3.6 %collective-permute-done.4 = f32[512,128]{1,0:T(8,128)S(1)} collective-permute-done((f32[512,128]{1,0:T(8,128)S(1)}, f32[512,128]{1,0:T(8,128)S(1)}, u32[]{:S(2)}, u32[]{:S(2)}) %collective-permute-start.4) | collective-permute-done | bytes 262176 | tf_op jit(solution)/shard_map/ppermute | solution.py:63
  65.4 2.7 %collective-permute-start.12 = (f32[512,128]{1,0:T(8,128)S(1)}, f32[512,128]{1,0:T(8,128)S(1)}, u32[]{:S(2)}, u32[]{:S(2)}) collective-permute-start(f32[512,128]{1,0:T(8,128)S(1)} %bitcast_add_fusion.2), channel_id=1, source_target_pairs={{0,28},{4,0},{8,4},{12,8},{16,12},{20,16},{24,20},{28,24},{1,29},{... | collective-permute-start | bytes 786440 | tf_op jit(solution)/shard_map/ppermute | solution.py:64
  68.1 3.6 %collective-permute-done.5 = f32[512,128]{1,0:T(8,128)S(1)} collective-permute-done((f32[512,128]{1,0:T(8,128)S(1)}, f32[512,128]{1,0:T(8,128)S(1)}, u32[]{:S(2)}, u32[]{:S(2)}) %collective-permute-start.5) | collective-permute-done | bytes 262176 | tf_op jit(solution)/shard_map/ppermute | solution.py:63
  73.1 2.7 %collective-permute-start.13 = (f32[512,128]{1,0:T(8,128)S(1)}, f32[512,128]{1,0:T(8,128)S(1)}, u32[]{:S(2)}, u32[]{:S(2)}) collective-permute-start(f32[512,128]{1,0:T(8,128)S(1)} %bitcast_add_fusion.1), channel_id=1, source_target_pairs={{0,28},{4,0},{8,4},{12,8},{16,12},{20,16},{24,20},{28,24},{1,29},{... | collective-permute-start | bytes 786440 | tf_op jit(solution)/shard_map/ppermute | solution.py:64
  75.8 4.5 %collective-permute-done.6 = f32[512,128]{1,0:T(8,128)S(1)} collective-permute-done((f32[512,128]{1,0:T(8,128)S(1)}, f32[512,128]{1,0:T(8,128)S(1)}, u32[]{:S(2)}, u32[]{:S(2)}) %collective-permute-start.6) | collective-permute-done | bytes 262176 | tf_op jit(solution)/shard_map/ppermute | solution.py:63
  82.2 5.1 %all-to-all-start = ((f32[8,128,128]{2,1,0:T(8,128)}), f32[8,128,128]{2,1,0:T(8,128)S(1)}, u32[]{:S(2)}, u32[]{:S(2)}) async-start(f32[8,128,128]{2,1,0:T(8,128)} %bitcast.20), calls=%async_computation | async-start | bytes 1048576 | tf_op jit(solution)/shard_map/all_to_all | solution.py:107
  88.2 6.6 %all-to-all-done = f32[8,128,128]{2,1,0:T(8,128)S(1)} async-done(((f32[8,128,128]{2,1,0:T(8,128)}), f32[8,128,128]{2,1,0:T(8,128)S(1)}, u32[]{:S(2)}, u32[]{:S(2)}) %all-to-all-start) | async-done | bytes 524320 | tf_op jit(solution)/shard_map/all_to_all | solution.py:107
  95.0 14.4 %all_to_all.15 = bf16[8,128,128]{2,1,0:T(8,128)(2,1)S(1)} all-to-all(bf16[8,128,128]{2,1,0:T(8,128)(2,1)S(1)} %broadcast_in_dim.6), channel_id=1, replica_groups=mesh['ylo'=2,'x'=4,'z'=8,'yhi'=2,'core'=2] {'z'}, dimensions={0} | all-to-all | bytes 524288 | tf_op jit(solution)/shard_map/all_to_all | solution.py:114
  109.8 19.5 %all_to_all.16 = bf16[8,8,128,128]{3,2,1,0:T(8,128)(2,1)} all-to-all(bf16[8,8,128,128]{3,2,1,0:T(8,128)(2,1)S(1)} %broadcast_in_dim.7), channel_id=1, replica_groups=mesh['ylo'=2,'x'=4,'z'=8,'yhi'=2,'core'=2] {'ylo','x'}, dimensions={0} | all-to-all | bytes 4194304 | tf_op jit(solution)/shard_map/all_to_all | solution.py:116
  129.4 8.9 %shard_map.78 = f32[8,128,128]{2,1,0:T(8,128)} custom-call(s32[1152]{0:T(1024)} %get-tuple-element.9.index_ref, bf16[64,128,128]{2,1,0:T(8,128)(2,1)} %a_ref.1, bf16[64,128,128]{2,1,0:T(8,128)(2,1)} %bitcast.70), custom_call_target="tpu_custom_call" | custom-call | tf_op jit(solution)/shard_map/pallas_call | solution.py:36
  138.2 11.7 %collective-permute-start.14 = (f32[1024,128]{1,0:T(8,128)}, f32[1024,128]{1,0:T(8,128)S(1)}, u32[]{:S(2)}, u32[]{:S(2)}) collective-permute-start(f32[1024,128]{1,0:T(8,128)} %bitcast.71), channel_id=1, source_target_pairs={{0,1},{1,0},{2,3},{3,2},{4,5},{5,4},{6,7},{7,6},{8,9},{9,8},{10,11... | collective-permute-start | bytes 1572872 | tf_op jit(solution)/shard_map/ppermute | solution.py:122
  150.0 1.7 %collective-permute-done.14 = f32[1024,128]{1,0:T(8,128)S(1)} collective-permute-done((f32[1024,128]{1,0:T(8,128)}, f32[1024,128]{1,0:T(8,128)S(1)}, u32[]{:S(2)}, u32[]{:S(2)}) %collective-permute-start.14) | collective-permute-done | bytes 524320 | tf_op jit(solution)/shard_map/ppermute | solution.py:122
  151.7 1.1 bitcast_add_fusion.15
  152.8 2.7 %collective-permute-start.15 = (f32[1024,128]{1,0:T(8,128)S(1)}, f32[1024,128]{1,0:T(8,128)S(1)}, u32[]{:S(2)}, u32[]{:S(2)}) collective-permute-start(f32[1024,128]{1,0:T(8,128)S(1)} %bitcast_add_fusion.15), channel_id=1, source_target_pairs={{0,2},{2,0},{1,3},{3,1},{4,6},{6,4},{5,7},{7,5},{8,10},{10,8},{9,1... | collective-permute-start | bytes 1572872 | tf_op jit(solution)/shard_map/ppermute | solution.py:123
  156.3 11.3 %collective-permute-done.15 = f32[1024,128]{1,0:T(8,128)S(1)} collective-permute-done((f32[1024,128]{1,0:T(8,128)S(1)}, f32[1024,128]{1,0:T(8,128)S(1)}, u32[]{:S(2)}, u32[]{:S(2)}) %collective-permute-start.15) | collective-permute-done | bytes 524320 | tf_op jit(solution)/shard_map/ppermute | solution.py:123
  (43 shorter events, 12.5 us)
Async XLA Ops:
  19.9 12.5 %collective-permute-start = (f32[512,128]{1,0:T(8,128)S(1)}, f32[512,128]{1,0:T(8,128)S(1)}, u32[]{:S(2)}, u32[]{:S(2)}) collective-permute-start(f32[512,128]{1,0:T(8,128)S(1)} %dynamic-slice_bitcast_fusion.1), channel_id=1, source_target_pairs={{0,4},{4,8},{8,12},{12,16},{16,20},{20,24},{24,28},{28,0},{1,5},{5... | collective-permute-start | bytes 786440 | tf_op jit(solution)/shard_map/ppermute | solution.py:63
  22.5 11.0 %collective-permute-start.7 = (f32[512,128]{1,0:T(8,128)S(1)}, f32[512,128]{1,0:T(8,128)S(1)}, u32[]{:S(2)}, u32[]{:S(2)}) collective-permute-start(f32[512,128]{1,0:T(8,128)S(1)} %dynamic-slice_bitcast_fusion), channel_id=1, source_target_pairs={{0,28},{4,0},{8,4},{12,8},{16,12},{20,16},{24,20},{28,24},{1,29},{... | collective-permute-start | bytes 786440 | tf_op jit(solution)/shard_map/ppermute | solution.py:64
  33.4 7.9 %collective-permute-start.1 = (f32[512,128]{1,0:T(8,128)S(1)}, f32[512,128]{1,0:T(8,128)S(1)}, u32[]{:S(2)}, u32[]{:S(2)}) collective-permute-start(f32[512,128]{1,0:T(8,128)S(1)} %bitcast_add_fusion.13), channel_id=1, source_target_pairs={{0,4},{4,8},{8,12},{12,16},{16,20},{20,24},{24,28},{28,0},{1,5},{5... | collective-permute-start | bytes 786440 | tf_op jit(solution)/shard_map/ppermute | solution.py:63
  33.5 8.8 %collective-permute-start.8 = (f32[512,128]{1,0:T(8,128)S(1)}, f32[512,128]{1,0:T(8,128)S(1)}, u32[]{:S(2)}, u32[]{:S(2)}) collective-permute-start(f32[512,128]{1,0:T(8,128)S(1)} %bitcast_add_fusion.6), channel_id=1, source_target_pairs={{0,28},{4,0},{8,4},{12,8},{16,12},{20,16},{24,20},{28,24},{1,29},{... | collective-permute-start | bytes 786440 | tf_op jit(solution)/shard_map/ppermute | solution.py:64
  42.2 7.0 %collective-permute-start.2 = (f32[512,128]{1,0:T(8,128)S(1)}, f32[512,128]{1,0:T(8,128)S(1)}, u32[]{:S(2)}, u32[]{:S(2)}) collective-permute-start(f32[512,128]{1,0:T(8,128)S(1)} %bitcast_add_fusion.12), channel_id=1, source_target_pairs={{0,4},{4,8},{8,12},{12,16},{16,20},{20,24},{24,28},{28,0},{1,5},{5... | collective-permute-start | bytes 786440 | tf_op jit(solution)/shard_map/ppermute | solution.py:63
  42.4 8.0 %collective-permute-start.9 = (f32[512,128]{1,0:T(8,128)S(1)}, f32[512,128]{1,0:T(8,128)S(1)}, u32[]{:S(2)}, u32[]{:S(2)}) collective-permute-start(f32[512,128]{1,0:T(8,128)S(1)} %bitcast_add_fusion.5), channel_id=1, source_target_pairs={{0,28},{4,0},{8,4},{12,8},{16,12},{20,16},{24,20},{28,24},{1,29},{... | collective-permute-start | bytes 786440 | tf_op jit(solution)/shard_map/ppermute | solution.py:64
  50.3 6.5 %collective-permute-start.3 = (f32[512,128]{1,0:T(8,128)S(1)}, f32[512,128]{1,0:T(8,128)S(1)}, u32[]{:S(2)}, u32[]{:S(2)}) collective-permute-start(f32[512,128]{1,0:T(8,128)S(1)} %bitcast_add_fusion.11), channel_id=1, source_target_pairs={{0,4},{4,8},{8,12},{12,16},{16,20},{20,24},{24,28},{28,0},{1,5},{5... | collective-permute-start | bytes 786440 | tf_op jit(solution)/shard_map/ppermute | solution.py:63
  50.4 7.4 %collective-permute-start.10 = (f32[512,128]{1,0:T(8,128)S(1)}, f32[512,128]{1,0:T(8,128)S(1)}, u32[]{:S(2)}, u32[]{:S(2)}) collective-permute-start(f32[512,128]{1,0:T(8,128)S(1)} %bitcast_add_fusion.4), channel_id=1, source_target_pairs={{0,28},{4,0},{8,4},{12,8},{16,12},{20,16},{24,20},{28,24},{1,29},{... | collective-permute-start | bytes 786440 | tf_op jit(solution)/shard_map/ppermute | solution.py:64
  57.8 6.5 %collective-permute-start.4 = (f32[512,128]{1,0:T(8,128)S(1)}, f32[512,128]{1,0:T(8,128)S(1)}, u32[]{:S(2)}, u32[]{:S(2)}) collective-permute-start(f32[512,128]{1,0:T(8,128)S(1)} %bitcast_add_fusion.10), channel_id=1, source_target_pairs={{0,4},{4,8},{8,12},{12,16},{16,20},{20,24},{24,28},{28,0},{1,5},{5... | collective-permute-start | bytes 786440 | tf_op jit(solution)/shard_map/ppermute | solution.py:63
  57.9 7.4 %collective-permute-start.11 = (f32[512,128]{1,0:T(8,128)S(1)}, f32[512,128]{1,0:T(8,128)S(1)}, u32[]{:S(2)}, u32[]{:S(2)}) collective-permute-start(f32[512,128]{1,0:T(8,128)S(1)} %bitcast_add_fusion.3), channel_id=1, source_target_pairs={{0,28},{4,0},{8,4},{12,8},{16,12},{20,16},{24,20},{28,24},{1,29},{... | collective-permute-start | bytes 786440 | tf_op jit(solution)/shard_map/ppermute | solution.py:64
  65.2 6.5 %collective-permute-start.5 = (f32[512,128]{1,0:T(8,128)S(1)}, f32[512,128]{1,0:T(8,128)S(1)}, u32[]{:S(2)}, u32[]{:S(2)}) collective-permute-start(f32[512,128]{1,0:T(8,128)S(1)} %bitcast_add_fusion.9), channel_id=1, source_target_pairs={{0,4},{4,8},{8,12},{12,16},{16,20},{20,24},{24,28},{28,0},{1,5},{5... | collective-permute-start | bytes 786440 | tf_op jit(solution)/shard_map/ppermute | solution.py:63
  65.4 7.6 %collective-permute-start.12 = (f32[512,128]{1,0:T(8,128)S(1)}, f32[512,128]{1,0:T(8,128)S(1)}, u32[]{:S(2)}, u32[]{:S(2)}) collective-permute-start(f32[512,128]{1,0:T(8,128)S(1)} %bitcast_add_fusion.2), channel_id=1, source_target_pairs={{0,28},{4,0},{8,4},{12,8},{16,12},{20,16},{24,20},{28,24},{1,29},{... | collective-permute-start | bytes 786440 | tf_op jit(solution)/shard_map/ppermute | solution.py:64
  72.7 7.6 %collective-permute-start.6 = (f32[512,128]{1,0:T(8,128)S(1)}, f32[512,128]{1,0:T(8,128)S(1)}, u32[]{:S(2)}, u32[]{:S(2)}) collective-permute-start(f32[512,128]{1,0:T(8,128)S(1)} %bitcast_add_fusion.8), channel_id=1, source_target_pairs={{0,4},{4,8},{8,12},{12,16},{16,20},{20,24},{24,28},{28,0},{1,5},{5... | collective-permute-start | bytes 786440 | tf_op jit(solution)/shard_map/ppermute | solution.py:63
  73.1 8.2 %collective-permute-start.13 = (f32[512,128]{1,0:T(8,128)S(1)}, f32[512,128]{1,0:T(8,128)S(1)}, u32[]{:S(2)}, u32[]{:S(2)}) collective-permute-start(f32[512,128]{1,0:T(8,128)S(1)} %bitcast_add_fusion.1), channel_id=1, source_target_pairs={{0,28},{4,0},{8,4},{12,8},{16,12},{20,16},{24,20},{28,24},{1,29},{... | collective-permute-start | bytes 786440 | tf_op jit(solution)/shard_map/ppermute | solution.py:64
  82.2 12.6 %all-to-all-start = ((f32[8,128,128]{2,1,0:T(8,128)}), f32[8,128,128]{2,1,0:T(8,128)S(1)}, u32[]{:S(2)}, u32[]{:S(2)}) async-start(f32[8,128,128]{2,1,0:T(8,128)} %bitcast.20), calls=%async_computation | async-start | bytes 1048576 | tf_op jit(solution)/shard_map/all_to_all | solution.py:107
  129.4 38.2 %copy-start = (f32[1024,128]{1,0:T(8,128)S(1)}, f32[1024,128]{1,0:T(8,128)}, u32[]{:S(2)}) copy-start(f32[1024,128]{1,0:T(8,128)} %param.6) | copy-start | bytes 1572868
  138.2 13.5 %collective-permute-start.14 = (f32[1024,128]{1,0:T(8,128)}, f32[1024,128]{1,0:T(8,128)S(1)}, u32[]{:S(2)}, u32[]{:S(2)}) collective-permute-start(f32[1024,128]{1,0:T(8,128)} %bitcast.71), channel_id=1, source_target_pairs={{0,1},{1,0},{2,3},{3,2},{4,5},{5,4},{6,7},{7,6},{8,9},{9,8},{10,11... | collective-permute-start | bytes 1572872 | tf_op jit(solution)/shard_map/ppermute | solution.py:122
  152.8 14.7 %collective-permute-start.15 = (f32[1024,128]{1,0:T(8,128)S(1)}, f32[1024,128]{1,0:T(8,128)S(1)}, u32[]{:S(2)}, u32[]{:S(2)}) collective-permute-start(f32[1024,128]{1,0:T(8,128)S(1)} %bitcast_add_fusion.15), channel_id=1, source_target_pairs={{0,2},{2,0},{1,3},{3,1},{4,6},{6,4},{5,7},{7,5},{8,10},{10,8},{9,1... | collective-permute-start | bytes 1572872 | tf_op jit(solution)/shard_map/ppermute | solution.py:123

commit v14 on v13

--- a/solution.py
+++ b/solution.py
@@ -111,7 +111,14 @@
     own_base = lax.dynamic_slice_in_dim(item_base[0], position * tile_rows, tile_rows, 0)
     own_emb = (1.0 - teleport) * own_sum + teleport * own_base
     own_bf = own_emb.astype(jnp.bfloat16)
-    t = lax.all_to_all(jnp.broadcast_to(own_bf[None], (n_z, tile_rows, width)), "z", 0, 0, tiled=True)
+    t = own_bf[None]
+    z_index = lax.axis_index("z")
+    step = 1
+    while step < n_z:
+        other = lax.ppermute(t, "z", [(j, j ^ step) for j in range(n_z)])
+        low = (z_index // step) % 2 == 0
+        t = jnp.where(low, jnp.concatenate([t, other], 0), jnp.concatenate([other, t], 0))
+        step *= 2
     t = jnp.broadcast_to(t[None], (n_ylo * n_x, n_z, tile_rows, width))
     t = lax.all_to_all(t, ("ylo", "x"), 0, 0, tiled=True)
     item_tiles = t.reshape(n_users, tile_rows, width)

time: 169 us -> 174 us (1.030)
  blocking collectives: 33.9 us -> 19.1 us
  starting transfers between devices: 43.1 us -> 53.5 us
  waiting for transfers between devices: 50.1 us -> 59.7 us
    all_to_all x1 -> x0, blocking collectives: 14.4 us -> none  [per_device(): lax.all_to_all(jnp.broadcast_to(own_bf[None], (n_z, tile_rows, width)), '...]
    ppermute x0 -> x3, waiting for transfers between devices: none -> 9.51 us  [per_device(): other = lax.ppermute(t, 'z', [(j, j ^ step) for j in range(n_z)])]
    ppermute x0 -> x3, starting transfers between devices: none -> 7.5 us  [per_device(): other = lax.ppermute(t, 'z', [(j, j ^ step) for j in range(n_z)])]
    ppermute x1, starting transfers between devices: 11.7 us -> 14.7 us  [per_device(): lax.ppermute(y, 'core', [(j, (j + 1) % n_core) for j in range(n_core)])]
  transfers between devices with their start and end apart: 17 -> 20, of which waited for: 10 -> 13; matrix products, arithmetic and copies ran while one was open for 5% -> 5% of each run, Pallas kernels for 0% -> 0%
where the time goes in v14:
time: 174 us
  waiting for transfers between devices  59.7 us (34%)
  starting transfers between devices  53.5 us (31%)
  blocking collectives  19.1 us (11%)
  Pallas kernels  18.5 us (11%)
  other arithmetic  13.8 us (8%)
  local copies, waits for them, and re-layouts  8.23 us (5%)
    ppermute x7, waiting for transfers between devices, ring_reduce_scatter_halves(): rl = lax.ppermute(bl, axis, right)  30.5 us
    ppermute x7, starting transfers between devices, ring_reduce_scatter_halves(): rr = lax.ppermute(br, axis, left)  20.4 us
    all_to_all x1, blocking collectives, per_device(): t = lax.all_to_all(t, ('ylo', 'x'), 0, 0, tiled=True)  19.1 us
    pallas_call x2, Pallas kernels, block_sums(): pl.pallas_call(functools.partial(block_sum_kernel, b_transposed=b_transpo...  18.5 us
    ppermute x1, starting transfers between devices, per_device(): lax.ppermute(y, 'core', [(j, (j + 1) % n_core) for j in range(n_core)])  14.7 us
    ppermute x1, waiting for transfers between devices, per_device(): y = y + lax.ppermute(y, 'yhi', [(j, (j + 1) % n_yhi) for j in range(n_yhi)])  11.3 us
    ppermute x3, waiting for transfers between devices, per_device(): other = lax.ppermute(t, 'z', [(j, j ^ step) for j in range(n_z)])  9.51 us
    ppermute x3, starting transfers between devices, per_device(): other = lax.ppermute(t, 'z', [(j, j ^ step) for j in range(n_z)])  7.5 us
  transfers between devices with their start and end apart: 20, of which 13 were waited for; matrix products, arithmetic and copies ran while one was open for 5% of the time, Pallas kernels for 0%

profile of v14, /device:TPU:1, one launch (start us, length us, event | category | flops | bytes accessed | tf_op | source)
XLA Modules:
  0.0 173.7 jit_solution(4096302804393935667)
XLA Ops:
  2.8 1.1 convert_element_type.6
  5.3 9.6 %shard_map.77 = f32[64,128,128]{2,1,0:T(8,128)} custom-call(s32[1152]{0:T(1024)} %get-tuple-element.8.index_ref, bf16[8,128,128]{2,1,0:T(8,128)(2,1)} %bitcast.74, bf16[64,128,128]{2,1,0:T(8,128)(2,1)} %a_ref.1), custom_call_target="tpu_custom_call" | custom-call | tf_op jit(solution)/shard_map/pallas_call | solution.py:36
  14.9 4.1 %fusion.8 = (f32[32,128,128]{2,1,0:T(8,128)}, f32[32,128,128]{2,1,0:T(8,128)S(1)}) fusion(f32[64,128,128]{2,1,0:T(8,128)} %shard_map.77), kind=kLoop, calls=%fused_computation.47 | loop fusion | bytes 8388608 | tf_op jit(solution)/shard_map/slice | solution.py:105
  19.9 2.5 %collective-permute-start = (f32[512,128]{1,0:T(8,128)S(1)}, f32[512,128]{1,0:T(8,128)S(1)}, u32[]{:S(2)}, u32[]{:S(2)}) collective-permute-start(f32[512,128]{1,0:T(8,128)S(1)} %dynamic-slice_bitcast_fusion.1), channel_id=1, source_target_pairs={{0,4},{4,8},{8,12},{12,16},{16,20},{20,24},{24,28},{28,0},{1,5},{5... | collective-permute-start | bytes 786440 | tf_op jit(solution)/shard_map/ppermute | solution.py:63
  22.5 4.1 %collective-permute-start.7 = (f32[512,128]{1,0:T(8,128)S(1)}, f32[512,128]{1,0:T(8,128)S(1)}, u32[]{:S(2)}, u32[]{:S(2)}) collective-permute-start(f32[512,128]{1,0:T(8,128)S(1)} %dynamic-slice_bitcast_fusion), channel_id=1, source_target_pairs={{0,28},{4,0},{8,4},{12,8},{16,12},{20,16},{24,20},{28,24},{1,29},{... | collective-permute-start | bytes 786440 | tf_op jit(solution)/shard_map/ppermute | solution.py:64
  26.5 5.9 %collective-permute-done = f32[512,128]{1,0:T(8,128)S(1)} collective-permute-done((f32[512,128]{1,0:T(8,128)S(1)}, f32[512,128]{1,0:T(8,128)S(1)}, u32[]{:S(2)}, u32[]{:S(2)}) %collective-permute-start) | collective-permute-done | bytes 262176 | tf_op jit(solution)/shard_map/ppermute | solution.py:63
  33.5 2.7 %collective-permute-start.8 = (f32[512,128]{1,0:T(8,128)S(1)}, f32[512,128]{1,0:T(8,128)S(1)}, u32[]{:S(2)}, u32[]{:S(2)}) collective-permute-start(f32[512,128]{1,0:T(8,128)S(1)} %bitcast_add_fusion.6), channel_id=1, source_target_pairs={{0,28},{4,0},{8,4},{12,8},{16,12},{20,16},{24,20},{28,24},{1,29},{... | collective-permute-start | bytes 786440 | tf_op jit(solution)/shard_map/ppermute | solution.py:64
  36.2 5.0 %collective-permute-done.1 = f32[512,128]{1,0:T(8,128)S(1)} collective-permute-done((f32[512,128]{1,0:T(8,128)S(1)}, f32[512,128]{1,0:T(8,128)S(1)}, u32[]{:S(2)}, u32[]{:S(2)}) %collective-permute-start.1) | collective-permute-done | bytes 262176 | tf_op jit(solution)/shard_map/ppermute | solution.py:63
  42.4 2.7 %collective-permute-start.9 = (f32[512,128]{1,0:T(8,128)S(1)}, f32[512,128]{1,0:T(8,128)S(1)}, u32[]{:S(2)}, u32[]{:S(2)}) collective-permute-start(f32[512,128]{1,0:T(8,128)S(1)} %bitcast_add_fusion.5), channel_id=1, source_target_pairs={{0,28},{4,0},{8,4},{12,8},{16,12},{20,16},{24,20},{28,24},{1,29},{... | collective-permute-start | bytes 786440 | tf_op jit(solution)/shard_map/ppermute | solution.py:64
  45.1 4.2 %collective-permute-done.2 = f32[512,128]{1,0:T(8,128)S(1)} collective-permute-done((f32[512,128]{1,0:T(8,128)S(1)}, f32[512,128]{1,0:T(8,128)S(1)}, u32[]{:S(2)}, u32[]{:S(2)}) %collective-permute-start.2) | collective-permute-done | bytes 262176 | tf_op jit(solution)/shard_map/ppermute | solution.py:63
  50.4 2.7 %collective-permute-start.10 = (f32[512,128]{1,0:T(8,128)S(1)}, f32[512,128]{1,0:T(8,128)S(1)}, u32[]{:S(2)}, u32[]{:S(2)}) collective-permute-start(f32[512,128]{1,0:T(8,128)S(1)} %bitcast_add_fusion.4), channel_id=1, source_target_pairs={{0,28},{4,0},{8,4},{12,8},{16,12},{20,16},{24,20},{28,24},{1,29},{... | collective-permute-start | bytes 786440 | tf_op jit(solution)/shard_map/ppermute | solution.py:64
  53.2 3.6 %collective-permute-done.3 = f32[512,128]{1,0:T(8,128)S(1)} collective-permute-done((f32[512,128]{1,0:T(8,128)S(1)}, f32[512,128]{1,0:T(8,128)S(1)}, u32[]{:S(2)}, u32[]{:S(2)}) %collective-permute-start.3) | collective-permute-done | bytes 262176 | tf_op jit(solution)/shard_map/ppermute | solution.py:63
  57.9 2.7 %collective-permute-start.11 = (f32[512,128]{1,0:T(8,128)S(1)}, f32[512,128]{1,0:T(8,128)S(1)}, u32[]{:S(2)}, u32[]{:S(2)}) collective-permute-start(f32[512,128]{1,0:T(8,128)S(1)} %bitcast_add_fusion.3), channel_id=1, source_target_pairs={{0,28},{4,0},{8,4},{12,8},{16,12},{20,16},{24,20},{28,24},{1,29},{... | collective-permute-start | bytes 786440 | tf_op jit(solution)/shard_map/ppermute | solution.py:64
  60.7 3.6 %collective-permute-done.4 = f32[512,128]{1,0:T(8,128)S(1)} collective-permute-done((f32[512,128]{1,0:T(8,128)S(1)}, f32[512,128]{1,0:T(8,128)S(1)}, u32[]{:S(2)}, u32[]{:S(2)}) %collective-permute-start.4) | collective-permute-done | bytes 262176 | tf_op jit(solution)/shard_map/ppermute | solution.py:63
  65.4 2.7 %collective-permute-start.12 = (f32[512,128]{1,0:T(8,128)S(1)}, f32[512,128]{1,0:T(8,128)S(1)}, u32[]{:S(2)}, u32[]{:S(2)}) collective-permute-start(f32[512,128]{1,0:T(8,128)S(1)} %bitcast_add_fusion.2), channel_id=1, source_target_pairs={{0,28},{4,0},{8,4},{12,8},{16,12},{20,16},{24,20},{28,24},{1,29},{... | collective-permute-start | bytes 786440 | tf_op jit(solution)/shard_map/ppermute | solution.py:64
  68.1 3.6 %collective-permute-done.5 = f32[512,128]{1,0:T(8,128)S(1)} collective-permute-done((f32[512,128]{1,0:T(8,128)S(1)}, f32[512,128]{1,0:T(8,128)S(1)}, u32[]{:S(2)}, u32[]{:S(2)}) %collective-permute-start.5) | collective-permute-done | bytes 262176 | tf_op jit(solution)/shard_map/ppermute | solution.py:63
  73.1 2.7 %collective-permute-start.13 = (f32[512,128]{1,0:T(8,128)S(1)}, f32[512,128]{1,0:T(8,128)S(1)}, u32[]{:S(2)}, u32[]{:S(2)}) collective-permute-start(f32[512,128]{1,0:T(8,128)S(1)} %bitcast_add_fusion.1), channel_id=1, source_target_pairs={{0,28},{4,0},{8,4},{12,8},{16,12},{20,16},{24,20},{28,24},{1,29},{... | collective-permute-start | bytes 786440 | tf_op jit(solution)/shard_map/ppermute | solution.py:64
  75.8 4.5 %collective-permute-done.6 = f32[512,128]{1,0:T(8,128)S(1)} collective-permute-done((f32[512,128]{1,0:T(8,128)S(1)}, f32[512,128]{1,0:T(8,128)S(1)}, u32[]{:S(2)}, u32[]{:S(2)}) %collective-permute-start.6) | collective-permute-done | bytes 262176 | tf_op jit(solution)/shard_map/ppermute | solution.py:63
  82.2 5.0 %all-to-all-start = ((f32[8,128,128]{2,1,0:T(8,128)}), f32[8,128,128]{2,1,0:T(8,128)S(1)}, u32[]{:S(2)}, u32[]{:S(2)}) async-start(f32[8,128,128]{2,1,0:T(8,128)} %bitcast.20), calls=%async_computation | async-start | bytes 1048576 | tf_op jit(solution)/shard_map/all_to_all | solution.py:107
  88.1 6.6 %all-to-all-done = f32[8,128,128]{2,1,0:T(8,128)S(1)} async-done(((f32[8,128,128]{2,1,0:T(8,128)}), f32[8,128,128]{2,1,0:T(8,128)S(1)}, u32[]{:S(2)}, u32[]{:S(2)}) %all-to-all-start) | async-done | bytes 524320 | tf_op jit(solution)/shard_map/all_to_all | solution.py:107
  94.9 2.7 %collective-permute-done.14 = bf16[1,128,128]{1,2,0:T(8,128)(2,1)S(1)} collective-permute-done((bf16[1,128,128]{1,2,0:T(8,128)(2,1)S(1)}, bf16[1,128,128]{1,2,0:T(8,128)(2,1)S(1)}, u32[]{:S(2)}, u32[]{:S(2)}) %collective-permute-start.14) | collective-permute-done | bytes 32800 | tf_op jit(solution)/shard_map/ppermute | solution.py:118
  97.7 2.9 %collective-permute-start.15 = (bf16[2,128,128]{1,2,0:T(8,128)(2,1)S(1)}, bf16[2,128,128]{1,2,0:T(8,128)(2,1)S(1)}, u32[]{:S(2)}, u32[]{:S(2)}) collective-permute-start(bf16[2,128,128]{1,2,0:T(8,128)(2,1)S(1)} %maximum_select_fusion.2), channel_id=1, source_target_pairs={{0,8},{4,12},{8,0},{12,4},{16,24},{20,28},{24,16},{28,20},{1,9},{5... | collective-permute-start | bytes 196616 | tf_op jit(solution)/shard_map/ppermute | solution.py:118
  100.5 1.8 %collective-permute-done.15 = bf16[2,128,128]{1,2,0:T(8,128)(2,1)S(1)} collective-permute-done((bf16[2,128,128]{1,2,0:T(8,128)(2,1)S(1)}, bf16[2,128,128]{1,2,0:T(8,128)(2,1)S(1)}, u32[]{:S(2)}, u32[]{:S(2)}) %collective-permute-start.15) | collective-permute-done | bytes 65568 | tf_op jit(solution)/shard_map/ppermute | solution.py:118
  102.3 4.6 %collective-permute-start.16 = (bf16[4,128,128]{1,2,0:T(8,128)(2,1)S(1)}, bf16[4,128,128]{1,2,0:T(8,128)(2,1)S(1)}, u32[]{:S(2)}, u32[]{:S(2)}) collective-permute-start(bf16[4,128,128]{1,2,0:T(8,128)(2,1)S(1)} %maximum_select_fusion.1), channel_id=1, source_target_pairs={{0,16},{4,20},{8,24},{12,28},{16,0},{20,4},{24,8},{28,12},{1,17},{... | collective-permute-start | bytes 393224 | tf_op jit(solution)/shard_map/ppermute | solution.py:118
  106.8 5.0 %collective-permute-done.16 = bf16[4,128,128]{1,2,0:T(8,128)(2,1)S(1)} collective-permute-done((bf16[4,128,128]{1,2,0:T(8,128)(2,1)S(1)}, bf16[4,128,128]{1,2,0:T(8,128)(2,1)S(1)}, u32[]{:S(2)}, u32[]{:S(2)}) %collective-permute-start.16) | collective-permute-done | bytes 131104 | tf_op jit(solution)/shard_map/ppermute | solution.py:118
  112.6 19.1 %all_to_all.10 = bf16[8,8,128,128]{3,2,1,0:T(8,128)(2,1)} all-to-all(bf16[8,8,128,128]{3,2,1,0:T(8,128)(2,1)S(1)} %broadcast_in_dim.13), channel_id=1, replica_groups=mesh['ylo'=2,'x'=4,'z'=8,'yhi'=2,'core'=2] {'ylo','x'}, dimensions={0} | all-to-all | bytes 4194304 | tf_op jit(solution)/shard_map/all_to_all | solution.py:123
  131.7 8.9 %shard_map.78 = f32[8,128,128]{2,1,0:T(8,128)} custom-call(s32[1152]{0:T(1024)} %get-tuple-element.9.index_ref, bf16[64,128,128]{2,1,0:T(8,128)(2,1)} %a_ref.1, bf16[64,128,128]{2,1,0:T(8,128)(2,1)} %bitcast.72), custom_call_target="tpu_custom_call" | custom-call | tf_op jit(solution)/shard_map/pallas_call | solution.py:36
  140.6 14.7 %collective-permute-start.17 = (f32[1024,128]{1,0:T(8,128)}, f32[1024,128]{1,0:T(8,128)S(1)}, u32[]{:S(2)}, u32[]{:S(2)}) collective-permute-start(f32[1024,128]{1,0:T(8,128)} %bitcast.73), channel_id=1, source_target_pairs={{0,1},{1,0},{2,3},{3,2},{4,5},{5,4},{6,7},{7,6},{8,9},{9,8},{10,11... | collective-permute-start | bytes 1572872 | tf_op jit(solution)/shard_map/ppermute | solution.py:129
  155.3 1.7 %collective-permute-done.17 = f32[1024,128]{1,0:T(8,128)S(1)} collective-permute-done((f32[1024,128]{1,0:T(8,128)}, f32[1024,128]{1,0:T(8,128)S(1)}, u32[]{:S(2)}, u32[]{:S(2)}) %collective-permute-start.17) | collective-permute-done | bytes 524320 | tf_op jit(solution)/shard_map/ppermute | solution.py:129
  157.0 1.1 bitcast_add_fusion.15
  158.1 2.7 %collective-permute-start.18 = (f32[1024,128]{1,0:T(8,128)S(1)}, f32[1024,128]{1,0:T(8,128)S(1)}, u32[]{:S(2)}, u32[]{:S(2)}) collective-permute-start(f32[1024,128]{1,0:T(8,128)S(1)} %bitcast_add_fusion.15), channel_id=1, source_target_pairs={{0,2},{2,0},{1,3},{3,1},{4,6},{6,4},{5,7},{7,5},{8,10},{10,8},{9,1... | collective-permute-start | bytes 1572872 | tf_op jit(solution)/shard_map/ppermute | solution.py:130
  161.6 11.3 %collective-permute-done.18 = f32[1024,128]{1,0:T(8,128)S(1)} collective-permute-done((f32[1024,128]{1,0:T(8,128)S(1)}, f32[1024,128]{1,0:T(8,128)S(1)}, u32[]{:S(2)}, u32[]{:S(2)}) %collective-permute-start.18) | collective-permute-done | bytes 524320 | tf_op jit(solution)/shard_map/ppermute | solution.py:130
  (50 shorter events, 16.6 us)
Async XLA Ops:
  19.9 12.5 %collective-permute-start = (f32[512,128]{1,0:T(8,128)S(1)}, f32[512,128]{1,0:T(8,128)S(1)}, u32[]{:S(2)}, u32[]{:S(2)}) collective-permute-start(f32[512,128]{1,0:T(8,128)S(1)} %dynamic-slice_bitcast_fusion.1), channel_id=1, source_target_pairs={{0,4},{4,8},{8,12},{12,16},{16,20},{20,24},{24,28},{28,0},{1,5},{5... | collective-permute-start | bytes 786440 | tf_op jit(solution)/shard_map/ppermute | solution.py:63
  22.5 11.0 %collective-permute-start.7 = (f32[512,128]{1,0:T(8,128)S(1)}, f32[512,128]{1,0:T(8,128)S(1)}, u32[]{:S(2)}, u32[]{:S(2)}) collective-permute-start(f32[512,128]{1,0:T(8,128)S(1)} %dynamic-slice_bitcast_fusion), channel_id=1, source_target_pairs={{0,28},{4,0},{8,4},{12,8},{16,12},{20,16},{24,20},{28,24},{1,29},{... | collective-permute-start | bytes 786440 | tf_op jit(solution)/shard_map/ppermute | solution.py:64
  33.4 7.9 %collective-permute-start.1 = (f32[512,128]{1,0:T(8,128)S(1)}, f32[512,128]{1,0:T(8,128)S(1)}, u32[]{:S(2)}, u32[]{:S(2)}) collective-permute-start(f32[512,128]{1,0:T(8,128)S(1)} %bitcast_add_fusion.13), channel_id=1, source_target_pairs={{0,4},{4,8},{8,12},{12,16},{16,20},{20,24},{24,28},{28,0},{1,5},{5... | collective-permute-start | bytes 786440 | tf_op jit(solution)/shard_map/ppermute | solution.py:63
  33.5 8.8 %collective-permute-start.8 = (f32[512,128]{1,0:T(8,128)S(1)}, f32[512,128]{1,0:T(8,128)S(1)}, u32[]{:S(2)}, u32[]{:S(2)}) collective-permute-start(f32[512,128]{1,0:T(8,128)S(1)} %bitcast_add_fusion.6), channel_id=1, source_target_pairs={{0,28},{4,0},{8,4},{12,8},{16,12},{20,16},{24,20},{28,24},{1,29},{... | collective-permute-start | bytes 786440 | tf_op jit(solution)/shard_map/ppermute | solution.py:64
  42.3 7.0 %collective-permute-start.2 = (f32[512,128]{1,0:T(8,128)S(1)}, f32[512,128]{1,0:T(8,128)S(1)}, u32[]{:S(2)}, u32[]{:S(2)}) collective-permute-start(f32[512,128]{1,0:T(8,128)S(1)} %bitcast_add_fusion.12), channel_id=1, source_target_pairs={{0,4},{4,8},{8,12},{12,16},{16,20},{20,24},{24,28},{28,0},{1,5},{5... | collective-permute-start | bytes 786440 | tf_op jit(solution)/shard_map/ppermute | solution.py:63
  42.4 8.0 %collective-permute-start.9 = (f32[512,128]{1,0:T(8,128)S(1)}, f32[512,128]{1,0:T(8,128)S(1)}, u32[]{:S(2)}, u32[]{:S(2)}) collective-permute-start(f32[512,128]{1,0:T(8,128)S(1)} %bitcast_add_fusion.5), channel_id=1, source_target_pairs={{0,28},{4,0},{8,4},{12,8},{16,12},{20,16},{24,20},{28,24},{1,29},{... | collective-permute-start | bytes 786440 | tf_op jit(solution)/shard_map/ppermute | solution.py:64
  50.3 6.5 %collective-permute-start.3 = (f32[512,128]{1,0:T(8,128)S(1)}, f32[512,128]{1,0:T(8,128)S(1)}, u32[]{:S(2)}, u32[]{:S(2)}) collective-permute-start(f32[512,128]{1,0:T(8,128)S(1)} %bitcast_add_fusion.11), channel_id=1, source_target_pairs={{0,4},{4,8},{8,12},{12,16},{16,20},{20,24},{24,28},{28,0},{1,5},{5... | collective-permute-start | bytes 786440 | tf_op jit(solution)/shard_map/ppermute | solution.py:63
  50.4 7.4 %collective-permute-start.10 = (f32[512,128]{1,0:T(8,128)S(1)}, f32[512,128]{1,0:T(8,128)S(1)}, u32[]{:S(2)}, u32[]{:S(2)}) collective-permute-start(f32[512,128]{1,0:T(8,128)S(1)} %bitcast_add_fusion.4), channel_id=1, source_target_pairs={{0,28},{4,0},{8,4},{12,8},{16,12},{20,16},{24,20},{28,24},{1,29},{... | collective-permute-start | bytes 786440 | tf_op jit(solution)/shard_map/ppermute | solution.py:64
  57.8 6.5 %collective-permute-start.4 = (f32[512,128]{1,0:T(8,128)S(1)}, f32[512,128]{1,0:T(8,128)S(1)}, u32[]{:S(2)}, u32[]{:S(2)}) collective-permute-start(f32[512,128]{1,0:T(8,128)S(1)} %bitcast_add_fusion.10), channel_id=1, source_target_pairs={{0,4},{4,8},{8,12},{12,16},{16,20},{20,24},{24,28},{28,0},{1,5},{5... | collective-permute-start | bytes 786440 | tf_op jit(solution)/shard_map/ppermute | solution.py:63
  57.9 7.4 %collective-permute-start.11 = (f32[512,128]{1,0:T(8,128)S(1)}, f32[512,128]{1,0:T(8,128)S(1)}, u32[]{:S(2)}, u32[]{:S(2)}) collective-permute-start(f32[512,128]{1,0:T(8,128)S(1)} %bitcast_add_fusion.3), channel_id=1, source_target_pairs={{0,28},{4,0},{8,4},{12,8},{16,12},{20,16},{24,20},{28,24},{1,29},{... | collective-permute-start | bytes 786440 | tf_op jit(solution)/shard_map/ppermute | solution.py:64
  65.3 6.5 %collective-permute-start.5 = (f32[512,128]{1,0:T(8,128)S(1)}, f32[512,128]{1,0:T(8,128)S(1)}, u32[]{:S(2)}, u32[]{:S(2)}) collective-permute-start(f32[512,128]{1,0:T(8,128)S(1)} %bitcast_add_fusion.9), channel_id=1, source_target_pairs={{0,4},{4,8},{8,12},{12,16},{16,20},{20,24},{24,28},{28,0},{1,5},{5... | collective-permute-start | bytes 786440 | tf_op jit(solution)/shard_map/ppermute | solution.py:63
  65.4 7.6 %collective-permute-start.12 = (f32[512,128]{1,0:T(8,128)S(1)}, f32[512,128]{1,0:T(8,128)S(1)}, u32[]{:S(2)}, u32[]{:S(2)}) collective-permute-start(f32[512,128]{1,0:T(8,128)S(1)} %bitcast_add_fusion.2), channel_id=1, source_target_pairs={{0,28},{4,0},{8,4},{12,8},{16,12},{20,16},{24,20},{28,24},{1,29},{... | collective-permute-start | bytes 786440 | tf_op jit(solution)/shard_map/ppermute | solution.py:64
  72.8 7.5 %collective-permute-start.6 = (f32[512,128]{1,0:T(8,128)S(1)}, f32[512,128]{1,0:T(8,128)S(1)}, u32[]{:S(2)}, u32[]{:S(2)}) collective-permute-start(f32[512,128]{1,0:T(8,128)S(1)} %bitcast_add_fusion.8), channel_id=1, source_target_pairs={{0,4},{4,8},{8,12},{12,16},{16,20},{20,24},{24,28},{28,0},{1,5},{5... | collective-permute-start | bytes 786440 | tf_op jit(solution)/shard_map/ppermute | solution.py:63
  73.1 8.2 %collective-permute-start.13 = (f32[512,128]{1,0:T(8,128)S(1)}, f32[512,128]{1,0:T(8,128)S(1)}, u32[]{:S(2)}, u32[]{:S(2)}) collective-permute-start(f32[512,128]{1,0:T(8,128)S(1)} %bitcast_add_fusion.1), channel_id=1, source_target_pairs={{0,28},{4,0},{8,4},{12,8},{16,12},{20,16},{24,20},{28,24},{1,29},{... | collective-permute-start | bytes 786440 | tf_op jit(solution)/shard_map/ppermute | solution.py:64
  82.2 12.5 %all-to-all-start = ((f32[8,128,128]{2,1,0:T(8,128)}), f32[8,128,128]{2,1,0:T(8,128)S(1)}, u32[]{:S(2)}, u32[]{:S(2)}) async-start(f32[8,128,128]{2,1,0:T(8,128)} %bitcast.20), calls=%async_computation | async-start | bytes 1048576 | tf_op jit(solution)/shard_map/all_to_all | solution.py:107
  94.8 2.9 %collective-permute-start.14 = (bf16[1,128,128]{1,2,0:T(8,128)(2,1)S(1)}, bf16[1,128,128]{1,2,0:T(8,128)(2,1)S(1)}, u32[]{:S(2)}, u32[]{:S(2)}) collective-permute-start(bf16[1,128,128]{1,2,0:T(8,128)(2,1)S(1)} %get-tuple-element.7), channel_id=1, source_target_pairs={{0,4},{4,0},{8,12},{12,8},{16,20},{20,16},{24,28},{28,24},{1,5},{5... | collective-permute-start | bytes 98312 | tf_op jit(solution)/shard_map/ppermute | solution.py:118
  97.7 4.6 %collective-permute-start.15 = (bf16[2,128,128]{1,2,0:T(8,128)(2,1)S(1)}, bf16[2,128,128]{1,2,0:T(8,128)(2,1)S(1)}, u32[]{:S(2)}, u32[]{:S(2)}) collective-permute-start(bf16[2,128,128]{1,2,0:T(8,128)(2,1)S(1)} %maximum_select_fusion.2), channel_id=1, source_target_pairs={{0,8},{4,12},{8,0},{12,4},{16,24},{20,28},{24,16},{28,20},{1,9},{5... | collective-permute-start | bytes 196616 | tf_op jit(solution)/shard_map/ppermute | solution.py:118
  102.3 9.6 %collective-permute-start.16 = (bf16[4,128,128]{1,2,0:T(8,128)(2,1)S(1)}, bf16[4,128,128]{1,2,0:T(8,128)(2,1)S(1)}, u32[]{:S(2)}, u32[]{:S(2)}) collective-permute-start(bf16[4,128,128]{1,2,0:T(8,128)(2,1)S(1)} %maximum_select_fusion.1), channel_id=1, source_target_pairs={{0,16},{4,20},{8,24},{12,28},{16,0},{20,4},{24,8},{28,12},{1,17},{... | collective-permute-start | bytes 393224 | tf_op jit(solution)/shard_map/ppermute | solution.py:118
  131.7 41.1 %copy-start = (f32[1024,128]{1,0:T(8,128)S(1)}, f32[1024,128]{1,0:T(8,128)}, u32[]{:S(2)}) copy-start(f32[1024,128]{1,0:T(8,128)} %param.6) | copy-start | bytes 1572868
  140.6 16.5 %collective-permute-start.17 = (f32[1024,128]{1,0:T(8,128)}, f32[1024,128]{1,0:T(8,128)S(1)}, u32[]{:S(2)}, u32[]{:S(2)}) collective-permute-start(f32[1024,128]{1,0:T(8,128)} %bitcast.73), channel_id=1, source_target_pairs={{0,1},{1,0},{2,3},{3,2},{4,5},{5,4},{6,7},{7,6},{8,9},{9,8},{10,11... | collective-permute-start | bytes 1572872 | tf_op jit(solution)/shard_map/ppermute | solution.py:129
  158.1 14.7 %collective-permute-start.18 = (f32[1024,128]{1,0:T(8,128)S(1)}, f32[1024,128]{1,0:T(8,128)S(1)}, u32[]{:S(2)}, u32[]{:S(2)}) collective-permute-start(f32[1024,128]{1,0:T(8,128)S(1)} %bitcast_add_fusion.15), channel_id=1, source_target_pairs={{0,2},{2,0},{1,3},{3,1},{4,6},{6,4},{5,7},{7,5},{8,10},{10,8},{9,1... | collective-permute-start | bytes 1572872 | tf_op jit(solution)/shard_map/ppermute | solution.py:130

commit v15 on v13

--- a/solution.py
+++ b/solution.py
@@ -103,8 +103,11 @@
     partial_t = block_sums(item_index, user_tiles_t, weight_tiles, n_users)
     halves = partial_t.reshape(n_ylo, n_z, n_x * tile_rows, width)
     bl, br = ring_reduce_scatter_halves(halves[0], halves[1], "z", n_z)
-    x = jnp.concatenate([bl, br], 0).reshape(n_ylo * n_x, tile_rows, width)
-    x = lax.all_to_all(x, ("ylo", "x"), 0, 0, tiled=True)
+    low = lax.axis_index("ylo") == 0
+    keep = jnp.where(low, bl, br)
+    send = jnp.where(low, br, bl)
+    x = keep + lax.ppermute(send, "ylo", [(j, (j + 1) % n_ylo) for j in range(n_ylo)])
+    x = lax.all_to_all(x.reshape(n_x, tile_rows, width), "x", 0, 0, tiled=True)
     own_sum = x.sum(0).T
 
     position = lax.axis_index(USER_AXES)

time: 169 us -> 174 us (1.030)
  starting transfers between devices: 43.1 us -> 47.5 us
  blocking collectives: 33.9 us -> 31 us
  waiting for transfers between devices: 50.1 us -> 52.2 us
    ppermute x7, waiting for transfers between devices: 30.5 us -> 23.2 us  [ring_reduce_scatter_halves(): rl = lax.ppermute(bl, axis, right)]
    ppermute x7, waiting for transfers between devices: 0.02 us -> 7.25 us  [ring_reduce_scatter_halves(): rr = lax.ppermute(br, axis, left)]
    ppermute x7, starting transfers between devices: 20.4 us -> 25.5 us  [ring_reduce_scatter_halves(): rr = lax.ppermute(br, axis, left)]
    ppermute x0 -> x1, waiting for transfers between devices: none -> 4.2 us  [per_device(): lax.ppermute(send, 'ylo', [(j, (j + 1) % n_ylo) for j in range(n_ylo)])]
    ppermute x7, starting transfers between devices: 3.21 us -> 0.59 us  [ring_reduce_scatter_halves(): rl = lax.ppermute(bl, axis, right)]
    all_to_all x1, blocking collectives: 14.4 us -> 11.8 us  [per_device(): lax.all_to_all(jnp.broadcast_to(own_bf[None], (n_z, tile_rows, width)), '...]
    all_to_all x1, waiting for transfers between devices: 6.6 us -> 4.59 us  [per_device(): x = lax.all_to_all(x.reshape(n_x, tile_rows, width), 'x', 0, 0, tiled=True)]
    add x0 -> x1, other arithmetic: none -> 1.74 us  [per_device(): keep + lax.ppermute(send, 'ylo', [(j, (j + 1) % n_ylo) for j in range(n_y...]
  transfers between devices with their start and end apart: 17 -> 18, of which waited for: 10 -> 15; matrix products, arithmetic and copies ran while one was open for 5% -> 5% of each run, Pallas kernels for 0% -> 0%
where the time goes in v15:
time: 174 us; the launch traced here: 173 us
  waiting for transfers between devices  52.2 us (30%)
  starting transfers between devices  47.5 us (27%)
  blocking collectives  31 us (18%)
  Pallas kernels  18.5 us (11%)
  other arithmetic  14.7 us (8%)
  local copies, waits for them, and re-layouts  8.19 us (5%)
    ppermute x7, starting transfers between devices, ring_reduce_scatter_halves(): rr = lax.ppermute(br, axis, left)  25.5 us
    ppermute x7, waiting for transfers between devices, ring_reduce_scatter_halves(): rl = lax.ppermute(bl, axis, right)  23.2 us
    all_to_all x1, blocking collectives, per_device(): t = lax.all_to_all(t, ('ylo', 'x'), 0, 0, tiled=True)  19.2 us
    pallas_call x2, Pallas kernels, block_sums(): pl.pallas_call(functools.partial(block_sum_kernel, b_transposed=b_transpo...  18.5 us
    ppermute x1, starting transfers between devices, per_device(): lax.ppermute(y, 'core', [(j, (j + 1) % n_core) for j in range(n_core)])  13.2 us
    all_to_all x1, blocking collectives, per_device(): lax.all_to_all(jnp.broadcast_to(own_bf[None], (n_z, tile_rows, width)), '...  11.8 us
    ppermute x1, waiting for transfers between devices, per_device(): y = y + lax.ppermute(y, 'yhi', [(j, (j + 1) % n_yhi) for j in range(n_yhi)])  11.1 us
    ppermute x7, waiting for transfers between devices, ring_reduce_scatter_halves(): rr = lax.ppermute(br, axis, left)  7.25 us
  transfers between devices with their start and end apart: 18, of which 15 were waited for; matrix products, arithmetic and copies ran while one was open for 5% of the time, Pallas kernels for 0%

profile of v15, /device:TPU:1, one launch (start us, length us, event | category | flops | bytes accessed | tf_op | source)
XLA Modules:
  0.0 173.1 jit_solution(16913958236443562798)
XLA Ops:
  2.8 1.1 convert_element_type.6
  5.3 9.6 %shard_map.77 = f32[64,128,128]{2,1,0:T(8,128)} custom-call(s32[1152]{0:T(1024)} %get-tuple-element.8.index_ref, bf16[8,128,128]{2,1,0:T(8,128)(2,1)} %bitcast.82, bf16[64,128,128]{2,1,0:T(8,128)(2,1)} %a_ref.1), custom_call_target="tpu_custom_call" | custom-call | tf_op jit(solution)/shard_map/pallas_call | solution.py:36
  14.9 4.0 %fusion.9 = (f32[32,128,128]{2,1,0:T(8,128)S(1)}, f32[32,128,128]{2,1,0:T(8,128)}) fusion(f32[64,128,128]{2,1,0:T(8,128)} %shard_map.77), kind=kLoop, calls=%fused_computation.45 | loop fusion | bytes 8388608 | tf_op jit(solution)/shard_map/slice | solution.py:105
  19.0 6.5 %collective-permute-start.7 = (f32[512,128]{1,0:T(8,128)S(1)}, f32[512,128]{1,0:T(8,128)S(1)}, u32[]{:S(2)}, u32[]{:S(2)}) collective-permute-start(f32[512,128]{1,0:T(8,128)S(1)} %dynamic-slice_bitcast_fusion), channel_id=1, source_target_pairs={{0,28},{4,0},{8,4},{12,8},{16,12},{20,16},{24,20},{28,24},{1,29},{... | collective-permute-start | bytes 786440 | tf_op jit(solution)/shard_map/ppermute | solution.py:64
  26.5 3.9 %collective-permute-done.7 = f32[512,128]{1,0:T(8,128)S(1)} collective-permute-done((f32[512,128]{1,0:T(8,128)S(1)}, f32[512,128]{1,0:T(8,128)S(1)}, u32[]{:S(2)}, u32[]{:S(2)}) %collective-permute-start.7) | collective-permute-done | bytes 262176 | tf_op jit(solution)/shard_map/ppermute | solution.py:64
  30.4 3.5 %collective-permute-start.8 = (f32[512,128]{1,0:T(8,128)S(1)}, f32[512,128]{1,0:T(8,128)S(1)}, u32[]{:S(2)}, u32[]{:S(2)}) collective-permute-start(f32[512,128]{1,0:T(8,128)S(1)} %bitcast_add_fusion.6), channel_id=1, source_target_pairs={{0,28},{4,0},{8,4},{12,8},{16,12},{20,16},{24,20},{28,24},{1,29},{... | collective-permute-start | bytes 786440 | tf_op jit(solution)/shard_map/ppermute | solution.py:64
  35.7 2.4 %collective-permute-done.8 = f32[512,128]{1,0:T(8,128)S(1)} collective-permute-done((f32[512,128]{1,0:T(8,128)S(1)}, f32[512,128]{1,0:T(8,128)S(1)}, u32[]{:S(2)}, u32[]{:S(2)}) %collective-permute-start.8) | collective-permute-done | bytes 262176 | tf_op jit(solution)/shard_map/ppermute | solution.py:64
  38.1 3.5 %collective-permute-start.9 = (f32[512,128]{1,0:T(8,128)S(1)}, f32[512,128]{1,0:T(8,128)S(1)}, u32[]{:S(2)}, u32[]{:S(2)}) collective-permute-start(f32[512,128]{1,0:T(8,128)S(1)} %bitcast_add_fusion.5), channel_id=1, source_target_pairs={{0,28},{4,0},{8,4},{12,8},{16,12},{20,16},{24,20},{28,24},{1,29},{... | collective-permute-start | bytes 786440 | tf_op jit(solution)/shard_map/ppermute | solution.py:64
  41.6 1.3 collective-permute-done.1
  44.9 3.2 %collective-permute-start.10 = (f32[512,128]{1,0:T(8,128)S(1)}, f32[512,128]{1,0:T(8,128)S(1)}, u32[]{:S(2)}, u32[]{:S(2)}) collective-permute-start(f32[512,128]{1,0:T(8,128)S(1)} %bitcast_add_fusion.4), channel_id=1, source_target_pairs={{0,28},{4,0},{8,4},{12,8},{16,12},{20,16},{24,20},{28,24},{1,29},{... | collective-permute-start | bytes 786440 | tf_op jit(solution)/shard_map/ppermute | solution.py:64
  48.1 2.3 %collective-permute-done.2 = f32[512,128]{1,0:T(8,128)S(1)} collective-permute-done((f32[512,128]{1,0:T(8,128)S(1)}, f32[512,128]{1,0:T(8,128)S(1)}, u32[]{:S(2)}, u32[]{:S(2)}) %collective-permute-start.2) | collective-permute-done | bytes 262176 | tf_op jit(solution)/shard_map/ppermute | solution.py:63
  51.6 3.1 %collective-permute-start.11 = (f32[512,128]{1,0:T(8,128)S(1)}, f32[512,128]{1,0:T(8,128)S(1)}, u32[]{:S(2)}, u32[]{:S(2)}) collective-permute-start(f32[512,128]{1,0:T(8,128)S(1)} %bitcast_add_fusion.3), channel_id=1, source_target_pairs={{0,28},{4,0},{8,4},{12,8},{16,12},{20,16},{24,20},{28,24},{1,29},{... | collective-permute-start | bytes 786440 | tf_op jit(solution)/shard_map/ppermute | solution.py:64
  54.7 3.2 %collective-permute-done.3 = f32[512,128]{1,0:T(8,128)S(1)} collective-permute-done((f32[512,128]{1,0:T(8,128)S(1)}, f32[512,128]{1,0:T(8,128)S(1)}, u32[]{:S(2)}, u32[]{:S(2)}) %collective-permute-start.3) | collective-permute-done | bytes 262176 | tf_op jit(solution)/shard_map/ppermute | solution.py:63
  59.1 2.7 %collective-permute-start.12 = (f32[512,128]{1,0:T(8,128)S(1)}, f32[512,128]{1,0:T(8,128)S(1)}, u32[]{:S(2)}, u32[]{:S(2)}) collective-permute-start(f32[512,128]{1,0:T(8,128)S(1)} %bitcast_add_fusion.2), channel_id=1, source_target_pairs={{0,28},{4,0},{8,4},{12,8},{16,12},{20,16},{24,20},{28,24},{1,29},{... | collective-permute-start | bytes 786440 | tf_op jit(solution)/shard_map/ppermute | solution.py:64
  61.7 3.6 %collective-permute-done.4 = f32[512,128]{1,0:T(8,128)S(1)} collective-permute-done((f32[512,128]{1,0:T(8,128)S(1)}, f32[512,128]{1,0:T(8,128)S(1)}, u32[]{:S(2)}, u32[]{:S(2)}) %collective-permute-start.4) | collective-permute-done | bytes 262176 | tf_op jit(solution)/shard_map/ppermute | solution.py:63
  66.5 3.1 %collective-permute-start.13 = (f32[512,128]{1,0:T(8,128)S(1)}, f32[512,128]{1,0:T(8,128)S(1)}, u32[]{:S(2)}, u32[]{:S(2)}) collective-permute-start(f32[512,128]{1,0:T(8,128)S(1)} %bitcast_add_fusion.1), channel_id=1, source_target_pairs={{0,28},{4,0},{8,4},{12,8},{16,12},{20,16},{24,20},{28,24},{1,29},{... | collective-permute-start | bytes 786440 | tf_op jit(solution)/shard_map/ppermute | solution.py:64
  69.6 4.1 %collective-permute-done.5 = f32[512,128]{1,0:T(8,128)} collective-permute-done((f32[512,128]{1,0:T(8,128)S(1)}, f32[512,128]{1,0:T(8,128)}, u32[]{:S(2)}, u32[]{:S(2)}) %collective-permute-start.5) | collective-permute-done | bytes 262176 | tf_op jit(solution)/shard_map/ppermute | solution.py:63
  73.7 1.1 bitcast_add_fusion.8
  75.0 8.0 %collective-permute-done.6 = f32[512,128]{1,0:T(8,128)S(1)} collective-permute-done((f32[512,128]{1,0:T(8,128)S(1)}, f32[512,128]{1,0:T(8,128)S(1)}, u32[]{:S(2)}, u32[]{:S(2)}) %collective-permute-start.6) | collective-permute-done | bytes 262176 | tf_op jit(solution)/shard_map/ppermute | solution.py:63
  84.0 1.4 collective-permute-start.14
  85.4 4.2 %collective-permute-done.14 = f32[512,128]{1,0:T(8,128)S(1)} collective-permute-done((f32[512,128]{1,0:T(8,128)S(1)}, f32[512,128]{1,0:T(8,128)S(1)}, u32[]{:S(2)}, u32[]{:S(2)}) %collective-permute-start.14) | collective-permute-done | bytes 262176 | tf_op jit(solution)/shard_map/ppermute | solution.py:109
  89.6 1.7 %select_add_fusion = f32[512,128]{1,0:T(8,128)} fusion(f32[512,128]{1,0:T(8,128)S(1)} %collective-permute-done.14, pred[]{:T(512)S(6)} %eq.23, f32[512,128]{1,0:T(8,128)S(1)} %collective-permute-done.6, f32[8,512,128]{2,1,0:T(8,128)} %bitcast.79, s32[]{:T(128)S(6)} %select_n.169, f32[512,128]{1,0:T(8,128)S(1)} %collective-permute-done.13, ...), kind=kLoop, calls=%fused_computation.15 | loop fusion | flops 262144 | bytes 1572873 | tf_op jit(solution)/shard_map/add | solution.py:109
  91.4 4.0 %all-to-all-start = ((f32[4,128,128]{2,1,0:T(8,128)}), f32[4,128,128]{2,1,0:T(8,128)S(1)}, u32[]{:S(2)}, u32[]{:S(2)}) async-start(f32[4,128,128]{2,1,0:T(8,128)} %bitcast.20), calls=%async_computation | async-start | bytes 524288 | tf_op jit(solution)/shard_map/all_to_all | solution.py:110
  96.3 4.6 %all-to-all-done = f32[4,128,128]{2,1,0:T(8,128)S(1)} async-done(((f32[4,128,128]{2,1,0:T(8,128)}), f32[4,128,128]{2,1,0:T(8,128)S(1)}, u32[]{:S(2)}, u32[]{:S(2)}) %all-to-all-start) | async-done | bytes 262176 | tf_op jit(solution)/shard_map/all_to_all | solution.py:110
  101.1 11.8 %all_to_all.15 = bf16[8,128,128]{2,1,0:T(8,128)(2,1)S(1)} all-to-all(bf16[8,128,128]{2,1,0:T(8,128)(2,1)S(1)} %broadcast_in_dim.6), channel_id=1, replica_groups=mesh['ylo'=2,'x'=4,'z'=8,'yhi'=2,'core'=2] {'z'}, dimensions={0} | all-to-all | bytes 524288 | tf_op jit(solution)/shard_map/all_to_all | solution.py:117
  113.4 19.2 %all_to_all.16 = bf16[8,8,128,128]{3,2,1,0:T(8,128)(2,1)} all-to-all(bf16[8,8,128,128]{3,2,1,0:T(8,128)(2,1)S(1)} %broadcast_in_dim.7), channel_id=1, replica_groups=mesh['ylo'=2,'x'=4,'z'=8,'yhi'=2,'core'=2] {'ylo','x'}, dimensions={0} | all-to-all | bytes 4194304 | tf_op jit(solution)/shard_map/all_to_all | solution.py:119
  132.6 8.9 %shard_map.78 = f32[8,128,128]{2,1,0:T(8,128)} custom-call(s32[1152]{0:T(1024)} %get-tuple-element.9.index_ref, bf16[64,128,128]{2,1,0:T(8,128)(2,1)} %a_ref.1, bf16[64,128,128]{2,1,0:T(8,128)(2,1)} %bitcast.80), custom_call_target="tpu_custom_call" | custom-call | tf_op jit(solution)/shard_map/pallas_call | solution.py:36
  141.5 13.2 %collective-permute-start.15 = (f32[1024,128]{1,0:T(8,128)}, f32[1024,128]{1,0:T(8,128)S(1)}, u32[]{:S(2)}, u32[]{:S(2)}) collective-permute-start(f32[1024,128]{1,0:T(8,128)} %bitcast.81), channel_id=1, source_target_pairs={{0,1},{1,0},{2,3},{3,2},{4,5},{5,4},{6,7},{7,6},{8,9},{9,8},{10,11... | collective-permute-start | bytes 1572872 | tf_op jit(solution)/shard_map/ppermute | solution.py:125
  154.7 1.7 %collective-permute-done.15 = f32[1024,128]{1,0:T(8,128)S(1)} collective-permute-done((f32[1024,128]{1,0:T(8,128)}, f32[1024,128]{1,0:T(8,128)S(1)}, u32[]{:S(2)}, u32[]{:S(2)}) %collective-permute-start.15) | collective-permute-done | bytes 524320 | tf_op jit(solution)/shard_map/ppermute | solution.py:125
  156.4 1.1 bitcast_add_fusion.15
  157.5 2.8 %collective-permute-start.16 = (f32[1024,128]{1,0:T(8,128)S(1)}, f32[1024,128]{1,0:T(8,128)S(1)}, u32[]{:S(2)}, u32[]{:S(2)}) collective-permute-start(f32[1024,128]{1,0:T(8,128)S(1)} %bitcast_add_fusion.15), channel_id=1, source_target_pairs={{0,2},{2,0},{1,3},{3,1},{4,6},{6,4},{5,7},{7,5},{8,10},{10,8},{9,1... | collective-permute-start | bytes 1572872 | tf_op jit(solution)/shard_map/ppermute | solution.py:126
  161.1 11.1 %collective-permute-done.16 = f32[1024,128]{1,0:T(8,128)S(1)} collective-permute-done((f32[1024,128]{1,0:T(8,128)S(1)}, f32[1024,128]{1,0:T(8,128)S(1)}, u32[]{:S(2)}, u32[]{:S(2)}) %collective-permute-start.16) | collective-permute-done | bytes 524320 | tf_op jit(solution)/shard_map/ppermute | solution.py:126
  (44 shorter events, 16.1 us)
Async XLA Ops:
  19.0 11.5 %collective-permute-start.7 = (f32[512,128]{1,0:T(8,128)S(1)}, f32[512,128]{1,0:T(8,128)S(1)}, u32[]{:S(2)}, u32[]{:S(2)}) collective-permute-start(f32[512,128]{1,0:T(8,128)S(1)} %dynamic-slice_bitcast_fusion), channel_id=1, source_target_pairs={{0,28},{4,0},{8,4},{12,8},{16,12},{20,16},{24,20},{28,24},{1,29},{... | collective-permute-start | bytes 786440 | tf_op jit(solution)/shard_map/ppermute | solution.py:64
  26.4 8.2 %collective-permute-start = (f32[512,128]{1,0:T(8,128)S(1)}, f32[512,128]{1,0:T(8,128)S(1)}, u32[]{:S(2)}, u32[]{:S(2)}) collective-permute-start(f32[512,128]{1,0:T(8,128)S(1)} %dynamic-slice_bitcast_fusion.1), channel_id=1, source_target_pairs={{0,4},{4,8},{8,12},{12,16},{16,20},{20,24},{24,28},{28,0},{1,5},{5... | collective-permute-start | bytes 786440 | tf_op jit(solution)/shard_map/ppermute | solution.py:63
  30.4 7.6 %collective-permute-start.8 = (f32[512,128]{1,0:T(8,128)S(1)}, f32[512,128]{1,0:T(8,128)S(1)}, u32[]{:S(2)}, u32[]{:S(2)}) collective-permute-start(f32[512,128]{1,0:T(8,128)S(1)} %bitcast_add_fusion.6), channel_id=1, source_target_pairs={{0,28},{4,0},{8,4},{12,8},{16,12},{20,16},{24,20},{28,24},{1,29},{... | collective-permute-start | bytes 786440 | tf_op jit(solution)/shard_map/ppermute | solution.py:64
  35.6 7.3 %collective-permute-start.1 = (f32[512,128]{1,0:T(8,128)S(1)}, f32[512,128]{1,0:T(8,128)S(1)}, u32[]{:S(2)}, u32[]{:S(2)}) collective-permute-start(f32[512,128]{1,0:T(8,128)S(1)} %bitcast_add_fusion.13), channel_id=1, source_target_pairs={{0,4},{4,8},{8,12},{12,16},{16,20},{20,24},{24,28},{28,0},{1,5},{5... | collective-permute-start | bytes 786440 | tf_op jit(solution)/shard_map/ppermute | solution.py:63
  38.1 6.8 %collective-permute-start.9 = (f32[512,128]{1,0:T(8,128)S(1)}, f32[512,128]{1,0:T(8,128)S(1)}, u32[]{:S(2)}, u32[]{:S(2)}) collective-permute-start(f32[512,128]{1,0:T(8,128)S(1)} %bitcast_add_fusion.5), channel_id=1, source_target_pairs={{0,28},{4,0},{8,4},{12,8},{16,12},{20,16},{24,20},{28,24},{1,29},{... | collective-permute-start | bytes 786440 | tf_op jit(solution)/shard_map/ppermute | solution.py:64
  43.9 6.5 %collective-permute-start.2 = (f32[512,128]{1,0:T(8,128)S(1)}, f32[512,128]{1,0:T(8,128)S(1)}, u32[]{:S(2)}, u32[]{:S(2)}) collective-permute-start(f32[512,128]{1,0:T(8,128)S(1)} %bitcast_add_fusion.12), channel_id=1, source_target_pairs={{0,4},{4,8},{8,12},{12,16},{16,20},{20,24},{24,28},{28,0},{1,5},{5... | collective-permute-start | bytes 786440 | tf_op jit(solution)/shard_map/ppermute | solution.py:63
  44.9 6.6 %collective-permute-start.10 = (f32[512,128]{1,0:T(8,128)S(1)}, f32[512,128]{1,0:T(8,128)S(1)}, u32[]{:S(2)}, u32[]{:S(2)}) collective-permute-start(f32[512,128]{1,0:T(8,128)S(1)} %bitcast_add_fusion.4), channel_id=1, source_target_pairs={{0,28},{4,0},{8,4},{12,8},{16,12},{20,16},{24,20},{28,24},{1,29},{... | collective-permute-start | bytes 786440 | tf_op jit(solution)/shard_map/ppermute | solution.py:64
  51.4 6.5 %collective-permute-start.3 = (f32[512,128]{1,0:T(8,128)S(1)}, f32[512,128]{1,0:T(8,128)S(1)}, u32[]{:S(2)}, u32[]{:S(2)}) collective-permute-start(f32[512,128]{1,0:T(8,128)S(1)} %bitcast_add_fusion.11), channel_id=1, source_target_pairs={{0,4},{4,8},{8,12},{12,16},{16,20},{20,24},{24,28},{28,0},{1,5},{5... | collective-permute-start | bytes 786440 | tf_op jit(solution)/shard_map/ppermute | solution.py:63
  51.6 7.4 %collective-permute-start.11 = (f32[512,128]{1,0:T(8,128)S(1)}, f32[512,128]{1,0:T(8,128)S(1)}, u32[]{:S(2)}, u32[]{:S(2)}) collective-permute-start(f32[512,128]{1,0:T(8,128)S(1)} %bitcast_add_fusion.3), channel_id=1, source_target_pairs={{0,28},{4,0},{8,4},{12,8},{16,12},{20,16},{24,20},{28,24},{1,29},{... | collective-permute-start | bytes 786440 | tf_op jit(solution)/shard_map/ppermute | solution.py:64
  58.9 6.5 %collective-permute-start.4 = (f32[512,128]{1,0:T(8,128)S(1)}, f32[512,128]{1,0:T(8,128)S(1)}, u32[]{:S(2)}, u32[]{:S(2)}) collective-permute-start(f32[512,128]{1,0:T(8,128)S(1)} %bitcast_add_fusion.10), channel_id=1, source_target_pairs={{0,4},{4,8},{8,12},{12,16},{16,20},{20,24},{24,28},{28,0},{1,5},{5... | collective-permute-start | bytes 786440 | tf_op jit(solution)/shard_map/ppermute | solution.py:63
  59.1 7.4 %collective-permute-start.12 = (f32[512,128]{1,0:T(8,128)S(1)}, f32[512,128]{1,0:T(8,128)S(1)}, u32[]{:S(2)}, u32[]{:S(2)}) collective-permute-start(f32[512,128]{1,0:T(8,128)S(1)} %bitcast_add_fusion.2), channel_id=1, source_target_pairs={{0,28},{4,0},{8,4},{12,8},{16,12},{20,16},{24,20},{28,24},{1,29},{... | collective-permute-start | bytes 786440 | tf_op jit(solution)/shard_map/ppermute | solution.py:64
  66.4 7.4 %collective-permute-start.5 = (f32[512,128]{1,0:T(8,128)S(1)}, f32[512,128]{1,0:T(8,128)}, u32[]{:S(2)}, u32[]{:S(2)}) collective-permute-start(f32[512,128]{1,0:T(8,128)S(1)} %bitcast_add_fusion.9), channel_id=1, source_target_pairs={{0,4},{4,8},{8,12},{12,16},{16,20},{20,24},{24,28},{28,0},{1,5},{5... | collective-permute-start | bytes 786440 | tf_op jit(solution)/shard_map/ppermute | solution.py:63
  66.5 8.5 %collective-permute-start.13 = (f32[512,128]{1,0:T(8,128)S(1)}, f32[512,128]{1,0:T(8,128)S(1)}, u32[]{:S(2)}, u32[]{:S(2)}) collective-permute-start(f32[512,128]{1,0:T(8,128)S(1)} %bitcast_add_fusion.1), channel_id=1, source_target_pairs={{0,28},{4,0},{8,4},{12,8},{16,12},{20,16},{24,20},{28,24},{1,29},{... | collective-permute-start | bytes 786440 | tf_op jit(solution)/shard_map/ppermute | solution.py:64
  74.8 8.2 %collective-permute-start.6 = (f32[512,128]{1,0:T(8,128)S(1)}, f32[512,128]{1,0:T(8,128)S(1)}, u32[]{:S(2)}, u32[]{:S(2)}) collective-permute-start(f32[512,128]{1,0:T(8,128)S(1)} %bitcast_add_fusion.8), channel_id=1, source_target_pairs={{0,4},{4,8},{8,12},{12,16},{16,20},{20,24},{24,28},{28,0},{1,5},{5... | collective-permute-start | bytes 786440 | tf_op jit(solution)/shard_map/ppermute | solution.py:63
  84.0 5.6 %collective-permute-start.14 = (f32[512,128]{1,0:T(8,128)S(1)}, f32[512,128]{1,0:T(8,128)S(1)}, u32[]{:S(2)}, u32[]{:S(2)}) collective-permute-start(f32[512,128]{1,0:T(8,128)S(1)} %broadcast_select_fusion), channel_id=1, source_target_pairs={{0,128},{128,0},{1,129},{129,1},{2,130},{130,2},{3,131},{131,3},{4... | collective-permute-start | bytes 786440 | tf_op jit(solution)/shard_map/ppermute | solution.py:109
  91.4 9.5 %all-to-all-start = ((f32[4,128,128]{2,1,0:T(8,128)}), f32[4,128,128]{2,1,0:T(8,128)S(1)}, u32[]{:S(2)}, u32[]{:S(2)}) async-start(f32[4,128,128]{2,1,0:T(8,128)} %bitcast.20), calls=%async_computation | async-start | bytes 524288 | tf_op jit(solution)/shard_map/all_to_all | solution.py:110
  132.6 39.6 %copy-start = (f32[1024,128]{1,0:T(8,128)S(1)}, f32[1024,128]{1,0:T(8,128)}, u32[]{:S(2)}) copy-start(f32[1024,128]{1,0:T(8,128)} %param.6) | copy-start | bytes 1572868
  141.5 14.9 %collective-permute-start.15 = (f32[1024,128]{1,0:T(8,128)}, f32[1024,128]{1,0:T(8,128)S(1)}, u32[]{:S(2)}, u32[]{:S(2)}) collective-permute-start(f32[1024,128]{1,0:T(8,128)} %bitcast.81), channel_id=1, source_target_pairs={{0,1},{1,0},{2,3},{3,2},{4,5},{5,4},{6,7},{7,6},{8,9},{9,8},{10,11... | collective-permute-start | bytes 1572872 | tf_op jit(solution)/shard_map/ppermute | solution.py:125
  157.5 14.7 %collective-permute-start.16 = (f32[1024,128]{1,0:T(8,128)S(1)}, f32[1024,128]{1,0:T(8,128)S(1)}, u32[]{:S(2)}, u32[]{:S(2)}) collective-permute-start(f32[1024,128]{1,0:T(8,128)S(1)} %bitcast_add_fusion.15), channel_id=1, source_target_pairs={{0,2},{2,0},{1,3},{3,1},{4,6},{6,4},{5,7},{7,5},{8,10},{10,8},{9,1... | collective-permute-start | bytes 1572872 | tf_op jit(solution)/shard_map/ppermute | solution.py:126

commit v16 on v13

--- a/solution.py
+++ b/solution.py
@@ -25,7 +25,7 @@
         )
         return carry
 
-    lax.fori_loop(0, n_blocks, body, 0, unroll=64)
+    lax.fori_loop(0, n_blocks, body, 0, unroll=128)
 
 
 def block_sums(index, a_tiles, b_tiles, n_out, b_transposed=False):

time: 169 us -> 169 us (level)
  no operation moved by 1% of the time
where the time goes in v16:
time: 169 us; the launch traced here: 168 us
  waiting for transfers between devices  50.1 us (30%)
  starting transfers between devices  43.1 us (26%)
  blocking collectives  33.9 us (20%)
  Pallas kernels  17.8 us (11%)
  other arithmetic  13.7 us (8%)
  local copies, waits for them, and re-layouts  8.2 us (5%)
    ppermute x7, waiting for transfers between devices, ring_reduce_scatter_halves(): rl = lax.ppermute(bl, axis, right)  30.5 us
    ppermute x7, starting transfers between devices, ring_reduce_scatter_halves(): rr = lax.ppermute(br, axis, left)  20.6 us
    all_to_all x1, blocking collectives, per_device(): t = lax.all_to_all(t, ('ylo', 'x'), 0, 0, tiled=True)  19.5 us
    pallas_call x2, Pallas kernels, block_sums(): pl.pallas_call(functools.partial(block_sum_kernel, b_transposed=b_transpo...  17.8 us
    all_to_all x1, blocking collectives, per_device(): lax.all_to_all(jnp.broadcast_to(own_bf[None], (n_z, tile_rows, width)), '...  14.4 us
    ppermute x1, starting transfers between devices, per_device(): lax.ppermute(y, 'core', [(j, (j + 1) % n_core) for j in range(n_core)])  11.7 us
    ppermute x1, waiting for transfers between devices, per_device(): y = y + lax.ppermute(y, 'yhi', [(j, (j + 1) % n_yhi) for j in range(n_yhi)])  11.3 us
    add x7, other arithmetic, ring_reduce_scatter_halves(): bl = rl + lax.dynamic_index_in_dim(xl, (i - s - 2) % n, 0, keepdims=False)  6.85 us
  transfers between devices with their start and end apart: 17, of which 10 were waited for; matrix products, arithmetic and copies ran while one was open for 5% of the time, Pallas kernels for 0%

profile of v16, /device:TPU:1, one launch (start us, length us, event | category | flops | bytes accessed | tf_op | source)
XLA Modules:
  0.0 167.8 jit_solution(16188511516459727722)
XLA Ops:
  2.8 1.1 convert_element_type.6
  5.3 9.3 %shard_map.77 = f32[64,128,128]{2,1,0:T(8,128)} custom-call(s32[1152]{0:T(1024)} %get-tuple-element.8.index_ref, bf16[8,128,128]{2,1,0:T(8,128)(2,1)} %bitcast.72, bf16[64,128,128]{2,1,0:T(8,128)(2,1)} %a_ref.1), custom_call_target="tpu_custom_call" | custom-call | tf_op jit(solution)/shard_map/pallas_call | solution.py:36
  14.6 4.0 %fusion.9 = (f32[32,128,128]{2,1,0:T(8,128)}, f32[32,128,128]{2,1,0:T(8,128)S(1)}) fusion(f32[64,128,128]{2,1,0:T(8,128)} %shard_map.77), kind=kLoop, calls=%fused_computation.44 | loop fusion | bytes 8388608 | tf_op jit(solution)/shard_map/slice | solution.py:105
  19.6 2.5 %collective-permute-start = (f32[512,128]{1,0:T(8,128)S(1)}, f32[512,128]{1,0:T(8,128)S(1)}, u32[]{:S(2)}, u32[]{:S(2)}) collective-permute-start(f32[512,128]{1,0:T(8,128)S(1)} %dynamic-slice_bitcast_fusion.1), channel_id=1, source_target_pairs={{0,4},{4,8},{8,12},{12,16},{16,20},{20,24},{24,28},{28,0},{1,5},{5... | collective-permute-start | bytes 786440 | tf_op jit(solution)/shard_map/ppermute | solution.py:63
  22.1 4.1 %collective-permute-start.7 = (f32[512,128]{1,0:T(8,128)S(1)}, f32[512,128]{1,0:T(8,128)S(1)}, u32[]{:S(2)}, u32[]{:S(2)}) collective-permute-start(f32[512,128]{1,0:T(8,128)S(1)} %dynamic-slice_bitcast_fusion), channel_id=1, source_target_pairs={{0,28},{4,0},{8,4},{12,8},{16,12},{20,16},{24,20},{28,24},{1,29},{... | collective-permute-start | bytes 786440 | tf_op jit(solution)/shard_map/ppermute | solution.py:64
  26.2 5.9 %collective-permute-done = f32[512,128]{1,0:T(8,128)S(1)} collective-permute-done((f32[512,128]{1,0:T(8,128)S(1)}, f32[512,128]{1,0:T(8,128)S(1)}, u32[]{:S(2)}, u32[]{:S(2)}) %collective-permute-start) | collective-permute-done | bytes 262176 | tf_op jit(solution)/shard_map/ppermute | solution.py:63
  32.1 1.0 bitcast_add_fusion.13
  33.2 2.7 %collective-permute-start.8 = (f32[512,128]{1,0:T(8,128)S(1)}, f32[512,128]{1,0:T(8,128)S(1)}, u32[]{:S(2)}, u32[]{:S(2)}) collective-permute-start(f32[512,128]{1,0:T(8,128)S(1)} %bitcast_add_fusion.6), channel_id=1, source_target_pairs={{0,28},{4,0},{8,4},{12,8},{16,12},{20,16},{24,20},{28,24},{1,29},{... | collective-permute-start | bytes 786440 | tf_op jit(solution)/shard_map/ppermute | solution.py:64
  35.9 5.0 %collective-permute-done.1 = f32[512,128]{1,0:T(8,128)S(1)} collective-permute-done((f32[512,128]{1,0:T(8,128)S(1)}, f32[512,128]{1,0:T(8,128)S(1)}, u32[]{:S(2)}, u32[]{:S(2)}) %collective-permute-start.1) | collective-permute-done | bytes 262176 | tf_op jit(solution)/shard_map/ppermute | solution.py:63
  40.9 1.0 bitcast_add_fusion.12
  42.1 2.7 %collective-permute-start.9 = (f32[512,128]{1,0:T(8,128)S(1)}, f32[512,128]{1,0:T(8,128)S(1)}, u32[]{:S(2)}, u32[]{:S(2)}) collective-permute-start(f32[512,128]{1,0:T(8,128)S(1)} %bitcast_add_fusion.5), channel_id=1, source_target_pairs={{0,28},{4,0},{8,4},{12,8},{16,12},{20,16},{24,20},{28,24},{1,29},{... | collective-permute-start | bytes 786440 | tf_op jit(solution)/shard_map/ppermute | solution.py:64
  44.8 4.2 %collective-permute-done.2 = f32[512,128]{1,0:T(8,128)S(1)} collective-permute-done((f32[512,128]{1,0:T(8,128)S(1)}, f32[512,128]{1,0:T(8,128)S(1)}, u32[]{:S(2)}, u32[]{:S(2)}) %collective-permute-start.2) | collective-permute-done | bytes 262176 | tf_op jit(solution)/shard_map/ppermute | solution.py:63
  49.0 1.0 bitcast_add_fusion.11
  50.1 2.7 %collective-permute-start.10 = (f32[512,128]{1,0:T(8,128)S(1)}, f32[512,128]{1,0:T(8,128)S(1)}, u32[]{:S(2)}, u32[]{:S(2)}) collective-permute-start(f32[512,128]{1,0:T(8,128)S(1)} %bitcast_add_fusion.4), channel_id=1, source_target_pairs={{0,28},{4,0},{8,4},{12,8},{16,12},{20,16},{24,20},{28,24},{1,29},{... | collective-permute-start | bytes 786440 | tf_op jit(solution)/shard_map/ppermute | solution.py:64
  52.8 3.6 %collective-permute-done.3 = f32[512,128]{1,0:T(8,128)S(1)} collective-permute-done((f32[512,128]{1,0:T(8,128)S(1)}, f32[512,128]{1,0:T(8,128)S(1)}, u32[]{:S(2)}, u32[]{:S(2)}) %collective-permute-start.3) | collective-permute-done | bytes 262176 | tf_op jit(solution)/shard_map/ppermute | solution.py:63
  57.6 2.7 %collective-permute-start.11 = (f32[512,128]{1,0:T(8,128)S(1)}, f32[512,128]{1,0:T(8,128)S(1)}, u32[]{:S(2)}, u32[]{:S(2)}) collective-permute-start(f32[512,128]{1,0:T(8,128)S(1)} %bitcast_add_fusion.3), channel_id=1, source_target_pairs={{0,28},{4,0},{8,4},{12,8},{16,12},{20,16},{24,20},{28,24},{1,29},{... | collective-permute-start | bytes 786440 | tf_op jit(solution)/shard_map/ppermute | solution.py:64
  60.3 3.6 %collective-permute-done.4 = f32[512,128]{1,0:T(8,128)S(1)} collective-permute-done((f32[512,128]{1,0:T(8,128)S(1)}, f32[512,128]{1,0:T(8,128)S(1)}, u32[]{:S(2)}, u32[]{:S(2)}) %collective-permute-start.4) | collective-permute-done | bytes 262176 | tf_op jit(solution)/shard_map/ppermute | solution.py:63
  65.1 2.9 %collective-permute-start.12 = (f32[512,128]{1,0:T(8,128)S(1)}, f32[512,128]{1,0:T(8,128)S(1)}, u32[]{:S(2)}, u32[]{:S(2)}) collective-permute-start(f32[512,128]{1,0:T(8,128)S(1)} %bitcast_add_fusion.2), channel_id=1, source_target_pairs={{0,28},{4,0},{8,4},{12,8},{16,12},{20,16},{24,20},{28,24},{1,29},{... | collective-permute-start | bytes 786440 | tf_op jit(solution)/shard_map/ppermute | solution.py:64
  68.0 3.5 %collective-permute-done.5 = f32[512,128]{1,0:T(8,128)S(1)} collective-permute-done((f32[512,128]{1,0:T(8,128)S(1)}, f32[512,128]{1,0:T(8,128)S(1)}, u32[]{:S(2)}, u32[]{:S(2)}) %collective-permute-start.5) | collective-permute-done | bytes 262176 | tf_op jit(solution)/shard_map/ppermute | solution.py:63
  71.4 1.0 bitcast_add_fusion.8
  72.6 2.7 %collective-permute-start.13 = (f32[512,128]{1,0:T(8,128)S(1)}, f32[512,128]{1,0:T(8,128)S(1)}, u32[]{:S(2)}, u32[]{:S(2)}) collective-permute-start(f32[512,128]{1,0:T(8,128)S(1)} %bitcast_add_fusion.1), channel_id=1, source_target_pairs={{0,28},{4,0},{8,4},{12,8},{16,12},{20,16},{24,20},{28,24},{1,29},{... | collective-permute-start | bytes 786440 | tf_op jit(solution)/shard_map/ppermute | solution.py:64
  75.3 4.7 %collective-permute-done.6 = f32[512,128]{1,0:T(8,128)S(1)} collective-permute-done((f32[512,128]{1,0:T(8,128)S(1)}, f32[512,128]{1,0:T(8,128)S(1)}, u32[]{:S(2)}, u32[]{:S(2)}) %collective-permute-start.6) | collective-permute-done | bytes 262176 | tf_op jit(solution)/shard_map/ppermute | solution.py:63
  81.8 5.0 %all-to-all-start = ((f32[8,128,128]{2,1,0:T(8,128)}), f32[8,128,128]{2,1,0:T(8,128)S(1)}, u32[]{:S(2)}, u32[]{:S(2)}) async-start(f32[8,128,128]{2,1,0:T(8,128)} %bitcast.20), calls=%async_computation | async-start | bytes 1048576 | tf_op jit(solution)/shard_map/all_to_all | solution.py:107
  87.8 6.6 %all-to-all-done = f32[8,128,128]{2,1,0:T(8,128)S(1)} async-done(((f32[8,128,128]{2,1,0:T(8,128)}), f32[8,128,128]{2,1,0:T(8,128)S(1)}, u32[]{:S(2)}, u32[]{:S(2)}) %all-to-all-start) | async-done | bytes 524320 | tf_op jit(solution)/shard_map/all_to_all | solution.py:107
  94.6 14.4 %all_to_all.15 = bf16[8,128,128]{2,1,0:T(8,128)(2,1)S(1)} all-to-all(bf16[8,128,128]{2,1,0:T(8,128)(2,1)S(1)} %broadcast_in_dim.6), channel_id=1, replica_groups=mesh['ylo'=2,'x'=4,'z'=8,'yhi'=2,'core'=2] {'z'}, dimensions={0} | all-to-all | bytes 524288 | tf_op jit(solution)/shard_map/all_to_all | solution.py:114
  109.5 19.5 %all_to_all.16 = bf16[8,8,128,128]{3,2,1,0:T(8,128)(2,1)} all-to-all(bf16[8,8,128,128]{3,2,1,0:T(8,128)(2,1)S(1)} %broadcast_in_dim.7), channel_id=1, replica_groups=mesh['ylo'=2,'x'=4,'z'=8,'yhi'=2,'core'=2] {'ylo','x'}, dimensions={0} | all-to-all | bytes 4194304 | tf_op jit(solution)/shard_map/all_to_all | solution.py:116
  129.1 8.6 %shard_map.78 = f32[8,128,128]{2,1,0:T(8,128)} custom-call(s32[1152]{0:T(1024)} %get-tuple-element.9.index_ref, bf16[64,128,128]{2,1,0:T(8,128)(2,1)} %a_ref.1, bf16[64,128,128]{2,1,0:T(8,128)(2,1)} %bitcast.70), custom_call_target="tpu_custom_call" | custom-call | tf_op jit(solution)/shard_map/pallas_call | solution.py:36
  137.6 11.7 %collective-permute-start.14 = (f32[1024,128]{1,0:T(8,128)}, f32[1024,128]{1,0:T(8,128)S(1)}, u32[]{:S(2)}, u32[]{:S(2)}) collective-permute-start(f32[1024,128]{1,0:T(8,128)} %bitcast.71), channel_id=1, source_target_pairs={{0,1},{1,0},{2,3},{3,2},{4,5},{5,4},{6,7},{7,6},{8,9},{9,8},{10,11... | collective-permute-start | bytes 1572872 | tf_op jit(solution)/shard_map/ppermute | solution.py:122
  149.3 1.7 %collective-permute-done.14 = f32[1024,128]{1,0:T(8,128)S(1)} collective-permute-done((f32[1024,128]{1,0:T(8,128)}, f32[1024,128]{1,0:T(8,128)S(1)}, u32[]{:S(2)}, u32[]{:S(2)}) %collective-permute-start.14) | collective-permute-done | bytes 524320 | tf_op jit(solution)/shard_map/ppermute | solution.py:122
  151.1 1.1 bitcast_add_fusion.15
  152.2 2.7 %collective-permute-start.15 = (f32[1024,128]{1,0:T(8,128)S(1)}, f32[1024,128]{1,0:T(8,128)S(1)}, u32[]{:S(2)}, u32[]{:S(2)}) collective-permute-start(f32[1024,128]{1,0:T(8,128)S(1)} %bitcast_add_fusion.15), channel_id=1, source_target_pairs={{0,2},{2,0},{1,3},{3,1},{4,6},{6,4},{5,7},{7,5},{8,10},{10,8},{9,1... | collective-permute-start | bytes 1572872 | tf_op jit(solution)/shard_map/ppermute | solution.py:123
  155.6 11.3 %collective-permute-done.15 = f32[1024,128]{1,0:T(8,128)S(1)} collective-permute-done((f32[1024,128]{1,0:T(8,128)S(1)}, f32[1024,128]{1,0:T(8,128)S(1)}, u32[]{:S(2)}, u32[]{:S(2)}) %collective-permute-start.15) | collective-permute-done | bytes 524320 | tf_op jit(solution)/shard_map/ppermute | solution.py:123
  (43 shorter events, 12.3 us)
Async XLA Ops:
  19.6 12.5 %collective-permute-start = (f32[512,128]{1,0:T(8,128)S(1)}, f32[512,128]{1,0:T(8,128)S(1)}, u32[]{:S(2)}, u32[]{:S(2)}) collective-permute-start(f32[512,128]{1,0:T(8,128)S(1)} %dynamic-slice_bitcast_fusion.1), channel_id=1, source_target_pairs={{0,4},{4,8},{8,12},{12,16},{16,20},{20,24},{24,28},{28,0},{1,5},{5... | collective-permute-start | bytes 786440 | tf_op jit(solution)/shard_map/ppermute | solution.py:63
  22.1 11.0 %collective-permute-start.7 = (f32[512,128]{1,0:T(8,128)S(1)}, f32[512,128]{1,0:T(8,128)S(1)}, u32[]{:S(2)}, u32[]{:S(2)}) collective-permute-start(f32[512,128]{1,0:T(8,128)S(1)} %dynamic-slice_bitcast_fusion), channel_id=1, source_target_pairs={{0,28},{4,0},{8,4},{12,8},{16,12},{20,16},{24,20},{28,24},{1,29},{... | collective-permute-start | bytes 786440 | tf_op jit(solution)/shard_map/ppermute | solution.py:64
  33.0 7.9 %collective-permute-start.1 = (f32[512,128]{1,0:T(8,128)S(1)}, f32[512,128]{1,0:T(8,128)S(1)}, u32[]{:S(2)}, u32[]{:S(2)}) collective-permute-start(f32[512,128]{1,0:T(8,128)S(1)} %bitcast_add_fusion.13), channel_id=1, source_target_pairs={{0,4},{4,8},{8,12},{12,16},{16,20},{20,24},{24,28},{28,0},{1,5},{5... | collective-permute-start | bytes 786440 | tf_op jit(solution)/shard_map/ppermute | solution.py:63
  33.2 8.8 %collective-permute-start.8 = (f32[512,128]{1,0:T(8,128)S(1)}, f32[512,128]{1,0:T(8,128)S(1)}, u32[]{:S(2)}, u32[]{:S(2)}) collective-permute-start(f32[512,128]{1,0:T(8,128)S(1)} %bitcast_add_fusion.6), channel_id=1, source_target_pairs={{0,28},{4,0},{8,4},{12,8},{16,12},{20,16},{24,20},{28,24},{1,29},{... | collective-permute-start | bytes 786440 | tf_op jit(solution)/shard_map/ppermute | solution.py:64
  41.9 7.0 %collective-permute-start.2 = (f32[512,128]{1,0:T(8,128)S(1)}, f32[512,128]{1,0:T(8,128)S(1)}, u32[]{:S(2)}, u32[]{:S(2)}) collective-permute-start(f32[512,128]{1,0:T(8,128)S(1)} %bitcast_add_fusion.12), channel_id=1, source_target_pairs={{0,4},{4,8},{8,12},{12,16},{16,20},{20,24},{24,28},{28,0},{1,5},{5... | collective-permute-start | bytes 786440 | tf_op jit(solution)/shard_map/ppermute | solution.py:63
  42.1 8.0 %collective-permute-start.9 = (f32[512,128]{1,0:T(8,128)S(1)}, f32[512,128]{1,0:T(8,128)S(1)}, u32[]{:S(2)}, u32[]{:S(2)}) collective-permute-start(f32[512,128]{1,0:T(8,128)S(1)} %bitcast_add_fusion.5), channel_id=1, source_target_pairs={{0,28},{4,0},{8,4},{12,8},{16,12},{20,16},{24,20},{28,24},{1,29},{... | collective-permute-start | bytes 786440 | tf_op jit(solution)/shard_map/ppermute | solution.py:64
  49.9 6.5 %collective-permute-start.3 = (f32[512,128]{1,0:T(8,128)S(1)}, f32[512,128]{1,0:T(8,128)S(1)}, u32[]{:S(2)}, u32[]{:S(2)}) collective-permute-start(f32[512,128]{1,0:T(8,128)S(1)} %bitcast_add_fusion.11), channel_id=1, source_target_pairs={{0,4},{4,8},{8,12},{12,16},{16,20},{20,24},{24,28},{28,0},{1,5},{5... | collective-permute-start | bytes 786440 | tf_op jit(solution)/shard_map/ppermute | solution.py:63
  50.1 7.4 %collective-permute-start.10 = (f32[512,128]{1,0:T(8,128)S(1)}, f32[512,128]{1,0:T(8,128)S(1)}, u32[]{:S(2)}, u32[]{:S(2)}) collective-permute-start(f32[512,128]{1,0:T(8,128)S(1)} %bitcast_add_fusion.4), channel_id=1, source_target_pairs={{0,28},{4,0},{8,4},{12,8},{16,12},{20,16},{24,20},{28,24},{1,29},{... | collective-permute-start | bytes 786440 | tf_op jit(solution)/shard_map/ppermute | solution.py:64
  57.4 6.5 %collective-permute-start.4 = (f32[512,128]{1,0:T(8,128)S(1)}, f32[512,128]{1,0:T(8,128)S(1)}, u32[]{:S(2)}, u32[]{:S(2)}) collective-permute-start(f32[512,128]{1,0:T(8,128)S(1)} %bitcast_add_fusion.10), channel_id=1, source_target_pairs={{0,4},{4,8},{8,12},{12,16},{16,20},{20,24},{24,28},{28,0},{1,5},{5... | collective-permute-start | bytes 786440 | tf_op jit(solution)/shard_map/ppermute | solution.py:63
  57.6 7.4 %collective-permute-start.11 = (f32[512,128]{1,0:T(8,128)S(1)}, f32[512,128]{1,0:T(8,128)S(1)}, u32[]{:S(2)}, u32[]{:S(2)}) collective-permute-start(f32[512,128]{1,0:T(8,128)S(1)} %bitcast_add_fusion.3), channel_id=1, source_target_pairs={{0,28},{4,0},{8,4},{12,8},{16,12},{20,16},{24,20},{28,24},{1,29},{... | collective-permute-start | bytes 786440 | tf_op jit(solution)/shard_map/ppermute | solution.py:64
  64.9 6.5 %collective-permute-start.5 = (f32[512,128]{1,0:T(8,128)S(1)}, f32[512,128]{1,0:T(8,128)S(1)}, u32[]{:S(2)}, u32[]{:S(2)}) collective-permute-start(f32[512,128]{1,0:T(8,128)S(1)} %bitcast_add_fusion.9), channel_id=1, source_target_pairs={{0,4},{4,8},{8,12},{12,16},{16,20},{20,24},{24,28},{28,0},{1,5},{5... | collective-permute-start | bytes 786440 | tf_op jit(solution)/shard_map/ppermute | solution.py:63
  65.1 7.4 %collective-permute-start.12 = (f32[512,128]{1,0:T(8,128)S(1)}, f32[512,128]{1,0:T(8,128)S(1)}, u32[]{:S(2)}, u32[]{:S(2)}) collective-permute-start(f32[512,128]{1,0:T(8,128)S(1)} %bitcast_add_fusion.2), channel_id=1, source_target_pairs={{0,28},{4,0},{8,4},{12,8},{16,12},{20,16},{24,20},{28,24},{1,29},{... | collective-permute-start | bytes 786440 | tf_op jit(solution)/shard_map/ppermute | solution.py:64
  72.4 7.6 %collective-permute-start.6 = (f32[512,128]{1,0:T(8,128)S(1)}, f32[512,128]{1,0:T(8,128)S(1)}, u32[]{:S(2)}, u32[]{:S(2)}) collective-permute-start(f32[512,128]{1,0:T(8,128)S(1)} %bitcast_add_fusion.8), channel_id=1, source_target_pairs={{0,4},{4,8},{8,12},{12,16},{16,20},{20,24},{24,28},{28,0},{1,5},{5... | collective-permute-start | bytes 786440 | tf_op jit(solution)/shard_map/ppermute | solution.py:63
  72.6 8.4 %collective-permute-start.13 = (f32[512,128]{1,0:T(8,128)S(1)}, f32[512,128]{1,0:T(8,128)S(1)}, u32[]{:S(2)}, u32[]{:S(2)}) collective-permute-start(f32[512,128]{1,0:T(8,128)S(1)} %bitcast_add_fusion.1), channel_id=1, source_target_pairs={{0,28},{4,0},{8,4},{12,8},{16,12},{20,16},{24,20},{28,24},{1,29},{... | collective-permute-start | bytes 786440 | tf_op jit(solution)/shard_map/ppermute | solution.py:64
  81.8 12.6 %all-to-all-start = ((f32[8,128,128]{2,1,0:T(8,128)}), f32[8,128,128]{2,1,0:T(8,128)S(1)}, u32[]{:S(2)}, u32[]{:S(2)}) async-start(f32[8,128,128]{2,1,0:T(8,128)} %bitcast.20), calls=%async_computation | async-start | bytes 1048576 | tf_op jit(solution)/shard_map/all_to_all | solution.py:107
  129.1 37.8 %copy-start = (f32[1024,128]{1,0:T(8,128)S(1)}, f32[1024,128]{1,0:T(8,128)}, u32[]{:S(2)}) copy-start(f32[1024,128]{1,0:T(8,128)} %param.6) | copy-start | bytes 1572868
  137.6 13.5 %collective-permute-start.14 = (f32[1024,128]{1,0:T(8,128)}, f32[1024,128]{1,0:T(8,128)S(1)}, u32[]{:S(2)}, u32[]{:S(2)}) collective-permute-start(f32[1024,128]{1,0:T(8,128)} %bitcast.71), channel_id=1, source_target_pairs={{0,1},{1,0},{2,3},{3,2},{4,5},{5,4},{6,7},{7,6},{8,9},{9,8},{10,11... | collective-permute-start | bytes 1572872 | tf_op jit(solution)/shard_map/ppermute | solution.py:122
  152.2 14.7 %collective-permute-start.15 = (f32[1024,128]{1,0:T(8,128)S(1)}, f32[1024,128]{1,0:T(8,128)S(1)}, u32[]{:S(2)}, u32[]{:S(2)}) collective-permute-start(f32[1024,128]{1,0:T(8,128)S(1)} %bitcast_add_fusion.15), channel_id=1, source_target_pairs={{0,2},{2,0},{1,3},{3,1},{4,6},{6,4},{5,7},{7,5},{8,10},{10,8},{9,1... | collective-permute-start | bytes 1572872 | tf_op jit(solution)/shard_map/ppermute | solution.py:123
